TPU v7x, 32 devices: a whole 2x2x4 slice. The times are simulated.
32 devices in a mesh: band: 4 (over z), gy: 2 (over x), gz: 4 (over y, core).
Axes of the slice: x: 2, y: 2, z: 4, core: 2. Of those that a mesh axis runs over, the one named last changes fastest.
Arguments:
- i_coeff: float32 [4, 96, 96, 96], P('band', 'gy', 'gz'), may hold values from -6 to 6
- j_coeff: float32 [8, 96, 96, 96], P('band', 'gy', 'gz'), may hold values from -6 to 6
- pair_orbital: int32 [4, 1], P('band'), may hold values from 0 to 7
- pair_occ: int32 [4, 1], P('band'), may hold values from 1 to 2
Outputs:
- exchange_applied: float32 [4, 96, 96, 96], P('band', 'gy', 'gz')
- pair_energy: float32 [4, 1], P('band')
All inputs are finite; a program needn't handle non-finite values.
Results may differ from a plain program's by a relative error of at most 0.00022.
Values sent between devices are 32-bit elements; how exact they have to be, the bound alone decides.
No kernel may reach another device: no remote copies, remote signals or barrier semaphores. Data moves between devices by JAX's collectives and lax.ppermute only.
A program may use at most 64 MiB of HBM per device.

v0:
```python
import math

import jax
import jax.numpy as jnp
import numpy as np
from jax import lax
from jax.sharding import PartitionSpec as P

tap_offsets = np.arange(-8, 8)
raw_taps = 0.6 ** np.abs(tap_offsets + 0.5) * np.where(tap_offsets % 2 == 0, 1.0, -0.6)
FILTER_TAPS = raw_taps / np.sqrt(np.sum(raw_taps**2))
SCREEN = 0.001
precise_mode = lax.Precision.HIGHEST
fast_mode = lax.Precision.HIGH


def extended(cells, sides, width):
    for axis, dim in sides:
        count = lax.axis_size(axis)
        ends = count - 1
        head = lax.slice_in_dim(cells, 0, width, axis=dim)
        tail = lax.slice_in_dim(cells, cells.shape[dim] - width, cells.shape[dim], axis=dim)
        cells = jnp.concatenate(
            [
                lax.ppermute(tail, axis, [(i, (i + 1) % count) for i in range(ends)]),
                cells,
                lax.ppermute(head, axis, [((i + 1) % count, i) for i in range(ends)]),
            ],
            axis=dim,
        )
    return cells


def band_matrix(row_count, col_count, shift_by):
    row_index = jnp.arange(row_count, dtype=jnp.int32)[:, None]
    col_index = jnp.arange(col_count, dtype=jnp.int32)[None, :]
    offset = row_index - shift_by - col_index
    picked = jnp.zeros((row_count, col_count), jnp.float32)
    for number in range(16):
        picked = picked + jnp.where(offset == number - 8, float(FILTER_TAPS[number]), 0.0)
    return picked


def synthesize(padded):
    wide_y, wide_z, length = (padded.shape[1], padded.shape[2], padded.shape[3])
    matrix_y = band_matrix(wide_y, wide_y - 16, 8)
    matrix_z = band_matrix(wide_z, wide_z - 16, 8)
    matrix_x = band_matrix(length, length, 0)
    step_one = jnp.einsum("oqzx,qy->oyzx", padded, matrix_y, precision=precise_mode)
    step_two = jnp.einsum("oyqx,qz->oyzx", step_one, matrix_z, precision=precise_mode)
    return jnp.matmul(step_two, matrix_x, precision=precise_mode)


def channel_of(channel, length):
    period = 2 * length
    frequency = jnp.where(channel <= length, channel, channel - length)
    angles = 2.0 * math.pi / period * (frequency % period).astype(jnp.float32)
    lattice = 2.0 - 2.0 * jnp.cos(angles)
    fold = jnp.where((channel == 0) | (channel == length), 1.0, 2.0)
    return frequency, lattice, fold


def channel_table(length):
    period = 2 * length
    channel = jnp.arange(period, dtype=jnp.int32)[None, :]
    frequency, _, _ = channel_of(channel, length)
    positions = jnp.arange(length, dtype=jnp.int32)[:, None] * frequency
    angles = 2.0 * math.pi / period * (positions % period).astype(jnp.float32)
    return jnp.where(channel <= length, jnp.cos(angles), jnp.sin(angles))


def contract(left, right, left_dim, right_dim):
    return lax.dot_general(
        left, right, (((left_dim,), (right_dim,)), ((), ())), precision=fast_mode
    )


def potentials(density):
    pair_count, rows_y, rows_z, length = density.shape
    period = 2 * length
    count_y = lax.axis_size("gy")
    count_z = lax.axis_size("gz")
    spread = count_y * count_z
    width = period // spread
    table = channel_table(length)
    flat = density.reshape(pair_count * rows_y * rows_z, length)
    along_x = contract(table, flat, 0, 1)
    send = along_x.reshape(spread, width, pair_count, rows_y * rows_z)
    got = lax.all_to_all(send, ("gy", "gz"), 0, 0, tiled=True)
    got = got.reshape(count_y, count_z, width, pair_count, rows_y, rows_z)
    got = got.transpose(2, 3, 0, 4, 1, 5).reshape(
        width, pair_count, count_y * rows_y, count_z * rows_z
    )
    along_z = contract(got, table, 3, 0)
    spectrum = contract(along_z, table, 2, 0)
    own = lax.axis_index(("gy", "gz")) * width + jnp.arange(width, dtype=jnp.int32)
    _, lattice_x, fold_x = channel_of(own, length)
    _, lattice_all, fold_all = channel_of(jnp.arange(period, dtype=jnp.int32), length)
    weight = (
        fold_x[:, None, None] * fold_all[None, :, None] * fold_all[None, None, :]
    ) / (
        (lattice_x[:, None, None] + lattice_all[None, :, None] + lattice_all[None, None, :] + SCREEN)
        * float(period**3)
    )
    weighted = spectrum * weight[:, None]
    energy_part = jnp.sum(weighted * spectrum, axis=(0, 2, 3))
    back_y = contract(weighted, table, 3, 1)
    back_z = contract(back_y, table, 2, 1)
    back = back_z.reshape(width, pair_count, count_y, rows_y, count_z, rows_z)
    back = back.transpose(2, 4, 0, 1, 3, 5).reshape(spread, width, pair_count, rows_y * rows_z)
    got = lax.all_to_all(back, ("gy", "gz"), 0, 0, tiled=True)
    got = got.reshape(period, pair_count, rows_y * rows_z)
    result = contract(got, table, 0, 1)
    return result.reshape(pair_count, rows_y, rows_z, length), energy_part


def shards(i_coeff, j_coeff, pair_orbital, pair_occ):
    fields = jnp.concatenate((i_coeff, j_coeff), 0)
    padded = extended(fields, (("gy", 1), ("gz", 2)), 8)
    orbitals = synthesize(padded)
    own_orbital = orbitals[0]
    local_partners = orbitals[1:]
    local_count = local_partners.shape[0]
    wanted = lax.all_gather(pair_orbital, "band", axis=0, tiled=True)
    first_owned = lax.axis_index("band") * local_count
    slots = jnp.zeros(wanted.shape + own_orbital.shape, jnp.float32)
    for number in range(local_count):
        hit = (wanted == first_owned + number)[:, :, None, None, None]
        slots = jnp.where(hit, local_partners[number][None, None], slots)
    partner = lax.psum_scatter(slots, "band", scatter_dimension=0, tiled=True)[0]
    density = own_orbital[None] * partner
    potential, energy_part = potentials(density)
    weights = pair_occ[0].astype(jnp.float32)
    applied = -jnp.sum(weights[:, None, None, None] * potential * partner, axis=0)
    length = own_orbital.shape[2]
    energy = lax.psum(energy_part, ("gy", "gz")) / float(length**3)
    return (applied[None], energy[None])


def solution(mesh):
    in_specs = (
        P("band", "gy", "gz", None),
        P("band", "gy", "gz", None),
        P("band", None),
        P("band", None),
    )
    out_specs = (P("band", "gy", "gz", None), P("band", None))
    return jax.shard_map(shards, mesh=mesh, in_specs=in_specs, out_specs=out_specs, check_vma=False)
```

profile of v0, /device:TPU:0, one launch (start us, length us, event | category | flops | bytes accessed | tf_op | source)
XLA Modules:
  0.0 186.8 jit_solution(6594772100901644955)
XLA Ops:
  7.2 0.0 reduce-scatter.2.cloned.1.call-start
  7.2 1.2 copy_dynamic-update-slice_fusion.1
  8.4 1.5 copy_dynamic-update-slice_fusion
  9.9 0.0 copy-start.7
  9.9 4.9 %collective-permute-start = (f32[3,8,24,96]{3,1,2,0:T(8,128)S(1)}, f32[3,8,24,96]{3,1,2,0:T(8,128)S(1)}, u32[]{:S(2)}, u32[]{:S(2)}) collective-permute-start(f32[3,8,24,96]{3,1,2,0:T(8,128)S(1)} %get-tuple-element.12), channel_id=1, source_target_pairs={{0,4},{1,5},{2,6},{3,7},{8,12},{9,13},{10,14},{11,15},{16,20},{17,... | collective-permute-start | bytes 663560 | tf_op jit(solution)/shard_map/ppermute | solution.py:25
  14.8 1.3 collective-permute-start.1
  16.1 4.9 %collective-permute-done = f32[3,8,24,96]{3,1,2,0:T(8,128)S(1)} collective-permute-done((f32[3,8,24,96]{3,1,2,0:T(8,128)S(1)}, f32[3,8,24,96]{3,1,2,0:T(8,128)S(1)}, u32[]{:S(2)}, u32[]{:S(2)}) %collective-permute-start) | collective-permute-done | bytes 221216 | tf_op jit(solution)/shard_map/ppermute | solution.py:25
  21.0 4.1 %collective-permute-done.1 = f32[3,8,24,96]{3,1,2,0:T(8,128)S(1)} collective-permute-done((f32[3,8,24,96]{3,1,2,0:T(8,128)S(1)}, f32[3,8,24,96]{3,1,2,0:T(8,128)S(1)}, u32[]{:S(2)}, u32[]{:S(2)}) %collective-permute-start.1) | collective-permute-done | bytes 221216 | tf_op jit(solution)/shard_map/ppermute | solution.py:27
  25.2 0.2 pad_maximum_fusion.2
  25.3 2.2 %collective-permute-start.2 = (f32[3,64,8,96]{3,1,2,0:T(8,128)S(1)}, f32[3,64,8,96]{3,1,2,0:T(8,128)}, u32[]{:S(2)}, u32[]{:S(2)}) collective-permute-start(f32[3,64,8,96]{3,1,2,0:T(8,128)S(1)} %get-tuple-element.8), channel_id=1, source_target_pairs={{0,1},{1,2},{2,3},{4,5},{5,6},{6,7},{8,9},{9,10},{10,11},{12,13},{... | collective-permute-start | bytes 1769480 | tf_op jit(solution)/shard_map/ppermute | solution.py:25
  27.6 1.3 collective-permute-start.3
  29.5 0.6 dynamic-slice
  30.1 0.7 bitcast_dynamic-update-slice_fusion
  30.8 8.5 %all-reduce = s32[4]{0:T(128)S(1)} all-reduce(s32[4]{0:T(128)S(1)} %bitcast_dynamic-update-slice_fusion), channel_id=1, replica_groups=mesh['band'=4,'gy'=2,'gz'=4] {'band'}, use_global_device_ids=true, to_apply=%add | all-reduce | flops 4 | bytes 32
  39.3 0.0 collective-permute-done.2
  39.3 0.0 collective-permute-done.3
  39.3 4.4 %fusion.19 = f32[3,48,40,96]{3,1,2,0:T(8,128)S(1)} fusion(f32[3,64,8,96]{3,1,2,0:T(8,128)} %collective-permute-done.3, f32[3,8,24,96]{3,1,2,0:T(8,128)} %copy-done.2, f32[3,48,24,96]{3,1,2,0:T(8,128)S(1)} %copy_dynamic-update-slice_fusion, f32[3,8,24,96]{3,1,2,0:T(8,128)} %copy-done.1, f32[3,64,8,96]{3,1,2,0:T(8,128)} %collective-permute-done.2, ...), kind=kOutput, calls=%fused_computation.23 | convolution fusion | flops 427769856 | bytes 5161216 | tf_op jit(solution)/shard_map/oqzx,qy->oyzx/dot_general | solution.py:49
  43.7 2.5 %fusion.24 = f32[3,48,24,96]{3,2,1,0:T(8,128)S(1)} fusion(f32[3,48,40,96]{3,1,2,0:T(8,128)S(1)} %fusion.19, s32[40]{0:T(128)S(1)} %iota_add_fusion.2), kind=kOutput, calls=%fused_computation.27 | convolution fusion | flops 159298560 | bytes 3539104 | tf_op jit(solution)/shard_map/oyqx,qz->oyzx/dot_general | solution.py:50
  46.2 1.7 fusion.22
  47.9 0.1 slice_bitcast_fusion.1
  48.0 1.7 select_select_fusion
  49.7 0.0 reduce-scatter.2.cloned.1.call-update
  49.7 0.1 or_select_fusion.1
  49.8 50.1 %reduce-scatter.2.cloned.1.call-done = f32[1,1,48,24,96]{4,2,3,1,0:T(8,128)} async-done(((f32[4,1,48,24,96]{4,2,3,1,0:T(8,128)}), f32[1,1,48,24,96]{4,2,3,1,0:T(8,128)}) %reduce-scatter.2.cloned.1.call-update) | async-done | bytes 442384 | tf_op jit(solution)/shard_map/reduce_scatter | solution.py:130
  99.9 1.1 slice_multiply_fusion
  101.0 0.2 copy.19
  101.2 1.9 %convolution_bitcast_fusion = f32[8,24,1,1152]{3,1,2,0:T(8,128)} fusion(f32[1152,96,1]{1,0,2:T(8,128)S(1)} %bitcast.96, s32[8,24]{1,0:T(8,128)S(1)} %add_select_fusion.3, pred[8,24]{1,0:T(8,128)(4,1)S(1)} %fusion.368), kind=kOutput, calls=%fused_computation.15 | convolution fusion | flops 127586304 | bytes 1328064 | tf_op jit(solution)/shard_map/dot_general | solution.py:73
  103.1 3.6 %all-to-all-start = ((f32[8,24,1,1152]{3,1,2,0:T(8,128)}), f32[8,24,1,1152]{3,1,2,0:T(8,128)S(1)}, u32[]{:S(2)}, u32[]{:S(2)}) async-start(f32[8,24,1,1152]{3,1,2,0:T(8,128)} %convolution_bitcast_fusion), calls=%async_computation.1 | async-start | bytes 1769472 | tf_op jit(solution)/shard_map/all_to_all | solution.py:89
  106.8 0.1 or_select_fusion
  106.8 0.7 broadcast_multiply_fusion
  107.5 0.7 broadcast_add_fusion
  108.2 11.3 %all-to-all-done = f32[8,24,1,1152]{3,1,2,0:T(8,128)S(1)} async-done(((f32[8,24,1,1152]{3,1,2,0:T(8,128)}), f32[8,24,1,1152]{3,1,2,0:T(8,128)S(1)}, u32[]{:S(2)}, u32[]{:S(2)}) %all-to-all-start) | async-done | bytes 884768 | tf_op jit(solution)/shard_map/all_to_all | solution.py:89
  119.5 4.3 %reshape.334 = f32[2,4,24,1,48,24]{5,4,2,1,0,3:T(8,128)} reshape(f32[8,24,1,1152]{3,1,2,0:T(8,128)S(1)} %all-to-all-done) | data formatting | bytes 1769472 | tf_op jit(solution)/shard_map/reshape | solution.py:90
  123.8 5.6 %copy.22 = f32[24,1,2,48,4,24]{3,2,5,4,0,1:T(2,128)S(1)} copy(f32[24,1,2,48,4,24]{5,3,0,4,2,1:T(8,128)} %bitcast.92) | data formatting | bytes 1769472 | tf_op jit(solution)/shard_map/transpose | solution.py:91
  129.4 1.3 reshape.335
  130.7 0.0 copy-start.4
  130.7 1.5 fusion.42
  132.3 3.9 %multiply_reduce_fusion = (f32[]{:T(128)}, f32[24,192,192]{2,1,0:T(8,128)S(1)}) fusion(f32[192]{0:T(256)S(1)} %copy-done.6, f32[24,192]{1,0:T(8,128)S(1)} %copy-done.4, f32[192]{0:T(256)S(1)} %get-tuple-element.20, f32[24,192]{1,0:T(8,128)S(1)} %copy-done.3, f32[24,96,192]{1,2,0:T(8,128)S(1)} %fusion.42, s32[192]{0:T(256)S(1)} %add_select_fusion.4, ...), kind=kOutput, calls=%fused_computation | convolution fusion | flops 516870144 | bytes 5347780 | tf_op jit(solution)/shard_map/dot_general | solution.py:73
  136.1 3.8 %fusion.12 = f32[24,192,96]{1,2,0:T(8,128)S(1)} fusion(f32[24,192,192]{2,1,0:T(8,128)S(1)} %get-tuple-element.17, f32[192]{0:T(256)S(1)} %copy-done.6, f32[24,192]{1,0:T(8,128)S(1)} %copy-done.4, f32[192]{0:T(256)S(1)} %get-tuple-element.20, f32[24,192]{1,0:T(8,128)S(1)} %copy-done.3, s32[192]{0:T(256)S(1)} %add_select_fusion.4, ...), kind=kOutput, calls=%fused_computation.14 | convolution fusion | flops 515100672 | bytes 5347776 | tf_op jit(solution)/shard_map/dot_general | solution.py:73
  140.0 2.6 %convolution_bitcast_fusion.1 = f32[2,4,24,1,48,24]{4,5,1,0,2,3:T(8,128)S(1)} fusion(f32[24,2,48,192,1]{3,2,4,1,0:T(8,128)S(1)} %bitcast.95, s32[192]{0:T(256)S(1)} %add_select_fusion.4, s32[4,24]{1,0:T(4,128)S(1)} %multiply_add_fusion.1, pred[192]{0:T(512)(128)(4,1)S(1)} %iota_compare_fusion), kind=kOutput, calls=%fused_computation.26 | convolution fusion | flops 254988288 | bytes 2655552 | tf_op jit(solution)/shard_map/dot_general | solution.py:73
  142.6 3.6 %copy.25 = f32[2,4,24,1,48,24]{5,4,2,1,0,3:T(8,128)} copy(f32[2,4,24,1,48,24]{4,5,1,0,2,3:T(8,128)S(1)} %convolution_bitcast_fusion.1) | data formatting | bytes 1769472 | tf_op jit(solution)/shard_map/transpose | solution.py:110
  146.3 5.0 %reshape.337 = f32[8,24,1,1152]{3,1,0,2:T(8,128)} reshape(f32[2,4,24,1,48,24]{5,4,2,1,0,3:T(8,128)} %copy.25) | data formatting | bytes 1769472 | tf_op jit(solution)/shard_map/reshape | solution.py:110
  151.3 3.7 %all-to-all-start.1 = ((f32[8,24,1,1152]{3,1,2,0:T(8,128)}), f32[8,24,1,1152]{3,1,2,0:T(8,128)S(1)}, u32[]{:S(2)}, u32[]{:S(2)}) async-start(f32[8,24,1,1152]{3,1,2,0:T(8,128)} %bitcast.29), calls=%async_computation.2 | async-start | bytes 1769472 | tf_op jit(solution)/shard_map/all_to_all | solution.py:111
  155.6 19.9 %psum.7 = f32[1]{0:T(128)} all-reduce(f32[1]{0:T(128)} %bitcast.35), channel_id=1, replica_groups=mesh['band'=4,'gy'=2,'gz'=4] {'gy','gz'}, use_global_device_ids=true, to_apply=%region_2.3 | all-reduce | flops 1 | bytes 8 | tf_op jit(solution)/shard_map/psum | solution.py:136
  176.1 0.0 all-to-all-done.1
  176.2 0.4 copy.27
  176.5 1.3 fusion.29
  177.8 1.0 copy.29
  (24 shorter events, 0.1 us)
Async XLA Ops:
  7.2 92.7 %reduce-scatter.2.cloned.1.call-start = ((), (), s32[]{:S(2)}) async-start(), calls=%async_computation.3 | async-start | bytes 2949120 | tf_op jit(solution)/shard_map/reduce_scatter | solution.py:130
  9.9 19.7 %copy-start.7 = (u32[32]{0:T(128)S(1)}, u32[32]{0:T(128)}, u32[]{:S(2)}) copy-start(u32[32]{0:T(128)} %constant.34) | copy-start | bytes 388
  9.9 11.1 %collective-permute-start = (f32[3,8,24,96]{3,1,2,0:T(8,128)S(1)}, f32[3,8,24,96]{3,1,2,0:T(8,128)S(1)}, u32[]{:S(2)}, u32[]{:S(2)}) collective-permute-start(f32[3,8,24,96]{3,1,2,0:T(8,128)S(1)} %get-tuple-element.12), channel_id=1, source_target_pairs={{0,4},{1,5},{2,6},{3,7},{8,12},{9,13},{10,14},{11,15},{16,20},{17,... | collective-permute-start | bytes 663560 | tf_op jit(solution)/shard_map/ppermute | solution.py:25
  14.8 10.4 %collective-permute-start.1 = (f32[3,8,24,96]{3,1,2,0:T(8,128)S(1)}, f32[3,8,24,96]{3,1,2,0:T(8,128)S(1)}, u32[]{:S(2)}, u32[]{:S(2)}) collective-permute-start(f32[3,8,24,96]{3,1,2,0:T(8,128)S(1)} %get-tuple-element.13), channel_id=1, source_target_pairs={{4,0},{5,1},{6,2},{7,3},{12,8},{13,9},{14,10},{15,11},{20,16},{21,... | collective-permute-start | bytes 663560 | tf_op jit(solution)/shard_map/ppermute | solution.py:27
  21.0 7.8 %copy-start.1 = (f32[3,8,24,96]{3,1,2,0:T(8,128)}, f32[3,8,24,96]{3,1,2,0:T(8,128)S(1)}, u32[]{:S(2)}) copy-start(f32[3,8,24,96]{3,1,2,0:T(8,128)S(1)} %collective-permute-done) | copy-start | bytes 663556
  25.1 3.7 %copy-start.2 = (f32[3,8,24,96]{3,1,2,0:T(8,128)}, f32[3,8,24,96]{3,1,2,0:T(8,128)S(1)}, u32[]{:S(2)}) copy-start(f32[3,8,24,96]{3,1,2,0:T(8,128)S(1)} %collective-permute-done.1) | copy-start | bytes 663556
  25.3 14.0 %collective-permute-start.2 = (f32[3,64,8,96]{3,1,2,0:T(8,128)S(1)}, f32[3,64,8,96]{3,1,2,0:T(8,128)}, u32[]{:S(2)}, u32[]{:S(2)}) collective-permute-start(f32[3,64,8,96]{3,1,2,0:T(8,128)S(1)} %get-tuple-element.8), channel_id=1, source_target_pairs={{0,1},{1,2},{2,3},{4,5},{5,6},{6,7},{8,9},{9,10},{10,11},{12,13},{... | collective-permute-start | bytes 1769480 | tf_op jit(solution)/shard_map/ppermute | solution.py:25
  27.6 11.7 %collective-permute-start.3 = (f32[3,64,8,96]{3,1,2,0:T(8,128)S(1)}, f32[3,64,8,96]{3,1,2,0:T(8,128)}, u32[]{:S(2)}, u32[]{:S(2)}) collective-permute-start(f32[3,64,8,96]{3,1,2,0:T(8,128)S(1)} %get-tuple-element.9), channel_id=1, source_target_pairs={{1,0},{2,1},{3,2},{5,4},{6,5},{7,6},{9,8},{10,9},{11,10},{13,12},{... | collective-permute-start | bytes 1769480 | tf_op jit(solution)/shard_map/ppermute | solution.py:27
  103.1 16.4 %all-to-all-start = ((f32[8,24,1,1152]{3,1,2,0:T(8,128)}), f32[8,24,1,1152]{3,1,2,0:T(8,128)S(1)}, u32[]{:S(2)}, u32[]{:S(2)}) async-start(f32[8,24,1,1152]{3,1,2,0:T(8,128)} %convolution_bitcast_fusion), calls=%async_computation.1 | async-start | bytes 1769472 | tf_op jit(solution)/shard_map/all_to_all | solution.py:89
  106.8 17.0 %copy-start.5 = (f32[192]{0:T(256)}, f32[192]{0:T(256)S(1)}, u32[]{:S(2)}) copy-start(f32[192]{0:T(256)S(1)} %get-tuple-element.21) | copy-start | bytes 2308
  130.7 1.6 copy-start.3
  130.7 1.6 copy-start.4
  130.7 1.6 copy-start.6
  151.3 25.3 %copy-start = (f32[1,1,48,24,96]{4,2,3,1,0:T(8,128)S(1)}, f32[1,1,48,24,96]{4,2,3,1,0:T(8,128)}, u32[]{:S(2)}) copy-start(f32[1,1,48,24,96]{4,2,3,1,0:T(8,128)} %reduce-scatter.2.cloned.1.call-done) | copy-start | bytes 1327108
  151.3 24.9 %all-to-all-start.1 = ((f32[8,24,1,1152]{3,1,2,0:T(8,128)}), f32[8,24,1,1152]{3,1,2,0:T(8,128)S(1)}, u32[]{:S(2)}, u32[]{:S(2)}) async-start(f32[8,24,1,1152]{3,1,2,0:T(8,128)} %bitcast.29), calls=%async_computation.2 | async-start | bytes 1769472 | tf_op jit(solution)/shard_map/all_to_all | solution.py:111
Sparse Core Ops, SparseCore 0:
  49.8 50.0 reduce-scatter.1
where the time goes:
time: 187 us
  waiting for transfers between devices  70.4 us (38%)
  blocking collectives  28.4 us (15%)
  local copies, waits for them, and re-layouts  25.5 us (14%)
  matrix products  23.6 us (13%)
  between operations  17.4 us (9%)
  starting transfers between devices  17 us (9%)
  other arithmetic  4.53 us (2%)
    reduce_scatter x1, waiting for transfers between devices, shards(): lax.psum_scatter(slots, 'band', scatter_dimension=0, tiled=True)[0]  50.1 us
    psum x1, blocking collectives, shards(): energy = lax.psum(energy_part, ('gy', 'gz')) / float(length ** 3)  19.9 us
    dot_general x6, matrix products, contract(): lax.dot_general(left, right, (((left_dim,), (right_dim,)), ((), ())), pre...  15 us
    all_to_all x1, waiting for transfers between devices, potentials(): got = lax.all_to_all(send, ('gy', 'gz'), 0, 0, tiled=True)  11.3 us
    unnamed x1, blocking collectives  8.48 us
    ppermute x2, starting transfers between devices, extended(): lax.ppermute(tail, axis, [(i, (i + 1) % count) for i in range(ends)])  7.09 us
    transpose x1, local copies, waits for them, and re-layouts, potentials(): got.transpose(2, 3, 0, 4, 1, 5)  5.61 us
    reshape x1, local copies, waits for them, and re-layouts, potentials(): back.transpose(2, 4, 0, 1, 3, 5)  4.99 us
  transfers between devices with their start and end apart: 7, of which 4 were waited for; matrix products, arithmetic and copies ran while one was open for 1% of the time, Pallas kernels for 0%

commit v1 on v0

--- a/solution.py
+++ b/solution.py
@@ -31,6 +31,20 @@
     return cells
 
 
+def group_sum(values, axes):
+    total = values
+    for axis in axes:
+        count = lax.axis_size(axis)
+        if count & (count - 1):
+            total = lax.psum(total, axis)
+            continue
+        step = 1
+        while step < count:
+            total = total + lax.ppermute(total, axis, [(i, i ^ step) for i in range(count)])
+            step *= 2
+    return total
+
+
 def band_matrix(row_count, col_count, shift_by):
     row_index = jnp.arange(row_count, dtype=jnp.int32)[:, None]
     col_index = jnp.arange(col_count, dtype=jnp.int32)[None, :]
@@ -46,9 +60,9 @@
     matrix_y = band_matrix(wide_y, wide_y - 16, 8)
     matrix_z = band_matrix(wide_z, wide_z - 16, 8)
     matrix_x = band_matrix(length, length, 0)
-    step_one = jnp.einsum("oqzx,qy->oyzx", padded, matrix_y, precision=precise_mode)
-    step_two = jnp.einsum("oyqx,qz->oyzx", step_one, matrix_z, precision=precise_mode)
-    return jnp.matmul(step_two, matrix_x, precision=precise_mode)
+    step_one = jnp.einsum("oqzx,qy->oyzx", padded, matrix_y, precision=fast_mode)
+    step_two = jnp.einsum("oyqx,qz->oyzx", step_one, matrix_z, precision=fast_mode)
+    return jnp.matmul(step_two, matrix_x, precision=fast_mode)
 
 
 def channel_of(channel, length):
@@ -121,7 +135,9 @@
     own_orbital = orbitals[0]
     local_partners = orbitals[1:]
     local_count = local_partners.shape[0]
-    wanted = lax.all_gather(pair_orbital, "band", axis=0, tiled=True)
+    band_count = lax.axis_size("band")
+    mine = lax.axis_index("band") == jnp.arange(band_count, dtype=jnp.int32)[:, None]
+    wanted = group_sum(jnp.where(mine, pair_orbital, 0), ("band",))
     first_owned = lax.axis_index("band") * local_count
     slots = jnp.zeros(wanted.shape + own_orbital.shape, jnp.float32)
     for number in range(local_count):
@@ -133,7 +149,7 @@
     weights = pair_occ[0].astype(jnp.float32)
     applied = -jnp.sum(weights[:, None, None, None] * potential * partner, axis=0)
     length = own_orbital.shape[2]
-    energy = lax.psum(energy_part, ("gy", "gz")) / float(length**3)
+    energy = group_sum(energy_part, ("gz", "gy")) / float(length**3)
     return (applied[None], energy[None])
 
 

time: 187 us -> 182 us (0.973)
  blocking collectives: 28.4 us -> 0 us
  starting transfers between devices: 17 us -> 31.9 us
  waiting for transfers between devices: 70.4 us -> 79 us
  matrix products: 23.6 us -> 20.9 us
  between operations: 17.4 us -> 19.3 us
    psum x1 -> x0, blocking collectives: 19.9 us -> none  [shards(): energy = lax.psum(energy_part, ('gy', 'gz')) / float(length ** 3)]
    ppermute x0 -> x5, starting transfers between devices: none -> 14.9 us  [group_sum(): lax.ppermute(total, axis, [(i, i ^ step) for i in range(count)])]
    unnamed x1 -> x0, blocking collectives: 8.48 us -> none
    reduce_scatter x1, waiting for transfers between devices: 50.1 us -> 56 us  [shards(): lax.psum_scatter(slots, 'band', scatter_dimension=0, tiled=True)[0]]
    ppermute x0 -> x5, waiting for transfers between devices: none -> 5.54 us  [group_sum(): lax.ppermute(total, axis, [(i, i ^ step) for i in range(count)])]
    dot_general x3, matrix products: 8.54 us -> 5.87 us  [the longest x1 3.02 us: synthesize(): jnp.einsum('oqzx,qy->oyzx', padded, matrix_y, precision=fast_mode)]
    ppermute x2, waiting for transfers between devices: 4.93 us -> 2.63 us  [extended(): lax.ppermute(tail, axis, [(i, (i + 1) % count) for i in range(ends)])]
  transfers between devices with their start and end apart: 7 -> 12, of which waited for: 4 -> 8; matrix products, arithmetic and copies ran while one was open for 1% -> 2% of each run, Pallas kernels for 0% -> 0%
where the time goes in v1:
time: 182 us
  waiting for transfers between devices  79 us (43%)
  starting transfers between devices  31.9 us (18%)
  local copies, waits for them, and re-layouts  25 us (14%)
  matrix products  20.9 us (11%)
  between operations  19.3 us (11%)
  other arithmetic  5.57 us (3%)
    reduce_scatter x1, waiting for transfers between devices, shards(): lax.psum_scatter(slots, 'band', scatter_dimension=0, tiled=True)[0]  56 us
    dot_general x6, matrix products, contract(): lax.dot_general(left, right, (((left_dim,), (right_dim,)), ((), ())), pre...  15 us
    ppermute x5, starting transfers between devices, group_sum(): lax.ppermute(total, axis, [(i, i ^ step) for i in range(count)])  14.9 us
    all_to_all x1, waiting for transfers between devices, potentials(): got = lax.all_to_all(send, ('gy', 'gz'), 0, 0, tiled=True)  11.3 us
    ppermute x2, starting transfers between devices, extended(): lax.ppermute(tail, axis, [(i, (i + 1) % count) for i in range(ends)])  7.08 us
    transpose x1, local copies, waits for them, and re-layouts, potentials(): got.transpose(2, 3, 0, 4, 1, 5)  5.61 us
    ppermute x5, waiting for transfers between devices, group_sum(): lax.ppermute(total, axis, [(i, i ^ step) for i in range(count)])  5.54 us
    reshape x1, local copies, waits for them, and re-layouts, potentials(): back.transpose(2, 4, 0, 1, 3, 5)  5.01 us
  transfers between devices with their start and end apart: 12, of which 8 were waited for; matrix products, arithmetic and copies ran while one was open for 2% of the time, Pallas kernels for 0%

profile of v1, /device:TPU:0, one launch (start us, length us, event | category | flops | bytes accessed | tf_op | source)
XLA Modules:
  0.0 181.6 jit_solution(11735921580768469074)
XLA Ops:
  7.2 0.0 reduce-scatter.2.cloned.1.call-start
  7.2 1.2 copy_dynamic-update-slice_fusion.1
  8.4 1.5 copy_dynamic-update-slice_fusion
  9.9 4.9 %collective-permute-start = (f32[3,8,24,96]{3,1,2,0:T(8,128)S(1)}, f32[3,8,24,96]{3,1,2,0:T(8,128)S(1)}, u32[]{:S(2)}, u32[]{:S(2)}) collective-permute-start(f32[3,8,24,96]{3,1,2,0:T(8,128)S(1)} %get-tuple-element.12), channel_id=1, source_target_pairs={{0,4},{1,5},{2,6},{3,7},{8,12},{9,13},{10,14},{11,15},{16,20},{17,... | collective-permute-start | bytes 663560 | tf_op jit(solution)/shard_map/ppermute | solution.py:25
  14.8 1.3 collective-permute-start.1
  16.7 1.6 collective-permute-start.4
  18.4 2.6 %collective-permute-done = f32[3,8,24,96]{3,1,2,0:T(8,128)S(1)} collective-permute-done((f32[3,8,24,96]{3,1,2,0:T(8,128)S(1)}, f32[3,8,24,96]{3,1,2,0:T(8,128)S(1)}, u32[]{:S(2)}, u32[]{:S(2)}) %collective-permute-start) | collective-permute-done | bytes 221216 | tf_op jit(solution)/shard_map/ppermute | solution.py:25
  21.0 0.7 copy-done.1
  21.7 3.5 %collective-permute-done.1 = f32[3,8,24,96]{3,1,2,0:T(8,128)} collective-permute-done((f32[3,8,24,96]{3,1,2,0:T(8,128)S(1)}, f32[3,8,24,96]{3,1,2,0:T(8,128)}, u32[]{:S(2)}, u32[]{:S(2)}) %collective-permute-start.1) | collective-permute-done | bytes 221216 | tf_op jit(solution)/shard_map/ppermute | solution.py:27
  25.2 1.2 pad_maximum_fusion.2
  26.5 2.2 %collective-permute-start.2 = (f32[3,64,8,96]{3,1,2,0:T(8,128)S(1)}, f32[3,64,8,96]{3,1,2,0:T(8,128)}, u32[]{:S(2)}, u32[]{:S(2)}) collective-permute-start(f32[3,64,8,96]{3,1,2,0:T(8,128)S(1)} %get-tuple-element.8), channel_id=1, source_target_pairs={{0,1},{1,2},{2,3},{4,5},{5,6},{6,7},{8,9},{9,10},{10,11},{12,13},{... | collective-permute-start | bytes 1769480 | tf_op jit(solution)/shard_map/ppermute | solution.py:25
  28.7 1.3 collective-permute-start.3
  30.0 2.7 %collective-permute-start.5 = (s32[4,1]{0,1:T(1,128)S(1)}, s32[4,1]{0,1:T(1,128)S(1)}, u32[]{:S(2)}, u32[]{:S(2)}) collective-permute-start(s32[4,1]{0,1:T(1,128)S(1)} %fusion.505), channel_id=1, source_target_pairs={{0,16},{8,24},{16,0},{24,8},{1,17},{9,25},{17,1},{25,9},{2,18},{10... | collective-permute-start | bytes 56 | tf_op jit(solution)/shard_map/ppermute | solution.py:43
  32.7 1.9 %collective-permute-done.5 = s32[4,1]{0,1:T(1,128)S(1)} collective-permute-done((s32[4,1]{0,1:T(1,128)S(1)}, s32[4,1]{0,1:T(1,128)S(1)}, u32[]{:S(2)}, u32[]{:S(2)}) %collective-permute-start.5) | collective-permute-done | bytes 48 | tf_op jit(solution)/shard_map/ppermute | solution.py:43
  34.6 3.0 %fusion.19 = f32[3,48,40,96]{3,1,2,0:T(8,128)S(1)} fusion(f32[3,64,8,96]{3,1,2,0:T(8,128)} %collective-permute-done.3, f32[3,8,24,96]{3,1,2,0:T(8,128)} %collective-permute-done.1, f32[3,48,24,96]{3,1,2,0:T(8,128)S(1)} %copy_dynamic-update-slice_fusion, f32[3,8,24,96]{3,1,2,0:T(8,128)} %copy-done.1, f32[3,64,8,96]{3,1,2,0:T(8,128)} %collective-permute-done.2, ...), kind=kOutput, calls=%fused_computation.23 | convolution fusion | flops 215433216 | bytes 5161216 | tf_op jit(solution)/shard_map/oqzx,qy->oyzx/dot_general | solution.py:63
  37.6 1.8 fusion.24
  39.3 1.1 fusion.22
  40.5 0.1 slice_bitcast_fusion.1
  40.5 1.7 select_select_fusion
  42.3 0.1 or_select_fusion.1
  42.4 56.0 %reduce-scatter.2.cloned.1.call-done = f32[1,1,48,24,96]{4,2,3,1,0:T(8,128)} async-done(((f32[4,1,48,24,96]{4,2,3,1,0:T(8,128)}), f32[1,1,48,24,96]{4,2,3,1,0:T(8,128)}) %reduce-scatter.2.cloned.1.call-update) | async-done | bytes 442384 | tf_op jit(solution)/shard_map/reduce_scatter | solution.py:146
  98.4 1.1 slice_multiply_fusion
  99.5 0.2 copy.19
  99.7 1.9 %convolution_bitcast_fusion = f32[8,24,1,1152]{3,1,2,0:T(8,128)} fusion(f32[1152,96,1]{1,0,2:T(8,128)S(1)} %bitcast.100, s32[8,24]{1,0:T(8,128)S(1)} %add_select_fusion.3, pred[8,24]{1,0:T(8,128)(4,1)S(1)} %fusion.368), kind=kOutput, calls=%fused_computation.15 | convolution fusion | flops 127586304 | bytes 1328064 | tf_op jit(solution)/shard_map/dot_general | solution.py:87
  101.6 3.7 %all-to-all-start = ((f32[8,24,1,1152]{3,1,2,0:T(8,128)}), f32[8,24,1,1152]{3,1,2,0:T(8,128)S(1)}, u32[]{:S(2)}, u32[]{:S(2)}) async-start(f32[8,24,1,1152]{3,1,2,0:T(8,128)} %convolution_bitcast_fusion), calls=%async_computation.1 | async-start | bytes 1769472 | tf_op jit(solution)/shard_map/all_to_all | solution.py:103
  105.3 0.1 or_select_fusion
  105.3 0.7 broadcast_multiply_fusion
  106.0 0.7 broadcast_add_fusion
  106.7 11.3 %all-to-all-done = f32[8,24,1,1152]{3,1,2,0:T(8,128)S(1)} async-done(((f32[8,24,1,1152]{3,1,2,0:T(8,128)}), f32[8,24,1,1152]{3,1,2,0:T(8,128)S(1)}, u32[]{:S(2)}, u32[]{:S(2)}) %all-to-all-start) | async-done | bytes 884768 | tf_op jit(solution)/shard_map/all_to_all | solution.py:103
  118.0 4.4 %reshape.348 = f32[2,4,24,1,48,24]{5,4,2,1,0,3:T(8,128)} reshape(f32[8,24,1,1152]{3,1,2,0:T(8,128)S(1)} %all-to-all-done) | data formatting | bytes 1769472 | tf_op jit(solution)/shard_map/reshape | solution.py:104
  122.3 5.6 %copy.22 = f32[24,1,2,48,4,24]{3,2,5,4,0,1:T(2,128)S(1)} copy(f32[24,1,2,48,4,24]{5,3,0,4,2,1:T(8,128)} %bitcast.96) | data formatting | bytes 1769472 | tf_op jit(solution)/shard_map/transpose | solution.py:105
  128.0 1.3 reshape.349
  129.3 1.5 fusion.42
  130.8 3.9 %multiply_reduce_fusion = (f32[]{:T(128)}, f32[24,192,192]{2,1,0:T(8,128)S(1)}) fusion(f32[192]{0:T(256)S(1)} %copy-done.5, f32[24,192]{1,0:T(8,128)S(1)} %copy-done.3, f32[192]{0:T(256)S(1)} %get-tuple-element.20, f32[24,192]{1,0:T(8,128)S(1)} %copy-done.2, f32[24,96,192]{1,2,0:T(8,128)S(1)} %fusion.42, s32[192]{0:T(256)S(1)} %add_select_fusion.4, ...), kind=kOutput, calls=%fused_computation | convolution fusion | flops 516870144 | bytes 5347780 | tf_op jit(solution)/shard_map/dot_general | solution.py:87
  134.7 3.8 %fusion.12 = f32[24,192,96]{1,2,0:T(8,128)S(1)} fusion(f32[24,192,192]{2,1,0:T(8,128)S(1)} %get-tuple-element.17, f32[192]{0:T(256)S(1)} %copy-done.5, f32[24,192]{1,0:T(8,128)S(1)} %copy-done.3, f32[192]{0:T(256)S(1)} %get-tuple-element.20, f32[24,192]{1,0:T(8,128)S(1)} %copy-done.2, s32[192]{0:T(256)S(1)} %add_select_fusion.4, ...), kind=kOutput, calls=%fused_computation.14 | convolution fusion | flops 515100672 | bytes 5347776 | tf_op jit(solution)/shard_map/dot_general | solution.py:87
  138.5 2.6 %convolution_bitcast_fusion.1 = f32[2,4,24,1,48,24]{4,5,1,0,2,3:T(8,128)S(1)} fusion(f32[24,2,48,192,1]{3,2,4,1,0:T(8,128)S(1)} %bitcast.99, s32[192]{0:T(256)S(1)} %add_select_fusion.4, s32[4,24]{1,0:T(4,128)S(1)} %multiply_add_fusion.1, pred[192]{0:T(512)(128)(4,1)S(1)} %iota_compare_fusion), kind=kOutput, calls=%fused_computation.26 | convolution fusion | flops 254988288 | bytes 2655552 | tf_op jit(solution)/shard_map/dot_general | solution.py:87
  141.2 3.7 %copy.25 = f32[2,4,24,1,48,24]{5,4,2,1,0,3:T(8,128)} copy(f32[2,4,24,1,48,24]{4,5,1,0,2,3:T(8,128)S(1)} %convolution_bitcast_fusion.1) | data formatting | bytes 1769472 | tf_op jit(solution)/shard_map/transpose | solution.py:124
  144.8 5.0 %reshape.351 = f32[8,24,1,1152]{3,1,0,2:T(8,128)} reshape(f32[2,4,24,1,48,24]{5,4,2,1,0,3:T(8,128)} %copy.25) | data formatting | bytes 1769472 | tf_op jit(solution)/shard_map/reshape | solution.py:124
  149.8 3.7 %all-to-all-start.1 = ((f32[8,24,1,1152]{3,1,2,0:T(8,128)}), f32[8,24,1,1152]{3,1,2,0:T(8,128)S(1)}, u32[]{:S(2)}, u32[]{:S(2)}) async-start(f32[8,24,1,1152]{3,1,2,0:T(8,128)} %bitcast.30), calls=%async_computation.2 | async-start | bytes 1769472 | tf_op jit(solution)/shard_map/all_to_all | solution.py:125
  154.2 0.5 collective-permute-start.6
  154.7 1.0 collective-permute-done.6
  156.9 7.2 %collective-permute-start.7 = (f32[1]{0:T(128)}, f32[1]{0:T(128)}, u32[]{:S(2)}, u32[]{:S(2)}) collective-permute-start(f32[1]{0:T(128)} %add.371), channel_id=1, source_target_pairs={{0,2},{1,3},{2,0},{3,1},{4,6},{5,7},{6,4},{7,5},{8,10},{9,11},{10,... | collective-permute-start | bytes 20 | tf_op jit(solution)/shard_map/ppermute | solution.py:43
  164.1 2.0 %collective-permute-done.7 = f32[1]{0:T(128)} collective-permute-done((f32[1]{0:T(128)}, f32[1]{0:T(128)}, u32[]{:S(2)}, u32[]{:S(2)}) %collective-permute-start.7) | collective-permute-done | bytes 36 | tf_op jit(solution)/shard_map/ppermute | solution.py:43
  166.8 2.9 %collective-permute-start.8 = (f32[1]{0:T(128)}, f32[1]{0:T(128)}, u32[]{:S(2)}, u32[]{:S(2)}) collective-permute-start(f32[1]{0:T(128)} %add.372), channel_id=1, source_target_pairs={{0,4},{4,0},{1,5},{5,1},{2,6},{6,2},{3,7},{7,3},{8,12},{12,8},{9,1... | collective-permute-start | bytes 20 | tf_op jit(solution)/shard_map/ppermute | solution.py:43
  169.6 0.7 collective-permute-done.8
  171.0 0.4 copy.27
  171.4 1.3 fusion.29
  172.7 1.0 copy.29
  (27 shorter events, 0.1 us)
Async XLA Ops:
  7.2 91.2 %reduce-scatter.2.cloned.1.call-start = ((), (), s32[]{:S(2)}) async-start(), calls=%async_computation.3 | async-start | bytes 2949120 | tf_op jit(solution)/shard_map/reduce_scatter | solution.py:146
  9.9 11.1 %collective-permute-start = (f32[3,8,24,96]{3,1,2,0:T(8,128)S(1)}, f32[3,8,24,96]{3,1,2,0:T(8,128)S(1)}, u32[]{:S(2)}, u32[]{:S(2)}) collective-permute-start(f32[3,8,24,96]{3,1,2,0:T(8,128)S(1)} %get-tuple-element.12), channel_id=1, source_target_pairs={{0,4},{1,5},{2,6},{3,7},{8,12},{9,13},{10,14},{11,15},{16,20},{17,... | collective-permute-start | bytes 663560 | tf_op jit(solution)/shard_map/ppermute | solution.py:25
  14.8 10.5 %collective-permute-start.1 = (f32[3,8,24,96]{3,1,2,0:T(8,128)S(1)}, f32[3,8,24,96]{3,1,2,0:T(8,128)}, u32[]{:S(2)}, u32[]{:S(2)}) collective-permute-start(f32[3,8,24,96]{3,1,2,0:T(8,128)S(1)} %get-tuple-element.13), channel_id=1, source_target_pairs={{4,0},{5,1},{6,2},{7,3},{12,8},{13,9},{14,10},{15,11},{20,16},{21,... | collective-permute-start | bytes 663560 | tf_op jit(solution)/shard_map/ppermute | solution.py:27
  16.7 13.3 %collective-permute-start.4 = (s32[4,1]{0,1:T(1,128)S(1)}, s32[4,1]{0,1:T(1,128)S(1)}, u32[]{:S(2)}, u32[]{:S(2)}) collective-permute-start(s32[4,1]{0,1:T(1,128)S(1)} %compare_select_fusion.1), channel_id=1, source_target_pairs={{0,8},{8,0},{16,24},{24,16},{1,9},{9,1},{17,25},{25,17},{2,10},{10... | collective-permute-start | bytes 56 | tf_op jit(solution)/shard_map/ppermute | solution.py:43
  21.0 0.7 copy-start.1
  26.5 8.1 %collective-permute-start.2 = (f32[3,64,8,96]{3,1,2,0:T(8,128)S(1)}, f32[3,64,8,96]{3,1,2,0:T(8,128)}, u32[]{:S(2)}, u32[]{:S(2)}) collective-permute-start(f32[3,64,8,96]{3,1,2,0:T(8,128)S(1)} %get-tuple-element.8), channel_id=1, source_target_pairs={{0,1},{1,2},{2,3},{4,5},{5,6},{6,7},{8,9},{9,10},{10,11},{12,13},{... | collective-permute-start | bytes 1769480 | tf_op jit(solution)/shard_map/ppermute | solution.py:25
  28.7 5.9 %collective-permute-start.3 = (f32[3,64,8,96]{3,1,2,0:T(8,128)S(1)}, f32[3,64,8,96]{3,1,2,0:T(8,128)}, u32[]{:S(2)}, u32[]{:S(2)}) collective-permute-start(f32[3,64,8,96]{3,1,2,0:T(8,128)S(1)} %get-tuple-element.9), channel_id=1, source_target_pairs={{1,0},{2,1},{3,2},{5,4},{6,5},{7,6},{9,8},{10,9},{11,10},{13,12},{... | collective-permute-start | bytes 1769480 | tf_op jit(solution)/shard_map/ppermute | solution.py:27
  30.0 4.5 %collective-permute-start.5 = (s32[4,1]{0,1:T(1,128)S(1)}, s32[4,1]{0,1:T(1,128)S(1)}, u32[]{:S(2)}, u32[]{:S(2)}) collective-permute-start(s32[4,1]{0,1:T(1,128)S(1)} %fusion.505), channel_id=1, source_target_pairs={{0,16},{8,24},{16,0},{24,8},{1,17},{9,25},{17,1},{25,9},{2,18},{10... | collective-permute-start | bytes 56 | tf_op jit(solution)/shard_map/ppermute | solution.py:43
  101.6 16.4 %all-to-all-start = ((f32[8,24,1,1152]{3,1,2,0:T(8,128)}), f32[8,24,1,1152]{3,1,2,0:T(8,128)S(1)}, u32[]{:S(2)}, u32[]{:S(2)}) async-start(f32[8,24,1,1152]{3,1,2,0:T(8,128)} %convolution_bitcast_fusion), calls=%async_computation.1 | async-start | bytes 1769472 | tf_op jit(solution)/shard_map/all_to_all | solution.py:103
  105.3 17.0 %copy-start.4 = (f32[192]{0:T(256)}, f32[192]{0:T(256)S(1)}, u32[]{:S(2)}) copy-start(f32[192]{0:T(256)S(1)} %get-tuple-element.21) | copy-start | bytes 2308
  129.2 1.6 copy-start.2
  129.2 1.6 copy-start.3
  129.3 1.6 copy-start.5
  149.8 21.5 %copy-start = (f32[1,1,48,24,96]{4,2,3,1,0:T(8,128)S(1)}, f32[1,1,48,24,96]{4,2,3,1,0:T(8,128)}, u32[]{:S(2)}) copy-start(f32[1,1,48,24,96]{4,2,3,1,0:T(8,128)} %reduce-scatter.2.cloned.1.call-done) | copy-start | bytes 1327108
  149.8 21.1 %all-to-all-start.1 = ((f32[8,24,1,1152]{3,1,2,0:T(8,128)}), f32[8,24,1,1152]{3,1,2,0:T(8,128)S(1)}, u32[]{:S(2)}, u32[]{:S(2)}) async-start(f32[8,24,1,1152]{3,1,2,0:T(8,128)} %bitcast.30), calls=%async_computation.2 | async-start | bytes 1769472 | tf_op jit(solution)/shard_map/all_to_all | solution.py:125
  154.2 1.4 collective-permute-start.6
  156.9 9.3 %collective-permute-start.7 = (f32[1]{0:T(128)}, f32[1]{0:T(128)}, u32[]{:S(2)}, u32[]{:S(2)}) collective-permute-start(f32[1]{0:T(128)} %add.371), channel_id=1, source_target_pairs={{0,2},{1,3},{2,0},{3,1},{4,6},{5,7},{6,4},{7,5},{8,10},{9,11},{10,... | collective-permute-start | bytes 20 | tf_op jit(solution)/shard_map/ppermute | solution.py:43
  166.8 3.6 %collective-permute-start.8 = (f32[1]{0:T(128)}, f32[1]{0:T(128)}, u32[]{:S(2)}, u32[]{:S(2)}) collective-permute-start(f32[1]{0:T(128)} %add.372), channel_id=1, source_target_pairs={{0,4},{4,0},{1,5},{5,1},{2,6},{6,2},{3,7},{7,3},{8,12},{12,8},{9,1... | collective-permute-start | bytes 20 | tf_op jit(solution)/shard_map/ppermute | solution.py:43
Sparse Core Ops, SparseCore 0:
  42.4 55.9 reduce-scatter.1

commit v2 on v1

--- a/solution.py
+++ b/solution.py
@@ -14,21 +14,38 @@
 fast_mode = lax.Precision.HIGH
 
 
-def extended(cells, sides, width):
-    for axis, dim in sides:
-        count = lax.axis_size(axis)
-        ends = count - 1
-        head = lax.slice_in_dim(cells, 0, width, axis=dim)
-        tail = lax.slice_in_dim(cells, cells.shape[dim] - width, cells.shape[dim], axis=dim)
-        cells = jnp.concatenate(
-            [
-                lax.ppermute(tail, axis, [(i, (i + 1) % count) for i in range(ends)]),
-                cells,
-                lax.ppermute(head, axis, [((i + 1) % count, i) for i in range(ends)]),
-            ],
-            axis=dim,
-        )
-    return cells
+def extended(cells, width):
+    count_y = lax.axis_size("gy")
+    count_z = lax.axis_size("gz")
+    rows_y, rows_z = cells.shape[1], cells.shape[2]
+    pieces_y = (
+        lax.slice_in_dim(cells, rows_y - width, rows_y, axis=1),
+        cells,
+        lax.slice_in_dim(cells, 0, width, axis=1),
+    )
+    grid = []
+    for shift_y in (-1, 0, 1):
+        row = []
+        for shift_z in (-1, 0, 1):
+            block = pieces_y[shift_y + 1]
+            block = (
+                lax.slice_in_dim(block, rows_z - width, rows_z, axis=2),
+                block,
+                lax.slice_in_dim(block, 0, width, axis=2),
+            )[shift_z + 1]
+            if shift_y == 0 and shift_z == 0:
+                row.append(block)
+                continue
+            pairs = []
+            for source_y in range(count_y):
+                for source_z in range(count_z):
+                    target_y = source_y - shift_y
+                    target_z = source_z - shift_z
+                    if 0 <= target_y < count_y and 0 <= target_z < count_z:
+                        pairs.append((source_y * count_z + source_z, target_y * count_z + target_z))
+            row.append(lax.ppermute(block, ("gy", "gz"), pairs))
+        grid.append(jnp.concatenate(row, axis=2))
+    return jnp.concatenate(grid, axis=1)
 
 
 def group_sum(values, axes):
@@ -60,9 +77,9 @@
     matrix_y = band_matrix(wide_y, wide_y - 16, 8)
     matrix_z = band_matrix(wide_z, wide_z - 16, 8)
     matrix_x = band_matrix(length, length, 0)
-    step_one = jnp.einsum("oqzx,qy->oyzx", padded, matrix_y, precision=fast_mode)
-    step_two = jnp.einsum("oyqx,qz->oyzx", step_one, matrix_z, precision=fast_mode)
-    return jnp.matmul(step_two, matrix_x, precision=fast_mode)
+    step_one = jnp.einsum("oqzx,qy->oyzx", padded, matrix_y, precision=precise_mode)
+    step_two = jnp.einsum("oyqx,qz->oyzx", step_one, matrix_z, precision=precise_mode)
+    return jnp.matmul(step_two, matrix_x, precision=precise_mode)
 
 
 def channel_of(channel, length):
@@ -122,34 +139,34 @@
     back_z = contract(back_y, table, 2, 1)
     back = back_z.reshape(width, pair_count, count_y, rows_y, count_z, rows_z)
     back = back.transpose(2, 4, 0, 1, 3, 5).reshape(spread, width, pair_count, rows_y * rows_z)
+    rider = jnp.broadcast_to(energy_part[None, None, :, None], (spread, width, pair_count, 128))
+    back = jnp.concatenate((back, rider), axis=3)
     got = lax.all_to_all(back, ("gy", "gz"), 0, 0, tiled=True)
-    got = got.reshape(period, pair_count, rows_y * rows_z)
+    energy_total = jnp.sum(got[:, 0, :, rows_y * rows_z], axis=0)
+    got = got[:, :, :, : rows_y * rows_z].reshape(period, pair_count, rows_y * rows_z)
     result = contract(got, table, 0, 1)
-    return result.reshape(pair_count, rows_y, rows_z, length), energy_part
+    return result.reshape(pair_count, rows_y, rows_z, length), energy_total
 
 
 def shards(i_coeff, j_coeff, pair_orbital, pair_occ):
-    fields = jnp.concatenate((i_coeff, j_coeff), 0)
-    padded = extended(fields, (("gy", 1), ("gz", 2)), 8)
-    orbitals = synthesize(padded)
-    own_orbital = orbitals[0]
-    local_partners = orbitals[1:]
+    local_partners = synthesize(extended(j_coeff, 8))
     local_count = local_partners.shape[0]
     band_count = lax.axis_size("band")
     mine = lax.axis_index("band") == jnp.arange(band_count, dtype=jnp.int32)[:, None]
     wanted = group_sum(jnp.where(mine, pair_orbital, 0), ("band",))
     first_owned = lax.axis_index("band") * local_count
-    slots = jnp.zeros(wanted.shape + own_orbital.shape, jnp.float32)
+    slots = jnp.zeros(wanted.shape + local_partners.shape[1:], jnp.float32)
     for number in range(local_count):
         hit = (wanted == first_owned + number)[:, :, None, None, None]
         slots = jnp.where(hit, local_partners[number][None, None], slots)
     partner = lax.psum_scatter(slots, "band", scatter_dimension=0, tiled=True)[0]
+    own_orbital = synthesize(extended(i_coeff, 8))[0]
     density = own_orbital[None] * partner
     potential, energy_part = potentials(density)
     weights = pair_occ[0].astype(jnp.float32)
     applied = -jnp.sum(weights[:, None, None, None] * potential * partner, axis=0)
     length = own_orbital.shape[2]
-    energy = group_sum(energy_part, ("gz", "gy")) / float(length**3)
+    energy = energy_part / float(length**3)
     return (applied[None], energy[None])
 
 

time: 182 us -> 184 us (1.011)
  starting transfers between devices: 31.9 us -> 44.7 us
  waiting for transfers between devices: 79 us -> 67.4 us
  matrix products: 20.9 us -> 25.3 us
    reduce_scatter x1, waiting for transfers between devices: 56 us -> 25.7 us  [shards(): lax.psum_scatter(slots, 'band', scatter_dimension=0, tiled=True)[0]]
    ppermute x4 -> x16, starting transfers between devices: 9.65 us -> 33.2 us  [extended(): row.append(lax.ppermute(block, ('gy', 'gz'), pairs))]
    all_to_all x1, waiting for transfers between devices: 0.01 us -> 13 us  [potentials(): got = lax.all_to_all(back, ('gy', 'gz'), 0, 0, tiled=True)]
    ppermute x5 -> x2, starting transfers between devices: 14.9 us -> 4.23 us  [group_sum(): lax.ppermute(total, axis, [(i, i ^ step) for i in range(count)])]
    ppermute x4 -> x16, waiting for transfers between devices: 6.15 us -> 13.7 us  [extended(): row.append(lax.ppermute(block, ('gy', 'gz'), pairs))]
    dot_general x3 -> x6, matrix products: 5.87 us -> 9.18 us  [the longest x2 3.65 us: synthesize(): jnp.einsum('oqzx,qy->oyzx', padded, matrix_y, precision=precise_mode)]
    ppermute x5 -> x2, waiting for transfers between devices: 5.54 us -> 3.77 us  [group_sum(): lax.ppermute(total, axis, [(i, i ^ step) for i in range(count)])]
  transfers between devices with their start and end apart: 12 -> 21, of which waited for: 8 -> 9; matrix products, arithmetic and copies ran while one was open for 2% -> 2% of each run, Pallas kernels for 0% -> 0%
where the time goes in v2:
time: 184 us; the launch traced here: 183 us
  waiting for transfers between devices  67.4 us (37%)
  starting transfers between devices  44.7 us (24%)
  matrix products  25.3 us (14%)
  local copies, waits for them, and re-layouts  24.3 us (13%)
  between operations  17.6 us (10%)
  other arithmetic  3.82 us (2%)
    ppermute x16, starting transfers between devices, extended(): row.append(lax.ppermute(block, ('gy', 'gz'), pairs))  33.2 us
    reduce_scatter x1, waiting for transfers between devices, shards(): lax.psum_scatter(slots, 'band', scatter_dimension=0, tiled=True)[0]  25.7 us
    dot_general x6, matrix products, contract(): lax.dot_general(left, right, (((left_dim,), (right_dim,)), ((), ())), pre...  16.1 us
    ppermute x16, waiting for transfers between devices, extended(): row.append(lax.ppermute(block, ('gy', 'gz'), pairs))  13.7 us
    all_to_all x1, waiting for transfers between devices, potentials(): got = lax.all_to_all(back, ('gy', 'gz'), 0, 0, tiled=True)  13 us
    all_to_all x1, waiting for transfers between devices, potentials(): got = lax.all_to_all(send, ('gy', 'gz'), 0, 0, tiled=True)  11.3 us
    transpose x1, local copies, waits for them, and re-layouts, potentials(): got.transpose(2, 3, 0, 4, 1, 5)  5.61 us
    reshape x1, local copies, waits for them, and re-layouts, potentials(): got = got.reshape(count_y, count_z, width, pair_count, rows_y, rows_z)  4.38 us
  transfers between devices with their start and end apart: 21, of which 9 were waited for; matrix products, arithmetic and copies ran while one was open for 2% of the time, Pallas kernels for 0%

profile of v2, /device:TPU:0, one launch (start us, length us, event | category | flops | bytes accessed | tf_op | source)
XLA Modules:
  0.0 183.2 jit_solution(6708064317259248569)
XLA Ops:
  7.2 1.5 copy.28
  8.7 4.3 %collective-permute-start.10 = (f32[2,8,8,96]{3,1,2,0:T(8,128)S(1)}, f32[2,8,8,96]{3,1,2,0:T(8,128)S(1)}, u32[]{:S(2)}, u32[]{:S(2)}) collective-permute-start(f32[2,8,8,96]{3,1,2,0:T(8,128)S(1)} %get-tuple-element.10), channel_id=1, source_target_pairs={{0,5},{1,6},{2,7},{8,13},{9,14},{10,15},{16,21},{17,22},{18,23},{2... | collective-permute-start | bytes 147464 | tf_op jit(solution)/shard_map/ppermute | solution.py:46
  13.7 1.3 collective-permute-start.15
  15.1 4.2 %collective-permute-start.13 = (f32[2,48,8,96]{3,1,2,0:T(8,128)S(1)}, f32[2,48,8,96]{3,1,2,0:T(8,128)S(1)}, u32[]{:S(2)}, u32[]{:S(2)}) collective-permute-start(f32[2,48,8,96]{3,1,2,0:T(8,128)S(1)} %get-tuple-element.16), channel_id=1, source_target_pairs={{0,1},{1,2},{2,3},{4,5},{5,6},{6,7},{8,9},{9,10},{10,11},{12,13},{... | collective-permute-start | bytes 884744 | tf_op jit(solution)/shard_map/ppermute | solution.py:46
  19.9 1.6 collective-permute-start.8
  21.6 1.9 %collective-permute-done.8 = s32[4,1]{0,1:T(1,128)S(1)} collective-permute-done((s32[4,1]{0,1:T(1,128)S(1)}, s32[4,1]{0,1:T(1,128)S(1)}, u32[]{:S(2)}, u32[]{:S(2)}) %collective-permute-start.8) | collective-permute-done | bytes 48 | tf_op jit(solution)/shard_map/ppermute | solution.py:60
  23.5 2.6 %collective-permute-start.9 = (s32[4,1]{0,1:T(1,128)S(1)}, s32[4,1]{0,1:T(1,128)S(1)}, u32[]{:S(2)}, u32[]{:S(2)}) collective-permute-start(s32[4,1]{0,1:T(1,128)S(1)} %fusion.398), channel_id=1, source_target_pairs={{0,16},{8,24},{16,0},{24,8},{1,17},{9,25},{17,1},{25,9},{2,18},{10... | collective-permute-start | bytes 56 | tf_op jit(solution)/shard_map/ppermute | solution.py:60
  26.1 1.9 %collective-permute-done.9 = s32[4,1]{0,1:T(1,128)S(1)} collective-permute-done((s32[4,1]{0,1:T(1,128)S(1)}, s32[4,1]{0,1:T(1,128)S(1)}, u32[]{:S(2)}, u32[]{:S(2)}) %collective-permute-start.9) | collective-permute-done | bytes 48 | tf_op jit(solution)/shard_map/ppermute | solution.py:60
  28.0 1.3 collective-permute-start.14
  29.3 1.3 collective-permute-start.17
  30.6 4.0 %collective-permute-start.11 = (f32[2,8,24,96]{3,1,2,0:T(8,128)S(1)}, f32[2,8,24,96]{3,1,2,0:T(8,128)S(1)}, u32[]{:S(2)}, u32[]{:S(2)}) collective-permute-start(f32[2,8,24,96]{3,1,2,0:T(8,128)S(1)} %get-tuple-element.14), channel_id=1, source_target_pairs={{0,4},{1,5},{2,6},{3,7},{8,12},{9,13},{10,14},{11,15},{16,20},{17,... | collective-permute-start | bytes 442376 | tf_op jit(solution)/shard_map/ppermute | solution.py:46
  34.6 1.3 collective-permute-start.16
  36.0 3.2 %collective-permute-done.11 = f32[2,8,24,96]{3,1,2,0:T(8,128)S(1)} collective-permute-done((f32[2,8,24,96]{3,1,2,0:T(8,128)S(1)}, f32[2,8,24,96]{3,1,2,0:T(8,128)S(1)}, u32[]{:S(2)}, u32[]{:S(2)}) %collective-permute-start.11) | collective-permute-done | bytes 147488 | tf_op jit(solution)/shard_map/ppermute | solution.py:46
  39.1 4.7 %collective-permute-done.16 = f32[2,8,24,96]{3,1,2,0:T(8,128)S(1)} collective-permute-done((f32[2,8,24,96]{3,1,2,0:T(8,128)S(1)}, f32[2,8,24,96]{3,1,2,0:T(8,128)S(1)}, u32[]{:S(2)}, u32[]{:S(2)}) %collective-permute-start.16) | collective-permute-done | bytes 147488 | tf_op jit(solution)/shard_map/ppermute | solution.py:46
  43.9 2.7 %fusion.27 = f32[2,48,40,96]{3,1,2,0:T(8,128)S(1)} fusion(f32[2,8,8,96]{3,1,2,0:T(8,128)S(1)} %collective-permute-done.17, f32[2,8,24,96]{3,1,2,0:T(8,128)S(1)} %collective-permute-done.16, f32[2,8,8,96]{3,1,2,0:T(8,128)} %collective-permute-done.15, f32[2,48,8,96]{3,1,2,0:T(8,128)S(1)} %collective-permute-done.14, f32[2,48,24,96]{3,1,2,0:T(8,128)S(1)} %copy.28, ...), kind=kOutput, calls=%fused_computation.32 | convolution fusion | flops 287195136 | bytes 3440896 | tf_op jit(solution)/shard_map/oqzx,qy->oyzx/dot_general | solution.py:80
  46.5 1.7 fusion.30
  48.2 1.2 fusion.54
  49.5 1.7 select_select_fusion
  51.4 1.6 collective-permute-start
  54.3 4.2 %collective-permute-start.3 = (f32[1,48,8,96]{3,1,2,0:T(8,128)S(1)}, f32[1,48,8,96]{3,1,2,0:T(8,128)S(1)}, u32[]{:S(2)}, u32[]{:S(2)}) collective-permute-start(f32[1,48,8,96]{3,1,2,0:T(8,128)S(1)} %get-tuple-element.24), channel_id=1, source_target_pairs={{0,1},{1,2},{2,3},{4,5},{5,6},{6,7},{8,9},{9,10},{10,11},{12,13},{... | collective-permute-start | bytes 442376 | tf_op jit(solution)/shard_map/ppermute | solution.py:46
  58.6 1.3 collective-permute-start.4
  60.0 1.3 collective-permute-start.7
  61.3 3.9 %collective-permute-start.1 = (f32[1,8,24,96]{3,1,2,0:T(8,128)S(1)}, f32[1,8,24,96]{3,1,2,0:T(8,128)S(1)}, u32[]{:S(2)}, u32[]{:S(2)}) collective-permute-start(f32[1,8,24,96]{3,1,2,0:T(8,128)S(1)} %get-tuple-element.22), channel_id=1, source_target_pairs={{0,4},{1,5},{2,6},{3,7},{8,12},{9,13},{10,14},{11,15},{16,20},{17,... | collective-permute-start | bytes 221192 | tf_op jit(solution)/shard_map/ppermute | solution.py:46
  65.2 1.3 collective-permute-start.6
  66.5 1.0 collective-permute-done.1
  67.6 4.7 %collective-permute-done.6 = f32[1,8,24,96]{3,1,2,0:T(8,128)S(1)} collective-permute-done((f32[1,8,24,96]{3,1,2,0:T(8,128)S(1)}, f32[1,8,24,96]{3,1,2,0:T(8,128)S(1)}, u32[]{:S(2)}, u32[]{:S(2)}) %collective-permute-start.6) | collective-permute-done | bytes 73760 | tf_op jit(solution)/shard_map/ppermute | solution.py:46
  72.3 1.0 fusion.33
  73.3 0.9 convolution_bitcast_fusion.2
  74.2 25.7 %reduce-scatter.2.cloned.1.call-done = f32[1,1,48,24,96]{4,2,3,1,0:T(8,128)} async-done(((f32[4,1,48,24,96]{4,2,3,1,0:T(8,128)}), f32[1,1,48,24,96]{4,2,3,1,0:T(8,128)}) %reduce-scatter.2.cloned.1.call-update) | async-done | bytes 442384 | tf_op jit(solution)/shard_map/reduce_scatter | solution.py:162
  99.9 1.8 convolution_multiply_fusion.1
  101.9 1.9 %convolution_bitcast_fusion = f32[8,24,1,1152]{3,1,2,0:T(8,128)} fusion(f32[1152,96,1]{1,0,2:T(8,128)S(1)} %bitcast.119, s32[8,24]{1,0:T(8,128)S(1)} %add_select_fusion.3, pred[8,24]{1,0:T(8,128)(4,1)S(1)} %fusion.156), kind=kOutput, calls=%fused_computation.21 | convolution fusion | flops 127586304 | bytes 1328064 | tf_op jit(solution)/shard_map/dot_general | solution.py:104
  103.8 3.6 %all-to-all-start = ((f32[8,24,1,1152]{3,1,2,0:T(8,128)}), f32[8,24,1,1152]{3,1,2,0:T(8,128)S(1)}, u32[]{:S(2)}, u32[]{:S(2)}) async-start(f32[8,24,1,1152]{3,1,2,0:T(8,128)} %convolution_bitcast_fusion), calls=%async_computation.1 | async-start | bytes 1769472 | tf_op jit(solution)/shard_map/all_to_all | solution.py:120
  107.5 0.7 broadcast_multiply_fusion
  108.9 11.3 %all-to-all-done = f32[8,24,1,1152]{3,1,2,0:T(8,128)S(1)} async-done(((f32[8,24,1,1152]{3,1,2,0:T(8,128)}), f32[8,24,1,1152]{3,1,2,0:T(8,128)S(1)}, u32[]{:S(2)}, u32[]{:S(2)}) %all-to-all-start) | async-done | bytes 884768 | tf_op jit(solution)/shard_map/all_to_all | solution.py:120
  120.1 4.4 %reshape.373 = f32[2,4,24,1,48,24]{5,4,2,1,0,3:T(8,128)} reshape(f32[8,24,1,1152]{3,1,2,0:T(8,128)S(1)} %all-to-all-done) | data formatting | bytes 1769472 | tf_op jit(solution)/shard_map/reshape | solution.py:121
  124.5 5.6 %copy.42 = f32[24,1,2,48,4,24]{3,2,5,4,0,1:T(2,128)S(1)} copy(f32[24,1,2,48,4,24]{5,3,0,4,2,1:T(8,128)} %bitcast.114) | data formatting | bytes 1769472 | tf_op jit(solution)/shard_map/transpose | solution.py:122
  130.1 1.3 reshape.374
  131.5 1.5 fusion.69
  133.0 3.9 %multiply_reduce_fusion = (f32[]{:T(128)}, f32[24,192,192]{2,1,0:T(8,128)S(1)}) fusion(f32[192]{0:T(256)S(1)} %copy-done.4, f32[24,192]{1,0:T(8,128)S(1)} %copy-done.2, f32[192]{0:T(256)S(1)} %get-tuple-element.32, f32[24,192]{1,0:T(8,128)S(1)} %copy-done.1, f32[24,96,192]{1,2,0:T(8,128)S(1)} %fusion.69, s32[192]{0:T(256)S(1)} %add_select_fusion.4, ...), kind=kOutput, calls=%fused_computation | convolution fusion | flops 516870144 | bytes 5347780 | tf_op jit(solution)/shard_map/dot_general | solution.py:104
  136.9 3.8 %fusion = f32[24,192,96]{1,2,0:T(8,128)S(1)} fusion(f32[24,192,192]{2,1,0:T(8,128)S(1)} %get-tuple-element.29, f32[192]{0:T(256)S(1)} %copy-done.4, f32[24,192]{1,0:T(8,128)S(1)} %copy-done.2, f32[192]{0:T(256)S(1)} %get-tuple-element.32, f32[24,192]{1,0:T(8,128)S(1)} %copy-done.1, s32[192]{0:T(256)S(1)} %add_select_fusion.4, ...), kind=kOutput, calls=%fused_computation.2 | convolution fusion | flops 515100672 | bytes 5347776 | tf_op jit(solution)/shard_map/dot_general | solution.py:104
  140.7 2.6 %convolution_bitcast_fusion.1 = f32[2,4,24,1,48,24]{4,5,1,0,2,3:T(8,128)S(1)} fusion(f32[24,2,48,192,1]{3,2,4,1,0:T(8,128)S(1)} %bitcast.118, s32[192]{0:T(256)S(1)} %add_select_fusion.4, s32[4,24]{1,0:T(4,128)S(1)} %multiply_add_fusion.1, pred[192]{0:T(512)(128)(4,1)S(1)} %iota_compare_fusion), kind=kOutput, calls=%fused_computation.31 | convolution fusion | flops 254988288 | bytes 2655552 | tf_op jit(solution)/shard_map/dot_general | solution.py:104
  143.3 3.7 %copy.45 = f32[2,4,24,1,48,24]{5,4,2,1,0,3:T(8,128)} copy(f32[2,4,24,1,48,24]{4,5,1,0,2,3:T(8,128)S(1)} %convolution_bitcast_fusion.1) | data formatting | bytes 1769472 | tf_op jit(solution)/shard_map/transpose | solution.py:141
  147.0 4.2 %reshape.376 = f32[8,24,1,1152]{3,1,0,2:T(8,128)S(1)} reshape(f32[2,4,24,1,48,24]{5,4,2,1,0,3:T(8,128)} %copy.45) | data formatting | bytes 1769472 | tf_op jit(solution)/shard_map/reshape | solution.py:141
  151.2 1.7 pad_bitcast_fusion
  152.9 3.6 %all-to-all-start.1 = ((f32[8,24,1,1280]{3,1,2,0:T(8,128)}), f32[8,24,1,1280]{3,1,2,0:T(8,128)S(1)}, u32[]{:S(2)}, u32[]{:S(2)}) async-start(f32[8,24,1,1280]{3,1,2,0:T(8,128)} %pad_bitcast_fusion), calls=%async_computation.2 | async-start | bytes 1966080 | tf_op jit(solution)/shard_map/all_to_all | solution.py:144
  157.1 13.0 %all-to-all-done.1 = f32[8,24,1,1280]{3,1,2,0:T(8,128)S(1)} async-done(((f32[8,24,1,1280]{3,1,2,0:T(8,128)}), f32[8,24,1,1280]{3,1,2,0:T(8,128)S(1)}, u32[]{:S(2)}, u32[]{:S(2)}) %all-to-all-start.1) | async-done | bytes 983072 | tf_op jit(solution)/shard_map/all_to_all | solution.py:144
  170.6 2.3 %fusion.52 = f32[1,48,24,96]{3,1,2,0:T(8,128)S(1)} fusion(f32[48,24,192]{2,1,0:T(8,128)S(1)} %bitcast.115, f32[1,1,48,24,96]{4,2,3,1,0:T(8,128)} %reduce-scatter.2.cloned.1.call-done, f32[]{:T(128)} %bitcast, s32[192]{0:T(256)S(1)} %add_select_fusion.4, pred[192]{0:T(512)(128)(4,1)S(1)} %iota_compare_fusion), kind=kOutput, calls=%fused_computation.55 | convolution fusion | flops 127918080 | bytes 1770436 | tf_op jit(solution)/shard_map/dot_general | solution.py:104
  172.9 1.0 copy.50
  (52 shorter events, 4.5 us)
Async XLA Ops:
  7.2 92.7 %reduce-scatter.2.cloned.1.call-start = ((), (), s32[]{:S(2)}) async-start(), calls=%async_computation.3 | async-start | bytes 2949120 | tf_op jit(solution)/shard_map/reduce_scatter | solution.py:162
  8.7 20.6 %collective-permute-start.10 = (f32[2,8,8,96]{3,1,2,0:T(8,128)S(1)}, f32[2,8,8,96]{3,1,2,0:T(8,128)S(1)}, u32[]{:S(2)}, u32[]{:S(2)}) collective-permute-start(f32[2,8,8,96]{3,1,2,0:T(8,128)S(1)} %get-tuple-element.10), channel_id=1, source_target_pairs={{0,5},{1,6},{2,7},{8,13},{9,14},{10,15},{16,21},{17,22},{18,23},{2... | collective-permute-start | bytes 147464 | tf_op jit(solution)/shard_map/ppermute | solution.py:46
  13.0 17.6 %collective-permute-start.12 = (f32[2,8,8,96]{3,1,2,0:T(8,128)S(1)}, f32[2,8,8,96]{3,1,2,0:T(8,128)S(1)}, u32[]{:S(2)}, u32[]{:S(2)}) collective-permute-start(f32[2,8,8,96]{3,1,2,0:T(8,128)S(1)} %get-tuple-element.13), channel_id=1, source_target_pairs={{1,4},{2,5},{3,6},{9,12},{10,13},{11,14},{17,20},{18,21},{19,22},{... | collective-permute-start | bytes 147464 | tf_op jit(solution)/shard_map/ppermute | solution.py:46
  13.7 20.9 %collective-permute-start.15 = (f32[2,8,8,96]{3,1,2,0:T(8,128)S(1)}, f32[2,8,8,96]{3,1,2,0:T(8,128)}, u32[]{:S(2)}, u32[]{:S(2)}) collective-permute-start(f32[2,8,8,96]{3,1,2,0:T(8,128)S(1)} %get-tuple-element.12), channel_id=1, source_target_pairs={{4,1},{5,2},{6,3},{12,9},{13,10},{14,11},{20,17},{21,18},{22,19},{... | collective-permute-start | bytes 147464 | tf_op jit(solution)/shard_map/ppermute | solution.py:46
  15.1 28.8 %collective-permute-start.13 = (f32[2,48,8,96]{3,1,2,0:T(8,128)S(1)}, f32[2,48,8,96]{3,1,2,0:T(8,128)S(1)}, u32[]{:S(2)}, u32[]{:S(2)}) collective-permute-start(f32[2,48,8,96]{3,1,2,0:T(8,128)S(1)} %get-tuple-element.16), channel_id=1, source_target_pairs={{0,1},{1,2},{2,3},{4,5},{5,6},{6,7},{8,9},{9,10},{10,11},{12,13},{... | collective-permute-start | bytes 884744 | tf_op jit(solution)/shard_map/ppermute | solution.py:46
  19.9 3.6 %collective-permute-start.8 = (s32[4,1]{0,1:T(1,128)S(1)}, s32[4,1]{0,1:T(1,128)S(1)}, u32[]{:S(2)}, u32[]{:S(2)}) collective-permute-start(s32[4,1]{0,1:T(1,128)S(1)} %compare_select_fusion.1), channel_id=1, source_target_pairs={{0,8},{8,0},{16,24},{24,16},{1,9},{9,1},{17,25},{25,17},{2,10},{10... | collective-permute-start | bytes 56 | tf_op jit(solution)/shard_map/ppermute | solution.py:60
  23.5 4.4 %collective-permute-start.9 = (s32[4,1]{0,1:T(1,128)S(1)}, s32[4,1]{0,1:T(1,128)S(1)}, u32[]{:S(2)}, u32[]{:S(2)}) collective-permute-start(s32[4,1]{0,1:T(1,128)S(1)} %fusion.398), channel_id=1, source_target_pairs={{0,16},{8,24},{16,0},{24,8},{1,17},{9,25},{17,1},{25,9},{2,18},{10... | collective-permute-start | bytes 56 | tf_op jit(solution)/shard_map/ppermute | solution.py:60
  28.0 15.9 %collective-permute-start.14 = (f32[2,48,8,96]{3,1,2,0:T(8,128)S(1)}, f32[2,48,8,96]{3,1,2,0:T(8,128)S(1)}, u32[]{:S(2)}, u32[]{:S(2)}) collective-permute-start(f32[2,48,8,96]{3,1,2,0:T(8,128)S(1)} %get-tuple-element.17), channel_id=1, source_target_pairs={{1,0},{2,1},{3,2},{5,4},{6,5},{7,6},{9,8},{10,9},{11,10},{13,12},{... | collective-permute-start | bytes 884744 | tf_op jit(solution)/shard_map/ppermute | solution.py:46
  29.3 6.7 %collective-permute-start.17 = (f32[2,8,8,96]{3,1,2,0:T(8,128)S(1)}, f32[2,8,8,96]{3,1,2,0:T(8,128)S(1)}, u32[]{:S(2)}, u32[]{:S(2)}) collective-permute-start(f32[2,8,8,96]{3,1,2,0:T(8,128)S(1)} %get-tuple-element.11), channel_id=1, source_target_pairs={{5,0},{6,1},{7,2},{13,8},{14,9},{15,10},{21,16},{22,17},{23,18},{2... | collective-permute-start | bytes 147464 | tf_op jit(solution)/shard_map/ppermute | solution.py:46
  30.6 8.5 %collective-permute-start.11 = (f32[2,8,24,96]{3,1,2,0:T(8,128)S(1)}, f32[2,8,24,96]{3,1,2,0:T(8,128)S(1)}, u32[]{:S(2)}, u32[]{:S(2)}) collective-permute-start(f32[2,8,24,96]{3,1,2,0:T(8,128)S(1)} %get-tuple-element.14), channel_id=1, source_target_pairs={{0,4},{1,5},{2,6},{3,7},{8,12},{9,13},{10,14},{11,15},{16,20},{17,... | collective-permute-start | bytes 442376 | tf_op jit(solution)/shard_map/ppermute | solution.py:46
  34.6 9.2 %collective-permute-start.16 = (f32[2,8,24,96]{3,1,2,0:T(8,128)S(1)}, f32[2,8,24,96]{3,1,2,0:T(8,128)S(1)}, u32[]{:S(2)}, u32[]{:S(2)}) collective-permute-start(f32[2,8,24,96]{3,1,2,0:T(8,128)S(1)} %get-tuple-element.15), channel_id=1, source_target_pairs={{4,0},{5,1},{6,2},{7,3},{12,8},{13,9},{14,10},{15,11},{20,16},{21,... | collective-permute-start | bytes 442376 | tf_op jit(solution)/shard_map/ppermute | solution.py:46
  49.5 1.7 copy-start
  51.4 8.6 %collective-permute-start = (f32[1,8,8,96]{3,1,2,0:T(8,128)S(1)}, f32[1,8,8,96]{3,1,2,0:T(8,128)S(1)}, u32[]{:S(2)}, u32[]{:S(2)}) collective-permute-start(f32[1,8,8,96]{3,1,2,0:T(8,128)S(1)} %get-tuple-element.18), channel_id=1, source_target_pairs={{0,5},{1,6},{2,7},{8,13},{9,14},{10,15},{16,21},{17,22},{18,23},{2... | collective-permute-start | bytes 73736 | tf_op jit(solution)/shard_map/ppermute | solution.py:46
  53.0 8.3 %collective-permute-start.2 = (f32[1,8,8,96]{3,1,2,0:T(8,128)S(1)}, f32[1,8,8,96]{3,1,2,0:T(8,128)S(1)}, u32[]{:S(2)}, u32[]{:S(2)}) collective-permute-start(f32[1,8,8,96]{3,1,2,0:T(8,128)S(1)} %get-tuple-element.21), channel_id=1, source_target_pairs={{1,4},{2,5},{3,6},{9,12},{10,13},{11,14},{17,20},{18,21},{19,22},{... | collective-permute-start | bytes 73736 | tf_op jit(solution)/shard_map/ppermute | solution.py:46
  53.6 11.5 %collective-permute-start.5 = (f32[1,8,8,96]{3,1,2,0:T(8,128)S(1)}, f32[1,8,8,96]{3,1,2,0:T(8,128)S(1)}, u32[]{:S(2)}, u32[]{:S(2)}) collective-permute-start(f32[1,8,8,96]{3,1,2,0:T(8,128)S(1)} %get-tuple-element.20), channel_id=1, source_target_pairs={{4,1},{5,2},{6,3},{12,9},{13,10},{14,11},{20,17},{21,18},{22,19},{... | collective-permute-start | bytes 73736 | tf_op jit(solution)/shard_map/ppermute | solution.py:46
  54.3 17.9 %collective-permute-start.3 = (f32[1,48,8,96]{3,1,2,0:T(8,128)S(1)}, f32[1,48,8,96]{3,1,2,0:T(8,128)S(1)}, u32[]{:S(2)}, u32[]{:S(2)}) collective-permute-start(f32[1,48,8,96]{3,1,2,0:T(8,128)S(1)} %get-tuple-element.24), channel_id=1, source_target_pairs={{0,1},{1,2},{2,3},{4,5},{5,6},{6,7},{8,9},{9,10},{10,11},{12,13},{... | collective-permute-start | bytes 442376 | tf_op jit(solution)/shard_map/ppermute | solution.py:46
  58.6 13.7 %collective-permute-start.4 = (f32[1,48,8,96]{3,1,2,0:T(8,128)S(1)}, f32[1,48,8,96]{3,1,2,0:T(8,128)S(1)}, u32[]{:S(2)}, u32[]{:S(2)}) collective-permute-start(f32[1,48,8,96]{3,1,2,0:T(8,128)S(1)} %get-tuple-element.25), channel_id=1, source_target_pairs={{1,0},{2,1},{3,2},{5,4},{6,5},{7,6},{9,8},{10,9},{11,10},{13,12},{... | collective-permute-start | bytes 442376 | tf_op jit(solution)/shard_map/ppermute | solution.py:46
  60.0 6.5 %collective-permute-start.7 = (f32[1,8,8,96]{3,1,2,0:T(8,128)S(1)}, f32[1,8,8,96]{3,1,2,0:T(8,128)S(1)}, u32[]{:S(2)}, u32[]{:S(2)}) collective-permute-start(f32[1,8,8,96]{3,1,2,0:T(8,128)S(1)} %get-tuple-element.19), channel_id=1, source_target_pairs={{5,0},{6,1},{7,2},{13,8},{14,9},{15,10},{21,16},{22,17},{23,18},{2... | collective-permute-start | bytes 73736 | tf_op jit(solution)/shard_map/ppermute | solution.py:46
  61.3 6.3 %collective-permute-start.1 = (f32[1,8,24,96]{3,1,2,0:T(8,128)S(1)}, f32[1,8,24,96]{3,1,2,0:T(8,128)S(1)}, u32[]{:S(2)}, u32[]{:S(2)}) collective-permute-start(f32[1,8,24,96]{3,1,2,0:T(8,128)S(1)} %get-tuple-element.22), channel_id=1, source_target_pairs={{0,4},{1,5},{2,6},{3,7},{8,12},{9,13},{10,14},{11,15},{16,20},{17,... | collective-permute-start | bytes 221192 | tf_op jit(solution)/shard_map/ppermute | solution.py:46
  65.2 7.1 %collective-permute-start.6 = (f32[1,8,24,96]{3,1,2,0:T(8,128)S(1)}, f32[1,8,24,96]{3,1,2,0:T(8,128)S(1)}, u32[]{:S(2)}, u32[]{:S(2)}) collective-permute-start(f32[1,8,24,96]{3,1,2,0:T(8,128)S(1)} %get-tuple-element.23), channel_id=1, source_target_pairs={{4,0},{5,1},{6,2},{7,3},{12,8},{13,9},{14,10},{15,11},{20,16},{21,... | collective-permute-start | bytes 221192 | tf_op jit(solution)/shard_map/ppermute | solution.py:46
  103.8 16.4 %all-to-all-start = ((f32[8,24,1,1152]{3,1,2,0:T(8,128)}), f32[8,24,1,1152]{3,1,2,0:T(8,128)S(1)}, u32[]{:S(2)}, u32[]{:S(2)}) async-start(f32[8,24,1,1152]{3,1,2,0:T(8,128)} %convolution_bitcast_fusion), calls=%async_computation.1 | async-start | bytes 1769472 | tf_op jit(solution)/shard_map/all_to_all | solution.py:120
  107.5 17.0 %copy-start.3 = (f32[192]{0:T(256)}, f32[192]{0:T(256)S(1)}, u32[]{:S(2)}) copy-start(f32[192]{0:T(256)S(1)} %get-tuple-element.33) | copy-start | bytes 2308
  131.4 1.6 copy-start.1
  131.4 1.6 copy-start.2
  131.4 1.6 copy-start.4
  152.9 17.2 %all-to-all-start.1 = ((f32[8,24,1,1280]{3,1,2,0:T(8,128)}), f32[8,24,1,1280]{3,1,2,0:T(8,128)S(1)}, u32[]{:S(2)}, u32[]{:S(2)}) async-start(f32[8,24,1,1280]{3,1,2,0:T(8,128)} %pad_bitcast_fusion), calls=%async_computation.2 | async-start | bytes 1966080 | tf_op jit(solution)/shard_map/all_to_all | solution.py:144
Sparse Core Ops, SparseCore 0:
  51.3 48.5 reduce-scatter.1

commit v3 on v1

--- a/solution.py
+++ b/solution.py
@@ -17,17 +17,19 @@
 def extended(cells, sides, width):
     for axis, dim in sides:
         count = lax.axis_size(axis)
-        ends = count - 1
+        extent = cells.shape[dim]
         head = lax.slice_in_dim(cells, 0, width, axis=dim)
-        tail = lax.slice_in_dim(cells, cells.shape[dim] - width, cells.shape[dim], axis=dim)
-        cells = jnp.concatenate(
-            [
-                lax.ppermute(tail, axis, [(i, (i + 1) % count) for i in range(ends)]),
-                cells,
-                lax.ppermute(head, axis, [((i + 1) % count, i) for i in range(ends)]),
-            ],
-            axis=dim,
-        )
+        tail = lax.slice_in_dim(cells, extent - width, extent, axis=dim)
+        if count == 2:
+            first = lax.axis_index(axis) == 0
+            got = lax.ppermute(jnp.where(first, tail, head), axis, [(0, 1), (1, 0)])
+            empty = jnp.zeros_like(got)
+            before = jnp.where(first, empty, got)
+            after = jnp.where(first, got, empty)
+        else:
+            before = lax.ppermute(tail, axis, [(i, i + 1) for i in range(count - 1)])
+            after = lax.ppermute(head, axis, [(i + 1, i) for i in range(count - 1)])
+        cells = jnp.concatenate([before, cells, after], axis=dim)
     return cells
 
 
@@ -60,9 +62,9 @@
     matrix_y = band_matrix(wide_y, wide_y - 16, 8)
     matrix_z = band_matrix(wide_z, wide_z - 16, 8)
     matrix_x = band_matrix(length, length, 0)
-    step_one = jnp.einsum("oqzx,qy->oyzx", padded, matrix_y, precision=fast_mode)
-    step_two = jnp.einsum("oyqx,qz->oyzx", step_one, matrix_z, precision=fast_mode)
-    return jnp.matmul(step_two, matrix_x, precision=fast_mode)
+    step_one = jnp.einsum("oqzx,qy->oyzx", padded, matrix_y, precision=precise_mode)
+    step_two = jnp.einsum("oyqx,qz->oyzx", step_one, matrix_z, precision=precise_mode)
+    return jnp.matmul(step_two, matrix_x, precision=precise_mode)
 
 
 def channel_of(channel, length):
@@ -122,34 +124,37 @@
     back_z = contract(back_y, table, 2, 1)
     back = back_z.reshape(width, pair_count, count_y, rows_y, count_z, rows_z)
     back = back.transpose(2, 4, 0, 1, 3, 5).reshape(spread, width, pair_count, rows_y * rows_z)
+    rider = jnp.broadcast_to(energy_part[None, None, :, None], (spread, width, pair_count, 128))
+    back = jnp.concatenate((back, rider), axis=3)
     got = lax.all_to_all(back, ("gy", "gz"), 0, 0, tiled=True)
-    got = got.reshape(period, pair_count, rows_y * rows_z)
+    energy_total = jnp.sum(got[:, 0, :, rows_y * rows_z], axis=0)
+    got = got[:, :, :, : rows_y * rows_z].reshape(period, pair_count, rows_y * rows_z)
     result = contract(got, table, 0, 1)
-    return result.reshape(pair_count, rows_y, rows_z, length), energy_part
+    return result.reshape(pair_count, rows_y, rows_z, length), energy_total
 
 
 def shards(i_coeff, j_coeff, pair_orbital, pair_occ):
     fields = jnp.concatenate((i_coeff, j_coeff), 0)
     padded = extended(fields, (("gy", 1), ("gz", 2)), 8)
-    orbitals = synthesize(padded)
-    own_orbital = orbitals[0]
-    local_partners = orbitals[1:]
+    own_count = i_coeff.shape[0]
+    local_partners = synthesize(padded[own_count:])
     local_count = local_partners.shape[0]
     band_count = lax.axis_size("band")
     mine = lax.axis_index("band") == jnp.arange(band_count, dtype=jnp.int32)[:, None]
     wanted = group_sum(jnp.where(mine, pair_orbital, 0), ("band",))
     first_owned = lax.axis_index("band") * local_count
-    slots = jnp.zeros(wanted.shape + own_orbital.shape, jnp.float32)
+    slots = jnp.zeros(wanted.shape + local_partners.shape[1:], jnp.float32)
     for number in range(local_count):
         hit = (wanted == first_owned + number)[:, :, None, None, None]
         slots = jnp.where(hit, local_partners[number][None, None], slots)
     partner = lax.psum_scatter(slots, "band", scatter_dimension=0, tiled=True)[0]
+    own_orbital = synthesize(padded[:own_count])[0]
     density = own_orbital[None] * partner
     potential, energy_part = potentials(density)
     weights = pair_occ[0].astype(jnp.float32)
     applied = -jnp.sum(weights[:, None, None, None] * potential * partner, axis=0)
     length = own_orbital.shape[2]
-    energy = group_sum(energy_part, ("gz", "gy")) / float(length**3)
+    energy = energy_part / float(length**3)
     return (applied[None], energy[None])
 
 

time: 182 us -> 178 us (0.978)
  starting transfers between devices: 31.9 us -> 17.4 us
  waiting for transfers between devices: 79 us -> 86 us
  matrix products: 20.9 us -> 26.4 us
  between operations: 19.3 us -> 17.4 us
    all_to_all x1, waiting for transfers between devices: 0.01 us -> 13 us  [potentials(): got = lax.all_to_all(back, ('gy', 'gz'), 0, 0, tiled=True)]
    ppermute x5 -> x2, starting transfers between devices: 14.9 us -> 4.54 us  [group_sum(): lax.ppermute(total, axis, [(i, i ^ step) for i in range(count)])]
    dot_general x3 -> x6, matrix products: 5.87 us -> 10.3 us  [the longest x2 4.79 us: synthesize(): jnp.einsum('oqzx,qy->oyzx', padded, matrix_y, precision=precise_mode)]
    ppermute x4 -> x3, starting transfers between devices: 9.65 us -> 5.62 us  [the longest x1 3 us: extended(): got = lax.ppermute(jnp.where(first, tail, head), axis, [(0, 1), (1, 0)])]
    ppermute x5 -> x2, waiting for transfers between devices: 5.54 us -> 1.6 us  [group_sum(): lax.ppermute(total, axis, [(i, i ^ step) for i in range(count)])]
    ppermute x4 -> x3, waiting for transfers between devices: 6.15 us -> 5.31 us  [the longest x1 4.7 us: extended(): got = lax.ppermute(jnp.where(first, tail, head), axis, [(0, 1), (1, 0)])]
  transfers between devices with their start and end apart: 12 -> 8, of which waited for: 8 -> 6; matrix products, arithmetic and copies ran while one was open for 2% -> 3% of each run, Pallas kernels for 0% -> 0%
where the time goes in v3:
time: 178 us
  waiting for transfers between devices  86 us (48%)
  matrix products  26.4 us (15%)
  local copies, waits for them, and re-layouts  25 us (14%)
  starting transfers between devices  17.4 us (10%)
  between operations  17.4 us (10%)
  other arithmetic  5.26 us (3%)
    reduce_scatter x1, waiting for transfers between devices, shards(): lax.psum_scatter(slots, 'band', scatter_dimension=0, tiled=True)[0]  54.8 us
    dot_general x6, matrix products, contract(): lax.dot_general(left, right, (((left_dim,), (right_dim,)), ((), ())), pre...  16.1 us
    all_to_all x1, waiting for transfers between devices, potentials(): got = lax.all_to_all(back, ('gy', 'gz'), 0, 0, tiled=True)  13 us
    all_to_all x1, waiting for transfers between devices, potentials(): got = lax.all_to_all(send, ('gy', 'gz'), 0, 0, tiled=True)  11.3 us
    transpose x1, local copies, waits for them, and re-layouts, potentials(): got.transpose(2, 3, 0, 4, 1, 5)  5.61 us
    dot_general x2, matrix products, synthesize(): jnp.einsum('oqzx,qy->oyzx', padded, matrix_y, precision=precise_mode)  4.79 us
    ppermute x1, waiting for transfers between devices, extended(): got = lax.ppermute(jnp.where(first, tail, head), axis, [(0, 1), (1, 0)])  4.7 us
    ppermute x2, starting transfers between devices, group_sum(): lax.ppermute(total, axis, [(i, i ^ step) for i in range(count)])  4.54 us
  transfers between devices with their start and end apart: 8, of which 6 were waited for; matrix products, arithmetic and copies ran while one was open for 3% of the time, Pallas kernels for 0%

profile of v3, /device:TPU:0, one launch (start us, length us, event | category | flops | bytes accessed | tf_op | source)
XLA Modules:
  0.0 177.5 jit_solution(862414485489735061)
XLA Ops:
  7.2 0.0 reduce-scatter.2.cloned.1.call-start
  7.2 1.2 copy_dynamic-update-slice_fusion.1
  8.4 1.5 copy_dynamic-update-slice_fusion
  9.9 3.0 %collective-permute-start = (f32[3,8,24,96]{3,1,2,0:T(8,128)S(1)}, f32[3,8,24,96]{3,1,2,0:T(8,128)S(1)}, u32[]{:S(2)}, u32[]{:S(2)}) collective-permute-start(f32[3,8,24,96]{3,1,2,0:T(8,128)S(1)} %slice_select_fusion), channel_id=1, source_target_pairs={{0,4},{4,0},{1,5},{5,1},{2,6},{6,2},{3,7},{7,3},{8,12},{12,8},{9,1... | collective-permute-start | bytes 663560 | tf_op jit(solution)/shard_map/ppermute | solution.py:25
  13.6 1.6 collective-permute-start.3
  15.2 4.7 %collective-permute-done = f32[3,8,24,96]{3,1,2,0:T(8,128)S(1)} collective-permute-done((f32[3,8,24,96]{3,1,2,0:T(8,128)S(1)}, f32[3,8,24,96]{3,1,2,0:T(8,128)S(1)}, u32[]{:S(2)}, u32[]{:S(2)}) %collective-permute-start) | collective-permute-done | bytes 221216 | tf_op jit(solution)/shard_map/ppermute | solution.py:25
  20.0 1.3 pad_maximum_fusion.12
  21.3 1.3 collective-permute-start.1
  22.6 1.3 collective-permute-start.2
  24.0 2.9 %collective-permute-start.4 = (s32[4,1]{0,1:T(1,128)S(1)}, s32[4,1]{0,1:T(1,128)S(1)}, u32[]{:S(2)}, u32[]{:S(2)}) collective-permute-start(s32[4,1]{0,1:T(1,128)S(1)} %fusion.366), channel_id=1, source_target_pairs={{0,16},{8,24},{16,0},{24,8},{1,17},{9,25},{17,1},{25,9},{2,18},{10... | collective-permute-start | bytes 56 | tf_op jit(solution)/shard_map/ppermute | solution.py:45
  26.9 1.6 collective-permute-done.4
  28.5 0.6 collective-permute-done.2
  29.1 2.8 %fusion.11 = f32[2,48,40,96]{3,1,2,0:T(8,128)S(1)} fusion(f32[3,64,8,96]{3,1,2,0:T(8,128)} %collective-permute-done.2, f32[3,64,8,96]{3,1,2,0:T(8,128)S(1)} %collective-permute-done.1, f32[3,8,24,96]{3,1,2,0:T(8,128)S(1)} %get-tuple-element.13, f32[3,48,24,96]{3,1,2,0:T(8,128)S(1)} %copy_dynamic-update-slice_fusion, ...), kind=kOutput, calls=%fused_computation.20 | convolution fusion | flops 285229056 | bytes 4423936 | tf_op jit(solution)/shard_map/oqzx,qy->oyzx/dot_general | solution.py:65
  32.0 1.7 fusion.12
  33.7 1.2 fusion.28
  34.9 0.1 slice_bitcast_fusion.1
  34.9 1.7 select_select_fusion
  36.6 0.0 reduce-scatter.2.cloned.1.call-update
  36.7 0.1 or_select_fusion.1
  36.8 1.9 %fusion.15 = f32[48,40,96]{2,0,1:T(8,128)S(1)} fusion(f32[3,64,8,96]{3,1,2,0:T(8,128)} %collective-permute-done.2, f32[3,64,8,96]{3,1,2,0:T(8,128)S(1)} %collective-permute-done.1, f32[3,8,24,96]{3,1,2,0:T(8,128)S(1)} %get-tuple-element.13, f32[3,48,24,96]{3,1,2,0:T(8,128)S(1)} %copy_dynamic-update-slice_fusion, ...), kind=kOutput, calls=%fused_computation.23 | convolution fusion | flops 142688256 | bytes 3686656 | tf_op jit(solution)/shard_map/oqzx,qy->oyzx/dot_general | solution.py:65
  38.7 0.9 convolution_bitcast_fusion.2
  39.6 54.8 %reduce-scatter.2.cloned.1.call-done = f32[1,1,48,24,96]{4,2,3,1,0:T(8,128)} async-done(((f32[4,1,48,24,96]{4,2,3,1,0:T(8,128)}), f32[1,1,48,24,96]{4,2,3,1,0:T(8,128)}) %reduce-scatter.2.cloned.1.call-update) | async-done | bytes 442384 | tf_op jit(solution)/shard_map/reduce_scatter | solution.py:150
  94.4 1.8 convolution_multiply_fusion.1
  96.2 0.2 copy.23
  96.4 1.9 %convolution_bitcast_fusion = f32[8,24,1,1152]{3,1,2,0:T(8,128)} fusion(f32[1152,96,1]{1,0,2:T(8,128)S(1)} %bitcast.119, s32[8,24]{1,0:T(8,128)S(1)} %add_select_fusion.3, pred[8,24]{1,0:T(8,128)(4,1)S(1)} %fusion.130), kind=kOutput, calls=%fused_computation.9 | convolution fusion | flops 127586304 | bytes 1328064 | tf_op jit(solution)/shard_map/dot_general | solution.py:89
  98.3 3.7 %all-to-all-start = ((f32[8,24,1,1152]{3,1,2,0:T(8,128)}), f32[8,24,1,1152]{3,1,2,0:T(8,128)S(1)}, u32[]{:S(2)}, u32[]{:S(2)}) async-start(f32[8,24,1,1152]{3,1,2,0:T(8,128)} %convolution_bitcast_fusion), calls=%async_computation.1 | async-start | bytes 1769472 | tf_op jit(solution)/shard_map/all_to_all | solution.py:105
  101.9 0.1 or_select_fusion
  102.0 0.7 broadcast_multiply_fusion
  102.7 0.7 broadcast_add_fusion
  103.4 11.3 %all-to-all-done = f32[8,24,1,1152]{3,1,2,0:T(8,128)S(1)} async-done(((f32[8,24,1,1152]{3,1,2,0:T(8,128)}), f32[8,24,1,1152]{3,1,2,0:T(8,128)S(1)}, u32[]{:S(2)}, u32[]{:S(2)}) %all-to-all-start) | async-done | bytes 884768 | tf_op jit(solution)/shard_map/all_to_all | solution.py:105
  114.6 4.3 %reshape.373 = f32[2,4,24,1,48,24]{5,4,2,1,0,3:T(8,128)} reshape(f32[8,24,1,1152]{3,1,2,0:T(8,128)S(1)} %all-to-all-done) | data formatting | bytes 1769472 | tf_op jit(solution)/shard_map/reshape | solution.py:106
  119.0 5.6 %copy.26 = f32[24,1,2,48,4,24]{3,2,5,4,0,1:T(2,128)S(1)} copy(f32[24,1,2,48,4,24]{5,3,0,4,2,1:T(8,128)} %bitcast.114) | data formatting | bytes 1769472 | tf_op jit(solution)/shard_map/transpose | solution.py:107
  124.6 1.3 reshape.374
  125.9 0.0 copy-start.1
  125.9 1.5 fusion.43
  127.5 3.8 %multiply_reduce_fusion = (f32[]{:T(128)}, f32[24,192,192]{2,1,0:T(8,128)S(1)}) fusion(f32[192]{0:T(256)S(1)} %copy-done.3, f32[24,192]{1,0:T(8,128)S(1)} %copy-done.1, f32[192]{0:T(256)S(1)} %get-tuple-element.20, f32[24,192]{1,0:T(8,128)S(1)} %copy-done, f32[24,96,192]{1,2,0:T(8,128)S(1)} %fusion.43, s32[192]{0:T(256)S(1)} %add_select_fusion.4, ...), kind=kOutput, calls=%fused_computation | convolution fusion | flops 516870144 | bytes 5347780 | tf_op jit(solution)/shard_map/dot_general | solution.py:89
  131.3 3.8 %fusion = f32[24,192,96]{1,2,0:T(8,128)S(1)} fusion(f32[24,192,192]{2,1,0:T(8,128)S(1)} %get-tuple-element.17, f32[192]{0:T(256)S(1)} %copy-done.3, f32[24,192]{1,0:T(8,128)S(1)} %copy-done.1, f32[192]{0:T(256)S(1)} %get-tuple-element.20, f32[24,192]{1,0:T(8,128)S(1)} %copy-done, s32[192]{0:T(256)S(1)} %add_select_fusion.4, ...), kind=kOutput, calls=%fused_computation.2 | convolution fusion | flops 515100672 | bytes 5347776 | tf_op jit(solution)/shard_map/dot_general | solution.py:89
  135.2 2.6 %convolution_bitcast_fusion.1 = f32[2,4,24,1,48,24]{4,5,1,0,2,3:T(8,128)S(1)} fusion(f32[24,2,48,192,1]{3,2,4,1,0:T(8,128)S(1)} %bitcast.118, s32[192]{0:T(256)S(1)} %add_select_fusion.4, s32[4,24]{1,0:T(4,128)S(1)} %multiply_add_fusion.1, pred[192]{0:T(512)(128)(4,1)S(1)} %iota_compare_fusion), kind=kOutput, calls=%fused_computation.19 | convolution fusion | flops 254988288 | bytes 2655552 | tf_op jit(solution)/shard_map/dot_general | solution.py:89
  137.8 3.6 %copy.29 = f32[2,4,24,1,48,24]{5,4,2,1,0,3:T(8,128)} copy(f32[2,4,24,1,48,24]{4,5,1,0,2,3:T(8,128)S(1)} %convolution_bitcast_fusion.1) | data formatting | bytes 1769472 | tf_op jit(solution)/shard_map/transpose | solution.py:126
  141.4 4.2 %reshape.376 = f32[8,24,1,1152]{3,1,0,2:T(8,128)S(1)} reshape(f32[2,4,24,1,48,24]{5,4,2,1,0,3:T(8,128)} %copy.29) | data formatting | bytes 1769472 | tf_op jit(solution)/shard_map/reshape | solution.py:126
  145.6 1.7 pad_bitcast_fusion
  147.3 3.6 %all-to-all-start.1 = ((f32[8,24,1,1280]{3,1,2,0:T(8,128)}), f32[8,24,1,1280]{3,1,2,0:T(8,128)S(1)}, u32[]{:S(2)}, u32[]{:S(2)}) async-start(f32[8,24,1,1280]{3,1,2,0:T(8,128)} %pad_bitcast_fusion), calls=%async_computation.2 | async-start | bytes 1966080 | tf_op jit(solution)/shard_map/all_to_all | solution.py:129
  151.5 13.0 %all-to-all-done.1 = f32[8,24,1,1280]{3,1,2,0:T(8,128)S(1)} async-done(((f32[8,24,1,1280]{3,1,2,0:T(8,128)}), f32[8,24,1,1280]{3,1,2,0:T(8,128)S(1)}, u32[]{:S(2)}, u32[]{:S(2)}) %all-to-all-start.1) | async-done | bytes 983072 | tf_op jit(solution)/shard_map/all_to_all | solution.py:129
  164.5 0.1 slice.44
  164.6 0.4 copy.32
  165.0 2.3 %fusion.26 = f32[1,48,24,96]{3,1,2,0:T(8,128)S(1)} fusion(f32[48,24,192]{2,1,0:T(8,128)S(1)} %bitcast.115, f32[1,1,48,24,96]{4,2,3,1,0:T(8,128)} %reduce-scatter.2.cloned.1.call-done, f32[]{:T(128)} %bitcast, s32[192]{0:T(256)S(1)} %add_select_fusion.4, pred[192]{0:T(512)(128)(4,1)S(1)} %iota_compare_fusion), kind=kOutput, calls=%fused_computation.35 | convolution fusion | flops 127918080 | bytes 1770436 | tf_op jit(solution)/shard_map/dot_general | solution.py:89
  167.3 1.0 copy.34
  168.3 0.6 slice_reduce_fusion
  (21 shorter events, 0.1 us)
Async XLA Ops:
  7.2 87.2 %reduce-scatter.2.cloned.1.call-start = ((), (), s32[]{:S(2)}) async-start(), calls=%async_computation.3 | async-start | bytes 2949120 | tf_op jit(solution)/shard_map/reduce_scatter | solution.py:150
  9.9 10.0 %collective-permute-start = (f32[3,8,24,96]{3,1,2,0:T(8,128)S(1)}, f32[3,8,24,96]{3,1,2,0:T(8,128)S(1)}, u32[]{:S(2)}, u32[]{:S(2)}) collective-permute-start(f32[3,8,24,96]{3,1,2,0:T(8,128)S(1)} %slice_select_fusion), channel_id=1, source_target_pairs={{0,4},{4,0},{1,5},{5,1},{2,6},{6,2},{3,7},{7,3},{8,12},{12,8},{9,1... | collective-permute-start | bytes 663560 | tf_op jit(solution)/shard_map/ppermute | solution.py:25
  13.6 10.4 %collective-permute-start.3 = (s32[4,1]{0,1:T(1,128)S(1)}, s32[4,1]{0,1:T(1,128)S(1)}, u32[]{:S(2)}, u32[]{:S(2)}) collective-permute-start(s32[4,1]{0,1:T(1,128)S(1)} %compare_select_fusion.1), channel_id=1, source_target_pairs={{0,8},{8,0},{16,24},{24,16},{1,9},{9,1},{17,25},{25,17},{2,10},{10... | collective-permute-start | bytes 56 | tf_op jit(solution)/shard_map/ppermute | solution.py:45
  21.3 7.2 %collective-permute-start.1 = (f32[3,64,8,96]{3,1,2,0:T(8,128)}, f32[3,64,8,96]{3,1,2,0:T(8,128)S(1)}, u32[]{:S(2)}, u32[]{:S(2)}) collective-permute-start(f32[3,64,8,96]{3,1,2,0:T(8,128)} %get-tuple-element.8), channel_id=1, source_target_pairs={{0,1},{1,2},{2,3},{4,5},{5,6},{6,7},{8,9},{9,10},{10,11},{12,13},{... | collective-permute-start | bytes 1769480 | tf_op jit(solution)/shard_map/ppermute | solution.py:30
  22.6 6.5 %collective-permute-start.2 = (f32[3,64,8,96]{3,1,2,0:T(8,128)}, f32[3,64,8,96]{3,1,2,0:T(8,128)}, u32[]{:S(2)}, u32[]{:S(2)}) collective-permute-start(f32[3,64,8,96]{3,1,2,0:T(8,128)} %get-tuple-element.9), channel_id=1, source_target_pairs={{1,0},{2,1},{3,2},{5,4},{6,5},{7,6},{9,8},{10,9},{11,10},{13,12},{... | collective-permute-start | bytes 1769480 | tf_op jit(solution)/shard_map/ppermute | solution.py:31
  24.0 4.5 %collective-permute-start.4 = (s32[4,1]{0,1:T(1,128)S(1)}, s32[4,1]{0,1:T(1,128)S(1)}, u32[]{:S(2)}, u32[]{:S(2)}) collective-permute-start(s32[4,1]{0,1:T(1,128)S(1)} %fusion.366), channel_id=1, source_target_pairs={{0,16},{8,24},{16,0},{24,8},{1,17},{9,25},{17,1},{25,9},{2,18},{10... | collective-permute-start | bytes 56 | tf_op jit(solution)/shard_map/ppermute | solution.py:45
  98.3 16.4 %all-to-all-start = ((f32[8,24,1,1152]{3,1,2,0:T(8,128)}), f32[8,24,1,1152]{3,1,2,0:T(8,128)S(1)}, u32[]{:S(2)}, u32[]{:S(2)}) async-start(f32[8,24,1,1152]{3,1,2,0:T(8,128)} %convolution_bitcast_fusion), calls=%async_computation.1 | async-start | bytes 1769472 | tf_op jit(solution)/shard_map/all_to_all | solution.py:105
  102.0 17.0 %copy-start.2 = (f32[192]{0:T(256)}, f32[192]{0:T(256)S(1)}, u32[]{:S(2)}) copy-start(f32[192]{0:T(256)S(1)} %get-tuple-element.21) | copy-start | bytes 2308
  125.9 1.6 copy-start
  125.9 1.6 copy-start.1
  125.9 1.6 copy-start.3
  147.3 17.2 %all-to-all-start.1 = ((f32[8,24,1,1280]{3,1,2,0:T(8,128)}), f32[8,24,1,1280]{3,1,2,0:T(8,128)S(1)}, u32[]{:S(2)}, u32[]{:S(2)}) async-start(f32[8,24,1,1280]{3,1,2,0:T(8,128)} %pad_bitcast_fusion), calls=%async_computation.2 | async-start | bytes 1966080 | tf_op jit(solution)/shard_map/all_to_all | solution.py:129
Sparse Core Ops, SparseCore 0:
  36.8 57.5 reduce-scatter.1

commit v4 on v3

--- a/solution.py
+++ b/solution.py
@@ -62,9 +62,9 @@
     matrix_y = band_matrix(wide_y, wide_y - 16, 8)
     matrix_z = band_matrix(wide_z, wide_z - 16, 8)
     matrix_x = band_matrix(length, length, 0)
-    step_one = jnp.einsum("oqzx,qy->oyzx", padded, matrix_y, precision=precise_mode)
+    step_one = jnp.matmul(padded, matrix_x, precision=precise_mode)
     step_two = jnp.einsum("oyqx,qz->oyzx", step_one, matrix_z, precision=precise_mode)
-    return jnp.matmul(step_two, matrix_x, precision=precise_mode)
+    return jnp.einsum("oqzx,qy->oyzx", step_two, matrix_y, precision=precise_mode)
 
 
 def channel_of(channel, length):

time: 178 us -> 178 us (level)
  waiting for transfers between devices: 86 us -> 82.9 us
  starting transfers between devices: 17.4 us -> 20 us
    ppermute x1, starting transfers between devices: 1.33 us -> 3.93 us  [extended(): before = lax.ppermute(tail, axis, [(i, i + 1) for i in range(count - 1)])]
    reduce_scatter x1, waiting for transfers between devices: 54.8 us -> 52.3 us  [shards(): lax.psum_scatter(slots, 'band', scatter_dimension=0, tiled=True)[0]]
  transfers between devices with their start and end apart: 8 -> 8, of which waited for: 6 -> 5; matrix products, arithmetic and copies ran while one was open for 3% -> 3% of each run, Pallas kernels for 0% -> 0%
where the time goes in v4:
time: 178 us
  waiting for transfers between devices  82.9 us (47%)
  matrix products  27.2 us (15%)
  local copies, waits for them, and re-layouts  24.9 us (14%)
  starting transfers between devices  20 us (11%)
  between operations  17.4 us (10%)
  other arithmetic  5.19 us (3%)
    reduce_scatter x1, waiting for transfers between devices, shards(): lax.psum_scatter(slots, 'band', scatter_dimension=0, tiled=True)[0]  52.3 us
    dot_general x6, matrix products, contract(): lax.dot_general(left, right, (((left_dim,), (right_dim,)), ((), ())), pre...  16.1 us
    all_to_all x1, waiting for transfers between devices, potentials(): got = lax.all_to_all(back, ('gy', 'gz'), 0, 0, tiled=True)  13 us
    all_to_all x1, waiting for transfers between devices, potentials(): got = lax.all_to_all(send, ('gy', 'gz'), 0, 0, tiled=True)  11.3 us
    transpose x1, local copies, waits for them, and re-layouts, potentials(): got.transpose(2, 3, 0, 4, 1, 5)  5.61 us
    dot_general x2, matrix products, synthesize(): step_one = jnp.matmul(padded, matrix_x, precision=precise_mode)  5.58 us
    ppermute x1, waiting for transfers between devices, extended(): got = lax.ppermute(jnp.where(first, tail, head), axis, [(0, 1), (1, 0)])  4.7 us
    ppermute x2, starting transfers between devices, group_sum(): lax.ppermute(total, axis, [(i, i ^ step) for i in range(count)])  4.54 us
  transfers between devices with their start and end apart: 8, of which 5 were waited for; matrix products, arithmetic and copies ran while one was open for 3% of the time, Pallas kernels for 0%

profile of v4, /device:TPU:0, one launch (start us, length us, event | category | flops | bytes accessed | tf_op | source)
XLA Modules:
  0.0 177.6 jit_solution(10884674966709982148)
XLA Ops:
  7.2 0.0 reduce-scatter.2.cloned.1.call-start
  7.2 1.1 constant_dynamic-update-slice_fusion.1
  8.3 1.4 constant_dynamic-update-slice_fusion
  9.7 3.0 %collective-permute-start = (f32[3,8,24,96]{3,2,1,0:T(8,128)S(1)}, f32[3,8,24,96]{3,2,1,0:T(8,128)S(1)}, u32[]{:S(2)}, u32[]{:S(2)}) collective-permute-start(f32[3,8,24,96]{3,2,1,0:T(8,128)S(1)} %slice_select_fusion), channel_id=1, source_target_pairs={{0,4},{4,0},{1,5},{5,1},{2,6},{6,2},{3,7},{7,3},{8,12},{12,8},{9,1... | collective-permute-start | bytes 663560 | tf_op jit(solution)/shard_map/ppermute | solution.py:25
  13.4 1.6 collective-permute-start.3
  15.0 4.7 %collective-permute-done = f32[3,8,24,96]{3,2,1,0:T(8,128)S(1)} collective-permute-done((f32[3,8,24,96]{3,2,1,0:T(8,128)S(1)}, f32[3,8,24,96]{3,2,1,0:T(8,128)S(1)}, u32[]{:S(2)}, u32[]{:S(2)}) %collective-permute-start) | collective-permute-done | bytes 221216 | tf_op jit(solution)/shard_map/ppermute | solution.py:25
  19.8 1.3 pad_maximum_fusion.2
  21.1 1.3 collective-permute-start.2
  22.3 3.9 %collective-permute-start.1 = (f32[3,64,8,96]{3,2,1,0:T(8,128)}, f32[3,64,8,96]{3,2,1,0:T(8,128)}, u32[]{:S(2)}, u32[]{:S(2)}) collective-permute-start(f32[3,64,8,96]{3,2,1,0:T(8,128)} %get-tuple-element.8), channel_id=1, source_target_pairs={{0,1},{1,2},{2,3},{4,5},{5,6},{6,7},{8,9},{9,10},{10,11},{12,13},{... | collective-permute-start | bytes 1769480 | tf_op jit(solution)/shard_map/ppermute | solution.py:30
  26.3 0.0 collective-permute-done.3
  26.3 2.9 %collective-permute-start.4 = (s32[4,1]{0,1:T(1,128)S(1)}, s32[4,1]{0,1:T(1,128)S(1)}, u32[]{:S(2)}, u32[]{:S(2)}) collective-permute-start(s32[4,1]{0,1:T(1,128)S(1)} %fusion.372), channel_id=1, source_target_pairs={{0,16},{8,24},{16,0},{24,8},{1,17},{9,25},{17,1},{25,9},{2,18},{10... | collective-permute-start | bytes 56 | tf_op jit(solution)/shard_map/ppermute | solution.py:45
  29.2 1.6 collective-permute-done.4
  30.8 3.4 %fusion = f32[2,64,40,96]{3,2,1,0:T(8,128)S(1)} fusion(f32[3,64,8,96]{3,2,1,0:T(8,128)S(1)} %collective-permute-done.2, f32[3,8,24,96]{3,2,1,0:T(8,128)S(1)} %get-tuple-element.13, f32[3,48,24,96]{3,2,1,0:T(8,128)S(1)} %constant_dynamic-update-slice_fusion, f32[3,8,24,96]{3,2,1,0:T(8,128)S(1)} %get-tuple-element.12, f32[3,64,8,96]{3,2,1,0:T(8,128)} %collective-permute-done.1), kind=kOutput, calls=%fused_computation.2 | convolution fusion | flops 569622528 | bytes 4915200 | tf_op jit(solution)/shard_map/dot_general | solution.py:65
  34.2 1.5 convolution_bitcast_fusion.2
  35.8 1.4 fusion.19
  37.1 0.1 slice_bitcast_fusion.1
  37.2 1.7 select_select_fusion
  38.9 0.0 reduce-scatter.2.cloned.1.call-update
  39.0 0.1 or_select_fusion.1
  39.0 2.2 %fusion.22 = f32[64,40,96]{2,1,0:T(8,128)S(1)} fusion(f32[3,64,8,96]{3,2,1,0:T(8,128)S(1)} %collective-permute-done.2, f32[3,64,8,96]{3,2,1,0:T(8,128)} %collective-permute-done.1, f32[3,8,24,96]{3,2,1,0:T(8,128)S(1)} %get-tuple-element.13, f32[3,48,24,96]{3,2,1,0:T(8,128)S(1)} %constant_dynamic-update-slice_fusion, f32[3,8,24,96]{3,2,1,0:T(8,128)S(1)} %get-tuple-element.12), kind=kOutput, calls=%fused_computation.27 | convolution fusion | flops 284540928 | bytes 3932160 | tf_op jit(solution)/shard_map/dot_general | solution.py:65
  41.2 0.8 convolution_bitcast_fusion.3
  42.1 52.3 %reduce-scatter.2.cloned.1.call-done = f32[1,1,48,24,96]{4,2,3,1,0:T(8,128)} async-done(((f32[4,1,48,24,96]{4,2,3,1,0:T(8,128)}), f32[1,1,48,24,96]{4,2,3,1,0:T(8,128)}) %reduce-scatter.2.cloned.1.call-update) | async-done | bytes 442384 | tf_op jit(solution)/shard_map/reduce_scatter | solution.py:150
  94.4 1.8 %convolution_multiply_fusion.1 = f32[48,24,96]{2,0,1:T(8,128)S(1)} fusion(f32[64,24,96]{2,1,0:T(8,128)S(1)} %convolution_bitcast_fusion.3, f32[1,1,48,24,96]{4,2,3,1,0:T(8,128)} %reduce-scatter.2.cloned.1.call-done, s32[64]{0:T(128)S(1)} %iota_add_fusion.2), kind=kOutput, calls=%fused_computation.41 | convolution fusion | flops 85192704 | bytes 1474816 | tf_op jit(solution)/shard_map/oqzx,qy->oyzx/dot_general | solution.py:67
  96.2 0.2 copy.19
  96.4 1.9 %convolution_bitcast_fusion = f32[8,24,1,1152]{3,1,2,0:T(8,128)} fusion(f32[1152,96,1]{1,0,2:T(8,128)S(1)} %bitcast.121, s32[8,24]{1,0:T(8,128)S(1)} %add_select_fusion.3, pred[8,24]{1,0:T(8,128)(4,1)S(1)} %fusion.134), kind=kOutput, calls=%fused_computation.13 | convolution fusion | flops 127586304 | bytes 1328064 | tf_op jit(solution)/shard_map/dot_general | solution.py:89
  98.4 3.7 %all-to-all-start = ((f32[8,24,1,1152]{3,1,2,0:T(8,128)}), f32[8,24,1,1152]{3,1,2,0:T(8,128)S(1)}, u32[]{:S(2)}, u32[]{:S(2)}) async-start(f32[8,24,1,1152]{3,1,2,0:T(8,128)} %convolution_bitcast_fusion), calls=%async_computation.1 | async-start | bytes 1769472 | tf_op jit(solution)/shard_map/all_to_all | solution.py:105
  102.0 0.1 or_select_fusion
  102.1 0.7 broadcast_add_fusion
  102.8 0.7 broadcast_multiply_fusion
  103.5 11.3 %all-to-all-done = f32[8,24,1,1152]{3,1,2,0:T(8,128)S(1)} async-done(((f32[8,24,1,1152]{3,1,2,0:T(8,128)}), f32[8,24,1,1152]{3,1,2,0:T(8,128)S(1)}, u32[]{:S(2)}, u32[]{:S(2)}) %all-to-all-start) | async-done | bytes 884768 | tf_op jit(solution)/shard_map/all_to_all | solution.py:105
  114.7 4.3 %reshape.373 = f32[2,4,24,1,48,24]{5,4,2,1,0,3:T(8,128)} reshape(f32[8,24,1,1152]{3,1,2,0:T(8,128)S(1)} %all-to-all-done) | data formatting | bytes 1769472 | tf_op jit(solution)/shard_map/reshape | solution.py:106
  119.1 5.6 %copy.22 = f32[24,1,2,48,4,24]{3,2,5,4,0,1:T(2,128)S(1)} copy(f32[24,1,2,48,4,24]{5,3,0,4,2,1:T(8,128)} %bitcast.116) | data formatting | bytes 1769472 | tf_op jit(solution)/shard_map/transpose | solution.py:107
  124.7 1.3 reshape.374
  126.0 0.0 copy-start
  126.0 1.5 fusion.47
  127.6 3.9 %multiply_reduce_fusion = (f32[]{:T(128)}, f32[24,192,192]{2,1,0:T(8,128)S(1)}) fusion(f32[192]{0:T(256)S(1)} %copy-done.3, f32[24,192]{1,0:T(8,128)S(1)} %copy-done, f32[192]{0:T(256)S(1)} %get-tuple-element.20, f32[24,192]{1,0:T(8,128)S(1)} %copy-done.1, f32[24,96,192]{1,2,0:T(8,128)S(1)} %fusion.47, s32[192]{0:T(256)S(1)} %add_select_fusion.4, ...), kind=kOutput, calls=%fused_computation | convolution fusion | flops 516870144 | bytes 5347780 | tf_op jit(solution)/shard_map/dot_general | solution.py:89
  131.4 3.8 %fusion.10 = f32[24,192,96]{1,2,0:T(8,128)S(1)} fusion(f32[24,192,192]{2,1,0:T(8,128)S(1)} %get-tuple-element.17, f32[192]{0:T(256)S(1)} %copy-done.3, f32[24,192]{1,0:T(8,128)S(1)} %copy-done, f32[192]{0:T(256)S(1)} %get-tuple-element.20, f32[24,192]{1,0:T(8,128)S(1)} %copy-done.1, s32[192]{0:T(256)S(1)} %add_select_fusion.4, ...), kind=kOutput, calls=%fused_computation.12 | convolution fusion | flops 515100672 | bytes 5347776 | tf_op jit(solution)/shard_map/dot_general | solution.py:89
  135.2 2.6 %convolution_bitcast_fusion.1 = f32[2,4,24,1,48,24]{4,5,1,0,2,3:T(8,128)S(1)} fusion(f32[24,2,48,192,1]{3,2,4,1,0:T(8,128)S(1)} %bitcast.120, s32[192]{0:T(256)S(1)} %add_select_fusion.4, s32[4,24]{1,0:T(4,128)S(1)} %multiply_add_fusion.1, pred[192]{0:T(512)(128)(4,1)S(1)} %iota_compare_fusion), kind=kOutput, calls=%fused_computation.21 | convolution fusion | flops 254988288 | bytes 2655552 | tf_op jit(solution)/shard_map/dot_general | solution.py:89
  137.9 3.6 %copy.25 = f32[2,4,24,1,48,24]{5,4,2,1,0,3:T(8,128)} copy(f32[2,4,24,1,48,24]{4,5,1,0,2,3:T(8,128)S(1)} %convolution_bitcast_fusion.1) | data formatting | bytes 1769472 | tf_op jit(solution)/shard_map/transpose | solution.py:126
  141.5 4.2 %reshape.376 = f32[8,24,1,1152]{3,1,0,2:T(8,128)S(1)} reshape(f32[2,4,24,1,48,24]{5,4,2,1,0,3:T(8,128)} %copy.25) | data formatting | bytes 1769472 | tf_op jit(solution)/shard_map/reshape | solution.py:126
  145.7 1.7 pad_bitcast_fusion
  147.4 3.6 %all-to-all-start.1 = ((f32[8,24,1,1280]{3,1,2,0:T(8,128)}), f32[8,24,1,1280]{3,1,2,0:T(8,128)S(1)}, u32[]{:S(2)}, u32[]{:S(2)}) async-start(f32[8,24,1,1280]{3,1,2,0:T(8,128)} %pad_bitcast_fusion), calls=%async_computation.2 | async-start | bytes 1966080 | tf_op jit(solution)/shard_map/all_to_all | solution.py:129
  151.6 13.0 %all-to-all-done.1 = f32[8,24,1,1280]{3,1,2,0:T(8,128)S(1)} async-done(((f32[8,24,1,1280]{3,1,2,0:T(8,128)}), f32[8,24,1,1280]{3,1,2,0:T(8,128)S(1)}, u32[]{:S(2)}, u32[]{:S(2)}) %all-to-all-start.1) | async-done | bytes 983072 | tf_op jit(solution)/shard_map/all_to_all | solution.py:129
  164.6 0.1 slice.44
  164.7 0.4 copy.28
  165.0 2.3 %fusion.33 = f32[1,48,24,96]{3,1,2,0:T(8,128)S(1)} fusion(f32[48,24,192]{2,1,0:T(8,128)S(1)} %bitcast.117, f32[1,1,48,24,96]{4,2,3,1,0:T(8,128)} %reduce-scatter.2.cloned.1.call-done, f32[]{:T(128)} %bitcast, s32[192]{0:T(256)S(1)} %add_select_fusion.4, pred[192]{0:T(512)(128)(4,1)S(1)} %iota_compare_fusion), kind=kOutput, calls=%fused_computation.40 | convolution fusion | flops 127918080 | bytes 1770436 | tf_op jit(solution)/shard_map/dot_general | solution.py:89
  167.4 1.0 copy.30
  168.4 0.6 slice_reduce_fusion
  (21 shorter events, 0.1 us)
Async XLA Ops:
  7.2 87.2 %reduce-scatter.2.cloned.1.call-start = ((), (), s32[]{:S(2)}) async-start(), calls=%async_computation.3 | async-start | bytes 2949120 | tf_op jit(solution)/shard_map/reduce_scatter | solution.py:150
  9.7 10.0 %collective-permute-start = (f32[3,8,24,96]{3,2,1,0:T(8,128)S(1)}, f32[3,8,24,96]{3,2,1,0:T(8,128)S(1)}, u32[]{:S(2)}, u32[]{:S(2)}) collective-permute-start(f32[3,8,24,96]{3,2,1,0:T(8,128)S(1)} %slice_select_fusion), channel_id=1, source_target_pairs={{0,4},{4,0},{1,5},{5,1},{2,6},{6,2},{3,7},{7,3},{8,12},{12,8},{9,1... | collective-permute-start | bytes 663560 | tf_op jit(solution)/shard_map/ppermute | solution.py:25
  13.4 12.9 %collective-permute-start.3 = (s32[4,1]{0,1:T(1,128)S(1)}, s32[4,1]{0,1:T(1,128)S(1)}, u32[]{:S(2)}, u32[]{:S(2)}) collective-permute-start(s32[4,1]{0,1:T(1,128)S(1)} %compare_select_fusion.1), channel_id=1, source_target_pairs={{0,8},{8,0},{16,24},{24,16},{1,9},{9,1},{17,25},{25,17},{2,10},{10... | collective-permute-start | bytes 56 | tf_op jit(solution)/shard_map/ppermute | solution.py:45
  21.1 9.7 %collective-permute-start.2 = (f32[3,64,8,96]{3,2,1,0:T(8,128)}, f32[3,64,8,96]{3,2,1,0:T(8,128)S(1)}, u32[]{:S(2)}, u32[]{:S(2)}) collective-permute-start(f32[3,64,8,96]{3,2,1,0:T(8,128)} %get-tuple-element.9), channel_id=1, source_target_pairs={{1,0},{2,1},{3,2},{5,4},{6,5},{7,6},{9,8},{10,9},{11,10},{13,12},{... | collective-permute-start | bytes 1769480 | tf_op jit(solution)/shard_map/ppermute | solution.py:31
  22.3 8.5 %collective-permute-start.1 = (f32[3,64,8,96]{3,2,1,0:T(8,128)}, f32[3,64,8,96]{3,2,1,0:T(8,128)}, u32[]{:S(2)}, u32[]{:S(2)}) collective-permute-start(f32[3,64,8,96]{3,2,1,0:T(8,128)} %get-tuple-element.8), channel_id=1, source_target_pairs={{0,1},{1,2},{2,3},{4,5},{5,6},{6,7},{8,9},{9,10},{10,11},{12,13},{... | collective-permute-start | bytes 1769480 | tf_op jit(solution)/shard_map/ppermute | solution.py:30
  26.3 4.5 %collective-permute-start.4 = (s32[4,1]{0,1:T(1,128)S(1)}, s32[4,1]{0,1:T(1,128)S(1)}, u32[]{:S(2)}, u32[]{:S(2)}) collective-permute-start(s32[4,1]{0,1:T(1,128)S(1)} %fusion.372), channel_id=1, source_target_pairs={{0,16},{8,24},{16,0},{24,8},{1,17},{9,25},{17,1},{25,9},{2,18},{10... | collective-permute-start | bytes 56 | tf_op jit(solution)/shard_map/ppermute | solution.py:45
  98.4 16.4 %all-to-all-start = ((f32[8,24,1,1152]{3,1,2,0:T(8,128)}), f32[8,24,1,1152]{3,1,2,0:T(8,128)S(1)}, u32[]{:S(2)}, u32[]{:S(2)}) async-start(f32[8,24,1,1152]{3,1,2,0:T(8,128)} %convolution_bitcast_fusion), calls=%async_computation.1 | async-start | bytes 1769472 | tf_op jit(solution)/shard_map/all_to_all | solution.py:105
  102.1 17.0 %copy-start.2 = (f32[192]{0:T(256)}, f32[192]{0:T(256)S(1)}, u32[]{:S(2)}) copy-start(f32[192]{0:T(256)S(1)} %get-tuple-element.21) | copy-start | bytes 2308
  126.0 1.6 copy-start
  126.0 1.6 copy-start.1
  126.0 1.6 copy-start.3
  147.4 17.2 %all-to-all-start.1 = ((f32[8,24,1,1280]{3,1,2,0:T(8,128)}), f32[8,24,1,1280]{3,1,2,0:T(8,128)S(1)}, u32[]{:S(2)}, u32[]{:S(2)}) async-start(f32[8,24,1,1280]{3,1,2,0:T(8,128)} %pad_bitcast_fusion), calls=%async_computation.2 | async-start | bytes 1966080 | tf_op jit(solution)/shard_map/all_to_all | solution.py:129
Sparse Core Ops, SparseCore 0:
  39.1 55.3 reduce-scatter.1

commit v5 on v4

--- a/solution.py
+++ b/solution.py
@@ -147,7 +147,7 @@
     for number in range(local_count):
         hit = (wanted == first_owned + number)[:, :, None, None, None]
         slots = jnp.where(hit, local_partners[number][None, None], slots)
-    partner = lax.psum_scatter(slots, "band", scatter_dimension=0, tiled=True)[0]
+    partner = jnp.sum(lax.all_to_all(slots, "band", 0, 0, tiled=True), axis=0)
     own_orbital = synthesize(padded[:own_count])[0]
     density = own_orbital[None] * partner
     potential, energy_part = potentials(density)

time: 178 us -> 171 us (0.961)
  between operations: 17.4 us -> 3.96 us
  starting transfers between devices: 20 us -> 24.3 us
  local copies, waits for them, and re-layouts: 24.9 us -> 27.2 us
    reduce_scatter x1 -> x0, waiting for transfers between devices: 52.3 us -> none  [shards(): lax.psum_scatter(slots, 'band', scatter_dimension=0, tiled=True)[0]]
    all_to_all x0 -> x1, waiting for transfers between devices: none -> 50.1 us  [shards(): partner = jnp.sum(lax.all_to_all(slots, 'band', 0, 0, tiled=True), axis=0)]
    all_to_all x0 -> x1, starting transfers between devices: none -> 4.87 us  [shards(): partner = jnp.sum(lax.all_to_all(slots, 'band', 0, 0, tiled=True), axis=0)]
    ppermute x1, starting transfers between devices: 3.93 us -> 1.33 us  [extended(): before = lax.ppermute(tail, axis, [(i, i + 1) for i in range(count - 1)])]
    all_to_all x1, starting transfers between devices: 3.66 us -> 5.67 us  [potentials(): got = lax.all_to_all(send, ('gy', 'gz'), 0, 0, tiled=True)]
    reduce_sum x0 -> x1, other arithmetic: none -> 1.89 us  [shards(): partner = jnp.sum(lax.all_to_all(slots, 'band', 0, 0, tiled=True), axis=0)]
  transfers between devices with their start and end apart: 8 -> 8, of which waited for: 5 -> 6; matrix products, arithmetic and copies ran while one was open for 3% -> 3% of each run, Pallas kernels for 0% -> 0%
where the time goes in v5:
time: 171 us
  waiting for transfers between devices  82.5 us (48%)
  local copies, waits for them, and re-layouts  27.2 us (16%)
  matrix products  26.9 us (16%)
  starting transfers between devices  24.3 us (14%)
  other arithmetic  5.78 us (3%)
  between operations  3.96 us (2%)
    all_to_all x1, waiting for transfers between devices, shards(): partner = jnp.sum(lax.all_to_all(slots, 'band', 0, 0, tiled=True), axis=0)  50.1 us
    dot_general x6, matrix products, contract(): lax.dot_general(left, right, (((left_dim,), (right_dim,)), ((), ())), pre...  16.8 us
    all_to_all x1, waiting for transfers between devices, potentials(): got = lax.all_to_all(back, ('gy', 'gz'), 0, 0, tiled=True)  13 us
    all_to_all x1, waiting for transfers between devices, potentials(): got = lax.all_to_all(send, ('gy', 'gz'), 0, 0, tiled=True)  12.5 us
    all_to_all x1, starting transfers between devices, potentials(): got = lax.all_to_all(send, ('gy', 'gz'), 0, 0, tiled=True)  5.67 us
    dot_general x2, matrix products, synthesize(): step_one = jnp.matmul(padded, matrix_x, precision=precise_mode)  5.58 us
    transpose x1, local copies, waits for them, and re-layouts, potentials(): got.transpose(2, 3, 0, 4, 1, 5)  5.43 us
    all_to_all x1, starting transfers between devices, shards(): partner = jnp.sum(lax.all_to_all(slots, 'band', 0, 0, tiled=True), axis=0)  4.87 us
  transfers between devices with their start and end apart: 8, of which 6 were waited for; matrix products, arithmetic and copies ran while one was open for 3% of the time, Pallas kernels for 0%

profile of v5, /device:TPU:0, one launch (start us, length us, event | category | flops | bytes accessed | tf_op | source)
XLA Modules:
  0.0 170.7 jit_solution(8053560660174844569)
XLA Ops:
  0.6 1.1 constant_dynamic-update-slice_fusion.1
  1.7 1.4 constant_dynamic-update-slice_fusion
  3.1 3.0 %collective-permute-start = (f32[3,8,24,96]{3,2,1,0:T(8,128)S(1)}, f32[3,8,24,96]{3,2,1,0:T(8,128)S(1)}, u32[]{:S(2)}, u32[]{:S(2)}) collective-permute-start(f32[3,8,24,96]{3,2,1,0:T(8,128)S(1)} %slice_select_fusion), channel_id=1, source_target_pairs={{0,4},{4,0},{1,5},{5,1},{2,6},{6,2},{3,7},{7,3},{8,12},{12,8},{9,1... | collective-permute-start | bytes 663560 | tf_op jit(solution)/shard_map/ppermute | solution.py:25
  6.8 1.6 collective-permute-start.3
  8.5 4.7 %collective-permute-done = f32[3,8,24,96]{3,2,1,0:T(8,128)S(1)} collective-permute-done((f32[3,8,24,96]{3,2,1,0:T(8,128)S(1)}, f32[3,8,24,96]{3,2,1,0:T(8,128)S(1)}, u32[]{:S(2)}, u32[]{:S(2)}) %collective-permute-start) | collective-permute-done | bytes 221216 | tf_op jit(solution)/shard_map/ppermute | solution.py:25
  13.2 1.3 pad_maximum_fusion.2
  14.5 1.3 collective-permute-start.1
  15.8 1.3 collective-permute-start.2
  17.1 2.9 %collective-permute-start.4 = (s32[4,1]{0,1:T(1,128)S(1)}, s32[4,1]{0,1:T(1,128)S(1)}, u32[]{:S(2)}, u32[]{:S(2)}) collective-permute-start(s32[4,1]{0,1:T(1,128)S(1)} %fusion.372), channel_id=1, source_target_pairs={{0,16},{8,24},{16,0},{24,8},{1,17},{9,25},{17,1},{25,9},{2,18},{10... | collective-permute-start | bytes 56 | tf_op jit(solution)/shard_map/ppermute | solution.py:45
  20.0 1.6 collective-permute-done.4
  21.7 0.6 collective-permute-done.2
  22.3 3.4 %fusion = f32[2,64,40,96]{3,2,1,0:T(8,128)S(1)} fusion(f32[3,64,8,96]{3,2,1,0:T(8,128)} %collective-permute-done.2, f32[3,8,24,96]{3,2,1,0:T(8,128)S(1)} %get-tuple-element.13, f32[3,48,24,96]{3,2,1,0:T(8,128)S(1)} %constant_dynamic-update-slice_fusion, f32[3,8,24,96]{3,2,1,0:T(8,128)S(1)} %get-tuple-element.12, f32[3,64,8,96]{3,2,1,0:T(8,128)S(1)} %collective-permute-done.1), kind=kOutput, calls=%fused_computation.2 | convolution fusion | flops 569622528 | bytes 4915200 | tf_op jit(solution)/shard_map/dot_general | solution.py:65
  25.7 1.5 convolution_bitcast_fusion.2
  27.2 1.4 fusion.19
  28.6 0.1 slice_bitcast_fusion.1
  28.7 0.2 copy.39
  28.9 0.2 copy.40
  29.1 1.6 select_select_fusion
  30.7 4.9 %all-to-all-start = ((f32[4,1,48,24,96]{4,3,2,1,0:T(8,128)}), f32[4,1,48,24,96]{4,3,2,1,0:T(8,128)}, u32[]{:S(2)}, u32[]{:S(2)}) async-start(f32[4,1,48,24,96]{4,3,2,1,0:T(8,128)} %select_select_fusion), calls=%async_computation | async-start | bytes 4718592 | tf_op jit(solution)/shard_map/all_to_all | solution.py:150
  35.6 0.1 or_select_fusion.1
  35.6 2.2 %fusion.22 = f32[64,40,96]{2,1,0:T(8,128)S(1)} fusion(f32[3,64,8,96]{3,2,1,0:T(8,128)} %collective-permute-done.2, f32[3,64,8,96]{3,2,1,0:T(8,128)S(1)} %collective-permute-done.1, f32[3,8,24,96]{3,2,1,0:T(8,128)S(1)} %get-tuple-element.13, f32[3,48,24,96]{3,2,1,0:T(8,128)S(1)} %constant_dynamic-update-slice_fusion, f32[3,8,24,96]{3,2,1,0:T(8,128)S(1)} %get-tuple-element.12), kind=kOutput, calls=%fused_computation.27 | convolution fusion | flops 284540928 | bytes 3932160 | tf_op jit(solution)/shard_map/dot_general | solution.py:65
  37.9 0.8 convolution_bitcast_fusion.3
  38.7 50.1 %all-to-all-done = f32[4,1,48,24,96]{4,3,2,1,0:T(8,128)} async-done(((f32[4,1,48,24,96]{4,3,2,1,0:T(8,128)}), f32[4,1,48,24,96]{4,3,2,1,0:T(8,128)}, u32[]{:S(2)}, u32[]{:S(2)}) %all-to-all-start) | async-done | bytes 1769504 | tf_op jit(solution)/shard_map/all_to_all | solution.py:150
  88.8 1.9 %reduce_sum.27 = f32[48,24,96]{2,1,0:T(8,128)S(1)} reduce(f32[4,1,48,24,96]{4,3,2,1,0:T(8,128)} %all-to-all-done, f32[]{:T(128)} %constant.54.clone.1), dimensions={0,1}, to_apply=%region_0.1 | reduce | flops 331776 | bytes 2211844 | tf_op jit(solution)/shard_map/reduce_sum | solution.py:150
  90.7 0.8 convolution_multiply_fusion.1
  91.5 0.2 copy.42
  91.7 1.9 %convolution_bitcast_fusion = f32[8,24,1,1152]{3,1,2,0:T(8,128)} fusion(f32[1152,96,1]{1,0,2:T(8,128)S(1)} %bitcast.119, s32[8,24]{1,0:T(8,128)S(1)} %add_select_fusion.3, pred[8,24]{1,0:T(8,128)(4,1)S(1)} %fusion.133), kind=kOutput, calls=%fused_computation.13 | convolution fusion | flops 127586304 | bytes 1328064 | tf_op jit(solution)/shard_map/dot_general | solution.py:89
  93.6 5.7 %all-to-all-start.1 = ((f32[8,24,1,1152]{3,1,2,0:T(8,128)}), f32[8,24,1,1152]{3,1,2,0:T(8,128)S(1)}, u32[]{:S(2)}, u32[]{:S(2)}) async-start(f32[8,24,1,1152]{3,1,2,0:T(8,128)} %convolution_bitcast_fusion), calls=%async_computation.1 | async-start | bytes 1769472 | tf_op jit(solution)/shard_map/all_to_all | solution.py:105
  99.3 0.1 or_select_fusion
  99.4 0.1 broadcast_multiply_fusion
  99.4 0.1 broadcast_add_fusion
  99.5 12.5 %all-to-all-done.1 = f32[8,24,1,1152]{3,1,2,0:T(8,128)S(1)} async-done(((f32[8,24,1,1152]{3,1,2,0:T(8,128)}), f32[8,24,1,1152]{3,1,2,0:T(8,128)S(1)}, u32[]{:S(2)}, u32[]{:S(2)}) %all-to-all-start.1) | async-done | bytes 884768 | tf_op jit(solution)/shard_map/all_to_all | solution.py:105
  112.0 4.3 %reshape.376 = f32[2,4,24,1,48,24]{5,4,2,1,0,3:T(8,128)} reshape(f32[8,24,1,1152]{3,1,2,0:T(8,128)S(1)} %all-to-all-done.1) | data formatting | bytes 1769472 | tf_op jit(solution)/shard_map/reshape | solution.py:106
  116.4 5.4 %copy.45 = f32[24,1,2,48,4,24]{3,2,5,4,0,1:T(2,128)S(1)} copy(f32[24,1,2,48,4,24]{5,3,0,4,2,1:T(8,128)} %bitcast.114) | data formatting | bytes 1769472 | tf_op jit(solution)/shard_map/transpose | solution.py:107
  121.8 2.3 %reshape.377 = f32[24,96,96]{1,2,0:T(8,128)} reshape(f32[24,1,2,48,4,24]{3,2,5,4,0,1:T(2,128)S(1)} %copy.45) | data formatting | bytes 1769472 | tf_op jit(solution)/shard_map/reshape.23
  124.1 2.8 %fusion.46 = f32[24,96,192]{1,2,0:T(8,128)S(1)} fusion(f32[24,96,96]{1,2,0:T(8,128)} %reshape.377, s32[192]{0:T(256)S(1)} %add_select_fusion.4, pred[192]{0:T(512)(128)(4,1)S(1)} %iota_compare_fusion), kind=kOutput, calls=%fused_computation.66 | convolution fusion | flops 254988288 | bytes 2655168 | tf_op jit(solution)/shard_map/dot_general | solution.py:89
  126.9 3.8 %multiply_reduce_fusion = (f32[]{:T(128)}, f32[24,192,192]{2,1,0:T(8,128)S(1)}) fusion(f32[192]{0:T(256)S(1)} %get-tuple-element.21, f32[24,192]{1,0:T(8,128)S(1)} %broadcast_add_fusion, f32[192]{0:T(256)S(1)} %get-tuple-element.20, f32[24,192]{1,0:T(8,128)S(1)} %broadcast_multiply_fusion, f32[24,96,192]{1,2,0:T(8,128)S(1)} %fusion.46, ...), kind=kOutput, calls=%fused_computation | convolution fusion | flops 516870144 | bytes 5347780 | tf_op jit(solution)/shard_map/dot_general | solution.py:89
  130.7 3.8 %fusion.10 = f32[24,192,96]{1,2,0:T(8,128)S(1)} fusion(f32[24,192,192]{2,1,0:T(8,128)S(1)} %get-tuple-element.17, f32[192]{0:T(256)S(1)} %get-tuple-element.21, f32[24,192]{1,0:T(8,128)S(1)} %broadcast_add_fusion, f32[192]{0:T(256)S(1)} %get-tuple-element.20, f32[24,192]{1,0:T(8,128)S(1)} %broadcast_multiply_fusion, s32[192]{0:T(256)S(1)} %add_select_fusion.4, ...), kind=kOutput, calls=%fused_computation.12 | convolution fusion | flops 515100672 | bytes 5347776 | tf_op jit(solution)/shard_map/dot_general | solution.py:89
  134.5 2.6 %convolution_bitcast_fusion.1 = f32[2,4,24,1,48,24]{4,5,1,0,2,3:T(8,128)S(1)} fusion(f32[24,2,48,192,1]{3,2,4,1,0:T(8,128)S(1)} %bitcast.118, s32[192]{0:T(256)S(1)} %add_select_fusion.4, s32[4,24]{1,0:T(4,128)S(1)} %multiply_add_fusion.1, pred[192]{0:T(512)(128)(4,1)S(1)} %iota_compare_fusion), kind=kOutput, calls=%fused_computation.21 | convolution fusion | flops 254988288 | bytes 2655552 | tf_op jit(solution)/shard_map/dot_general | solution.py:89
  137.2 3.7 %copy.48 = f32[2,4,24,1,48,24]{5,4,2,1,0,3:T(8,128)} copy(f32[2,4,24,1,48,24]{4,5,1,0,2,3:T(8,128)S(1)} %convolution_bitcast_fusion.1) | data formatting | bytes 1769472 | tf_op jit(solution)/shard_map/transpose | solution.py:126
  140.8 4.2 %reshape.379 = f32[8,24,1,1152]{3,1,0,2:T(8,128)S(1)} reshape(f32[2,4,24,1,48,24]{5,4,2,1,0,3:T(8,128)} %copy.48) | data formatting | bytes 1769472 | tf_op jit(solution)/shard_map/reshape | solution.py:126
  145.0 1.7 pad_bitcast_fusion
  146.7 3.6 %all-to-all-start.2 = ((f32[8,24,1,1280]{3,1,2,0:T(8,128)}), f32[8,24,1,1280]{3,1,2,0:T(8,128)S(1)}, u32[]{:S(2)}, u32[]{:S(2)}) async-start(f32[8,24,1,1280]{3,1,2,0:T(8,128)} %pad_bitcast_fusion), calls=%async_computation.2 | async-start | bytes 1966080 | tf_op jit(solution)/shard_map/all_to_all | solution.py:129
  150.9 13.0 %all-to-all-done.2 = f32[8,24,1,1280]{3,1,2,0:T(8,128)S(1)} async-done(((f32[8,24,1,1280]{3,1,2,0:T(8,128)}), f32[8,24,1,1280]{3,1,2,0:T(8,128)S(1)}, u32[]{:S(2)}, u32[]{:S(2)}) %all-to-all-start.2) | async-done | bytes 983072 | tf_op jit(solution)/shard_map/all_to_all | solution.py:129
  163.9 1.0 slice.44
  164.9 1.5 copy.51
  166.4 0.6 slice_reduce_fusion
  167.7 1.9 %fusion.33 = f32[1,48,24,96]{3,2,1,0:T(8,128)} fusion(f32[48,24,96]{2,1,0:T(8,128)S(1)} %reduce_sum.27, f32[48,24,192]{2,1,0:T(8,128)S(1)} %bitcast.115, f32[]{:T(128)} %bitcast, s32[192]{0:T(256)S(1)} %add_select_fusion.4, pred[192]{0:T(512)(128)(4,1)S(1)} %iota_compare_fusion), kind=kOutput, calls=%fused_computation.40 | convolution fusion | flops 127918080 | bytes 1770436 | tf_op jit(solution)/shard_map/dot_general | solution.py:89
  (14 shorter events, 0.1 us)
Async XLA Ops:
  3.1 10.0 %collective-permute-start = (f32[3,8,24,96]{3,2,1,0:T(8,128)S(1)}, f32[3,8,24,96]{3,2,1,0:T(8,128)S(1)}, u32[]{:S(2)}, u32[]{:S(2)}) collective-permute-start(f32[3,8,24,96]{3,2,1,0:T(8,128)S(1)} %slice_select_fusion), channel_id=1, source_target_pairs={{0,4},{4,0},{1,5},{5,1},{2,6},{6,2},{3,7},{7,3},{8,12},{12,8},{9,1... | collective-permute-start | bytes 663560 | tf_op jit(solution)/shard_map/ppermute | solution.py:25
  6.8 10.3 %collective-permute-start.3 = (s32[4,1]{0,1:T(1,128)S(1)}, s32[4,1]{0,1:T(1,128)S(1)}, u32[]{:S(2)}, u32[]{:S(2)}) collective-permute-start(s32[4,1]{0,1:T(1,128)S(1)} %compare_select_fusion.1), channel_id=1, source_target_pairs={{0,8},{8,0},{16,24},{24,16},{1,9},{9,1},{17,25},{25,17},{2,10},{10... | collective-permute-start | bytes 56 | tf_op jit(solution)/shard_map/ppermute | solution.py:45
  14.5 7.2 %collective-permute-start.1 = (f32[3,64,8,96]{3,2,1,0:T(8,128)}, f32[3,64,8,96]{3,2,1,0:T(8,128)S(1)}, u32[]{:S(2)}, u32[]{:S(2)}) collective-permute-start(f32[3,64,8,96]{3,2,1,0:T(8,128)} %get-tuple-element.8), channel_id=1, source_target_pairs={{0,1},{1,2},{2,3},{4,5},{5,6},{6,7},{8,9},{9,10},{10,11},{12,13},{... | collective-permute-start | bytes 1769480 | tf_op jit(solution)/shard_map/ppermute | solution.py:30
  15.8 6.5 %collective-permute-start.2 = (f32[3,64,8,96]{3,2,1,0:T(8,128)}, f32[3,64,8,96]{3,2,1,0:T(8,128)}, u32[]{:S(2)}, u32[]{:S(2)}) collective-permute-start(f32[3,64,8,96]{3,2,1,0:T(8,128)} %get-tuple-element.9), channel_id=1, source_target_pairs={{1,0},{2,1},{3,2},{5,4},{6,5},{7,6},{9,8},{10,9},{11,10},{13,12},{... | collective-permute-start | bytes 1769480 | tf_op jit(solution)/shard_map/ppermute | solution.py:31
  17.1 4.5 %collective-permute-start.4 = (s32[4,1]{0,1:T(1,128)S(1)}, s32[4,1]{0,1:T(1,128)S(1)}, u32[]{:S(2)}, u32[]{:S(2)}) collective-permute-start(s32[4,1]{0,1:T(1,128)S(1)} %fusion.372), channel_id=1, source_target_pairs={{0,16},{8,24},{16,0},{24,8},{1,17},{9,25},{17,1},{25,9},{2,18},{10... | collective-permute-start | bytes 56 | tf_op jit(solution)/shard_map/ppermute | solution.py:45
  30.7 58.1 %all-to-all-start = ((f32[4,1,48,24,96]{4,3,2,1,0:T(8,128)}), f32[4,1,48,24,96]{4,3,2,1,0:T(8,128)}, u32[]{:S(2)}, u32[]{:S(2)}) async-start(f32[4,1,48,24,96]{4,3,2,1,0:T(8,128)} %select_select_fusion), calls=%async_computation | async-start | bytes 4718592 | tf_op jit(solution)/shard_map/all_to_all | solution.py:150
  93.6 18.4 %all-to-all-start.1 = ((f32[8,24,1,1152]{3,1,2,0:T(8,128)}), f32[8,24,1,1152]{3,1,2,0:T(8,128)S(1)}, u32[]{:S(2)}, u32[]{:S(2)}) async-start(f32[8,24,1,1152]{3,1,2,0:T(8,128)} %convolution_bitcast_fusion), calls=%async_computation.1 | async-start | bytes 1769472 | tf_op jit(solution)/shard_map/all_to_all | solution.py:105
  146.7 17.2 %all-to-all-start.2 = ((f32[8,24,1,1280]{3,1,2,0:T(8,128)}), f32[8,24,1,1280]{3,1,2,0:T(8,128)S(1)}, u32[]{:S(2)}, u32[]{:S(2)}) async-start(f32[8,24,1,1280]{3,1,2,0:T(8,128)} %pad_bitcast_fusion), calls=%async_computation.2 | async-start | bytes 1966080 | tf_op jit(solution)/shard_map/all_to_all | solution.py:129

commit v6 on v5

--- a/solution.py
+++ b/solution.py
@@ -147,7 +147,11 @@
     for number in range(local_count):
         hit = (wanted == first_owned + number)[:, :, None, None, None]
         slots = jnp.where(hit, local_partners[number][None, None], slots)
-    partner = jnp.sum(lax.all_to_all(slots, "band", 0, 0, tiled=True), axis=0)
+    arrived = lax.all_to_all(slots, "band", 0, 0, tiled=True)
+    owners = wanted[lax.axis_index("band")] // local_count
+    partner = jnp.stack(
+        [lax.dynamic_index_in_dim(arrived[:, pair], owners[pair], 0, False) for pair in range(owners.shape[0])]
+    )
     own_orbital = synthesize(padded[:own_count])[0]
     density = own_orbital[None] * partner
     potential, energy_part = potentials(density)

time: 171 us -> 171 us (level)
  waiting for transfers between devices: 82.5 us -> 79 us
  local copies, waits for them, and re-layouts: 27.2 us -> 30.6 us
  other arithmetic: 5.78 us -> 2.79 us
  between operations: 3.96 us -> 6.56 us
    all_to_all x1, waiting for transfers between devices: 50.1 us -> 46.9 us  [shards(): arrived = lax.all_to_all(slots, 'band', 0, 0, tiled=True)]
    reduce_sum x1 -> x0, other arithmetic: 1.89 us -> none  [shards(): partner = jnp.sum(lax.all_to_all(slots, 'band', 0, 0, tiled=True), axis=0)]
  transfers between devices with their start and end apart: 8 -> 8, of which waited for: 6 -> 6; matrix products, arithmetic and copies ran while one was open for 3% -> 2% of each run, Pallas kernels for 0% -> 0%
where the time goes in v6:
time: 171 us; the launch traced here: 170 us
  waiting for transfers between devices  79 us (46%)
  local copies, waits for them, and re-layouts  30.6 us (18%)
  matrix products  27.6 us (16%)
  starting transfers between devices  23.8 us (14%)
  between operations  6.56 us (4%)
  other arithmetic  2.79 us (2%)
    all_to_all x1, waiting for transfers between devices, shards(): arrived = lax.all_to_all(slots, 'band', 0, 0, tiled=True)  46.9 us
    dot_general x6, matrix products, contract(): lax.dot_general(left, right, (((left_dim,), (right_dim,)), ((), ())), pre...  17.5 us
    all_to_all x1, waiting for transfers between devices, potentials(): got = lax.all_to_all(back, ('gy', 'gz'), 0, 0, tiled=True)  13 us
    all_to_all x1, waiting for transfers between devices, potentials(): got = lax.all_to_all(send, ('gy', 'gz'), 0, 0, tiled=True)  12.5 us
    transpose x1, local copies, waits for them, and re-layouts, potentials(): got.transpose(2, 3, 0, 4, 1, 5)  5.85 us
    all_to_all x1, starting transfers between devices, potentials(): got = lax.all_to_all(send, ('gy', 'gz'), 0, 0, tiled=True)  5.2 us
    transpose x1, local copies, waits for them, and re-layouts, potentials(): back.transpose(2, 4, 0, 1, 3, 5)  4.99 us
    all_to_all x1, starting transfers between devices, shards(): arrived = lax.all_to_all(slots, 'band', 0, 0, tiled=True)  4.87 us
  transfers between devices with their start and end apart: 8, of which 6 were waited for; matrix products, arithmetic and copies ran while one was open for 2% of the time, Pallas kernels for 0%

profile of v6, /device:TPU:0, one launch (start us, length us, event | category | flops | bytes accessed | tf_op | source)
XLA Modules:
  0.0 170.3 jit_solution(2433006472123923613)
XLA Ops:
  0.6 1.1 constant_dynamic-update-slice_fusion.1
  1.7 1.4 constant_dynamic-update-slice_fusion
  3.1 3.0 %collective-permute-start = (f32[3,8,24,96]{3,2,1,0:T(8,128)S(1)}, f32[3,8,24,96]{3,2,1,0:T(8,128)S(1)}, u32[]{:S(2)}, u32[]{:S(2)}) collective-permute-start(f32[3,8,24,96]{3,2,1,0:T(8,128)S(1)} %slice_select_fusion), channel_id=1, source_target_pairs={{0,4},{4,0},{1,5},{5,1},{2,6},{6,2},{3,7},{7,3},{8,12},{12,8},{9,1... | collective-permute-start | bytes 663560 | tf_op jit(solution)/shard_map/ppermute | solution.py:25
  6.8 1.6 collective-permute-start.3
  8.5 4.7 %collective-permute-done = f32[3,8,24,96]{3,2,1,0:T(8,128)S(1)} collective-permute-done((f32[3,8,24,96]{3,2,1,0:T(8,128)S(1)}, f32[3,8,24,96]{3,2,1,0:T(8,128)S(1)}, u32[]{:S(2)}, u32[]{:S(2)}) %collective-permute-start) | collective-permute-done | bytes 221216 | tf_op jit(solution)/shard_map/ppermute | solution.py:25
  13.2 0.1 pad_maximum_fusion.2
  13.3 1.3 collective-permute-start.1
  14.7 1.3 collective-permute-start.2
  16.0 0.0 collective-permute-done.3
  16.0 2.9 %collective-permute-start.4 = (s32[4,1]{0,1:T(1,128)S(1)}, s32[4,1]{0,1:T(1,128)S(1)}, u32[]{:S(2)}, u32[]{:S(2)}) collective-permute-start(s32[4,1]{0,1:T(1,128)S(1)} %fusion.372), channel_id=1, source_target_pairs={{0,16},{8,24},{16,0},{24,8},{1,17},{9,25},{17,1},{25,9},{2,18},{10... | collective-permute-start | bytes 56 | tf_op jit(solution)/shard_map/ppermute | solution.py:45
  18.9 1.6 collective-permute-done.4
  20.5 0.3 collective-permute-done.2
  20.8 2.3 %fusion = f32[2,64,40,96]{3,2,1,0:T(8,128)S(1)} fusion(f32[3,64,8,96]{3,2,1,0:T(8,128)S(1)} %collective-permute-done.2, f32[3,8,24,96]{3,2,1,0:T(8,128)S(1)} %get-tuple-element.15, f32[3,48,24,96]{3,2,1,0:T(8,128)S(1)} %constant_dynamic-update-slice_fusion, f32[3,8,24,96]{3,2,1,0:T(8,128)S(1)} %get-tuple-element.14, ...), kind=kOutput, calls=%fused_computation.2 | convolution fusion | flops 569622528 | bytes 4915200 | tf_op jit(solution)/shard_map/dot_general | solution.py:65
  23.2 1.5 convolution_bitcast_fusion.2
  24.7 1.4 fusion.19
  26.1 0.1 slice_bitcast_fusion.1
  26.2 1.7 select_select_fusion
  27.8 4.9 %all-to-all-start = ((f32[4,1,48,24,96]{4,2,3,1,0:T(8,128)}), f32[4,1,48,24,96]{4,2,3,1,0:T(8,128)}, u32[]{:S(2)}, u32[]{:S(2)}) async-start(f32[4,1,48,24,96]{4,2,3,1,0:T(8,128)} %select_select_fusion), calls=%async_computation | async-start | bytes 4718592 | tf_op jit(solution)/shard_map/all_to_all | solution.py:150
  32.7 0.1 or_select_fusion.1
  32.8 0.6 constant_dynamic-slice_fusion
  36.0 2.2 %fusion.22 = f32[64,40,96]{2,1,0:T(8,128)S(1)} fusion(f32[3,64,8,96]{3,2,1,0:T(8,128)} %copy-done, f32[3,64,8,96]{3,2,1,0:T(8,128)S(1)} %collective-permute-done.1, f32[3,8,24,96]{3,2,1,0:T(8,128)S(1)} %get-tuple-element.15, f32[3,48,24,96]{3,2,1,0:T(8,128)S(1)} %constant_dynamic-update-slice_fusion, f32[3,8,24,96]{3,2,1,0:T(8,128)S(1)} %get-tuple-element.14), kind=kOutput, calls=%fused_computation.27 | convolution fusion | flops 284540928 | bytes 3932160 | tf_op jit(solution)/shard_map/dot_general | solution.py:65
  38.2 0.8 convolution_bitcast_fusion.3
  39.0 46.9 %all-to-all-done = f32[4,1,48,24,96]{4,2,3,1,0:T(8,128)} async-done(((f32[4,1,48,24,96]{4,2,3,1,0:T(8,128)}), f32[4,1,48,24,96]{4,2,3,1,0:T(8,128)}, u32[]{:S(2)}, u32[]{:S(2)}) %all-to-all-start) | async-done | bytes 1769504 | tf_op jit(solution)/shard_map/all_to_all | solution.py:150
  85.9 1.8 %convolution_multiply_fusion.1 = f32[48,24,96]{2,0,1:T(8,128)S(1)} fusion(f32[64,24,96]{2,1,0:T(8,128)S(1)} %convolution_bitcast_fusion.3, f32[4,1,48,24,96]{4,2,3,1,0:T(8,128)} %all-to-all-done, s32[]{:T(128)S(6)} %select_n.570, s32[64]{0:T(128)S(1)} %iota_add_fusion.2), kind=kOutput, calls=%fused_computation.41 | convolution fusion | flops 85192704 | bytes 1474820 | tf_op jit(solution)/shard_map/oqzx,qy->oyzx/dot_general | solution.py:67
  87.7 0.2 copy.19
  87.9 1.9 %convolution_bitcast_fusion = f32[8,24,1,1152]{3,1,2,0:T(8,128)} fusion(f32[1152,96,1]{1,0,2:T(8,128)S(1)} %bitcast.123, s32[8,24]{1,0:T(8,128)S(1)} %add_select_fusion.3, pred[8,24]{1,0:T(8,128)(4,1)S(1)} %fusion.134), kind=kOutput, calls=%fused_computation.13 | convolution fusion | flops 127586304 | bytes 1328064 | tf_op jit(solution)/shard_map/dot_general | solution.py:89
  89.9 5.2 %all-to-all-start.1 = ((f32[8,24,1,1152]{3,1,2,0:T(8,128)}), f32[8,24,1,1152]{3,1,2,0:T(8,128)S(1)}, u32[]{:S(2)}, u32[]{:S(2)}) async-start(f32[8,24,1,1152]{3,1,2,0:T(8,128)} %convolution_bitcast_fusion), calls=%async_computation.1 | async-start | bytes 1769472 | tf_op jit(solution)/shard_map/all_to_all | solution.py:105
  95.1 0.1 or_select_fusion
  95.1 0.1 broadcast_multiply_fusion
  95.2 0.1 broadcast_add_fusion
  95.3 12.5 %all-to-all-done.1 = f32[8,24,1,1152]{3,1,2,0:T(8,128)S(1)} async-done(((f32[8,24,1,1152]{3,1,2,0:T(8,128)}), f32[8,24,1,1152]{3,1,2,0:T(8,128)S(1)}, u32[]{:S(2)}, u32[]{:S(2)}) %all-to-all-start.1) | async-done | bytes 884768 | tf_op jit(solution)/shard_map/all_to_all | solution.py:105
  107.8 4.3 %reshape.378 = f32[2,4,24,1,48,24]{5,4,2,1,0,3:T(8,128)} reshape(f32[8,24,1,1152]{3,1,2,0:T(8,128)S(1)} %all-to-all-done.1) | data formatting | bytes 1769472 | tf_op jit(solution)/shard_map/reshape | solution.py:106
  112.1 5.9 %copy.22 = f32[24,1,2,48,4,24]{3,2,5,4,0,1:T(2,128)} copy(f32[24,1,2,48,4,24]{5,3,0,4,2,1:T(8,128)} %bitcast.118) | data formatting | bytes 1769472 | tf_op jit(solution)/shard_map/transpose | solution.py:107
  118.0 2.7 %reshape.379 = f32[24,96,96]{1,2,0:T(8,128)S(1)} reshape(f32[24,1,2,48,4,24]{3,2,5,4,0,1:T(2,128)} %copy.22) | data formatting | bytes 1769472 | tf_op jit(solution)/shard_map/reshape.24
  120.7 1.5 fusion.47
  122.2 3.8 %multiply_reduce_fusion = (f32[]{:T(128)}, f32[24,192,192]{2,1,0:T(8,128)S(1)}) fusion(f32[192]{0:T(256)S(1)} %get-tuple-element.21, f32[24,192]{1,0:T(8,128)S(1)} %broadcast_add_fusion, f32[192]{0:T(256)S(1)} %get-tuple-element.20, f32[24,192]{1,0:T(8,128)S(1)} %broadcast_multiply_fusion, f32[24,96,192]{1,2,0:T(8,128)S(1)} %fusion.47, ...), kind=kOutput, calls=%fused_computation | convolution fusion | flops 516870144 | bytes 5347780 | tf_op jit(solution)/shard_map/dot_general | solution.py:89
  126.0 3.8 %fusion.10 = f32[24,192,96]{1,2,0:T(8,128)S(1)} fusion(f32[24,192,192]{2,1,0:T(8,128)S(1)} %get-tuple-element.17, f32[192]{0:T(256)S(1)} %get-tuple-element.21, f32[24,192]{1,0:T(8,128)S(1)} %broadcast_add_fusion, f32[192]{0:T(256)S(1)} %get-tuple-element.20, f32[24,192]{1,0:T(8,128)S(1)} %broadcast_multiply_fusion, s32[192]{0:T(256)S(1)} %add_select_fusion.4, ...), kind=kOutput, calls=%fused_computation.12 | convolution fusion | flops 515100672 | bytes 5347776 | tf_op jit(solution)/shard_map/dot_general | solution.py:89
  129.8 4.1 %convolution_bitcast_fusion.1 = f32[2,4,24,1,48,24]{4,5,1,0,2,3:T(8,128)} fusion(f32[24,2,48,192,1]{3,2,4,1,0:T(8,128)S(1)} %bitcast.122, s32[192]{0:T(256)S(1)} %add_select_fusion.4, s32[4,24]{1,0:T(4,128)S(1)} %multiply_add_fusion.1, pred[192]{0:T(512)(128)(4,1)S(1)} %iota_compare_fusion), kind=kOutput, calls=%fused_computation.21 | convolution fusion | flops 254988288 | bytes 2655552 | tf_op jit(solution)/shard_map/dot_general | solution.py:89
  134.0 5.0 %copy.25 = f32[2,4,24,1,48,24]{5,4,2,1,0,3:T(8,128)} copy(f32[2,4,24,1,48,24]{4,5,1,0,2,3:T(8,128)} %convolution_bitcast_fusion.1) | data formatting | bytes 1769472 | tf_op jit(solution)/shard_map/transpose | solution.py:126
  139.0 4.2 %reshape.381 = f32[8,24,1,1152]{3,1,0,2:T(8,128)S(1)} reshape(f32[2,4,24,1,48,24]{5,4,2,1,0,3:T(8,128)} %copy.25) | data formatting | bytes 1769472 | tf_op jit(solution)/shard_map/reshape | solution.py:126
  143.1 1.7 pad_bitcast_fusion
  144.8 3.6 %all-to-all-start.2 = ((f32[8,24,1,1280]{3,1,2,0:T(8,128)}), f32[8,24,1,1280]{3,1,2,0:T(8,128)S(1)}, u32[]{:S(2)}, u32[]{:S(2)}) async-start(f32[8,24,1,1280]{3,1,2,0:T(8,128)} %pad_bitcast_fusion), calls=%async_computation.2 | async-start | bytes 1966080 | tf_op jit(solution)/shard_map/all_to_all | solution.py:129
  149.0 13.0 %all-to-all-done.2 = f32[8,24,1,1280]{3,1,2,0:T(8,128)S(1)} async-done(((f32[8,24,1,1280]{3,1,2,0:T(8,128)}), f32[8,24,1,1280]{3,1,2,0:T(8,128)S(1)}, u32[]{:S(2)}, u32[]{:S(2)}) %all-to-all-start.2) | async-done | bytes 983072 | tf_op jit(solution)/shard_map/all_to_all | solution.py:129
  162.0 1.0 slice.44
  163.0 1.5 copy.28
  164.5 2.4 %fusion.33 = f32[1,48,24,96]{3,1,2,0:T(8,128)S(1)} fusion(f32[48,24,192]{2,1,0:T(8,128)S(1)} %bitcast.119, f32[4,1,48,24,96]{4,2,3,1,0:T(8,128)} %all-to-all-done, s32[]{:T(128)S(6)} %select_n.570, f32[]{:T(128)} %bitcast, s32[192]{0:T(256)S(1)} %add_select_fusion.4, pred[192]{0:T(512)(128)(4,1)S(1)} %iota_compare_fusion), kind=kOutput, calls=%fused_computation.40 | convolution fusion | flops 127918080 | bytes 1770440 | tf_op jit(solution)/shard_map/dot_general | solution.py:89
  166.9 1.0 copy.30
  167.9 0.6 slice_reduce_fusion
  (16 shorter events, 0.1 us)
Async XLA Ops:
  3.1 10.0 %collective-permute-start = (f32[3,8,24,96]{3,2,1,0:T(8,128)S(1)}, f32[3,8,24,96]{3,2,1,0:T(8,128)S(1)}, u32[]{:S(2)}, u32[]{:S(2)}) collective-permute-start(f32[3,8,24,96]{3,2,1,0:T(8,128)S(1)} %slice_select_fusion), channel_id=1, source_target_pairs={{0,4},{4,0},{1,5},{5,1},{2,6},{6,2},{3,7},{7,3},{8,12},{12,8},{9,1... | collective-permute-start | bytes 663560 | tf_op jit(solution)/shard_map/ppermute | solution.py:25
  6.8 9.2 %collective-permute-start.3 = (s32[4,1]{0,1:T(1,128)S(1)}, s32[4,1]{0,1:T(1,128)S(1)}, u32[]{:S(2)}, u32[]{:S(2)}) collective-permute-start(s32[4,1]{0,1:T(1,128)S(1)} %compare_select_fusion.1), channel_id=1, source_target_pairs={{0,8},{8,0},{16,24},{24,16},{1,9},{9,1},{17,25},{25,17},{2,10},{10... | collective-permute-start | bytes 56 | tf_op jit(solution)/shard_map/ppermute | solution.py:45
  13.3 7.2 %collective-permute-start.1 = (f32[3,64,8,96]{3,2,1,0:T(8,128)S(1)}, f32[3,64,8,96]{3,2,1,0:T(8,128)S(1)}, u32[]{:S(2)}, u32[]{:S(2)}) collective-permute-start(f32[3,64,8,96]{3,2,1,0:T(8,128)S(1)} %get-tuple-element.10), channel_id=1, source_target_pairs={{0,1},{1,2},{2,3},{4,5},{5,6},{6,7},{8,9},{9,10},{10,11},{12,13},{... | collective-permute-start | bytes 1769480 | tf_op jit(solution)/shard_map/ppermute | solution.py:30
  14.7 6.1 %collective-permute-start.2 = (f32[3,64,8,96]{3,2,1,0:T(8,128)S(1)}, f32[3,64,8,96]{3,2,1,0:T(8,128)S(1)}, u32[]{:S(2)}, u32[]{:S(2)}) collective-permute-start(f32[3,64,8,96]{3,2,1,0:T(8,128)S(1)} %get-tuple-element.11), channel_id=1, source_target_pairs={{1,0},{2,1},{3,2},{5,4},{6,5},{7,6},{9,8},{10,9},{11,10},{13,12},{... | collective-permute-start | bytes 1769480 | tf_op jit(solution)/shard_map/ppermute | solution.py:31
  16.0 4.5 %collective-permute-start.4 = (s32[4,1]{0,1:T(1,128)S(1)}, s32[4,1]{0,1:T(1,128)S(1)}, u32[]{:S(2)}, u32[]{:S(2)}) collective-permute-start(s32[4,1]{0,1:T(1,128)S(1)} %fusion.372), channel_id=1, source_target_pairs={{0,16},{8,24},{16,0},{24,8},{1,17},{9,25},{17,1},{25,9},{2,18},{10... | collective-permute-start | bytes 56 | tf_op jit(solution)/shard_map/ppermute | solution.py:45
  20.8 2.4 %copy-start = (f32[3,64,8,96]{3,2,1,0:T(8,128)}, f32[3,64,8,96]{3,2,1,0:T(8,128)S(1)}, u32[]{:S(2)}) copy-start(f32[3,64,8,96]{3,2,1,0:T(8,128)S(1)} %collective-permute-done.2) | copy-start | bytes 1769476
  27.8 58.1 %all-to-all-start = ((f32[4,1,48,24,96]{4,2,3,1,0:T(8,128)}), f32[4,1,48,24,96]{4,2,3,1,0:T(8,128)}, u32[]{:S(2)}, u32[]{:S(2)}) async-start(f32[4,1,48,24,96]{4,2,3,1,0:T(8,128)} %select_select_fusion), calls=%async_computation | async-start | bytes 4718592 | tf_op jit(solution)/shard_map/all_to_all | solution.py:150
  89.9 17.9 %all-to-all-start.1 = ((f32[8,24,1,1152]{3,1,2,0:T(8,128)}), f32[8,24,1,1152]{3,1,2,0:T(8,128)S(1)}, u32[]{:S(2)}, u32[]{:S(2)}) async-start(f32[8,24,1,1152]{3,1,2,0:T(8,128)} %convolution_bitcast_fusion), calls=%async_computation.1 | async-start | bytes 1769472 | tf_op jit(solution)/shard_map/all_to_all | solution.py:105
  144.8 17.2 %all-to-all-start.2 = ((f32[8,24,1,1280]{3,1,2,0:T(8,128)}), f32[8,24,1,1280]{3,1,2,0:T(8,128)S(1)}, u32[]{:S(2)}, u32[]{:S(2)}) async-start(f32[8,24,1,1280]{3,1,2,0:T(8,128)} %pad_bitcast_fusion), calls=%async_computation.2 | async-start | bytes 1966080 | tf_op jit(solution)/shard_map/all_to_all | solution.py:129

commit v7 on v5

--- a/solution.py
+++ b/solution.py
@@ -99,13 +99,13 @@
     spread = count_y * count_z
     width = period // spread
     table = channel_table(length)
-    flat = density.reshape(pair_count * rows_y * rows_z, length)
+    flat = density.transpose(0, 2, 1, 3).reshape(pair_count * rows_y * rows_z, length)
     along_x = contract(table, flat, 0, 1)
     send = along_x.reshape(spread, width, pair_count, rows_y * rows_z)
     got = lax.all_to_all(send, ("gy", "gz"), 0, 0, tiled=True)
-    got = got.reshape(count_y, count_z, width, pair_count, rows_y, rows_z)
-    got = got.transpose(2, 3, 0, 4, 1, 5).reshape(
-        width, pair_count, count_y * rows_y, count_z * rows_z
+    got = got.reshape(count_y, count_z, width, pair_count, rows_z, rows_y)
+    got = got.transpose(2, 3, 1, 4, 0, 5).reshape(
+        width, pair_count, count_z * rows_z, count_y * rows_y
     )
     along_z = contract(got, table, 3, 0)
     spectrum = contract(along_z, table, 2, 0)
@@ -122,8 +122,8 @@
     energy_part = jnp.sum(weighted * spectrum, axis=(0, 2, 3))
     back_y = contract(weighted, table, 3, 1)
     back_z = contract(back_y, table, 2, 1)
-    back = back_z.reshape(width, pair_count, count_y, rows_y, count_z, rows_z)
-    back = back.transpose(2, 4, 0, 1, 3, 5).reshape(spread, width, pair_count, rows_y * rows_z)
+    back = back_z.reshape(width, pair_count, count_z, rows_z, count_y, rows_y)
+    back = back.transpose(4, 2, 0, 1, 5, 3).reshape(spread, width, pair_count, rows_y * rows_z)
     rider = jnp.broadcast_to(energy_part[None, None, :, None], (spread, width, pair_count, 128))
     back = jnp.concatenate((back, rider), axis=3)
     got = lax.all_to_all(back, ("gy", "gz"), 0, 0, tiled=True)

time: 171 us -> 165 us (0.965)
  local copies, waits for them, and re-layouts: 27.2 us -> 22.8 us
  matrix products: 26.9 us -> 24.9 us
    transpose x2 -> x1, local copies, waits for them, and re-layouts: 9.09 us -> 3.44 us  [potentials(): back.transpose(4, 2, 0, 1, 5, 3)]
    dot_general x6, matrix products: 16.8 us -> 14.8 us  [contract(): lax.dot_general(left, right, (((left_dim,), (right_dim,)), ((), ())), pre...]
    reshape x2 -> x3, local copies, waits for them, and re-layouts: 8.51 us -> 9.5 us  [the longest x2 5.34 us: potentials(): got = got.reshape(count_y, count_z, width, pair_count, rows_z, rows_y)]
where the time goes in v7:
time: 165 us; the launch traced here: 164 us
  waiting for transfers between devices  82.6 us (50%)
  matrix products  24.9 us (15%)
  starting transfers between devices  24.3 us (15%)
  local copies, waits for them, and re-layouts  22.8 us (14%)
  other arithmetic  5.78 us (4%)
  between operations  3.96 us (2%)
    all_to_all x1, waiting for transfers between devices, shards(): partner = jnp.sum(lax.all_to_all(slots, 'band', 0, 0, tiled=True), axis=0)  50.2 us
    dot_general x6, matrix products, contract(): lax.dot_general(left, right, (((left_dim,), (right_dim,)), ((), ())), pre...  14.8 us
    all_to_all x1, waiting for transfers between devices, potentials(): got = lax.all_to_all(back, ('gy', 'gz'), 0, 0, tiled=True)  13 us
    all_to_all x1, waiting for transfers between devices, potentials(): got = lax.all_to_all(send, ('gy', 'gz'), 0, 0, tiled=True)  12.5 us
    all_to_all x1, starting transfers between devices, potentials(): got = lax.all_to_all(send, ('gy', 'gz'), 0, 0, tiled=True)  5.66 us
    dot_general x2, matrix products, synthesize(): step_one = jnp.matmul(padded, matrix_x, precision=precise_mode)  5.58 us
    reshape x2, local copies, waits for them, and re-layouts, potentials(): got = got.reshape(count_y, count_z, width, pair_count, rows_z, rows_y)  5.34 us
    all_to_all x1, starting transfers between devices, shards(): partner = jnp.sum(lax.all_to_all(slots, 'band', 0, 0, tiled=True), axis=0)  4.87 us
  transfers between devices with their start and end apart: 8, of which 6 were waited for; matrix products, arithmetic and copies ran while one was open for 3% of the time, Pallas kernels for 0%

profile of v7, /device:TPU:0, one launch (start us, length us, event | category | flops | bytes accessed | tf_op | source)
XLA Modules:
  0.0 164.3 jit_solution(2400133441484488521)
XLA Ops:
  0.6 1.1 constant_dynamic-update-slice_fusion.1
  1.7 1.4 constant_dynamic-update-slice_fusion
  3.1 3.0 %collective-permute-start = (f32[3,8,24,96]{3,2,1,0:T(8,128)S(1)}, f32[3,8,24,96]{3,2,1,0:T(8,128)S(1)}, u32[]{:S(2)}, u32[]{:S(2)}) collective-permute-start(f32[3,8,24,96]{3,2,1,0:T(8,128)S(1)} %slice_select_fusion), channel_id=1, source_target_pairs={{0,4},{4,0},{1,5},{5,1},{2,6},{6,2},{3,7},{7,3},{8,12},{12,8},{9,1... | collective-permute-start | bytes 663560 | tf_op jit(solution)/shard_map/ppermute | solution.py:25
  6.8 1.6 collective-permute-start.3
  8.5 4.7 %collective-permute-done = f32[3,8,24,96]{3,2,1,0:T(8,128)S(1)} collective-permute-done((f32[3,8,24,96]{3,2,1,0:T(8,128)S(1)}, f32[3,8,24,96]{3,2,1,0:T(8,128)S(1)}, u32[]{:S(2)}, u32[]{:S(2)}) %collective-permute-start) | collective-permute-done | bytes 221216 | tf_op jit(solution)/shard_map/ppermute | solution.py:25
  13.2 1.3 pad_maximum_fusion.2
  14.5 1.3 collective-permute-start.1
  15.8 1.3 collective-permute-start.2
  17.1 0.0 collective-permute-done.3
  17.1 2.9 %collective-permute-start.4 = (s32[4,1]{0,1:T(1,128)S(1)}, s32[4,1]{0,1:T(1,128)S(1)}, u32[]{:S(2)}, u32[]{:S(2)}) collective-permute-start(s32[4,1]{0,1:T(1,128)S(1)} %fusion.372), channel_id=1, source_target_pairs={{0,16},{8,24},{16,0},{24,8},{1,17},{9,25},{17,1},{25,9},{2,18},{10... | collective-permute-start | bytes 56 | tf_op jit(solution)/shard_map/ppermute | solution.py:45
  20.0 1.6 collective-permute-done.4
  21.7 0.6 collective-permute-done.2
  22.3 3.4 %fusion = f32[2,64,40,96]{3,2,1,0:T(8,128)S(1)} fusion(f32[3,64,8,96]{3,2,1,0:T(8,128)} %collective-permute-done.2, f32[3,8,24,96]{3,2,1,0:T(8,128)S(1)} %get-tuple-element.13, f32[3,48,24,96]{3,2,1,0:T(8,128)S(1)} %constant_dynamic-update-slice_fusion, f32[3,8,24,96]{3,2,1,0:T(8,128)S(1)} %get-tuple-element.12, f32[3,64,8,96]{3,2,1,0:T(8,128)S(1)} %collective-permute-done.1), kind=kOutput, calls=%fused_computation.2 | convolution fusion | flops 569622528 | bytes 4915200 | tf_op jit(solution)/shard_map/dot_general | solution.py:65
  25.7 1.5 convolution_bitcast_fusion.2
  27.2 1.4 fusion.19
  28.6 0.1 slice_bitcast_fusion.1
  28.7 0.2 copy.37
  28.9 0.2 copy.38
  29.1 1.6 select_select_fusion
  30.7 4.9 %all-to-all-start = ((f32[4,1,48,24,96]{4,3,2,1,0:T(8,128)}), f32[4,1,48,24,96]{4,3,2,1,0:T(8,128)}, u32[]{:S(2)}, u32[]{:S(2)}) async-start(f32[4,1,48,24,96]{4,3,2,1,0:T(8,128)} %select_select_fusion), calls=%async_computation | async-start | bytes 4718592 | tf_op jit(solution)/shard_map/all_to_all | solution.py:150
  35.6 2.2 %fusion.22 = f32[64,40,96]{2,1,0:T(8,128)S(1)} fusion(f32[3,64,8,96]{3,2,1,0:T(8,128)} %collective-permute-done.2, f32[3,64,8,96]{3,2,1,0:T(8,128)S(1)} %collective-permute-done.1, f32[3,8,24,96]{3,2,1,0:T(8,128)S(1)} %get-tuple-element.13, f32[3,48,24,96]{3,2,1,0:T(8,128)S(1)} %constant_dynamic-update-slice_fusion, f32[3,8,24,96]{3,2,1,0:T(8,128)S(1)} %get-tuple-element.12), kind=kOutput, calls=%fused_computation.28 | convolution fusion | flops 284540928 | bytes 3932160 | tf_op jit(solution)/shard_map/dot_general | solution.py:65
  37.8 0.8 convolution_bitcast_fusion.3
  38.6 50.2 %all-to-all-done = f32[4,1,48,24,96]{4,3,2,1,0:T(8,128)} async-done(((f32[4,1,48,24,96]{4,3,2,1,0:T(8,128)}), f32[4,1,48,24,96]{4,3,2,1,0:T(8,128)}, u32[]{:S(2)}, u32[]{:S(2)}) %all-to-all-start) | async-done | bytes 1769504 | tf_op jit(solution)/shard_map/all_to_all | solution.py:150
  88.8 1.9 %reduce_sum.27 = f32[48,24,96]{2,1,0:T(8,128)S(1)} reduce(f32[4,1,48,24,96]{4,3,2,1,0:T(8,128)} %all-to-all-done, f32[]{:T(128)} %constant.55.clone.1), dimensions={0,1}, to_apply=%region_0.1 | reduce | flops 331776 | bytes 2211844 | tf_op jit(solution)/shard_map/reduce_sum | solution.py:150
  90.7 0.8 convolution_multiply_fusion.1
  91.5 1.9 %convolution_bitcast_fusion = f32[8,24,1,1152]{3,1,2,0:T(8,128)} fusion(f32[1152,96,1]{1,0,2:T(8,128)S(1)} %bitcast.125, s32[8,24]{1,0:T(8,128)S(1)} %add_select_fusion.3, pred[8,24]{1,0:T(8,128)(4,1)S(1)} %fusion.133), kind=kOutput, calls=%fused_computation.13 | convolution fusion | flops 127586304 | bytes 1328064 | tf_op jit(solution)/shard_map/dot_general | solution.py:89
  93.4 5.7 %all-to-all-start.1 = ((f32[8,24,1,1152]{3,1,2,0:T(8,128)}), f32[8,24,1,1152]{3,1,2,0:T(8,128)}, u32[]{:S(2)}, u32[]{:S(2)}) async-start(f32[8,24,1,1152]{3,1,2,0:T(8,128)} %convolution_bitcast_fusion), calls=%async_computation.1 | async-start | bytes 1769472 | tf_op jit(solution)/shard_map/all_to_all | solution.py:105
  99.1 0.1 or_select_fusion.1
  99.2 0.1 or_select_fusion
  99.2 0.1 broadcast_multiply_fusion
  99.3 0.1 broadcast_add_fusion
  99.4 12.5 %all-to-all-done.1 = f32[8,24,1,1152]{3,1,2,0:T(8,128)} async-done(((f32[8,24,1,1152]{3,1,2,0:T(8,128)}), f32[8,24,1,1152]{3,1,2,0:T(8,128)}, u32[]{:S(2)}, u32[]{:S(2)}) %all-to-all-start.1) | async-done | bytes 884768 | tf_op jit(solution)/shard_map/all_to_all | solution.py:105
  111.9 2.1 %reshape.375 = f32[2,4,24,1,24,48]{5,4,2,1,0,3:T(8,128)S(1)} reshape(f32[8,24,1,1152]{3,1,2,0:T(8,128)} %all-to-all-done.1) | data formatting | bytes 1769472 | tf_op jit(solution)/shard_map/reshape | solution.py:106
  114.0 3.2 %copy.64 = f32[2,4,24,1,24,48]{5,0,4,1,2,3:T(2,128)} copy(f32[2,4,24,1,24,48]{5,4,2,1,0,3:T(8,128)S(1)} %reshape.375) | data formatting | bytes 1769472 | tf_op jit(solution)/shard_map/reshape | solution.py:106
  117.3 2.7 %reshape.376 = f32[24,96,96]{2,1,0:T(8,128)S(1)} reshape(f32[24,1,4,24,2,48]{5,4,3,2,0,1:T(2,128)} %bitcast.120) | data formatting | bytes 1769472 | tf_op jit(solution)/shard_map/reshape.23
  120.0 1.9 %fusion.46 = f32[24,96,192]{1,2,0:T(8,128)S(1)} fusion(f32[24,96,96]{2,1,0:T(8,128)S(1)} %reshape.376, s32[192]{0:T(256)S(1)} %add_select_fusion.4, pred[192]{0:T(512)(128)(4,1)S(1)} %iota_compare_fusion), kind=kOutput, calls=%fused_computation.67 | convolution fusion | flops 254988288 | bytes 2655168 | tf_op jit(solution)/shard_map/dot_general | solution.py:89
  121.9 3.8 %multiply_reduce_fusion = (f32[]{:T(128)}, f32[24,192,192]{2,1,0:T(8,128)S(1)}) fusion(f32[192]{0:T(256)S(1)} %get-tuple-element.21, f32[24,192]{1,0:T(8,128)S(1)} %broadcast_add_fusion, f32[192]{0:T(256)S(1)} %get-tuple-element.20, f32[24,192]{1,0:T(8,128)S(1)} %broadcast_multiply_fusion, f32[24,96,192]{1,2,0:T(8,128)S(1)} %fusion.46, ...), kind=kOutput, calls=%fused_computation | convolution fusion | flops 516870144 | bytes 5347780 | tf_op jit(solution)/shard_map/dot_general | solution.py:89
  125.7 3.8 %fusion.10 = f32[24,192,96]{1,2,0:T(8,128)S(1)} fusion(f32[24,192,192]{2,1,0:T(8,128)S(1)} %get-tuple-element.17, f32[192]{0:T(256)S(1)} %get-tuple-element.21, f32[24,192]{1,0:T(8,128)S(1)} %broadcast_add_fusion, f32[192]{0:T(256)S(1)} %get-tuple-element.20, f32[24,192]{1,0:T(8,128)S(1)} %broadcast_multiply_fusion, s32[192]{0:T(256)S(1)} %add_select_fusion.4, ...), kind=kOutput, calls=%fused_computation.12 | convolution fusion | flops 515100672 | bytes 5347776 | tf_op jit(solution)/shard_map/dot_general | solution.py:89
  129.5 1.6 convolution_bitcast_fusion.1
  131.0 3.4 %copy.44 = f32[2,4,24,1,48,24]{5,4,2,1,0,3:T(8,128)} copy(f32[2,4,24,1,48,24]{4,5,0,1,2,3:T(8,128)S(1)} %convolution_bitcast_fusion.1) | data formatting | bytes 1769472 | tf_op jit(solution)/shard_map/transpose | solution.py:126
  134.5 4.2 %reshape.378 = f32[8,24,1,1152]{3,1,0,2:T(8,128)S(1)} reshape(f32[2,4,24,1,48,24]{5,4,2,1,0,3:T(8,128)} %copy.44) | data formatting | bytes 1769472 | tf_op jit(solution)/shard_map/reshape | solution.py:126
  138.6 1.7 %pad_bitcast_fusion = f32[8,24,1,1280]{3,1,2,0:T(8,128)} fusion(f32[8,24,1,1152]{3,1,0,2:T(8,128)S(1)} %reshape.378, f32[]{:T(128)} %get-tuple-element.16), kind=kLoop, calls=%fused_computation.43 | loop fusion | bytes 1867780 | tf_op jit(solution)/shard_map/concatenate | solution.py:128
  140.3 3.6 %all-to-all-start.2 = ((f32[8,24,1,1280]{3,1,2,0:T(8,128)}), f32[8,24,1,1280]{3,1,2,0:T(8,128)S(1)}, u32[]{:S(2)}, u32[]{:S(2)}) async-start(f32[8,24,1,1280]{3,1,2,0:T(8,128)} %pad_bitcast_fusion), calls=%async_computation.2 | async-start | bytes 1966080 | tf_op jit(solution)/shard_map/all_to_all | solution.py:129
  144.5 13.0 %all-to-all-done.2 = f32[8,24,1,1280]{3,1,2,0:T(8,128)S(1)} async-done(((f32[8,24,1,1280]{3,1,2,0:T(8,128)}), f32[8,24,1,1280]{3,1,2,0:T(8,128)S(1)}, u32[]{:S(2)}, u32[]{:S(2)}) %all-to-all-start.2) | async-done | bytes 983072 | tf_op jit(solution)/shard_map/all_to_all | solution.py:129
  157.6 1.0 slice.44
  158.5 1.5 copy.47
  160.1 0.6 slice_reduce_fusion
  161.3 1.9 %fusion.33 = f32[1,48,24,96]{3,2,1,0:T(8,128)} fusion(f32[48,24,96]{2,1,0:T(8,128)S(1)} %reduce_sum.27, f32[48,24,192]{2,1,0:T(8,128)S(1)} %bitcast.121, f32[]{:T(128)} %bitcast, s32[192]{0:T(256)S(1)} %add_select_fusion.4, pred[192]{0:T(512)(128)(4,1)S(1)} %iota_compare_fusion), kind=kOutput, calls=%fused_computation.41 | convolution fusion | flops 127918080 | bytes 1770436 | tf_op jit(solution)/shard_map/dot_general | solution.py:89
  (13 shorter events, 0.1 us)
Async XLA Ops:
  3.1 10.0 %collective-permute-start = (f32[3,8,24,96]{3,2,1,0:T(8,128)S(1)}, f32[3,8,24,96]{3,2,1,0:T(8,128)S(1)}, u32[]{:S(2)}, u32[]{:S(2)}) collective-permute-start(f32[3,8,24,96]{3,2,1,0:T(8,128)S(1)} %slice_select_fusion), channel_id=1, source_target_pairs={{0,4},{4,0},{1,5},{5,1},{2,6},{6,2},{3,7},{7,3},{8,12},{12,8},{9,1... | collective-permute-start | bytes 663560 | tf_op jit(solution)/shard_map/ppermute | solution.py:25
  6.8 10.3 %collective-permute-start.3 = (s32[4,1]{0,1:T(1,128)S(1)}, s32[4,1]{0,1:T(1,128)S(1)}, u32[]{:S(2)}, u32[]{:S(2)}) collective-permute-start(s32[4,1]{0,1:T(1,128)S(1)} %compare_select_fusion.1), channel_id=1, source_target_pairs={{0,8},{8,0},{16,24},{24,16},{1,9},{9,1},{17,25},{25,17},{2,10},{10... | collective-permute-start | bytes 56 | tf_op jit(solution)/shard_map/ppermute | solution.py:45
  14.5 7.2 %collective-permute-start.1 = (f32[3,64,8,96]{3,2,1,0:T(8,128)}, f32[3,64,8,96]{3,2,1,0:T(8,128)S(1)}, u32[]{:S(2)}, u32[]{:S(2)}) collective-permute-start(f32[3,64,8,96]{3,2,1,0:T(8,128)} %get-tuple-element.8), channel_id=1, source_target_pairs={{0,1},{1,2},{2,3},{4,5},{5,6},{6,7},{8,9},{9,10},{10,11},{12,13},{... | collective-permute-start | bytes 1769480 | tf_op jit(solution)/shard_map/ppermute | solution.py:30
  15.8 6.5 %collective-permute-start.2 = (f32[3,64,8,96]{3,2,1,0:T(8,128)}, f32[3,64,8,96]{3,2,1,0:T(8,128)}, u32[]{:S(2)}, u32[]{:S(2)}) collective-permute-start(f32[3,64,8,96]{3,2,1,0:T(8,128)} %get-tuple-element.9), channel_id=1, source_target_pairs={{1,0},{2,1},{3,2},{5,4},{6,5},{7,6},{9,8},{10,9},{11,10},{13,12},{... | collective-permute-start | bytes 1769480 | tf_op jit(solution)/shard_map/ppermute | solution.py:31
  17.1 4.5 %collective-permute-start.4 = (s32[4,1]{0,1:T(1,128)S(1)}, s32[4,1]{0,1:T(1,128)S(1)}, u32[]{:S(2)}, u32[]{:S(2)}) collective-permute-start(s32[4,1]{0,1:T(1,128)S(1)} %fusion.372), channel_id=1, source_target_pairs={{0,16},{8,24},{16,0},{24,8},{1,17},{9,25},{17,1},{25,9},{2,18},{10... | collective-permute-start | bytes 56 | tf_op jit(solution)/shard_map/ppermute | solution.py:45
  30.7 58.1 %all-to-all-start = ((f32[4,1,48,24,96]{4,3,2,1,0:T(8,128)}), f32[4,1,48,24,96]{4,3,2,1,0:T(8,128)}, u32[]{:S(2)}, u32[]{:S(2)}) async-start(f32[4,1,48,24,96]{4,3,2,1,0:T(8,128)} %select_select_fusion), calls=%async_computation | async-start | bytes 4718592 | tf_op jit(solution)/shard_map/all_to_all | solution.py:150
  93.4 18.5 %all-to-all-start.1 = ((f32[8,24,1,1152]{3,1,2,0:T(8,128)}), f32[8,24,1,1152]{3,1,2,0:T(8,128)}, u32[]{:S(2)}, u32[]{:S(2)}) async-start(f32[8,24,1,1152]{3,1,2,0:T(8,128)} %convolution_bitcast_fusion), calls=%async_computation.1 | async-start | bytes 1769472 | tf_op jit(solution)/shard_map/all_to_all | solution.py:105
  140.3 17.2 %all-to-all-start.2 = ((f32[8,24,1,1280]{3,1,2,0:T(8,128)}), f32[8,24,1,1280]{3,1,2,0:T(8,128)S(1)}, u32[]{:S(2)}, u32[]{:S(2)}) async-start(f32[8,24,1,1280]{3,1,2,0:T(8,128)} %pad_bitcast_fusion), calls=%async_computation.2 | async-start | bytes 1966080 | tf_op jit(solution)/shard_map/all_to_all | solution.py:129

commit v8 on v7

--- a/solution.py
+++ b/solution.py
@@ -123,14 +123,15 @@
     back_y = contract(weighted, table, 3, 1)
     back_z = contract(back_y, table, 2, 1)
     back = back_z.reshape(width, pair_count, count_z, rows_z, count_y, rows_y)
-    back = back.transpose(4, 2, 0, 1, 5, 3).reshape(spread, width, pair_count, rows_y * rows_z)
+    back = back.transpose(4, 2, 0, 1, 3, 5).reshape(spread, width, pair_count, rows_y * rows_z)
     rider = jnp.broadcast_to(energy_part[None, None, :, None], (spread, width, pair_count, 128))
     back = jnp.concatenate((back, rider), axis=3)
     got = lax.all_to_all(back, ("gy", "gz"), 0, 0, tiled=True)
     energy_total = jnp.sum(got[:, 0, :, rows_y * rows_z], axis=0)
     got = got[:, :, :, : rows_y * rows_z].reshape(period, pair_count, rows_y * rows_z)
     result = contract(got, table, 0, 1)
-    return result.reshape(pair_count, rows_y, rows_z, length), energy_total
+    result = result.reshape(pair_count, rows_z, rows_y, length).transpose(0, 2, 1, 3)
+    return result, energy_total
 
 
 def shards(i_coeff, j_coeff, pair_orbital, pair_occ):

time: 165 us -> 163 us (0.988)
  local copies, waits for them, and re-layouts: 22.8 us -> 19.2 us
    transpose x1, local copies, waits for them, and re-layouts: 3.44 us -> 0.15 us  [potentials(): back.transpose(4, 2, 0, 1, 3, 5)]
    ppermute x1, starting transfers between devices: 1.33 us -> 3.96 us  [extended(): before = lax.ppermute(tail, axis, [(i, i + 1) for i in range(count - 1)])]
    reshape x1, local copies, waits for them, and re-layouts: 4.17 us -> 1.69 us  [potentials(): back.transpose(4, 2, 0, 1, 3, 5)]
  transfers between devices with their start and end apart: 8 -> 8, of which waited for: 6 -> 5; matrix products, arithmetic and copies ran while one was open for 3% -> 3% of each run, Pallas kernels for 0% -> 0%
where the time goes in v8:
time: 163 us; the launch traced here: 162 us
  waiting for transfers between devices  83.2 us (51%)
  starting transfers between devices  25.9 us (16%)
  matrix products  24.1 us (15%)
  local copies, waits for them, and re-layouts  19.2 us (12%)
  other arithmetic  5.78 us (4%)
  between operations  3.95 us (2%)
    all_to_all x1, waiting for transfers between devices, shards(): partner = jnp.sum(lax.all_to_all(slots, 'band', 0, 0, tiled=True), axis=0)  51.2 us
    dot_general x6, matrix products, contract(): lax.dot_general(left, right, (((left_dim,), (right_dim,)), ((), ())), pre...  14 us
    all_to_all x1, waiting for transfers between devices, potentials(): got = lax.all_to_all(back, ('gy', 'gz'), 0, 0, tiled=True)  13 us
    all_to_all x1, waiting for transfers between devices, potentials(): got = lax.all_to_all(send, ('gy', 'gz'), 0, 0, tiled=True)  12.7 us
    dot_general x2, matrix products, synthesize(): step_one = jnp.matmul(padded, matrix_x, precision=precise_mode)  5.58 us
    reshape x2, local copies, waits for them, and re-layouts, potentials(): got = got.reshape(count_y, count_z, width, pair_count, rows_z, rows_y)  5.34 us
    all_to_all x1, starting transfers between devices, shards(): partner = jnp.sum(lax.all_to_all(slots, 'band', 0, 0, tiled=True), axis=0)  5.12 us
    ppermute x1, waiting for transfers between devices, extended(): got = lax.ppermute(jnp.where(first, tail, head), axis, [(0, 1), (1, 0)])  4.7 us
  transfers between devices with their start and end apart: 8, of which 5 were waited for; matrix products, arithmetic and copies ran while one was open for 3% of the time, Pallas kernels for 0%

profile of v8, /device:TPU:0, one launch (start us, length us, event | category | flops | bytes accessed | tf_op | source)
XLA Modules:
  0.0 162.1 jit_solution(17828273445424762401)
XLA Ops:
  0.6 1.1 constant_dynamic-update-slice_fusion.1
  1.7 1.4 constant_dynamic-update-slice_fusion
  3.1 3.0 %collective-permute-start = (f32[3,8,24,96]{3,2,1,0:T(8,128)S(1)}, f32[3,8,24,96]{3,2,1,0:T(8,128)S(1)}, u32[]{:S(2)}, u32[]{:S(2)}) collective-permute-start(f32[3,8,24,96]{3,2,1,0:T(8,128)S(1)} %slice_select_fusion), channel_id=1, source_target_pairs={{0,4},{4,0},{1,5},{5,1},{2,6},{6,2},{3,7},{7,3},{8,12},{12,8},{9,1... | collective-permute-start | bytes 663560 | tf_op jit(solution)/shard_map/ppermute | solution.py:25
  6.8 1.6 %collective-permute-start.3 = (s32[4,1]{0,1:T(1,128)S(1)}, s32[4,1]{0,1:T(1,128)S(1)}, u32[]{:S(2)}, u32[]{:S(2)}) collective-permute-start(s32[4,1]{0,1:T(1,128)S(1)} %compare_select_fusion.1), channel_id=1, source_target_pairs={{0,8},{8,0},{16,24},{24,16},{1,9},{9,1},{17,25},{25,17},{2,10},{10... | collective-permute-start | bytes 56 | tf_op jit(solution)/shard_map/ppermute | solution.py:45
  8.4 4.7 %collective-permute-done = f32[3,8,24,96]{3,2,1,0:T(8,128)S(1)} collective-permute-done((f32[3,8,24,96]{3,2,1,0:T(8,128)S(1)}, f32[3,8,24,96]{3,2,1,0:T(8,128)S(1)}, u32[]{:S(2)}, u32[]{:S(2)}) %collective-permute-start) | collective-permute-done | bytes 221216 | tf_op jit(solution)/shard_map/ppermute | solution.py:25
  13.2 1.3 pad_maximum_fusion.2
  14.5 1.3 collective-permute-start.2
  15.7 4.0 %collective-permute-start.1 = (f32[3,64,8,96]{3,2,1,0:T(8,128)}, f32[3,64,8,96]{3,2,1,0:T(8,128)}, u32[]{:S(2)}, u32[]{:S(2)}) collective-permute-start(f32[3,64,8,96]{3,2,1,0:T(8,128)} %get-tuple-element.10), channel_id=1, source_target_pairs={{0,1},{1,2},{2,3},{4,5},{5,6},{6,7},{8,9},{9,10},{10,11},{12,13},{... | collective-permute-start | bytes 1769480 | tf_op jit(solution)/shard_map/ppermute | solution.py:30
  19.7 2.9 %collective-permute-start.4 = (s32[4,1]{0,1:T(1,128)S(1)}, s32[4,1]{0,1:T(1,128)S(1)}, u32[]{:S(2)}, u32[]{:S(2)}) collective-permute-start(s32[4,1]{0,1:T(1,128)S(1)} %fusion.372), channel_id=1, source_target_pairs={{0,16},{8,24},{16,0},{24,8},{1,17},{9,25},{17,1},{25,9},{2,18},{10... | collective-permute-start | bytes 56 | tf_op jit(solution)/shard_map/ppermute | solution.py:45
  22.6 1.6 collective-permute-done.4
  24.2 0.0 collective-permute-done.2
  24.3 3.4 %fusion = f32[2,64,40,96]{3,2,1,0:T(8,128)S(1)} fusion(f32[3,64,8,96]{3,2,1,0:T(8,128)S(1)} %collective-permute-done.2, f32[3,8,24,96]{3,2,1,0:T(8,128)S(1)} %get-tuple-element.15, f32[3,48,24,96]{3,2,1,0:T(8,128)S(1)} %constant_dynamic-update-slice_fusion, f32[3,8,24,96]{3,2,1,0:T(8,128)S(1)} %get-tuple-element.14, f32[3,64,8,96]{3,2,1,0:T(8,128)} %collective-permute-done.1), kind=kOutput, calls=%fused_computation.2 | convolution fusion | flops 569622528 | bytes 4915200 | tf_op jit(solution)/shard_map/dot_general | solution.py:65
  27.6 1.5 convolution_bitcast_fusion.2
  29.2 1.4 fusion.19
  30.6 0.1 slice_bitcast_fusion.1
  30.6 0.2 copy.35
  30.8 0.2 copy.34
  31.0 1.6 %select_select_fusion = f32[4,1,48,24,96]{4,3,2,1,0:T(8,128)} fusion(f32[48,24,96]{2,1,0:T(8,128)S(1)} %copy.35, f32[48,24,96]{2,1,0:T(8,128)S(1)} %copy.34, pred[4]{0:T(512)(128)(4,1)S(1)} %get-tuple-element.17, pred[4]{0:T(512)(128)(4,1)S(1)} %get-tuple-element.16), kind=kLoop, calls=%fused_computation.21 | loop fusion | flops 884736 | bytes 2654216 | tf_op jit(solution)/shard_map/jit(_where)/select_n | solution.py:150
  32.7 5.1 %all-to-all-start = ((f32[4,1,48,24,96]{4,3,2,1,0:T(8,128)}), f32[4,1,48,24,96]{4,3,2,1,0:T(8,128)}, u32[]{:S(2)}, u32[]{:S(2)}) async-start(f32[4,1,48,24,96]{4,3,2,1,0:T(8,128)} %select_select_fusion), calls=%async_computation | async-start | bytes 4718592 | tf_op jit(solution)/shard_map/all_to_all | solution.py:151
  37.8 2.2 %fusion.22 = f32[64,40,96]{2,1,0:T(8,128)S(1)} fusion(f32[3,64,8,96]{3,2,1,0:T(8,128)S(1)} %collective-permute-done.2, f32[3,64,8,96]{3,2,1,0:T(8,128)} %collective-permute-done.1, f32[3,8,24,96]{3,2,1,0:T(8,128)S(1)} %get-tuple-element.15, f32[3,48,24,96]{3,2,1,0:T(8,128)S(1)} %constant_dynamic-update-slice_fusion, f32[3,8,24,96]{3,2,1,0:T(8,128)S(1)} %get-tuple-element.14), kind=kOutput, calls=%fused_computation.28 | convolution fusion | flops 284540928 | bytes 3932160 | tf_op jit(solution)/shard_map/dot_general | solution.py:65
  40.0 0.8 convolution_bitcast_fusion.3
  40.9 51.2 %all-to-all-done = f32[4,1,48,24,96]{4,3,2,1,0:T(8,128)} async-done(((f32[4,1,48,24,96]{4,3,2,1,0:T(8,128)}), f32[4,1,48,24,96]{4,3,2,1,0:T(8,128)}, u32[]{:S(2)}, u32[]{:S(2)}) %all-to-all-start) | async-done | bytes 1769504 | tf_op jit(solution)/shard_map/all_to_all | solution.py:151
  92.1 1.9 %reduce_sum.33 = f32[48,24,96]{2,1,0:T(8,128)S(1)} reduce(f32[4,1,48,24,96]{4,3,2,1,0:T(8,128)} %all-to-all-done, f32[]{:T(128)} %constant.55.clone.1), dimensions={0,1}, to_apply=%region_0.1 | reduce | flops 331776 | bytes 2211844 | tf_op jit(solution)/shard_map/reduce_sum | solution.py:151
  94.0 0.8 convolution_multiply_fusion.1
  94.8 1.9 %convolution_bitcast_fusion = f32[8,24,1,1152]{3,1,2,0:T(8,128)} fusion(f32[1152,96,1]{1,0,2:T(8,128)S(1)} %bitcast.133, s32[8,24]{1,0:T(8,128)S(1)} %add_select_fusion.3, pred[8,24]{1,0:T(8,128)(4,1)S(1)} %fusion.133), kind=kOutput, calls=%fused_computation.13 | convolution fusion | flops 127586304 | bytes 1328064 | tf_op jit(solution)/shard_map/dot_general | solution.py:89
  96.7 4.4 %all-to-all-start.1 = ((f32[8,24,1,1152]{3,1,2,0:T(8,128)}), f32[8,24,1,1152]{3,1,2,0:T(8,128)}, u32[]{:S(2)}, u32[]{:S(2)}) async-start(f32[8,24,1,1152]{3,1,2,0:T(8,128)} %convolution_bitcast_fusion), calls=%async_computation.1 | async-start | bytes 1769472 | tf_op jit(solution)/shard_map/all_to_all | solution.py:105
  101.1 0.1 or_select_fusion.1
  101.2 0.1 or_select_fusion
  101.3 0.1 broadcast_add_fusion
  101.3 0.1 broadcast_multiply_fusion
  101.4 12.7 %all-to-all-done.1 = f32[8,24,1,1152]{3,1,2,0:T(8,128)} async-done(((f32[8,24,1,1152]{3,1,2,0:T(8,128)}), f32[8,24,1,1152]{3,1,2,0:T(8,128)}, u32[]{:S(2)}, u32[]{:S(2)}) %all-to-all-start.1) | async-done | bytes 884768 | tf_op jit(solution)/shard_map/all_to_all | solution.py:105
  114.1 2.1 %reshape.376 = f32[2,4,24,1,24,48]{5,4,2,1,0,3:T(8,128)S(1)} reshape(f32[8,24,1,1152]{3,1,2,0:T(8,128)} %all-to-all-done.1) | data formatting | bytes 1769472 | tf_op jit(solution)/shard_map/reshape | solution.py:106
  116.2 3.2 %copy.64 = f32[2,4,24,1,24,48]{5,0,4,1,2,3:T(2,128)} copy(f32[2,4,24,1,24,48]{5,4,2,1,0,3:T(8,128)S(1)} %reshape.376) | data formatting | bytes 1769472 | tf_op jit(solution)/shard_map/reshape | solution.py:106
  119.4 2.7 %reshape.377 = f32[24,96,96]{2,1,0:T(8,128)S(1)} reshape(f32[24,1,4,24,2,48]{5,4,3,2,0,1:T(2,128)} %bitcast.128) | data formatting | bytes 1769472 | tf_op jit(solution)/shard_map/reshape.23
  122.2 1.9 %fusion.46 = f32[24,96,192]{1,2,0:T(8,128)S(1)} fusion(f32[24,96,96]{2,1,0:T(8,128)S(1)} %reshape.377, s32[192]{0:T(256)S(1)} %add_select_fusion.4, pred[192]{0:T(512)(128)(4,1)S(1)} %iota_compare_fusion), kind=kOutput, calls=%fused_computation.67 | convolution fusion | flops 254988288 | bytes 2655168 | tf_op jit(solution)/shard_map/dot_general | solution.py:89
  124.0 3.8 %multiply_reduce_fusion = (f32[]{:T(128)}, f32[24,192,192]{2,1,0:T(8,128)S(1)}) fusion(f32[192]{0:T(256)S(1)} %get-tuple-element.23, f32[24,192]{1,0:T(8,128)S(1)} %broadcast_add_fusion, f32[192]{0:T(256)S(1)} %get-tuple-element.22, f32[24,192]{1,0:T(8,128)S(1)} %broadcast_multiply_fusion, f32[24,96,192]{1,2,0:T(8,128)S(1)} %fusion.46, ...), kind=kOutput, calls=%fused_computation | convolution fusion | flops 516870144 | bytes 5347780 | tf_op jit(solution)/shard_map/dot_general | solution.py:89
  127.8 3.8 %fusion.10 = f32[24,192,96]{1,2,0:T(8,128)S(1)} fusion(f32[24,192,192]{2,1,0:T(8,128)S(1)} %get-tuple-element.19, f32[192]{0:T(256)S(1)} %get-tuple-element.23, f32[24,192]{1,0:T(8,128)S(1)} %broadcast_add_fusion, f32[192]{0:T(256)S(1)} %get-tuple-element.22, f32[24,192]{1,0:T(8,128)S(1)} %broadcast_multiply_fusion, s32[192]{0:T(256)S(1)} %add_select_fusion.4, ...), kind=kOutput, calls=%fused_computation.12 | convolution fusion | flops 515100672 | bytes 5347776 | tf_op jit(solution)/shard_map/dot_general | solution.py:89
  131.6 1.6 convolution_bitcast_fusion.1
  133.2 0.2 copy.41
  133.4 1.7 %reshape.379 = f32[8,24,1,1152]{3,1,0,2:T(8,128)} reshape(f32[2,4,24,1,24,48]{5,4,2,1,0,3:T(8,128)S(1)} %copy.41) | data formatting | bytes 1769472 | tf_op jit(solution)/shard_map/reshape | solution.py:126
  135.1 2.8 %pad_bitcast_fusion = f32[8,24,1,1280]{3,1,2,0:T(8,128)} fusion(f32[8,24,1,1152]{3,1,0,2:T(8,128)} %reshape.379, f32[]{:T(128)} %get-tuple-element.18), kind=kLoop, calls=%fused_computation.43 | loop fusion | bytes 1867780 | tf_op jit(solution)/shard_map/concatenate | solution.py:128
  137.9 3.6 %all-to-all-start.2 = ((f32[8,24,1,1280]{3,1,2,0:T(8,128)}), f32[8,24,1,1280]{3,1,2,0:T(8,128)S(1)}, u32[]{:S(2)}, u32[]{:S(2)}) async-start(f32[8,24,1,1280]{3,1,2,0:T(8,128)} %pad_bitcast_fusion), calls=%async_computation.2 | async-start | bytes 1966080 | tf_op jit(solution)/shard_map/all_to_all | solution.py:129
  142.1 13.0 %all-to-all-done.2 = f32[8,24,1,1280]{3,1,2,0:T(8,128)S(1)} async-done(((f32[8,24,1,1280]{3,1,2,0:T(8,128)}), f32[8,24,1,1280]{3,1,2,0:T(8,128)S(1)}, u32[]{:S(2)}, u32[]{:S(2)}) %all-to-all-start.2) | async-done | bytes 983072 | tf_op jit(solution)/shard_map/all_to_all | solution.py:129
  155.1 1.0 slice.44
  156.1 1.5 copy.44
  157.7 1.0 fusion.33
  158.7 1.0 copy.46
  159.7 0.6 slice_reduce_fusion
  (14 shorter events, 0.1 us)
Async XLA Ops:
  3.1 10.0 %collective-permute-start = (f32[3,8,24,96]{3,2,1,0:T(8,128)S(1)}, f32[3,8,24,96]{3,2,1,0:T(8,128)S(1)}, u32[]{:S(2)}, u32[]{:S(2)}) collective-permute-start(f32[3,8,24,96]{3,2,1,0:T(8,128)S(1)} %slice_select_fusion), channel_id=1, source_target_pairs={{0,4},{4,0},{1,5},{5,1},{2,6},{6,2},{3,7},{7,3},{8,12},{12,8},{9,1... | collective-permute-start | bytes 663560 | tf_op jit(solution)/shard_map/ppermute | solution.py:25
  6.8 12.9 %collective-permute-start.3 = (s32[4,1]{0,1:T(1,128)S(1)}, s32[4,1]{0,1:T(1,128)S(1)}, u32[]{:S(2)}, u32[]{:S(2)}) collective-permute-start(s32[4,1]{0,1:T(1,128)S(1)} %compare_select_fusion.1), channel_id=1, source_target_pairs={{0,8},{8,0},{16,24},{24,16},{1,9},{9,1},{17,25},{25,17},{2,10},{10... | collective-permute-start | bytes 56 | tf_op jit(solution)/shard_map/ppermute | solution.py:45
  14.5 9.8 %collective-permute-start.2 = (f32[3,64,8,96]{3,2,1,0:T(8,128)}, f32[3,64,8,96]{3,2,1,0:T(8,128)S(1)}, u32[]{:S(2)}, u32[]{:S(2)}) collective-permute-start(f32[3,64,8,96]{3,2,1,0:T(8,128)} %get-tuple-element.11), channel_id=1, source_target_pairs={{1,0},{2,1},{3,2},{5,4},{6,5},{7,6},{9,8},{10,9},{11,10},{13,12},{... | collective-permute-start | bytes 1769480 | tf_op jit(solution)/shard_map/ppermute | solution.py:31
  15.7 8.5 %collective-permute-start.1 = (f32[3,64,8,96]{3,2,1,0:T(8,128)}, f32[3,64,8,96]{3,2,1,0:T(8,128)}, u32[]{:S(2)}, u32[]{:S(2)}) collective-permute-start(f32[3,64,8,96]{3,2,1,0:T(8,128)} %get-tuple-element.10), channel_id=1, source_target_pairs={{0,1},{1,2},{2,3},{4,5},{5,6},{6,7},{8,9},{9,10},{10,11},{12,13},{... | collective-permute-start | bytes 1769480 | tf_op jit(solution)/shard_map/ppermute | solution.py:30
  19.7 4.5 %collective-permute-start.4 = (s32[4,1]{0,1:T(1,128)S(1)}, s32[4,1]{0,1:T(1,128)S(1)}, u32[]{:S(2)}, u32[]{:S(2)}) collective-permute-start(s32[4,1]{0,1:T(1,128)S(1)} %fusion.372), channel_id=1, source_target_pairs={{0,16},{8,24},{16,0},{24,8},{1,17},{9,25},{17,1},{25,9},{2,18},{10... | collective-permute-start | bytes 56 | tf_op jit(solution)/shard_map/ppermute | solution.py:45
  32.7 59.4 %all-to-all-start = ((f32[4,1,48,24,96]{4,3,2,1,0:T(8,128)}), f32[4,1,48,24,96]{4,3,2,1,0:T(8,128)}, u32[]{:S(2)}, u32[]{:S(2)}) async-start(f32[4,1,48,24,96]{4,3,2,1,0:T(8,128)} %select_select_fusion), calls=%async_computation | async-start | bytes 4718592 | tf_op jit(solution)/shard_map/all_to_all | solution.py:151
  96.7 17.4 %all-to-all-start.1 = ((f32[8,24,1,1152]{3,1,2,0:T(8,128)}), f32[8,24,1,1152]{3,1,2,0:T(8,128)}, u32[]{:S(2)}, u32[]{:S(2)}) async-start(f32[8,24,1,1152]{3,1,2,0:T(8,128)} %convolution_bitcast_fusion), calls=%async_computation.1 | async-start | bytes 1769472 | tf_op jit(solution)/shard_map/all_to_all | solution.py:105
  137.9 17.2 %all-to-all-start.2 = ((f32[8,24,1,1280]{3,1,2,0:T(8,128)}), f32[8,24,1,1280]{3,1,2,0:T(8,128)S(1)}, u32[]{:S(2)}, u32[]{:S(2)}) async-start(f32[8,24,1,1280]{3,1,2,0:T(8,128)} %pad_bitcast_fusion), calls=%async_computation.2 | async-start | bytes 1966080 | tf_op jit(solution)/shard_map/all_to_all | solution.py:129

commit v9 on v8

--- a/solution.py
+++ b/solution.py
@@ -135,21 +135,19 @@
 
 
 def shards(i_coeff, j_coeff, pair_orbital, pair_occ):
-    fields = jnp.concatenate((i_coeff, j_coeff), 0)
-    padded = extended(fields, (("gy", 1), ("gz", 2)), 8)
-    own_count = i_coeff.shape[0]
-    local_partners = synthesize(padded[own_count:])
-    local_count = local_partners.shape[0]
+    sides = (("gy", 1), ("gz", 2))
+    local_count = j_coeff.shape[0]
     band_count = lax.axis_size("band")
     mine = lax.axis_index("band") == jnp.arange(band_count, dtype=jnp.int32)[:, None]
     wanted = group_sum(jnp.where(mine, pair_orbital, 0), ("band",))
     first_owned = lax.axis_index("band") * local_count
-    slots = jnp.zeros(wanted.shape + local_partners.shape[1:], jnp.float32)
+    slots = jnp.zeros(wanted.shape + j_coeff.shape[1:], jnp.float32)
     for number in range(local_count):
         hit = (wanted == first_owned + number)[:, :, None, None, None]
-        slots = jnp.where(hit, local_partners[number][None, None], slots)
-    partner = jnp.sum(lax.all_to_all(slots, "band", 0, 0, tiled=True), axis=0)
-    own_orbital = synthesize(padded[:own_count])[0]
+        slots = jnp.where(hit, j_coeff[number][None, None], slots)
+    arrived = lax.all_to_all(slots, "band", 0, 0, tiled=True)
+    own_orbital = synthesize(extended(i_coeff, sides, 8))[0]
+    partner = synthesize(extended(jnp.sum(arrived, axis=0), sides, 8))
     density = own_orbital[None] * partner
     potential, energy_part = potentials(density)
     weights = pair_occ[0].astype(jnp.float32)

time: 163 us -> 155 us (0.951)
  waiting for transfers between devices: 83.2 us -> 75.6 us
  starting transfers between devices: 25.9 us -> 31.1 us
  matrix products: 24.1 us -> 20.8 us
    all_to_all x1, waiting for transfers between devices: 51.2 us -> 42.6 us  [shards(): arrived = lax.all_to_all(slots, 'band', 0, 0, tiled=True)]
    ppermute x1 -> x2, waiting for transfers between devices: 0.01 us -> 3.03 us  [extended(): after = lax.ppermute(head, axis, [(i + 1, i) for i in range(count - 1)])]
    all_to_all x1, starting transfers between devices: 4.41 us -> 7.13 us  [potentials(): got = lax.all_to_all(send, ('gy', 'gz'), 0, 0, tiled=True)]
    ppermute x1 -> x2, waiting for transfers between devices: 4.7 us -> 2.65 us  [extended(): got = lax.ppermute(jnp.where(first, tail, head), axis, [(0, 1), (1, 0)])]
    dot_general x2, matrix products: 5.58 us -> 3.62 us  [synthesize(): step_one = jnp.matmul(padded, matrix_x, precision=precise_mode)]
    reduce_sum x1, other arithmetic: 1.89 us -> 0.2 us  [shards(): partner = synthesize(extended(jnp.sum(arrived, axis=0), sides, 8))]
    ppermute x1 -> x2, starting transfers between devices: 3.96 us -> 3.32 us  [extended(): before = lax.ppermute(tail, axis, [(i, i + 1) for i in range(count - 1)])]
  transfers between devices with their start and end apart: 8 -> 11, of which waited for: 5 -> 8; matrix products, arithmetic and copies ran while one was open for 3% -> 5% of each run, Pallas kernels for 0% -> 0%
where the time goes in v9:
time: 155 us; the launch traced here: 154 us
  waiting for transfers between devices  75.6 us (49%)
  starting transfers between devices  31.1 us (20%)
  matrix products  20.8 us (13%)
  local copies, waits for them, and re-layouts  17.6 us (11%)
  other arithmetic  4.86 us (3%)
  between operations  3.97 us (3%)
    all_to_all x1, waiting for transfers between devices, shards(): arrived = lax.all_to_all(slots, 'band', 0, 0, tiled=True)  42.6 us
    dot_general x6, matrix products, contract(): lax.dot_general(left, right, (((left_dim,), (right_dim,)), ((), ())), pre...  14 us
    all_to_all x1, waiting for transfers between devices, potentials(): got = lax.all_to_all(back, ('gy', 'gz'), 0, 0, tiled=True)  13 us
    all_to_all x1, waiting for transfers between devices, potentials(): got = lax.all_to_all(send, ('gy', 'gz'), 0, 0, tiled=True)  12.5 us
    all_to_all x1, starting transfers between devices, potentials(): got = lax.all_to_all(send, ('gy', 'gz'), 0, 0, tiled=True)  7.13 us
    ppermute x2, starting transfers between devices, group_sum(): lax.ppermute(total, axis, [(i, i ^ step) for i in range(count)])  6.12 us
    reshape x2, local copies, waits for them, and re-layouts, potentials(): got = got.reshape(count_y, count_z, width, pair_count, rows_z, rows_y)  5.35 us
    all_to_all x1, starting transfers between devices, shards(): arrived = lax.all_to_all(slots, 'band', 0, 0, tiled=True)  5.33 us
  transfers between devices with their start and end apart: 11, of which 8 were waited for; matrix products, arithmetic and copies ran while one was open for 5% of the time, Pallas kernels for 0%

profile of v9, /device:TPU:0, one launch (start us, length us, event | category | flops | bytes accessed | tf_op | source)
XLA Modules:
  0.0 154.0 jit_solution(14347928541265673739)
XLA Ops:
  1.3 3.1 %collective-permute-start.3 = (s32[4,1]{0,1:T(1,128)S(1)}, s32[4,1]{0,1:T(1,128)S(1)}, u32[]{:S(2)}, u32[]{:S(2)}) collective-permute-start(s32[4,1]{0,1:T(1,128)S(1)} %compare_select_fusion.1), channel_id=1, source_target_pairs={{0,8},{8,0},{16,24},{24,16},{1,9},{9,1},{17,25},{25,17},{2,10},{10... | collective-permute-start | bytes 56 | tf_op jit(solution)/shard_map/ppermute | solution.py:45
  4.4 1.3 slice_bitcast_fusion.1
  5.7 0.2 collective-permute-done.3
  5.9 3.0 %collective-permute-start.4 = (s32[4,1]{0,1:T(1,128)S(1)}, s32[4,1]{0,1:T(1,128)S(1)}, u32[]{:S(2)}, u32[]{:S(2)}) collective-permute-start(s32[4,1]{0,1:T(1,128)S(1)} %fusion.368), channel_id=1, source_target_pairs={{0,16},{8,24},{16,0},{24,8},{1,17},{9,25},{17,1},{25,9},{2,18},{10... | collective-permute-start | bytes 56 | tf_op jit(solution)/shard_map/ppermute | solution.py:45
  8.9 1.5 collective-permute-done.4
  10.5 1.7 %select_select_fusion = f32[4,1,48,24,96]{4,3,2,1,0:T(8,128)} fusion(f32[48,24,96]{2,1,0:T(8,128)S(1)} %get-tuple-element.11, f32[48,24,96]{2,1,0:T(8,128)S(1)} %get-tuple-element.10, pred[4]{0:T(512)(128)(4,1)S(1)} %get-tuple-element.21, pred[4]{0:T(512)(128)(4,1)S(1)} %get-tuple-element.20), kind=kLoop, calls=%fused_computation.11 | loop fusion | flops 884736 | bytes 2654216 | tf_op jit(solution)/shard_map/jit(_where)/select_n | solution.py:147
  12.1 5.3 %all-to-all-start = ((f32[4,1,48,24,96]{4,3,2,1,0:T(8,128)}), f32[4,1,48,24,96]{4,3,2,1,0:T(8,128)S(1)}, u32[]{:S(2)}, u32[]{:S(2)}) async-start(f32[4,1,48,24,96]{4,3,2,1,0:T(8,128)} %select_select_fusion), calls=%async_computation | async-start | bytes 4718592 | tf_op jit(solution)/shard_map/all_to_all | solution.py:148
  17.5 1.6 %collective-permute-start = (f32[1,8,24,96]{3,2,1,0:T(8,128)S(1)}, f32[1,8,24,96]{3,2,1,0:T(8,128)S(1)}, u32[]{:S(2)}, u32[]{:S(2)}) collective-permute-start(f32[1,8,24,96]{3,2,1,0:T(8,128)S(1)} %slice_select_fusion.1), channel_id=1, source_target_pairs={{0,4},{4,0},{1,5},{5,1},{2,6},{6,2},{3,7},{7,3},{8,12},{12,8},{9,1... | collective-permute-start | bytes 221192 | tf_op jit(solution)/shard_map/ppermute | solution.py:25
  19.0 0.6 fusion.129
  19.6 0.6 multiply_add_fusion.1
  20.2 1.9 %collective-permute-done = f32[1,8,24,96]{3,2,1,0:T(8,128)S(1)} collective-permute-done((f32[1,8,24,96]{3,2,1,0:T(8,128)S(1)}, f32[1,8,24,96]{3,2,1,0:T(8,128)S(1)}, u32[]{:S(2)}, u32[]{:S(2)}) %collective-permute-start) | collective-permute-done | bytes 73760 | tf_op jit(solution)/shard_map/ppermute | solution.py:25
  22.2 0.8 pad_maximum_fusion.5
  23.0 2.0 %collective-permute-start.1 = (f32[1,64,8,96]{3,2,1,0:T(8,128)}, f32[1,64,8,96]{3,2,1,0:T(8,128)}, u32[]{:S(2)}, u32[]{:S(2)}) collective-permute-start(f32[1,64,8,96]{3,2,1,0:T(8,128)} %get-tuple-element.12), channel_id=1, source_target_pairs={{0,1},{1,2},{2,3},{4,5},{5,6},{6,7},{8,9},{9,10},{10,11},{12,13},{... | collective-permute-start | bytes 589832 | tf_op jit(solution)/shard_map/ppermute | solution.py:30
  25.0 1.3 collective-permute-start.2
  26.3 42.6 %all-to-all-done = f32[4,1,48,24,96]{4,3,2,1,0:T(8,128)S(1)} async-done(((f32[4,1,48,24,96]{4,3,2,1,0:T(8,128)}), f32[4,1,48,24,96]{4,3,2,1,0:T(8,128)S(1)}, u32[]{:S(2)}, u32[]{:S(2)}) %all-to-all-start) | async-done | bytes 1769504 | tf_op jit(solution)/shard_map/all_to_all | solution.py:148
  69.0 0.2 reduce_sum.33
  69.2 1.6 %collective-permute-start.5 = (f32[1,8,24,96]{3,2,1,0:T(8,128)S(1)}, f32[1,8,24,96]{3,2,1,0:T(8,128)S(1)}, u32[]{:S(2)}, u32[]{:S(2)}) collective-permute-start(f32[1,8,24,96]{3,2,1,0:T(8,128)S(1)} %slice_select_fusion), channel_id=1, source_target_pairs={{0,4},{4,0},{1,5},{5,1},{2,6},{6,2},{3,7},{7,3},{8,12},{12,8},{9,1... | collective-permute-start | bytes 221192 | tf_op jit(solution)/shard_map/ppermute | solution.py:25
  70.8 2.4 %fusion.7 = f32[64,40,96]{2,1,0:T(8,128)S(1)} fusion(f32[1,64,8,96]{3,2,1,0:T(8,128)} %collective-permute-done.2, f32[1,8,24,96]{3,2,1,0:T(8,128)} %copy-done.2, f32[1,48,24,96]{3,2,1,0:T(8,128)S(1)} %copy-done, f32[1,8,24,96]{3,2,1,0:T(8,128)} %copy-done.1, f32[1,64,8,96]{3,2,1,0:T(8,128)} %collective-permute-done.1), kind=kOutput, calls=%fused_computation.14 | convolution fusion | flops 284540928 | bytes 1966080 | tf_op jit(solution)/shard_map/dot_general | solution.py:65
  73.1 0.7 collective-permute-done.5
  73.9 1.3 collective-permute-start.6
  75.3 1.3 collective-permute-start.7
  76.6 0.8 convolution_bitcast_fusion.3
  77.4 3.0 %collective-permute-done.7 = f32[1,64,8,96]{3,2,1,0:T(8,128)S(1)} collective-permute-done((f32[1,64,8,96]{3,2,1,0:T(8,128)S(1)}, f32[1,64,8,96]{3,2,1,0:T(8,128)S(1)}, u32[]{:S(2)}, u32[]{:S(2)}) %collective-permute-start.7) | collective-permute-done | bytes 196640 | tf_op jit(solution)/shard_map/ppermute | solution.py:31
  80.4 1.2 fusion.16
  81.7 0.8 convolution_bitcast_fusion.2
  82.5 0.8 fusion.28
  83.3 0.8 convolution_multiply_fusion.1
  84.1 2.0 %convolution_bitcast_fusion = f32[8,24,1,1152]{3,1,2,0:T(8,128)} fusion(f32[1152,96,1]{1,0,2:T(8,128)S(1)} %bitcast.133, s32[8,24]{1,0:T(8,128)S(1)} %add_select_fusion.3, pred[8,24]{1,0:T(8,128)(4,1)S(1)} %copy-done.4), kind=kOutput, calls=%fused_computation.3 | convolution fusion | flops 127586304 | bytes 1328064 | tf_op jit(solution)/shard_map/dot_general | solution.py:89
  86.0 7.1 %all-to-all-start.1 = ((f32[8,24,1,1152]{3,1,2,0:T(8,128)}), f32[8,24,1,1152]{3,1,2,0:T(8,128)}, u32[]{:S(2)}, u32[]{:S(2)}) async-start(f32[8,24,1,1152]{3,1,2,0:T(8,128)} %convolution_bitcast_fusion), calls=%async_computation.1 | async-start | bytes 1769472 | tf_op jit(solution)/shard_map/all_to_all | solution.py:105
  93.3 0.1 broadcast_multiply_fusion
  93.4 12.5 %all-to-all-done.1 = f32[8,24,1,1152]{3,1,2,0:T(8,128)} async-done(((f32[8,24,1,1152]{3,1,2,0:T(8,128)}), f32[8,24,1,1152]{3,1,2,0:T(8,128)}, u32[]{:S(2)}, u32[]{:S(2)}) %all-to-all-start.1) | async-done | bytes 884768 | tf_op jit(solution)/shard_map/all_to_all | solution.py:105
  106.0 2.1 %reshape.388 = f32[2,4,24,1,24,48]{5,4,2,1,0,3:T(8,128)S(1)} reshape(f32[8,24,1,1152]{3,1,2,0:T(8,128)} %all-to-all-done.1) | data formatting | bytes 1769472 | tf_op jit(solution)/shard_map/reshape | solution.py:106
  108.1 3.2 %copy.49 = f32[2,4,24,1,24,48]{5,0,4,1,2,3:T(2,128)} copy(f32[2,4,24,1,24,48]{5,4,2,1,0,3:T(8,128)S(1)} %reshape.388) | data formatting | bytes 1769472 | tf_op jit(solution)/shard_map/reshape | solution.py:106
  111.3 2.7 %reshape.389 = f32[24,96,96]{2,1,0:T(8,128)S(1)} reshape(f32[24,1,4,24,2,48]{5,4,3,2,0,1:T(2,128)} %bitcast.125) | data formatting | bytes 1769472 | tf_op jit(solution)/shard_map/reshape.30
  114.1 1.9 %fusion.42 = f32[24,96,192]{1,2,0:T(8,128)S(1)} fusion(f32[24,96,96]{2,1,0:T(8,128)S(1)} %reshape.389, s32[192]{0:T(256)S(1)} %add_select_fusion.4, pred[192]{0:T(512)(128)(4,1)S(1)} %iota_compare_fusion), kind=kOutput, calls=%fused_computation.67 | convolution fusion | flops 254988288 | bytes 2655168 | tf_op jit(solution)/shard_map/dot_general | solution.py:89
  115.9 3.8 %multiply_reduce_fusion = (f32[]{:T(128)}, f32[24,192,192]{2,1,0:T(8,128)S(1)}) fusion(f32[192]{0:T(256)S(1)} %get-tuple-element.27, f32[24,192]{1,0:T(8,128)S(1)} %broadcast_add_fusion, f32[192]{0:T(256)S(1)} %get-tuple-element.26, f32[24,192]{1,0:T(8,128)S(1)} %broadcast_multiply_fusion, f32[24,96,192]{1,2,0:T(8,128)S(1)} %fusion.42, ...), kind=kOutput, calls=%fused_computation | convolution fusion | flops 516870144 | bytes 5347780 | tf_op jit(solution)/shard_map/dot_general | solution.py:89
  119.7 3.8 %fusion = f32[24,192,96]{1,2,0:T(8,128)S(1)} fusion(f32[24,192,192]{2,1,0:T(8,128)S(1)} %get-tuple-element.23, f32[192]{0:T(256)S(1)} %get-tuple-element.27, f32[24,192]{1,0:T(8,128)S(1)} %broadcast_add_fusion, f32[192]{0:T(256)S(1)} %get-tuple-element.26, f32[24,192]{1,0:T(8,128)S(1)} %broadcast_multiply_fusion, s32[192]{0:T(256)S(1)} %add_select_fusion.4, ...), kind=kOutput, calls=%fused_computation.2 | convolution fusion | flops 515100672 | bytes 5347776 | tf_op jit(solution)/shard_map/dot_general | solution.py:89
  123.6 1.6 %convolution_bitcast_fusion.1 = f32[2,4,24,1,24,48]{5,4,0,1,2,3:T(8,128)S(1)} fusion(f32[24,4,24,192,1]{3,2,4,1,0:T(8,128)S(1)} %bitcast.132, s32[192]{0:T(256)S(1)} %add_select_fusion.4, s32[2,48]{1,0:T(2,128)S(1)} %copy-done.3, pred[192]{0:T(512)(128)(4,1)S(1)} %iota_compare_fusion), kind=kOutput, calls=%fused_computation.12 | convolution fusion | flops 254988288 | bytes 2655552 | tf_op jit(solution)/shard_map/dot_general | solution.py:89
  125.1 0.2 copy.34
  125.3 1.7 %reshape.391 = f32[8,24,1,1152]{3,1,0,2:T(8,128)} reshape(f32[2,4,24,1,24,48]{5,4,2,1,0,3:T(8,128)S(1)} %copy.34) | data formatting | bytes 1769472 | tf_op jit(solution)/shard_map/reshape | solution.py:126
  127.0 2.8 %pad_bitcast_fusion = f32[8,24,1,1280]{3,1,2,0:T(8,128)} fusion(f32[8,24,1,1152]{3,1,0,2:T(8,128)} %reshape.391, f32[]{:T(128)} %get-tuple-element.22), kind=kLoop, calls=%fused_computation.40 | loop fusion | bytes 1867780 | tf_op jit(solution)/shard_map/concatenate | solution.py:128
  129.8 3.6 %all-to-all-start.2 = ((f32[8,24,1,1280]{3,1,2,0:T(8,128)}), f32[8,24,1,1280]{3,1,2,0:T(8,128)S(1)}, u32[]{:S(2)}, u32[]{:S(2)}) async-start(f32[8,24,1,1280]{3,1,2,0:T(8,128)} %pad_bitcast_fusion), calls=%async_computation.2 | async-start | bytes 1966080 | tf_op jit(solution)/shard_map/all_to_all | solution.py:129
  134.0 13.0 %all-to-all-done.2 = f32[8,24,1,1280]{3,1,2,0:T(8,128)S(1)} async-done(((f32[8,24,1,1280]{3,1,2,0:T(8,128)}), f32[8,24,1,1280]{3,1,2,0:T(8,128)S(1)}, u32[]{:S(2)}, u32[]{:S(2)}) %all-to-all-start.2) | async-done | bytes 983072 | tf_op jit(solution)/shard_map/all_to_all | solution.py:129
  147.1 1.0 slice.50
  148.0 1.5 copy.37
  149.6 1.0 fusion.27
  150.6 1.0 copy.38
  151.6 0.6 slice_reduce_fusion
  (29 shorter events, 0.3 us)
Async XLA Ops:
  1.3 4.6 %collective-permute-start.3 = (s32[4,1]{0,1:T(1,128)S(1)}, s32[4,1]{0,1:T(1,128)S(1)}, u32[]{:S(2)}, u32[]{:S(2)}) collective-permute-start(s32[4,1]{0,1:T(1,128)S(1)} %compare_select_fusion.1), channel_id=1, source_target_pairs={{0,8},{8,0},{16,24},{24,16},{1,9},{9,1},{17,25},{25,17},{2,10},{10... | collective-permute-start | bytes 56 | tf_op jit(solution)/shard_map/ppermute | solution.py:45
  5.9 4.6 %collective-permute-start.4 = (s32[4,1]{0,1:T(1,128)S(1)}, s32[4,1]{0,1:T(1,128)S(1)}, u32[]{:S(2)}, u32[]{:S(2)}) collective-permute-start(s32[4,1]{0,1:T(1,128)S(1)} %fusion.368), channel_id=1, source_target_pairs={{0,16},{8,24},{16,0},{24,8},{1,17},{9,25},{17,1},{25,9},{2,18},{10... | collective-permute-start | bytes 56 | tf_op jit(solution)/shard_map/ppermute | solution.py:45
  12.1 5.3 %copy-start = (f32[1,48,24,96]{3,2,1,0:T(8,128)S(1)}, f32[1,48,24,96]{3,2,1,0:T(8,128)}, u32[]{:S(2)}) copy-start(f32[1,48,24,96]{3,2,1,0:T(8,128)} %param.4) | copy-start | bytes 1327108
  12.1 56.9 %all-to-all-start = ((f32[4,1,48,24,96]{4,3,2,1,0:T(8,128)}), f32[4,1,48,24,96]{4,3,2,1,0:T(8,128)S(1)}, u32[]{:S(2)}, u32[]{:S(2)}) async-start(f32[4,1,48,24,96]{4,3,2,1,0:T(8,128)} %select_select_fusion), calls=%async_computation | async-start | bytes 4718592 | tf_op jit(solution)/shard_map/all_to_all | solution.py:148
  17.5 4.7 %collective-permute-start = (f32[1,8,24,96]{3,2,1,0:T(8,128)S(1)}, f32[1,8,24,96]{3,2,1,0:T(8,128)S(1)}, u32[]{:S(2)}, u32[]{:S(2)}) collective-permute-start(f32[1,8,24,96]{3,2,1,0:T(8,128)S(1)} %slice_select_fusion.1), channel_id=1, source_target_pairs={{0,4},{4,0},{1,5},{5,1},{2,6},{6,2},{3,7},{7,3},{8,12},{12,8},{9,1... | collective-permute-start | bytes 221192 | tf_op jit(solution)/shard_map/ppermute | solution.py:25
  22.2 4.1 %copy-start.1 = (f32[1,8,24,96]{3,2,1,0:T(8,128)}, f32[1,8,24,96]{3,2,1,0:T(8,128)S(1)}, u32[]{:S(2)}) copy-start(f32[1,8,24,96]{3,2,1,0:T(8,128)S(1)} %get-tuple-element.16) | copy-start | bytes 221188
  22.2 4.1 %copy-start.2 = (f32[1,8,24,96]{3,2,1,0:T(8,128)}, f32[1,8,24,96]{3,2,1,0:T(8,128)S(1)}, u32[]{:S(2)}) copy-start(f32[1,8,24,96]{3,2,1,0:T(8,128)S(1)} %get-tuple-element.17) | copy-start | bytes 221188
  23.0 47.7 %collective-permute-start.1 = (f32[1,64,8,96]{3,2,1,0:T(8,128)}, f32[1,64,8,96]{3,2,1,0:T(8,128)}, u32[]{:S(2)}, u32[]{:S(2)}) collective-permute-start(f32[1,64,8,96]{3,2,1,0:T(8,128)} %get-tuple-element.12), channel_id=1, source_target_pairs={{0,1},{1,2},{2,3},{4,5},{5,6},{6,7},{8,9},{9,10},{10,11},{12,13},{... | collective-permute-start | bytes 589832 | tf_op jit(solution)/shard_map/ppermute | solution.py:30
  25.0 45.7 %collective-permute-start.2 = (f32[1,64,8,96]{3,2,1,0:T(8,128)}, f32[1,64,8,96]{3,2,1,0:T(8,128)}, u32[]{:S(2)}, u32[]{:S(2)}) collective-permute-start(f32[1,64,8,96]{3,2,1,0:T(8,128)} %get-tuple-element.13), channel_id=1, source_target_pairs={{1,0},{2,1},{3,2},{5,4},{6,5},{7,6},{9,8},{10,9},{11,10},{13,12},{... | collective-permute-start | bytes 589832 | tf_op jit(solution)/shard_map/ppermute | solution.py:31
  69.2 4.7 %collective-permute-start.5 = (f32[1,8,24,96]{3,2,1,0:T(8,128)S(1)}, f32[1,8,24,96]{3,2,1,0:T(8,128)S(1)}, u32[]{:S(2)}, u32[]{:S(2)}) collective-permute-start(f32[1,8,24,96]{3,2,1,0:T(8,128)S(1)} %slice_select_fusion), channel_id=1, source_target_pairs={{0,4},{4,0},{1,5},{5,1},{2,6},{6,2},{3,7},{7,3},{8,12},{12,8},{9,1... | collective-permute-start | bytes 221192 | tf_op jit(solution)/shard_map/ppermute | solution.py:25
  73.9 3.4 %collective-permute-start.6 = (f32[1,64,8,96]{3,2,1,0:T(8,128)S(1)}, f32[1,64,8,96]{3,2,1,0:T(8,128)S(1)}, u32[]{:S(2)}, u32[]{:S(2)}) collective-permute-start(f32[1,64,8,96]{3,2,1,0:T(8,128)S(1)} %get-tuple-element.14), channel_id=1, source_target_pairs={{0,1},{1,2},{2,3},{4,5},{5,6},{6,7},{8,9},{9,10},{10,11},{12,13},{... | collective-permute-start | bytes 589832 | tf_op jit(solution)/shard_map/ppermute | solution.py:30
  75.3 5.2 %collective-permute-start.7 = (f32[1,64,8,96]{3,2,1,0:T(8,128)S(1)}, f32[1,64,8,96]{3,2,1,0:T(8,128)S(1)}, u32[]{:S(2)}, u32[]{:S(2)}) collective-permute-start(f32[1,64,8,96]{3,2,1,0:T(8,128)S(1)} %get-tuple-element.15), channel_id=1, source_target_pairs={{1,0},{2,1},{3,2},{5,4},{6,5},{7,6},{9,8},{10,9},{11,10},{13,12},{... | collective-permute-start | bytes 589832 | tf_op jit(solution)/shard_map/ppermute | solution.py:31
  81.7 2.4 %copy-start.4 = (pred[8,24]{1,0:T(8,128)(4,1)S(1)}, pred[8,24]{1,0:T(8,128)(4,1)}, u32[]{:S(2)}) copy-start(pred[8,24]{1,0:T(8,128)(4,1)} %fusion.129) | copy-start | bytes 580
  86.0 19.9 %all-to-all-start.1 = ((f32[8,24,1,1152]{3,1,2,0:T(8,128)}), f32[8,24,1,1152]{3,1,2,0:T(8,128)}, u32[]{:S(2)}, u32[]{:S(2)}) async-start(f32[8,24,1,1152]{3,1,2,0:T(8,128)} %convolution_bitcast_fusion), calls=%async_computation.1 | async-start | bytes 1769472 | tf_op jit(solution)/shard_map/all_to_all | solution.py:105
  119.7 3.8 %copy-start.3 = (s32[2,48]{1,0:T(2,128)S(1)}, s32[2,48]{1,0:T(2,128)}, u32[]{:S(2)}) copy-start(s32[2,48]{1,0:T(2,128)} %multiply_add_fusion.1) | copy-start | bytes 1156
  129.8 17.2 %all-to-all-start.2 = ((f32[8,24,1,1280]{3,1,2,0:T(8,128)}), f32[8,24,1,1280]{3,1,2,0:T(8,128)S(1)}, u32[]{:S(2)}, u32[]{:S(2)}) async-start(f32[8,24,1,1280]{3,1,2,0:T(8,128)} %pad_bitcast_fusion), calls=%async_computation.2 | async-start | bytes 1966080 | tf_op jit(solution)/shard_map/all_to_all | solution.py:129

commit v10 on v9

--- a/solution.py
+++ b/solution.py
@@ -138,8 +138,8 @@
     sides = (("gy", 1), ("gz", 2))
     local_count = j_coeff.shape[0]
     band_count = lax.axis_size("band")
-    mine = lax.axis_index("band") == jnp.arange(band_count, dtype=jnp.int32)[:, None]
-    wanted = group_sum(jnp.where(mine, pair_orbital, 0), ("band",))
+    requests = jnp.broadcast_to(pair_orbital, (band_count,) + pair_orbital.shape[1:])
+    wanted = lax.all_to_all(requests, "band", 0, 0, tiled=True)
     first_owned = lax.axis_index("band") * local_count
     slots = jnp.zeros(wanted.shape + j_coeff.shape[1:], jnp.float32)
     for number in range(local_count):

time: 155 us -> 158 us (1.019)
  waiting for transfers between devices: 75.6 us -> 79.2 us
    all_to_all x0 -> x1, starting transfers between devices: none -> 6.32 us  [shards(): wanted = lax.all_to_all(requests, 'band', 0, 0, tiled=True)]
    ppermute x2 -> x0, starting transfers between devices: 6.12 us -> none  [group_sum(): lax.ppermute(total, axis, [(i, i ^ step) for i in range(count)])]
    all_to_all x0 -> x1, waiting for transfers between devices: none -> 4.14 us  [shards(): wanted = lax.all_to_all(requests, 'band', 0, 0, tiled=True)]
    ppermute x2 -> x0, waiting for transfers between devices: 1.71 us -> none  [group_sum(): lax.ppermute(total, axis, [(i, i ^ step) for i in range(count)])]
  transfers between devices with their start and end apart: 11 -> 10, of which waited for: 8 -> 7; matrix products, arithmetic and copies ran while one was open for 5% -> 4% of each run, Pallas kernels for 0% -> 0%
where the time goes in v10:
time: 158 us; the launch traced here: 157 us
  waiting for transfers between devices  79.2 us (50%)
  starting transfers between devices  29.7 us (19%)
  matrix products  20.8 us (13%)
  local copies, waits for them, and re-layouts  18.2 us (12%)
  other arithmetic  5.05 us (3%)
  between operations  3.99 us (3%)
    all_to_all x1, waiting for transfers between devices, shards(): arrived = lax.all_to_all(slots, 'band', 0, 0, tiled=True)  43.7 us
    dot_general x6, matrix products, contract(): lax.dot_general(left, right, (((left_dim,), (right_dim,)), ((), ())), pre...  14 us
    all_to_all x1, waiting for transfers between devices, potentials(): got = lax.all_to_all(back, ('gy', 'gz'), 0, 0, tiled=True)  13 us
    all_to_all x1, waiting for transfers between devices, potentials(): got = lax.all_to_all(send, ('gy', 'gz'), 0, 0, tiled=True)  12.5 us
    all_to_all x1, starting transfers between devices, potentials(): got = lax.all_to_all(send, ('gy', 'gz'), 0, 0, tiled=True)  7.11 us
    all_to_all x1, starting transfers between devices, shards(): wanted = lax.all_to_all(requests, 'band', 0, 0, tiled=True)  6.32 us
    reshape x2, local copies, waits for them, and re-layouts, potentials(): got = got.reshape(count_y, count_z, width, pair_count, rows_z, rows_y)  5.34 us
    all_to_all x1, waiting for transfers between devices, shards(): wanted = lax.all_to_all(requests, 'band', 0, 0, tiled=True)  4.14 us
  transfers between devices with their start and end apart: 10, of which 7 were waited for; matrix products, arithmetic and copies ran while one was open for 4% of the time, Pallas kernels for 0%

profile of v10, /device:TPU:0, one launch (start us, length us, event | category | flops | bytes accessed | tf_op | source)
XLA Modules:
  0.0 156.9 jit_solution(5692225714892390753)
XLA Ops:
  1.3 0.6 broadcast_in_dim.459
  1.9 6.3 %all-to-all-start = ((s32[4,1,1]{2,1,0:T(1,128)}), s32[4,1,1]{2,1,0:T(1,128)S(1)}, u32[]{:S(2)}, u32[]{:S(2)}) async-start(s32[4,1,1]{2,1,0:T(1,128)} %broadcast_in_dim.459), calls=%async_computation | async-start | bytes 4096 | tf_op jit(solution)/shard_map/all_to_all | solution.py:142
  8.2 1.3 slice_bitcast_fusion.1
  9.5 4.1 %all-to-all-done = s32[4,1,1]{2,1,0:T(1,128)S(1)} async-done(((s32[4,1,1]{2,1,0:T(1,128)}), s32[4,1,1]{2,1,0:T(1,128)S(1)}, u32[]{:S(2)}, u32[]{:S(2)}) %all-to-all-start) | async-done | bytes 48 | tf_op jit(solution)/shard_map/all_to_all | solution.py:142
  13.6 0.2 compare_reduce_fusion.1
  13.9 1.7 %select_select_fusion = f32[4,1,48,24,96]{4,3,2,1,0:T(8,128)} fusion(f32[48,24,96]{2,1,0:T(8,128)S(1)} %get-tuple-element.15, f32[48,24,96]{2,1,0:T(8,128)S(1)} %get-tuple-element.14, pred[4]{0:T(512)(128)(4,1)S(1)} %get-tuple-element.13, pred[4]{0:T(512)(128)(4,1)S(1)} %get-tuple-element.12), kind=kLoop, calls=%fused_computation.11 | loop fusion | flops 884736 | bytes 2654216 | tf_op jit(solution)/shard_map/jit(_where)/select_n | solution.py:147
  15.5 3.8 %all-to-all-start.1 = ((f32[4,1,48,24,96]{4,3,2,1,0:T(8,128)}), f32[4,1,48,24,96]{4,3,2,1,0:T(8,128)S(1)}, u32[]{:S(2)}, u32[]{:S(2)}) async-start(f32[4,1,48,24,96]{4,3,2,1,0:T(8,128)} %select_select_fusion), calls=%async_computation.1 | async-start | bytes 4718592 | tf_op jit(solution)/shard_map/all_to_all | solution.py:148
  19.3 1.6 collective-permute-start
  20.9 0.6 fusion.129
  21.5 0.5 multiply_add_fusion.1
  22.0 2.0 %collective-permute-done = f32[1,8,24,96]{3,2,1,0:T(8,128)S(1)} collective-permute-done((f32[1,8,24,96]{3,2,1,0:T(8,128)S(1)}, f32[1,8,24,96]{3,2,1,0:T(8,128)S(1)}, u32[]{:S(2)}, u32[]{:S(2)}) %collective-permute-start) | collective-permute-done | bytes 73760 | tf_op jit(solution)/shard_map/ppermute | solution.py:25
  24.1 0.9 pad_maximum_fusion.5
  24.9 2.0 %collective-permute-start.1 = (f32[1,64,8,96]{3,2,1,0:T(8,128)}, f32[1,64,8,96]{3,2,1,0:T(8,128)}, u32[]{:S(2)}, u32[]{:S(2)}) collective-permute-start(f32[1,64,8,96]{3,2,1,0:T(8,128)} %get-tuple-element.16), channel_id=1, source_target_pairs={{0,1},{1,2},{2,3},{4,5},{5,6},{6,7},{8,9},{9,10},{10,11},{12,13},{... | collective-permute-start | bytes 589832 | tf_op jit(solution)/shard_map/ppermute | solution.py:30
  26.9 1.3 collective-permute-start.2
  28.2 43.7 %all-to-all-done.1 = f32[4,1,48,24,96]{4,3,2,1,0:T(8,128)S(1)} async-done(((f32[4,1,48,24,96]{4,3,2,1,0:T(8,128)}), f32[4,1,48,24,96]{4,3,2,1,0:T(8,128)S(1)}, u32[]{:S(2)}, u32[]{:S(2)}) %all-to-all-start.1) | async-done | bytes 1769504 | tf_op jit(solution)/shard_map/all_to_all | solution.py:148
  71.9 0.2 reduce_sum.33
  72.2 1.6 collective-permute-start.3
  73.7 2.4 %fusion.7 = f32[64,40,96]{2,1,0:T(8,128)S(1)} fusion(f32[1,64,8,96]{3,2,1,0:T(8,128)} %collective-permute-done.2, f32[1,8,24,96]{3,2,1,0:T(8,128)} %copy-done.2, f32[1,48,24,96]{3,2,1,0:T(8,128)S(1)} %copy-done, f32[1,8,24,96]{3,2,1,0:T(8,128)} %copy-done.1, f32[1,64,8,96]{3,2,1,0:T(8,128)} %collective-permute-done.1), kind=kOutput, calls=%fused_computation.14 | convolution fusion | flops 284540928 | bytes 1966080 | tf_op jit(solution)/shard_map/dot_general | solution.py:65
  76.1 0.7 collective-permute-done.3
  76.9 1.3 collective-permute-start.4
  78.2 1.3 collective-permute-start.5
  79.5 0.8 convolution_bitcast_fusion.3
  80.4 3.0 %collective-permute-done.5 = f32[1,64,8,96]{3,2,1,0:T(8,128)S(1)} collective-permute-done((f32[1,64,8,96]{3,2,1,0:T(8,128)S(1)}, f32[1,64,8,96]{3,2,1,0:T(8,128)S(1)}, u32[]{:S(2)}, u32[]{:S(2)}) %collective-permute-start.5) | collective-permute-done | bytes 196640 | tf_op jit(solution)/shard_map/ppermute | solution.py:31
  83.4 1.2 fusion.16
  84.7 0.8 convolution_bitcast_fusion.2
  85.5 0.8 fusion.28
  86.3 0.8 convolution_multiply_fusion.1
  87.0 2.0 %convolution_bitcast_fusion = f32[8,24,1,1152]{3,1,2,0:T(8,128)} fusion(f32[1152,96,1]{1,0,2:T(8,128)S(1)} %bitcast.128, s32[8,24]{1,0:T(8,128)S(1)} %add_select_fusion.3, pred[8,24]{1,0:T(8,128)(4,1)S(1)} %copy-done.4), kind=kOutput, calls=%fused_computation.3 | convolution fusion | flops 127586304 | bytes 1328064 | tf_op jit(solution)/shard_map/dot_general | solution.py:89
  89.0 7.1 %all-to-all-start.2 = ((f32[8,24,1,1152]{3,1,2,0:T(8,128)}), f32[8,24,1,1152]{3,1,2,0:T(8,128)}, u32[]{:S(2)}, u32[]{:S(2)}) async-start(f32[8,24,1,1152]{3,1,2,0:T(8,128)} %convolution_bitcast_fusion), calls=%async_computation.2 | async-start | bytes 1769472 | tf_op jit(solution)/shard_map/all_to_all | solution.py:105
  96.2 0.1 broadcast_multiply_fusion
  96.4 12.5 %all-to-all-done.2 = f32[8,24,1,1152]{3,1,2,0:T(8,128)} async-done(((f32[8,24,1,1152]{3,1,2,0:T(8,128)}), f32[8,24,1,1152]{3,1,2,0:T(8,128)}, u32[]{:S(2)}, u32[]{:S(2)}) %all-to-all-start.2) | async-done | bytes 884768 | tf_op jit(solution)/shard_map/all_to_all | solution.py:105
  108.9 2.1 %reshape.396 = f32[2,4,24,1,24,48]{5,4,2,1,0,3:T(8,128)S(1)} reshape(f32[8,24,1,1152]{3,1,2,0:T(8,128)} %all-to-all-done.2) | data formatting | bytes 1769472 | tf_op jit(solution)/shard_map/reshape | solution.py:106
  111.0 3.2 %copy.60 = f32[2,4,24,1,24,48]{5,0,4,1,2,3:T(2,128)} copy(f32[2,4,24,1,24,48]{5,4,2,1,0,3:T(8,128)S(1)} %reshape.396) | data formatting | bytes 1769472 | tf_op jit(solution)/shard_map/reshape | solution.py:106
  114.3 2.7 %reshape.397 = f32[24,96,96]{2,1,0:T(8,128)S(1)} reshape(f32[24,1,4,24,2,48]{5,4,3,2,0,1:T(2,128)} %bitcast.120) | data formatting | bytes 1769472 | tf_op jit(solution)/shard_map/reshape.30
  117.0 1.9 %fusion.42 = f32[24,96,192]{1,2,0:T(8,128)S(1)} fusion(f32[24,96,96]{2,1,0:T(8,128)S(1)} %reshape.397, s32[192]{0:T(256)S(1)} %add_select_fusion.4, pred[192]{0:T(512)(128)(4,1)S(1)} %iota_compare_fusion), kind=kOutput, calls=%fused_computation.67 | convolution fusion | flops 254988288 | bytes 2655168 | tf_op jit(solution)/shard_map/dot_general | solution.py:89
  118.9 3.8 %multiply_reduce_fusion = (f32[]{:T(128)}, f32[24,192,192]{2,1,0:T(8,128)S(1)}) fusion(f32[192]{0:T(256)S(1)} %get-tuple-element.29, f32[24,192]{1,0:T(8,128)S(1)} %broadcast_add_fusion, f32[192]{0:T(256)S(1)} %get-tuple-element.28, f32[24,192]{1,0:T(8,128)S(1)} %broadcast_multiply_fusion, f32[24,96,192]{1,2,0:T(8,128)S(1)} %fusion.42, ...), kind=kOutput, calls=%fused_computation | convolution fusion | flops 516870144 | bytes 5347780 | tf_op jit(solution)/shard_map/dot_general | solution.py:89
  122.7 3.8 %fusion = f32[24,192,96]{1,2,0:T(8,128)S(1)} fusion(f32[24,192,192]{2,1,0:T(8,128)S(1)} %get-tuple-element.25, f32[192]{0:T(256)S(1)} %get-tuple-element.29, f32[24,192]{1,0:T(8,128)S(1)} %broadcast_add_fusion, f32[192]{0:T(256)S(1)} %get-tuple-element.28, f32[24,192]{1,0:T(8,128)S(1)} %broadcast_multiply_fusion, s32[192]{0:T(256)S(1)} %add_select_fusion.4, ...), kind=kOutput, calls=%fused_computation.2 | convolution fusion | flops 515100672 | bytes 5347776 | tf_op jit(solution)/shard_map/dot_general | solution.py:89
  126.5 1.6 %convolution_bitcast_fusion.1 = f32[2,4,24,1,24,48]{5,4,0,1,2,3:T(8,128)S(1)} fusion(f32[24,4,24,192,1]{3,2,4,1,0:T(8,128)S(1)} %bitcast.127, s32[192]{0:T(256)S(1)} %add_select_fusion.4, s32[2,48]{1,0:T(2,128)S(1)} %copy-done.3, pred[192]{0:T(512)(128)(4,1)S(1)} %iota_compare_fusion), kind=kOutput, calls=%fused_computation.12 | convolution fusion | flops 254988288 | bytes 2655552 | tf_op jit(solution)/shard_map/dot_general | solution.py:89
  128.1 0.2 copy.45
  128.2 1.7 %reshape.399 = f32[8,24,1,1152]{3,1,0,2:T(8,128)} reshape(f32[2,4,24,1,24,48]{5,4,2,1,0,3:T(8,128)S(1)} %copy.45) | data formatting | bytes 1769472 | tf_op jit(solution)/shard_map/reshape | solution.py:126
  129.9 2.8 %pad_bitcast_fusion = f32[8,24,1,1280]{3,1,2,0:T(8,128)} fusion(f32[8,24,1,1152]{3,1,0,2:T(8,128)} %reshape.399, f32[]{:T(128)} %get-tuple-element.24), kind=kLoop, calls=%fused_computation.40 | loop fusion | bytes 1867780 | tf_op jit(solution)/shard_map/concatenate | solution.py:128
  132.8 3.6 %all-to-all-start.3 = ((f32[8,24,1,1280]{3,1,2,0:T(8,128)}), f32[8,24,1,1280]{3,1,2,0:T(8,128)S(1)}, u32[]{:S(2)}, u32[]{:S(2)}) async-start(f32[8,24,1,1280]{3,1,2,0:T(8,128)} %pad_bitcast_fusion), calls=%async_computation.3 | async-start | bytes 1966080 | tf_op jit(solution)/shard_map/all_to_all | solution.py:129
  137.0 13.0 %all-to-all-done.3 = f32[8,24,1,1280]{3,1,2,0:T(8,128)S(1)} async-done(((f32[8,24,1,1280]{3,1,2,0:T(8,128)}), f32[8,24,1,1280]{3,1,2,0:T(8,128)S(1)}, u32[]{:S(2)}, u32[]{:S(2)}) %all-to-all-start.3) | async-done | bytes 983072 | tf_op jit(solution)/shard_map/all_to_all | solution.py:129
  150.0 1.0 slice.50
  151.0 1.5 copy.48
  152.5 1.0 fusion.27
  153.6 1.0 copy.49
  154.6 0.6 slice_reduce_fusion
  (26 shorter events, 0.3 us)
Async XLA Ops:
  1.9 11.8 %all-to-all-start = ((s32[4,1,1]{2,1,0:T(1,128)}), s32[4,1,1]{2,1,0:T(1,128)S(1)}, u32[]{:S(2)}, u32[]{:S(2)}) async-start(s32[4,1,1]{2,1,0:T(1,128)} %broadcast_in_dim.459), calls=%async_computation | async-start | bytes 4096 | tf_op jit(solution)/shard_map/all_to_all | solution.py:142
  15.5 3.8 %copy-start = (f32[1,48,24,96]{3,2,1,0:T(8,128)S(1)}, f32[1,48,24,96]{3,2,1,0:T(8,128)}, u32[]{:S(2)}) copy-start(f32[1,48,24,96]{3,2,1,0:T(8,128)} %param.4) | copy-start | bytes 1327108
  15.5 56.4 %all-to-all-start.1 = ((f32[4,1,48,24,96]{4,3,2,1,0:T(8,128)}), f32[4,1,48,24,96]{4,3,2,1,0:T(8,128)S(1)}, u32[]{:S(2)}, u32[]{:S(2)}) async-start(f32[4,1,48,24,96]{4,3,2,1,0:T(8,128)} %select_select_fusion), calls=%async_computation.1 | async-start | bytes 4718592 | tf_op jit(solution)/shard_map/all_to_all | solution.py:148
  19.3 4.7 %collective-permute-start = (f32[1,8,24,96]{3,2,1,0:T(8,128)S(1)}, f32[1,8,24,96]{3,2,1,0:T(8,128)S(1)}, u32[]{:S(2)}, u32[]{:S(2)}) collective-permute-start(f32[1,8,24,96]{3,2,1,0:T(8,128)S(1)} %slice_select_fusion.1), channel_id=1, source_target_pairs={{0,4},{4,0},{1,5},{5,1},{2,6},{6,2},{3,7},{7,3},{8,12},{12,8},{9,1... | collective-permute-start | bytes 221192 | tf_op jit(solution)/shard_map/ppermute | solution.py:25
  24.0 4.2 %copy-start.1 = (f32[1,8,24,96]{3,2,1,0:T(8,128)}, f32[1,8,24,96]{3,2,1,0:T(8,128)S(1)}, u32[]{:S(2)}) copy-start(f32[1,8,24,96]{3,2,1,0:T(8,128)S(1)} %get-tuple-element.20) | copy-start | bytes 221188
  24.1 4.2 %copy-start.2 = (f32[1,8,24,96]{3,2,1,0:T(8,128)}, f32[1,8,24,96]{3,2,1,0:T(8,128)S(1)}, u32[]{:S(2)}) copy-start(f32[1,8,24,96]{3,2,1,0:T(8,128)S(1)} %get-tuple-element.21) | copy-start | bytes 221188
  24.9 48.8 %collective-permute-start.1 = (f32[1,64,8,96]{3,2,1,0:T(8,128)}, f32[1,64,8,96]{3,2,1,0:T(8,128)}, u32[]{:S(2)}, u32[]{:S(2)}) collective-permute-start(f32[1,64,8,96]{3,2,1,0:T(8,128)} %get-tuple-element.16), channel_id=1, source_target_pairs={{0,1},{1,2},{2,3},{4,5},{5,6},{6,7},{8,9},{9,10},{10,11},{12,13},{... | collective-permute-start | bytes 589832 | tf_op jit(solution)/shard_map/ppermute | solution.py:30
  26.9 46.8 %collective-permute-start.2 = (f32[1,64,8,96]{3,2,1,0:T(8,128)}, f32[1,64,8,96]{3,2,1,0:T(8,128)}, u32[]{:S(2)}, u32[]{:S(2)}) collective-permute-start(f32[1,64,8,96]{3,2,1,0:T(8,128)} %get-tuple-element.17), channel_id=1, source_target_pairs={{1,0},{2,1},{3,2},{5,4},{6,5},{7,6},{9,8},{10,9},{11,10},{13,12},{... | collective-permute-start | bytes 589832 | tf_op jit(solution)/shard_map/ppermute | solution.py:31
  72.2 4.7 %collective-permute-start.3 = (f32[1,8,24,96]{3,2,1,0:T(8,128)S(1)}, f32[1,8,24,96]{3,2,1,0:T(8,128)S(1)}, u32[]{:S(2)}, u32[]{:S(2)}) collective-permute-start(f32[1,8,24,96]{3,2,1,0:T(8,128)S(1)} %slice_select_fusion), channel_id=1, source_target_pairs={{0,4},{4,0},{1,5},{5,1},{2,6},{6,2},{3,7},{7,3},{8,12},{12,8},{9,1... | collective-permute-start | bytes 221192 | tf_op jit(solution)/shard_map/ppermute | solution.py:25
  76.9 3.5 %collective-permute-start.4 = (f32[1,64,8,96]{3,2,1,0:T(8,128)S(1)}, f32[1,64,8,96]{3,2,1,0:T(8,128)S(1)}, u32[]{:S(2)}, u32[]{:S(2)}) collective-permute-start(f32[1,64,8,96]{3,2,1,0:T(8,128)S(1)} %get-tuple-element.18), channel_id=1, source_target_pairs={{0,1},{1,2},{2,3},{4,5},{5,6},{6,7},{8,9},{9,10},{10,11},{12,13},{... | collective-permute-start | bytes 589832 | tf_op jit(solution)/shard_map/ppermute | solution.py:30
  78.2 5.2 %collective-permute-start.5 = (f32[1,64,8,96]{3,2,1,0:T(8,128)S(1)}, f32[1,64,8,96]{3,2,1,0:T(8,128)S(1)}, u32[]{:S(2)}, u32[]{:S(2)}) collective-permute-start(f32[1,64,8,96]{3,2,1,0:T(8,128)S(1)} %get-tuple-element.19), channel_id=1, source_target_pairs={{1,0},{2,1},{3,2},{5,4},{6,5},{7,6},{9,8},{10,9},{11,10},{13,12},{... | collective-permute-start | bytes 589832 | tf_op jit(solution)/shard_map/ppermute | solution.py:31
  84.6 2.4 %copy-start.4 = (pred[8,24]{1,0:T(8,128)(4,1)S(1)}, pred[8,24]{1,0:T(8,128)(4,1)}, u32[]{:S(2)}) copy-start(pred[8,24]{1,0:T(8,128)(4,1)} %fusion.129) | copy-start | bytes 580
  89.0 19.9 %all-to-all-start.2 = ((f32[8,24,1,1152]{3,1,2,0:T(8,128)}), f32[8,24,1,1152]{3,1,2,0:T(8,128)}, u32[]{:S(2)}, u32[]{:S(2)}) async-start(f32[8,24,1,1152]{3,1,2,0:T(8,128)} %convolution_bitcast_fusion), calls=%async_computation.2 | async-start | bytes 1769472 | tf_op jit(solution)/shard_map/all_to_all | solution.py:105
  122.7 3.8 %copy-start.3 = (s32[2,48]{1,0:T(2,128)S(1)}, s32[2,48]{1,0:T(2,128)}, u32[]{:S(2)}) copy-start(s32[2,48]{1,0:T(2,128)} %multiply_add_fusion.1) | copy-start | bytes 1156
  132.8 17.2 %all-to-all-start.3 = ((f32[8,24,1,1280]{3,1,2,0:T(8,128)}), f32[8,24,1,1280]{3,1,2,0:T(8,128)S(1)}, u32[]{:S(2)}, u32[]{:S(2)}) async-start(f32[8,24,1,1280]{3,1,2,0:T(8,128)} %pad_bitcast_fusion), calls=%async_computation.3 | async-start | bytes 1966080 | tf_op jit(solution)/shard_map/all_to_all | solution.py:129

commit v11 on v9

--- a/solution.py
+++ b/solution.py
@@ -57,14 +57,17 @@
     return picked
 
 
-def synthesize(padded):
-    wide_y, wide_z, length = (padded.shape[1], padded.shape[2], padded.shape[3])
+def filter_x(cells):
+    length = cells.shape[3]
+    return jnp.matmul(cells, band_matrix(length, length, 0), precision=precise_mode)
+
+
+def filter_yz(padded):
+    wide_y, wide_z = padded.shape[1], padded.shape[2]
     matrix_y = band_matrix(wide_y, wide_y - 16, 8)
     matrix_z = band_matrix(wide_z, wide_z - 16, 8)
-    matrix_x = band_matrix(length, length, 0)
-    step_one = jnp.matmul(padded, matrix_x, precision=precise_mode)
-    step_two = jnp.einsum("oyqx,qz->oyzx", step_one, matrix_z, precision=precise_mode)
-    return jnp.einsum("oqzx,qy->oyzx", step_two, matrix_y, precision=precise_mode)
+    step_one = jnp.einsum("oyqx,qz->oyzx", padded, matrix_z, precision=precise_mode)
+    return jnp.einsum("oqzx,qy->oyzx", step_one, matrix_y, precision=precise_mode)
 
 
 def channel_of(channel, length):
@@ -141,13 +144,14 @@
     mine = lax.axis_index("band") == jnp.arange(band_count, dtype=jnp.int32)[:, None]
     wanted = group_sum(jnp.where(mine, pair_orbital, 0), ("band",))
     first_owned = lax.axis_index("band") * local_count
+    filtered = filter_x(j_coeff)
     slots = jnp.zeros(wanted.shape + j_coeff.shape[1:], jnp.float32)
     for number in range(local_count):
         hit = (wanted == first_owned + number)[:, :, None, None, None]
-        slots = jnp.where(hit, j_coeff[number][None, None], slots)
+        slots = jnp.where(hit, filtered[number][None, None], slots)
     arrived = lax.all_to_all(slots, "band", 0, 0, tiled=True)
-    own_orbital = synthesize(extended(i_coeff, sides, 8))[0]
-    partner = synthesize(extended(jnp.sum(arrived, axis=0), sides, 8))
+    own_orbital = filter_yz(extended(filter_x(i_coeff), sides, 8))[0]
+    partner = filter_yz(extended(jnp.sum(arrived, axis=0), sides, 8))
     density = own_orbital[None] * partner
     potential, energy_part = potentials(density)
     weights = pair_occ[0].astype(jnp.float32)

time: 155 us -> 158 us (1.019)
  other arithmetic: 4.86 us -> 11.9 us
  waiting for transfers between devices: 75.6 us -> 69.4 us
  local copies, waits for them, and re-layouts: 17.6 us -> 19.8 us
    all_to_all x1, waiting for transfers between devices: 42.6 us -> 37.2 us  [shards(): arrived = lax.all_to_all(slots, 'band', 0, 0, tiled=True)]
    unnamed x11 -> x23, local copies, waits for them, and re-layouts: 1.02 us -> 2.89 us
    another operation x0 -> x2, other arithmetic: none -> 1.6 us
  transfers between devices with their start and end apart: 11 -> 11, of which waited for: 8 -> 7; matrix products, arithmetic and copies ran while one was open for 5% -> 9% of each run, Pallas kernels for 0% -> 0%
where the time goes in v11:
time: 158 us
  waiting for transfers between devices  69.4 us (44%)
  starting transfers between devices  30.7 us (19%)
  matrix products  21.6 us (14%)
  local copies, waits for them, and re-layouts  19.8 us (13%)
  other arithmetic  11.9 us (8%)
  between operations  4.23 us (3%)
    all_to_all x1, waiting for transfers between devices, shards(): arrived = lax.all_to_all(slots, 'band', 0, 0, tiled=True)  37.2 us
    dot_general x6, matrix products, contract(): lax.dot_general(left, right, (((left_dim,), (right_dim,)), ((), ())), pre...  14.1 us
    all_to_all x1, waiting for transfers between devices, potentials(): got = lax.all_to_all(back, ('gy', 'gz'), 0, 0, tiled=True)  13 us
    all_to_all x1, waiting for transfers between devices, potentials(): got = lax.all_to_all(send, ('gy', 'gz'), 0, 0, tiled=True)  11.3 us
    all_to_all x1, starting transfers between devices, potentials(): got = lax.all_to_all(send, ('gy', 'gz'), 0, 0, tiled=True)  7.12 us
    ppermute x2, starting transfers between devices, group_sum(): lax.ppermute(total, axis, [(i, i ^ step) for i in range(count)])  5.97 us
    reshape x2, local copies, waits for them, and re-layouts, potentials(): got = got.reshape(count_y, count_z, width, pair_count, rows_z, rows_y)  5.35 us
    all_to_all x1, starting transfers between devices, shards(): arrived = lax.all_to_all(slots, 'band', 0, 0, tiled=True)  5.1 us
  transfers between devices with their start and end apart: 11, of which 7 were waited for; matrix products, arithmetic and copies ran while one was open for 9% of the time, Pallas kernels for 0%

profile of v11, /device:TPU:0, one launch (start us, length us, event | category | flops | bytes accessed | tf_op | source)
XLA Modules:
  0.0 157.6 jit_solution(2613012020562139979)
XLA Ops:
  1.4 3.1 %collective-permute-start.3 = (s32[4,1]{0,1:T(1,128)S(1)}, s32[4,1]{0,1:T(1,128)S(1)}, u32[]{:S(2)}, u32[]{:S(2)}) collective-permute-start(s32[4,1]{0,1:T(1,128)S(1)} %compare_select_fusion.1), channel_id=1, source_target_pairs={{0,8},{8,0},{16,24},{24,16},{1,9},{9,1},{17,25},{25,17},{2,10},{10... | collective-permute-start | bytes 56 | tf_op jit(solution)/shard_map/ppermute | solution.py:45
  4.5 1.1 convolution_bitcast_fusion.2
  6.2 2.9 %collective-permute-start.4 = (s32[4,1]{0,1:T(1,128)S(1)}, s32[4,1]{0,1:T(1,128)S(1)}, u32[]{:S(2)}, u32[]{:S(2)}) collective-permute-start(s32[4,1]{0,1:T(1,128)S(1)} %fusion.358), channel_id=1, source_target_pairs={{0,16},{8,24},{16,0},{24,8},{1,17},{9,25},{17,1},{25,9},{2,18},{10... | collective-permute-start | bytes 56 | tf_op jit(solution)/shard_map/ppermute | solution.py:45
  9.1 1.6 %collective-permute-done.4 = s32[4,1]{0,1:T(1,128)S(1)} collective-permute-done((s32[4,1]{0,1:T(1,128)S(1)}, s32[4,1]{0,1:T(1,128)S(1)}, u32[]{:S(2)}, u32[]{:S(2)}) %collective-permute-start.4) | collective-permute-done | bytes 48 | tf_op jit(solution)/shard_map/ppermute | solution.py:45
  10.7 1.7 %select_select_fusion = f32[4,1,48,24,96]{4,3,2,1,0:T(8,128)} fusion(f32[48,24,96]{2,1,0:T(8,128)S(1)} %copy.51, f32[48,24,96]{2,1,0:T(8,128)S(1)} %copy.50, pred[4]{0:T(512)(128)(4,1)S(1)} %get-tuple-element.21, pred[4]{0:T(512)(128)(4,1)S(1)} %get-tuple-element.20), kind=kLoop, calls=%fused_computation.11 | loop fusion | flops 884736 | bytes 2654216 | tf_op jit(solution)/shard_map/jit(_where)/select_n | solution.py:151
  12.3 5.1 %all-to-all-start = ((f32[4,1,48,24,96]{4,3,2,1,0:T(8,128)}), f32[4,1,48,24,96]{4,3,2,1,0:T(8,128)S(1)}, u32[]{:S(2)}, u32[]{:S(2)}) async-start(f32[4,1,48,24,96]{4,3,2,1,0:T(8,128)} %select_select_fusion), calls=%async_computation | async-start | bytes 4718592 | tf_op jit(solution)/shard_map/all_to_all | solution.py:152
  17.4 1.8 %convolution_bitcast_fusion.3 = f32[1,48,24,96]{3,1,2,0:T(8,128)S(1)} fusion(f32[48,24,96]{2,1,0:T(8,128)} %bitcast.142), kind=kOutput, calls=%fused_computation.25 | convolution fusion | flops 127844352 | bytes 884736 | tf_op jit(solution)/shard_map/dot_general | solution.py:62
  19.2 0.8 copy-done.1
  20.7 1.5 collective-permute-start
  23.4 2.3 %collective-permute-done = f32[1,8,24,96]{3,1,2,0:T(8,128)} collective-permute-done((f32[1,8,24,96]{3,1,2,0:T(8,128)}, f32[1,8,24,96]{3,1,2,0:T(8,128)}, u32[]{:S(2)}, u32[]{:S(2)}) %collective-permute-start) | collective-permute-done | bytes 73760 | tf_op jit(solution)/shard_map/ppermute | solution.py:25
  25.6 0.9 broadcast_select_fusion.3
  26.6 1.9 %pad_maximum_fusion.5 = (f32[1,64,8,96]{3,1,2,0:T(8,128)}, f32[1,64,8,96]{3,1,2,0:T(8,128)}) fusion(f32[1,8,24,96]{3,1,2,0:T(8,128)S(1)} %get-tuple-element.17, f32[1,48,24,96]{3,1,2,0:T(8,128)} %copy-done.1, f32[1,8,24,96]{3,1,2,0:T(8,128)S(1)} %get-tuple-element.16), kind=kLoop, calls=%fused_computation.42 | loop fusion | flops 196608 | bytes 983040 | tf_op jit(solution)/shard_map/slice | solution.py:22
  28.5 2.0 %collective-permute-start.1 = (f32[1,64,8,96]{3,1,2,0:T(8,128)}, f32[1,64,8,96]{3,1,2,0:T(8,128)}, u32[]{:S(2)}, u32[]{:S(2)}) collective-permute-start(f32[1,64,8,96]{3,1,2,0:T(8,128)} %get-tuple-element.12), channel_id=1, source_target_pairs={{0,1},{1,2},{2,3},{4,5},{5,6},{6,7},{8,9},{9,10},{10,11},{12,13},{... | collective-permute-start | bytes 589832 | tf_op jit(solution)/shard_map/ppermute | solution.py:30
  30.5 1.3 collective-permute-start.2
  31.8 37.2 %all-to-all-done = f32[4,1,48,24,96]{4,3,2,1,0:T(8,128)S(1)} async-done(((f32[4,1,48,24,96]{4,3,2,1,0:T(8,128)}), f32[4,1,48,24,96]{4,3,2,1,0:T(8,128)S(1)}, u32[]{:S(2)}, u32[]{:S(2)}) %all-to-all-start) | async-done | bytes 1769504 | tf_op jit(solution)/shard_map/all_to_all | solution.py:152
  69.0 1.1 reduce_sum.33
  70.0 1.2 copy.89
  71.2 1.6 collective-permute-start.5
  72.8 1.4 maximum_bitcast_fusion
  74.2 1.7 %collective-permute-done.5 = f32[1,8,24,96]{3,1,2,0:T(8,128)S(1)} collective-permute-done((f32[1,8,24,96]{3,1,2,0:T(8,128)S(1)}, f32[1,8,24,96]{3,1,2,0:T(8,128)S(1)}, u32[]{:S(2)}, u32[]{:S(2)}) %collective-permute-start.5) | collective-permute-done | bytes 73760 | tf_op jit(solution)/shard_map/ppermute | solution.py:25
  76.0 1.3 collective-permute-start.6
  77.3 1.3 collective-permute-start.7
  78.6 1.6 fusion.11
  80.2 2.3 %collective-permute-done.7 = f32[1,64,8,96]{3,1,2,0:T(8,128)S(1)} collective-permute-done((f32[1,64,8,96]{3,1,2,0:T(8,128)S(1)}, f32[1,64,8,96]{3,1,2,0:T(8,128)S(1)}, u32[]{:S(2)}, u32[]{:S(2)}) %collective-permute-start.7) | collective-permute-done | bytes 196640 | tf_op jit(solution)/shard_map/ppermute | solution.py:31
  82.6 1.5 fusion.14
  84.2 0.8 fusion.21
  85.0 0.8 copy-done.2
  85.8 0.8 convolution_multiply_fusion.1
  86.6 2.0 %convolution_bitcast_fusion = f32[8,24,1,1152]{3,1,2,0:T(8,128)} fusion(f32[1152,96,1]{1,0,2:T(8,128)S(1)} %bitcast.141, s32[8,24]{1,0:T(8,128)S(1)} %add_select_fusion.3, pred[8,24]{1,0:T(8,128)(4,1)S(1)} %copy-done.10), kind=kOutput, calls=%fused_computation.3 | convolution fusion | flops 127586304 | bytes 1328064 | tf_op jit(solution)/shard_map/dot_general | solution.py:92
  88.5 7.1 %all-to-all-start.1 = ((f32[8,24,1,1152]{3,1,2,0:T(8,128)}), f32[8,24,1,1152]{3,1,2,0:T(8,128)}, u32[]{:S(2)}, u32[]{:S(2)}) async-start(f32[8,24,1,1152]{3,1,2,0:T(8,128)} %convolution_bitcast_fusion), calls=%async_computation.1 | async-start | bytes 1769472 | tf_op jit(solution)/shard_map/all_to_all | solution.py:108
  95.8 0.7 broadcast_multiply_fusion
  97.1 11.3 %all-to-all-done.1 = f32[8,24,1,1152]{3,1,2,0:T(8,128)} async-done(((f32[8,24,1,1152]{3,1,2,0:T(8,128)}), f32[8,24,1,1152]{3,1,2,0:T(8,128)}, u32[]{:S(2)}, u32[]{:S(2)}) %all-to-all-start.1) | async-done | bytes 884768 | tf_op jit(solution)/shard_map/all_to_all | solution.py:108
  108.5 2.1 %reshape.387 = f32[2,4,24,1,24,48]{5,4,2,1,0,3:T(8,128)S(1)} reshape(f32[8,24,1,1152]{3,1,2,0:T(8,128)} %all-to-all-done.1) | data formatting | bytes 1769472 | tf_op jit(solution)/shard_map/reshape | solution.py:109
  110.6 3.3 %copy.88 = f32[2,4,24,1,24,48]{5,0,4,1,2,3:T(2,128)} copy(f32[2,4,24,1,24,48]{5,4,2,1,0,3:T(8,128)S(1)} %reshape.387) | data formatting | bytes 1769472 | tf_op jit(solution)/shard_map/reshape | solution.py:109
  113.8 2.7 %reshape.388 = f32[24,96,96]{2,1,0:T(8,128)S(1)} reshape(f32[24,1,4,24,2,48]{5,4,3,2,0,1:T(2,128)} %bitcast.133) | data formatting | bytes 1769472 | tf_op jit(solution)/shard_map/reshape.28
  116.6 1.9 %fusion.36 = f32[24,96,192]{1,2,0:T(8,128)S(1)} fusion(f32[24,96,96]{2,1,0:T(8,128)S(1)} %reshape.388, s32[192]{0:T(256)S(1)} %add_select_fusion.4, pred[192]{0:T(512)(128)(4,1)S(1)} %iota_compare_fusion), kind=kOutput, calls=%fused_computation.59 | convolution fusion | flops 254988288 | bytes 2655168 | tf_op jit(solution)/shard_map/dot_general | solution.py:92
  118.4 3.9 %multiply_reduce_fusion = (f32[]{:T(128)}, f32[24,192,192]{2,1,0:T(8,128)S(1)}) fusion(f32[192]{0:T(256)S(1)} %get-tuple-element.27, f32[24,192]{1,0:T(8,128)S(1)} %copy-done.8, f32[192]{0:T(256)S(1)} %get-tuple-element.26, f32[24,192]{1,0:T(8,128)S(1)} %copy-done.7, f32[24,96,192]{1,2,0:T(8,128)S(1)} %fusion.36, s32[192]{0:T(256)S(1)} %add_select_fusion.4, ...), kind=kOutput, calls=%fused_computation | convolution fusion | flops 516870144 | bytes 5347780 | tf_op jit(solution)/shard_map/dot_general | solution.py:92
  122.3 3.8 %fusion = f32[24,192,96]{1,2,0:T(8,128)S(1)} fusion(f32[24,192,192]{2,1,0:T(8,128)S(1)} %get-tuple-element.23, f32[192]{0:T(256)S(1)} %get-tuple-element.27, f32[24,192]{1,0:T(8,128)S(1)} %copy-done.8, f32[192]{0:T(256)S(1)} %get-tuple-element.26, f32[24,192]{1,0:T(8,128)S(1)} %copy-done.7, s32[192]{0:T(256)S(1)} %add_select_fusion.4, ...), kind=kOutput, calls=%fused_computation.2 | convolution fusion | flops 515100672 | bytes 5347776 | tf_op jit(solution)/shard_map/dot_general | solution.py:92
  126.1 1.6 %convolution_bitcast_fusion.1 = f32[2,4,24,1,24,48]{5,4,0,1,2,3:T(8,128)S(1)} fusion(f32[24,4,24,192,1]{3,2,4,1,0:T(8,128)S(1)} %bitcast.140, s32[192]{0:T(256)S(1)} %add_select_fusion.4, s32[2,48]{1,0:T(2,128)S(1)} %copy-done.9, pred[192]{0:T(512)(128)(4,1)S(1)} %iota_compare_fusion), kind=kOutput, calls=%fused_computation.12 | convolution fusion | flops 254988288 | bytes 2655552 | tf_op jit(solution)/shard_map/dot_general | solution.py:92
  127.9 1.6 %reshape.390 = f32[8,24,1,1152]{3,1,0,2:T(8,128)} reshape(f32[2,4,24,1,24,48]{5,4,2,1,0,3:T(8,128)S(1)} %copy.59) | data formatting | bytes 1769472 | tf_op jit(solution)/shard_map/reshape | solution.py:129
  129.5 2.8 %pad_bitcast_fusion = f32[8,24,1,1280]{3,1,2,0:T(8,128)} fusion(f32[8,24,1,1152]{3,1,0,2:T(8,128)} %reshape.390, f32[]{:T(128)} %get-tuple-element.22), kind=kLoop, calls=%fused_computation.29 | loop fusion | bytes 1867780 | tf_op jit(solution)/shard_map/concatenate | solution.py:131
  132.4 3.6 %all-to-all-start.2 = ((f32[8,24,1,1280]{3,1,2,0:T(8,128)}), f32[8,24,1,1280]{3,1,2,0:T(8,128)S(1)}, u32[]{:S(2)}, u32[]{:S(2)}) async-start(f32[8,24,1,1280]{3,1,2,0:T(8,128)} %pad_bitcast_fusion), calls=%async_computation.2 | async-start | bytes 1966080 | tf_op jit(solution)/shard_map/all_to_all | solution.py:132
  136.7 13.0 %all-to-all-done.2 = f32[8,24,1,1280]{3,1,2,0:T(8,128)S(1)} async-done(((f32[8,24,1,1280]{3,1,2,0:T(8,128)}), f32[8,24,1,1280]{3,1,2,0:T(8,128)S(1)}, u32[]{:S(2)}, u32[]{:S(2)}) %all-to-all-start.2) | async-done | bytes 983072 | tf_op jit(solution)/shard_map/all_to_all | solution.py:132
  149.6 1.0 slice.54
  150.9 1.5 copy.62
  152.4 1.0 fusion.19
  153.5 1.0 copy.63
  154.5 1.4 slice_reduce_fusion
  (46 shorter events, 3.8 us)
Async XLA Ops:
  0.6 3.9 %copy-start = (f32[2,48,24,96]{3,2,1,0:T(8,128)S(1)}, f32[2,48,24,96]{3,2,1,0:T(8,128)}, u32[]{:S(2)}) copy-start(f32[2,48,24,96]{3,2,1,0:T(8,128)} %param.5) | copy-start | bytes 2654212
  1.4 4.7 %collective-permute-start.3 = (s32[4,1]{0,1:T(1,128)S(1)}, s32[4,1]{0,1:T(1,128)S(1)}, u32[]{:S(2)}, u32[]{:S(2)}) collective-permute-start(s32[4,1]{0,1:T(1,128)S(1)} %compare_select_fusion.1), channel_id=1, source_target_pairs={{0,8},{8,0},{16,24},{24,16},{1,9},{9,1},{17,25},{25,17},{2,10},{10... | collective-permute-start | bytes 56 | tf_op jit(solution)/shard_map/ppermute | solution.py:45
  6.2 4.5 %collective-permute-start.4 = (s32[4,1]{0,1:T(1,128)S(1)}, s32[4,1]{0,1:T(1,128)S(1)}, u32[]{:S(2)}, u32[]{:S(2)}) collective-permute-start(s32[4,1]{0,1:T(1,128)S(1)} %fusion.358), channel_id=1, source_target_pairs={{0,16},{8,24},{16,0},{24,8},{1,17},{9,25},{17,1},{25,9},{2,18},{10... | collective-permute-start | bytes 56 | tf_op jit(solution)/shard_map/ppermute | solution.py:45
  12.3 56.6 %all-to-all-start = ((f32[4,1,48,24,96]{4,3,2,1,0:T(8,128)}), f32[4,1,48,24,96]{4,3,2,1,0:T(8,128)S(1)}, u32[]{:S(2)}, u32[]{:S(2)}) async-start(f32[4,1,48,24,96]{4,3,2,1,0:T(8,128)} %select_select_fusion), calls=%async_computation | async-start | bytes 4718592 | tf_op jit(solution)/shard_map/all_to_all | solution.py:152
  19.2 0.8 copy-start.1
  20.7 4.9 %collective-permute-start = (f32[1,8,24,96]{3,1,2,0:T(8,128)}, f32[1,8,24,96]{3,1,2,0:T(8,128)}, u32[]{:S(2)}, u32[]{:S(2)}) collective-permute-start(f32[1,8,24,96]{3,1,2,0:T(8,128)} %slice_select_fusion.1), channel_id=1, source_target_pairs={{0,4},{4,0},{1,5},{5,1},{2,6},{6,2},{3,7},{7,3},{8,12},{12,8},{9,1... | collective-permute-start | bytes 221192 | tf_op jit(solution)/shard_map/ppermute | solution.py:25
  26.5 3.9 %copy-start.5 = (f32[1,8,24,96]{3,1,2,0:T(8,128)}, f32[1,8,24,96]{3,1,2,0:T(8,128)S(1)}, u32[]{:S(2)}) copy-start(f32[1,8,24,96]{3,1,2,0:T(8,128)S(1)} %get-tuple-element.16) | copy-start | bytes 221188
  26.5 3.9 %copy-start.6 = (f32[1,8,24,96]{3,1,2,0:T(8,128)}, f32[1,8,24,96]{3,1,2,0:T(8,128)S(1)}, u32[]{:S(2)}) copy-start(f32[1,8,24,96]{3,1,2,0:T(8,128)S(1)} %get-tuple-element.17) | copy-start | bytes 221188
  28.5 44.3 %collective-permute-start.1 = (f32[1,64,8,96]{3,1,2,0:T(8,128)}, f32[1,64,8,96]{3,1,2,0:T(8,128)}, u32[]{:S(2)}, u32[]{:S(2)}) collective-permute-start(f32[1,64,8,96]{3,1,2,0:T(8,128)} %get-tuple-element.12), channel_id=1, source_target_pairs={{0,1},{1,2},{2,3},{4,5},{5,6},{6,7},{8,9},{9,10},{10,11},{12,13},{... | collective-permute-start | bytes 589832 | tf_op jit(solution)/shard_map/ppermute | solution.py:30
  30.5 42.3 %collective-permute-start.2 = (f32[1,64,8,96]{3,1,2,0:T(8,128)}, f32[1,64,8,96]{3,1,2,0:T(8,128)}, u32[]{:S(2)}, u32[]{:S(2)}) collective-permute-start(f32[1,64,8,96]{3,1,2,0:T(8,128)} %get-tuple-element.13), channel_id=1, source_target_pairs={{1,0},{2,1},{3,2},{5,4},{6,5},{7,6},{9,8},{10,9},{11,10},{13,12},{... | collective-permute-start | bytes 589832 | tf_op jit(solution)/shard_map/ppermute | solution.py:31
  71.2 4.7 %collective-permute-start.5 = (f32[1,8,24,96]{3,1,2,0:T(8,128)S(1)}, f32[1,8,24,96]{3,1,2,0:T(8,128)S(1)}, u32[]{:S(2)}, u32[]{:S(2)}) collective-permute-start(f32[1,8,24,96]{3,1,2,0:T(8,128)S(1)} %slice_select_fusion), channel_id=1, source_target_pairs={{0,4},{4,0},{1,5},{5,1},{2,6},{6,2},{3,7},{7,3},{8,12},{12,8},{9,1... | collective-permute-start | bytes 221192 | tf_op jit(solution)/shard_map/ppermute | solution.py:25
  76.0 4.2 %collective-permute-start.6 = (f32[1,64,8,96]{3,1,2,0:T(8,128)S(1)}, f32[1,64,8,96]{3,1,2,0:T(8,128)S(1)}, u32[]{:S(2)}, u32[]{:S(2)}) collective-permute-start(f32[1,64,8,96]{3,1,2,0:T(8,128)S(1)} %get-tuple-element.14), channel_id=1, source_target_pairs={{0,1},{1,2},{2,3},{4,5},{5,6},{6,7},{8,9},{9,10},{10,11},{12,13},{... | collective-permute-start | bytes 589832 | tf_op jit(solution)/shard_map/ppermute | solution.py:30
  77.3 5.2 %collective-permute-start.7 = (f32[1,64,8,96]{3,1,2,0:T(8,128)S(1)}, f32[1,64,8,96]{3,1,2,0:T(8,128)S(1)}, u32[]{:S(2)}, u32[]{:S(2)}) collective-permute-start(f32[1,64,8,96]{3,1,2,0:T(8,128)S(1)} %get-tuple-element.15), channel_id=1, source_target_pairs={{1,0},{2,1},{3,2},{5,4},{6,5},{7,6},{9,8},{10,9},{11,10},{13,12},{... | collective-permute-start | bytes 589832 | tf_op jit(solution)/shard_map/ppermute | solution.py:31
  82.6 3.9 %copy-start.10 = (pred[8,24]{1,0:T(8,128)(4,1)S(1)}, pred[8,24]{1,0:T(8,128)(4,1)}, u32[]{:S(2)}) copy-start(pred[8,24]{1,0:T(8,128)(4,1)} %fusion.123) | copy-start | bytes 580
  85.0 0.8 copy-start.2
  88.5 19.9 %all-to-all-start.1 = ((f32[8,24,1,1152]{3,1,2,0:T(8,128)}), f32[8,24,1,1152]{3,1,2,0:T(8,128)}, u32[]{:S(2)}, u32[]{:S(2)}) async-start(f32[8,24,1,1152]{3,1,2,0:T(8,128)} %convolution_bitcast_fusion), calls=%async_computation.1 | async-start | bytes 1769472 | tf_op jit(solution)/shard_map/all_to_all | solution.py:108
  116.5 1.9 %copy-start.7 = (f32[24,192]{1,0:T(8,128)S(1)}, f32[24,192]{1,0:T(8,128)}, u32[]{:S(2)}) copy-start(f32[24,192]{1,0:T(8,128)} %broadcast_multiply_fusion) | copy-start | bytes 55300
  116.6 1.9 %copy-start.8 = (f32[24,192]{1,0:T(8,128)S(1)}, f32[24,192]{1,0:T(8,128)}, u32[]{:S(2)}) copy-start(f32[24,192]{1,0:T(8,128)} %broadcast_add_fusion) | copy-start | bytes 55300
  122.3 3.8 %copy-start.9 = (s32[2,48]{1,0:T(2,128)S(1)}, s32[2,48]{1,0:T(2,128)}, u32[]{:S(2)}) copy-start(s32[2,48]{1,0:T(2,128)} %multiply_add_fusion.1) | copy-start | bytes 1156
  132.4 17.2 %all-to-all-start.2 = ((f32[8,24,1,1280]{3,1,2,0:T(8,128)}), f32[8,24,1,1280]{3,1,2,0:T(8,128)S(1)}, u32[]{:S(2)}, u32[]{:S(2)}) async-start(f32[8,24,1,1280]{3,1,2,0:T(8,128)} %pad_bitcast_fusion), calls=%async_computation.2 | async-start | bytes 1966080 | tf_op jit(solution)/shard_map/all_to_all | solution.py:132
  136.0 16.5 %copy-start.3 = (f32[48,24,96]{2,0,1:T(8,128)S(1)}, f32[48,24,96]{2,0,1:T(8,128)}, u32[]{:S(2)}) copy-start(f32[48,24,96]{2,0,1:T(8,128)} %copy-done.2) | copy-start | bytes 1327108
  149.6 1.3 copy-start.4

commit v12 on v9

--- a/solution.py
+++ b/solution.py
@@ -147,7 +147,11 @@
         slots = jnp.where(hit, j_coeff[number][None, None], slots)
     arrived = lax.all_to_all(slots, "band", 0, 0, tiled=True)
     own_orbital = synthesize(extended(i_coeff, sides, 8))[0]
-    partner = synthesize(extended(jnp.sum(arrived, axis=0), sides, 8))
+    owners = wanted[lax.axis_index("band")] // local_count
+    picked = jnp.stack(
+        [lax.dynamic_index_in_dim(arrived[:, pair], owners[pair], 0, False) for pair in range(owners.shape[0])]
+    )
+    partner = synthesize(extended(picked, sides, 8))
     density = own_orbital[None] * partner
     potential, energy_part = potentials(density)
     weights = pair_occ[0].astype(jnp.float32)

time: 155 us -> 154 us (level)
  between operations: 3.97 us -> 6.56 us
  waiting for transfers between devices: 75.6 us -> 73.8 us
    ppermute x2, waiting for transfers between devices: 2.65 us -> 0.84 us  [extended(): got = lax.ppermute(jnp.where(first, tail, head), axis, [(0, 1), (1, 0)])]
  transfers between devices with their start and end apart: 11 -> 11, of which waited for: 8 -> 7; matrix products, arithmetic and copies ran while one was open for 5% -> 4% of each run, Pallas kernels for 0% -> 0%
where the time goes in v12:
time: 154 us
  waiting for transfers between devices  73.8 us (48%)
  starting transfers between devices  31.1 us (20%)
  matrix products  20.8 us (14%)
  local copies, waits for them, and re-layouts  18.2 us (12%)
  between operations  6.56 us (4%)
  other arithmetic  3.42 us (2%)
    all_to_all x1, waiting for transfers between devices, shards(): arrived = lax.all_to_all(slots, 'band', 0, 0, tiled=True)  42.6 us
    dot_general x6, matrix products, contract(): lax.dot_general(left, right, (((left_dim,), (right_dim,)), ((), ())), pre...  14.1 us
    all_to_all x1, waiting for transfers between devices, potentials(): got = lax.all_to_all(back, ('gy', 'gz'), 0, 0, tiled=True)  13 us
    all_to_all x1, waiting for transfers between devices, potentials(): got = lax.all_to_all(send, ('gy', 'gz'), 0, 0, tiled=True)  12.5 us
    all_to_all x1, starting transfers between devices, potentials(): got = lax.all_to_all(send, ('gy', 'gz'), 0, 0, tiled=True)  7.13 us
    ppermute x2, starting transfers between devices, group_sum(): lax.ppermute(total, axis, [(i, i ^ step) for i in range(count)])  6.12 us
    reshape x2, local copies, waits for them, and re-layouts, potentials(): got = got.reshape(count_y, count_z, width, pair_count, rows_z, rows_y)  5.35 us
    all_to_all x1, starting transfers between devices, shards(): arrived = lax.all_to_all(slots, 'band', 0, 0, tiled=True)  5.33 us
  transfers between devices with their start and end apart: 11, of which 7 were waited for; matrix products, arithmetic and copies ran while one was open for 4% of the time, Pallas kernels for 0%

profile of v12, /device:TPU:0, one launch (start us, length us, event | category | flops | bytes accessed | tf_op | source)
XLA Modules:
  0.0 153.8 jit_solution(18216021996038162981)
XLA Ops:
  1.3 3.1 %collective-permute-start.3 = (s32[4,1]{0,1:T(1,128)S(1)}, s32[4,1]{0,1:T(1,128)S(1)}, u32[]{:S(2)}, u32[]{:S(2)}) collective-permute-start(s32[4,1]{0,1:T(1,128)S(1)} %compare_select_fusion.1), channel_id=1, source_target_pairs={{0,8},{8,0},{16,24},{24,16},{1,9},{9,1},{17,25},{25,17},{2,10},{10... | collective-permute-start | bytes 56 | tf_op jit(solution)/shard_map/ppermute | solution.py:45
  4.4 1.3 slice_bitcast_fusion.1
  5.7 0.2 collective-permute-done.3
  5.9 3.0 %collective-permute-start.4 = (s32[4,1]{0,1:T(1,128)S(1)}, s32[4,1]{0,1:T(1,128)S(1)}, u32[]{:S(2)}, u32[]{:S(2)}) collective-permute-start(s32[4,1]{0,1:T(1,128)S(1)} %fusion.368), channel_id=1, source_target_pairs={{0,16},{8,24},{16,0},{24,8},{1,17},{9,25},{17,1},{25,9},{2,18},{10... | collective-permute-start | bytes 56 | tf_op jit(solution)/shard_map/ppermute | solution.py:45
  8.9 1.5 collective-permute-done.4
  10.5 1.7 %select_select_fusion = f32[4,1,48,24,96]{4,3,2,1,0:T(8,128)} fusion(f32[48,24,96]{2,1,0:T(8,128)S(1)} %get-tuple-element.11, f32[48,24,96]{2,1,0:T(8,128)S(1)} %get-tuple-element.10, pred[4]{0:T(512)(128)(4,1)S(1)} %compare_bitcast_fusion, pred[4]{0:T(512)(128)(4,1)S(1)} %get-tuple-element.8), kind=kLoop, calls=%fused_computation.11 | loop fusion | flops 884736 | bytes 2654216 | tf_op jit(solution)/shard_map/jit(_where)/select_n | solution.py:147
  12.1 5.3 %all-to-all-start = ((f32[4,1,48,24,96]{4,3,2,1,0:T(8,128)}), f32[4,1,48,24,96]{4,3,2,1,0:T(8,128)S(1)}, u32[]{:S(2)}, u32[]{:S(2)}) async-start(f32[4,1,48,24,96]{4,3,2,1,0:T(8,128)} %select_select_fusion), calls=%async_computation | async-start | bytes 4718592 | tf_op jit(solution)/shard_map/all_to_all | solution.py:148
  17.5 1.6 %collective-permute-start = (f32[1,8,24,96]{3,2,1,0:T(8,128)S(1)}, f32[1,8,24,96]{3,2,1,0:T(8,128)S(1)}, u32[]{:S(2)}, u32[]{:S(2)}) collective-permute-start(f32[1,8,24,96]{3,2,1,0:T(8,128)S(1)} %slice_select_fusion.1), channel_id=1, source_target_pairs={{0,4},{4,0},{1,5},{5,1},{2,6},{6,2},{3,7},{7,3},{8,12},{12,8},{9,1... | collective-permute-start | bytes 221192 | tf_op jit(solution)/shard_map/ppermute | solution.py:25
  19.1 0.6 constant_dynamic-slice_fusion
  22.3 0.7 pad_maximum_fusion.5
  23.1 2.0 %collective-permute-start.1 = (f32[1,64,8,96]{3,2,1,0:T(8,128)}, f32[1,64,8,96]{3,2,1,0:T(8,128)}, u32[]{:S(2)}, u32[]{:S(2)}) collective-permute-start(f32[1,64,8,96]{3,2,1,0:T(8,128)} %get-tuple-element.12), channel_id=1, source_target_pairs={{0,1},{1,2},{2,3},{4,5},{5,6},{6,7},{8,9},{9,10},{10,11},{12,13},{... | collective-permute-start | bytes 589832 | tf_op jit(solution)/shard_map/ppermute | solution.py:30
  25.1 1.3 collective-permute-start.2
  26.4 42.6 %all-to-all-done = f32[4,1,48,24,96]{4,3,2,1,0:T(8,128)S(1)} async-done(((f32[4,1,48,24,96]{4,3,2,1,0:T(8,128)}), f32[4,1,48,24,96]{4,3,2,1,0:T(8,128)S(1)}, u32[]{:S(2)}, u32[]{:S(2)}) %all-to-all-start) | async-done | bytes 1769504 | tf_op jit(solution)/shard_map/all_to_all | solution.py:148
  69.0 1.6 %collective-permute-start.5 = (f32[1,8,24,96]{3,2,1,0:T(8,128)S(1)}, f32[1,8,24,96]{3,2,1,0:T(8,128)S(1)}, u32[]{:S(2)}, u32[]{:S(2)}) collective-permute-start(f32[1,8,24,96]{3,2,1,0:T(8,128)S(1)} %slice_select_fusion), channel_id=1, source_target_pairs={{0,4},{4,0},{1,5},{5,1},{2,6},{6,2},{3,7},{7,3},{8,12},{12,8},{9,1... | collective-permute-start | bytes 221192 | tf_op jit(solution)/shard_map/ppermute | solution.py:25
  70.6 2.3 %fusion.7 = f32[64,40,96]{2,1,0:T(8,128)S(1)} fusion(f32[1,64,8,96]{3,2,1,0:T(8,128)} %collective-permute-done.2, f32[1,8,24,96]{3,2,1,0:T(8,128)S(1)} %get-tuple-element.17, f32[1,48,24,96]{3,2,1,0:T(8,128)S(1)} %copy-done, f32[1,8,24,96]{3,2,1,0:T(8,128)S(1)} %get-tuple-element.16, f32[1,64,8,96]{3,2,1,0:T(8,128)} %collective-permute-done.1), kind=kOutput, calls=%fused_computation.14 | convolution fusion | flops 284540928 | bytes 1966080 | tf_op jit(solution)/shard_map/dot_general | solution.py:65
  72.9 0.8 collective-permute-done.5
  73.8 1.3 collective-permute-start.6
  75.1 1.3 collective-permute-start.7
  76.4 0.8 convolution_bitcast_fusion.3
  77.3 3.0 %collective-permute-done.7 = f32[1,64,8,96]{3,2,1,0:T(8,128)S(1)} collective-permute-done((f32[1,64,8,96]{3,2,1,0:T(8,128)S(1)}, f32[1,64,8,96]{3,2,1,0:T(8,128)S(1)}, u32[]{:S(2)}, u32[]{:S(2)}) %collective-permute-start.7) | collective-permute-done | bytes 196640 | tf_op jit(solution)/shard_map/ppermute | solution.py:31
  80.3 1.2 fusion.16
  81.5 0.8 convolution_bitcast_fusion.2
  82.4 0.8 fusion.28
  83.1 0.8 convolution_multiply_fusion.1
  83.9 2.0 %convolution_bitcast_fusion = f32[8,24,1,1152]{3,1,2,0:T(8,128)} fusion(f32[1152,96,1]{1,0,2:T(8,128)S(1)} %bitcast.133, s32[8,24]{1,0:T(8,128)S(1)} %add_select_fusion.3, pred[8,24]{1,0:T(8,128)(4,1)S(1)} %fusion.129), kind=kOutput, calls=%fused_computation.3 | convolution fusion | flops 127586304 | bytes 1328064 | tf_op jit(solution)/shard_map/dot_general | solution.py:89
  85.9 7.1 %all-to-all-start.1 = ((f32[8,24,1,1152]{3,1,2,0:T(8,128)}), f32[8,24,1,1152]{3,1,2,0:T(8,128)}, u32[]{:S(2)}, u32[]{:S(2)}) async-start(f32[8,24,1,1152]{3,1,2,0:T(8,128)} %convolution_bitcast_fusion), calls=%async_computation.1 | async-start | bytes 1769472 | tf_op jit(solution)/shard_map/all_to_all | solution.py:105
  93.0 0.1 or_select_fusion.1
  93.1 0.1 or_select_fusion
  93.1 0.1 broadcast_multiply_fusion
  93.2 0.1 broadcast_add_fusion
  93.3 12.5 %all-to-all-done.1 = f32[8,24,1,1152]{3,1,2,0:T(8,128)} async-done(((f32[8,24,1,1152]{3,1,2,0:T(8,128)}), f32[8,24,1,1152]{3,1,2,0:T(8,128)}, u32[]{:S(2)}, u32[]{:S(2)}) %all-to-all-start.1) | async-done | bytes 884768 | tf_op jit(solution)/shard_map/all_to_all | solution.py:105
  105.8 2.1 %reshape.392 = f32[2,4,24,1,24,48]{5,4,2,1,0,3:T(8,128)S(1)} reshape(f32[8,24,1,1152]{3,1,2,0:T(8,128)} %all-to-all-done.1) | data formatting | bytes 1769472 | tf_op jit(solution)/shard_map/reshape | solution.py:106
  107.9 3.2 %copy.38 = f32[2,4,24,1,24,48]{5,0,4,1,2,3:T(2,128)} copy(f32[2,4,24,1,24,48]{5,4,2,1,0,3:T(8,128)S(1)} %reshape.392) | data formatting | bytes 1769472 | tf_op jit(solution)/shard_map/reshape | solution.py:106
  111.2 2.7 %reshape.393 = f32[24,96,96]{2,1,0:T(8,128)S(1)} reshape(f32[24,1,4,24,2,48]{5,4,3,2,0,1:T(2,128)} %bitcast.128) | data formatting | bytes 1769472 | tf_op jit(solution)/shard_map/reshape.31
  113.9 1.9 %fusion.42 = f32[24,96,192]{1,2,0:T(8,128)S(1)} fusion(f32[24,96,96]{2,1,0:T(8,128)S(1)} %reshape.393, s32[192]{0:T(256)S(1)} %add_select_fusion.4, pred[192]{0:T(512)(128)(4,1)S(1)} %iota_compare_fusion), kind=kOutput, calls=%fused_computation.68 | convolution fusion | flops 254988288 | bytes 2655168 | tf_op jit(solution)/shard_map/dot_general | solution.py:89
  115.8 3.8 %multiply_reduce_fusion = (f32[]{:T(128)}, f32[24,192,192]{2,1,0:T(8,128)S(1)}) fusion(f32[192]{0:T(256)S(1)} %get-tuple-element.25, f32[24,192]{1,0:T(8,128)S(1)} %broadcast_add_fusion, f32[192]{0:T(256)S(1)} %get-tuple-element.24, f32[24,192]{1,0:T(8,128)S(1)} %broadcast_multiply_fusion, f32[24,96,192]{1,2,0:T(8,128)S(1)} %fusion.42, ...), kind=kOutput, calls=%fused_computation | convolution fusion | flops 516870144 | bytes 5347780 | tf_op jit(solution)/shard_map/dot_general | solution.py:89
  119.6 3.8 %fusion = f32[24,192,96]{1,2,0:T(8,128)S(1)} fusion(f32[24,192,192]{2,1,0:T(8,128)S(1)} %get-tuple-element.21, f32[192]{0:T(256)S(1)} %get-tuple-element.25, f32[24,192]{1,0:T(8,128)S(1)} %broadcast_add_fusion, f32[192]{0:T(256)S(1)} %get-tuple-element.24, f32[24,192]{1,0:T(8,128)S(1)} %broadcast_multiply_fusion, s32[192]{0:T(256)S(1)} %add_select_fusion.4, ...), kind=kOutput, calls=%fused_computation.2 | convolution fusion | flops 515100672 | bytes 5347776 | tf_op jit(solution)/shard_map/dot_general | solution.py:89
  123.4 1.6 %convolution_bitcast_fusion.1 = f32[2,4,24,1,24,48]{5,4,0,1,2,3:T(8,128)S(1)} fusion(f32[24,4,24,192,1]{3,2,4,1,0:T(8,128)S(1)} %bitcast.132, s32[192]{0:T(256)S(1)} %add_select_fusion.4, s32[2,48]{1,0:T(2,128)S(1)} %multiply_add_fusion.1, pred[192]{0:T(512)(128)(4,1)S(1)} %iota_compare_fusion), kind=kOutput, calls=%fused_computation.12 | convolution fusion | flops 254988288 | bytes 2655552 | tf_op jit(solution)/shard_map/dot_general | solution.py:89
  125.0 0.2 copy.23
  125.1 1.7 %reshape.395 = f32[8,24,1,1152]{3,1,0,2:T(8,128)} reshape(f32[2,4,24,1,24,48]{5,4,2,1,0,3:T(8,128)S(1)} %copy.23) | data formatting | bytes 1769472 | tf_op jit(solution)/shard_map/reshape | solution.py:126
  126.8 2.8 %pad_bitcast_fusion = f32[8,24,1,1280]{3,1,2,0:T(8,128)} fusion(f32[8,24,1,1152]{3,1,0,2:T(8,128)} %reshape.395, f32[]{:T(128)} %get-tuple-element.20), kind=kLoop, calls=%fused_computation.40 | loop fusion | bytes 1867780 | tf_op jit(solution)/shard_map/concatenate | solution.py:128
  129.6 3.6 %all-to-all-start.2 = ((f32[8,24,1,1280]{3,1,2,0:T(8,128)}), f32[8,24,1,1280]{3,1,2,0:T(8,128)S(1)}, u32[]{:S(2)}, u32[]{:S(2)}) async-start(f32[8,24,1,1280]{3,1,2,0:T(8,128)} %pad_bitcast_fusion), calls=%async_computation.2 | async-start | bytes 1966080 | tf_op jit(solution)/shard_map/all_to_all | solution.py:129
  133.9 13.0 %all-to-all-done.2 = f32[8,24,1,1280]{3,1,2,0:T(8,128)S(1)} async-done(((f32[8,24,1,1280]{3,1,2,0:T(8,128)}), f32[8,24,1,1280]{3,1,2,0:T(8,128)S(1)}, u32[]{:S(2)}, u32[]{:S(2)}) %all-to-all-start.2) | async-done | bytes 983072 | tf_op jit(solution)/shard_map/all_to_all | solution.py:129
  146.9 1.0 slice.50
  147.9 1.5 copy.26
  149.4 1.0 fusion.27
  150.4 1.0 copy.27
  151.4 0.6 slice_reduce_fusion
  (23 shorter events, 0.2 us)
Async XLA Ops:
  1.3 4.6 %collective-permute-start.3 = (s32[4,1]{0,1:T(1,128)S(1)}, s32[4,1]{0,1:T(1,128)S(1)}, u32[]{:S(2)}, u32[]{:S(2)}) collective-permute-start(s32[4,1]{0,1:T(1,128)S(1)} %compare_select_fusion.1), channel_id=1, source_target_pairs={{0,8},{8,0},{16,24},{24,16},{1,9},{9,1},{17,25},{25,17},{2,10},{10... | collective-permute-start | bytes 56 | tf_op jit(solution)/shard_map/ppermute | solution.py:45
  5.9 4.6 %collective-permute-start.4 = (s32[4,1]{0,1:T(1,128)S(1)}, s32[4,1]{0,1:T(1,128)S(1)}, u32[]{:S(2)}, u32[]{:S(2)}) collective-permute-start(s32[4,1]{0,1:T(1,128)S(1)} %fusion.368), channel_id=1, source_target_pairs={{0,16},{8,24},{16,0},{24,8},{1,17},{9,25},{17,1},{25,9},{2,18},{10... | collective-permute-start | bytes 56 | tf_op jit(solution)/shard_map/ppermute | solution.py:45
  12.1 5.3 %copy-start = (f32[1,48,24,96]{3,2,1,0:T(8,128)S(1)}, f32[1,48,24,96]{3,2,1,0:T(8,128)}, u32[]{:S(2)}) copy-start(f32[1,48,24,96]{3,2,1,0:T(8,128)} %param.4) | copy-start | bytes 1327108
  12.1 56.9 %all-to-all-start = ((f32[4,1,48,24,96]{4,3,2,1,0:T(8,128)}), f32[4,1,48,24,96]{4,3,2,1,0:T(8,128)S(1)}, u32[]{:S(2)}, u32[]{:S(2)}) async-start(f32[4,1,48,24,96]{4,3,2,1,0:T(8,128)} %select_select_fusion), calls=%async_computation | async-start | bytes 4718592 | tf_op jit(solution)/shard_map/all_to_all | solution.py:148
  17.5 4.8 %collective-permute-start = (f32[1,8,24,96]{3,2,1,0:T(8,128)S(1)}, f32[1,8,24,96]{3,2,1,0:T(8,128)S(1)}, u32[]{:S(2)}, u32[]{:S(2)}) collective-permute-start(f32[1,8,24,96]{3,2,1,0:T(8,128)S(1)} %slice_select_fusion.1), channel_id=1, source_target_pairs={{0,4},{4,0},{1,5},{5,1},{2,6},{6,2},{3,7},{7,3},{8,12},{12,8},{9,1... | collective-permute-start | bytes 221192 | tf_op jit(solution)/shard_map/ppermute | solution.py:25
  23.1 47.5 %collective-permute-start.1 = (f32[1,64,8,96]{3,2,1,0:T(8,128)}, f32[1,64,8,96]{3,2,1,0:T(8,128)}, u32[]{:S(2)}, u32[]{:S(2)}) collective-permute-start(f32[1,64,8,96]{3,2,1,0:T(8,128)} %get-tuple-element.12), channel_id=1, source_target_pairs={{0,1},{1,2},{2,3},{4,5},{5,6},{6,7},{8,9},{9,10},{10,11},{12,13},{... | collective-permute-start | bytes 589832 | tf_op jit(solution)/shard_map/ppermute | solution.py:30
  25.1 45.5 %collective-permute-start.2 = (f32[1,64,8,96]{3,2,1,0:T(8,128)S(1)}, f32[1,64,8,96]{3,2,1,0:T(8,128)}, u32[]{:S(2)}, u32[]{:S(2)}) collective-permute-start(f32[1,64,8,96]{3,2,1,0:T(8,128)S(1)} %get-tuple-element.13), channel_id=1, source_target_pairs={{1,0},{2,1},{3,2},{5,4},{6,5},{7,6},{9,8},{10,9},{11,10},{13,12},{... | collective-permute-start | bytes 589832 | tf_op jit(solution)/shard_map/ppermute | solution.py:31
  69.0 4.7 %collective-permute-start.5 = (f32[1,8,24,96]{3,2,1,0:T(8,128)S(1)}, f32[1,8,24,96]{3,2,1,0:T(8,128)S(1)}, u32[]{:S(2)}, u32[]{:S(2)}) collective-permute-start(f32[1,8,24,96]{3,2,1,0:T(8,128)S(1)} %slice_select_fusion), channel_id=1, source_target_pairs={{0,4},{4,0},{1,5},{5,1},{2,6},{6,2},{3,7},{7,3},{8,12},{12,8},{9,1... | collective-permute-start | bytes 221192 | tf_op jit(solution)/shard_map/ppermute | solution.py:25
  73.8 3.5 %collective-permute-start.6 = (f32[1,64,8,96]{3,2,1,0:T(8,128)S(1)}, f32[1,64,8,96]{3,2,1,0:T(8,128)S(1)}, u32[]{:S(2)}, u32[]{:S(2)}) collective-permute-start(f32[1,64,8,96]{3,2,1,0:T(8,128)S(1)} %get-tuple-element.14), channel_id=1, source_target_pairs={{0,1},{1,2},{2,3},{4,5},{5,6},{6,7},{8,9},{9,10},{10,11},{12,13},{... | collective-permute-start | bytes 589832 | tf_op jit(solution)/shard_map/ppermute | solution.py:30
  75.1 5.2 %collective-permute-start.7 = (f32[1,64,8,96]{3,2,1,0:T(8,128)S(1)}, f32[1,64,8,96]{3,2,1,0:T(8,128)S(1)}, u32[]{:S(2)}, u32[]{:S(2)}) collective-permute-start(f32[1,64,8,96]{3,2,1,0:T(8,128)S(1)} %get-tuple-element.15), channel_id=1, source_target_pairs={{1,0},{2,1},{3,2},{5,4},{6,5},{7,6},{9,8},{10,9},{11,10},{13,12},{... | collective-permute-start | bytes 589832 | tf_op jit(solution)/shard_map/ppermute | solution.py:31
  85.9 19.9 %all-to-all-start.1 = ((f32[8,24,1,1152]{3,1,2,0:T(8,128)}), f32[8,24,1,1152]{3,1,2,0:T(8,128)}, u32[]{:S(2)}, u32[]{:S(2)}) async-start(f32[8,24,1,1152]{3,1,2,0:T(8,128)} %convolution_bitcast_fusion), calls=%async_computation.1 | async-start | bytes 1769472 | tf_op jit(solution)/shard_map/all_to_all | solution.py:105
  129.6 17.2 %all-to-all-start.2 = ((f32[8,24,1,1280]{3,1,2,0:T(8,128)}), f32[8,24,1,1280]{3,1,2,0:T(8,128)S(1)}, u32[]{:S(2)}, u32[]{:S(2)}) async-start(f32[8,24,1,1280]{3,1,2,0:T(8,128)} %pad_bitcast_fusion), calls=%async_computation.2 | async-start | bytes 1966080 | tf_op jit(solution)/shard_map/all_to_all | solution.py:129

commit v13 on v9

--- a/solution.py
+++ b/solution.py
@@ -124,11 +124,9 @@
     back_z = contract(back_y, table, 2, 1)
     back = back_z.reshape(width, pair_count, count_z, rows_z, count_y, rows_y)
     back = back.transpose(4, 2, 0, 1, 3, 5).reshape(spread, width, pair_count, rows_y * rows_z)
-    rider = jnp.broadcast_to(energy_part[None, None, :, None], (spread, width, pair_count, 128))
-    back = jnp.concatenate((back, rider), axis=3)
+    energy_total = group_sum(energy_part, ("gz", "gy"))
     got = lax.all_to_all(back, ("gy", "gz"), 0, 0, tiled=True)
-    energy_total = jnp.sum(got[:, 0, :, rows_y * rows_z], axis=0)
-    got = got[:, :, :, : rows_y * rows_z].reshape(period, pair_count, rows_y * rows_z)
+    got = got.reshape(period, pair_count, rows_y * rows_z)
     result = contract(got, table, 0, 1)
     result = result.reshape(pair_count, rows_z, rows_y, length).transpose(0, 2, 1, 3)
     return result, energy_total

time: 155 us -> 152 us (0.981)
  starting transfers between devices: 31.1 us -> 41.7 us
  waiting for transfers between devices: 75.6 us -> 66.4 us
  local copies, waits for them, and re-layouts: 17.6 us -> 12.6 us
  between operations: 3.97 us -> 5.87 us
    all_to_all x1, waiting for transfers between devices: 13 us -> 0.01 us  [potentials(): got = lax.all_to_all(back, ('gy', 'gz'), 0, 0, tiled=True)]
    ppermute x2 -> x5, starting transfers between devices: 6.12 us -> 16.7 us  [group_sum(): lax.ppermute(total, axis, [(i, i ^ step) for i in range(count)])]
    ppermute x2 -> x5, waiting for transfers between devices: 1.71 us -> 5.4 us  [group_sum(): lax.ppermute(total, axis, [(i, i ^ step) for i in range(count)])]
    concatenate x1 -> x0, local copies, waits for them, and re-layouts: 2.84 us -> none  [potentials(): back = jnp.concatenate((back, rider), axis=3)]
  transfers between devices with their start and end apart: 11 -> 14, of which waited for: 8 -> 10; matrix products, arithmetic and copies ran while one was open for 5% -> 5% of each run, Pallas kernels for 0% -> 0%
where the time goes in v13:
time: 152 us
  waiting for transfers between devices  66.4 us (44%)
  starting transfers between devices  41.7 us (27%)
  matrix products  20.8 us (14%)
  local copies, waits for them, and re-layouts  12.6 us (8%)
  between operations  5.87 us (4%)
  other arithmetic  4.14 us (3%)
    all_to_all x1, waiting for transfers between devices, shards(): arrived = lax.all_to_all(slots, 'band', 0, 0, tiled=True)  42.6 us
    ppermute x5, starting transfers between devices, group_sum(): lax.ppermute(total, axis, [(i, i ^ step) for i in range(count)])  16.7 us
    dot_general x6, matrix products, contract(): lax.dot_general(left, right, (((left_dim,), (right_dim,)), ((), ())), pre...  14 us
    all_to_all x1, waiting for transfers between devices, potentials(): got = lax.all_to_all(send, ('gy', 'gz'), 0, 0, tiled=True)  12.5 us
    all_to_all x1, starting transfers between devices, potentials(): got = lax.all_to_all(send, ('gy', 'gz'), 0, 0, tiled=True)  7.13 us
    ppermute x5, waiting for transfers between devices, group_sum(): lax.ppermute(total, axis, [(i, i ^ step) for i in range(count)])  5.4 us
    reshape x2, local copies, waits for them, and re-layouts, potentials(): got = got.reshape(count_y, count_z, width, pair_count, rows_z, rows_y)  5.35 us
    all_to_all x1, starting transfers between devices, shards(): arrived = lax.all_to_all(slots, 'band', 0, 0, tiled=True)  5.33 us
  transfers between devices with their start and end apart: 14, of which 10 were waited for; matrix products, arithmetic and copies ran while one was open for 5% of the time, Pallas kernels for 0%

profile of v13, /device:TPU:0, one launch (start us, length us, event | category | flops | bytes accessed | tf_op | source)
XLA Modules:
  0.0 151.5 jit_solution(4132234066705134273)
XLA Ops:
  1.3 3.1 %collective-permute-start.3 = (s32[4,1]{0,1:T(1,128)S(1)}, s32[4,1]{0,1:T(1,128)S(1)}, u32[]{:S(2)}, u32[]{:S(2)}) collective-permute-start(s32[4,1]{0,1:T(1,128)S(1)} %compare_select_fusion.1), channel_id=1, source_target_pairs={{0,8},{8,0},{16,24},{24,16},{1,9},{9,1},{17,25},{25,17},{2,10},{10... | collective-permute-start | bytes 56 | tf_op jit(solution)/shard_map/ppermute | solution.py:45
  4.4 1.3 slice_bitcast_fusion.1
  5.7 0.2 collective-permute-done.3
  5.9 3.0 %collective-permute-start.4 = (s32[4,1]{0,1:T(1,128)S(1)}, s32[4,1]{0,1:T(1,128)S(1)}, u32[]{:S(2)}, u32[]{:S(2)}) collective-permute-start(s32[4,1]{0,1:T(1,128)S(1)} %fusion.368), channel_id=1, source_target_pairs={{0,16},{8,24},{16,0},{24,8},{1,17},{9,25},{17,1},{25,9},{2,18},{10... | collective-permute-start | bytes 56 | tf_op jit(solution)/shard_map/ppermute | solution.py:45
  8.9 1.5 %collective-permute-done.4 = s32[4,1]{0,1:T(1,128)S(1)} collective-permute-done((s32[4,1]{0,1:T(1,128)S(1)}, s32[4,1]{0,1:T(1,128)S(1)}, u32[]{:S(2)}, u32[]{:S(2)}) %collective-permute-start.4) | collective-permute-done | bytes 48 | tf_op jit(solution)/shard_map/ppermute | solution.py:45
  10.5 1.7 %select_select_fusion = f32[4,1,48,24,96]{4,3,2,1,0:T(8,128)} fusion(f32[48,24,96]{2,1,0:T(8,128)S(1)} %get-tuple-element.11, f32[48,24,96]{2,1,0:T(8,128)S(1)} %get-tuple-element.10, pred[4]{0:T(512)(128)(4,1)S(1)} %get-tuple-element.21, pred[4]{0:T(512)(128)(4,1)S(1)} %get-tuple-element.20), kind=kLoop, calls=%fused_computation.11 | loop fusion | flops 884736 | bytes 2654216 | tf_op jit(solution)/shard_map/jit(_where)/select_n | solution.py:145
  12.1 5.3 %all-to-all-start = ((f32[4,1,48,24,96]{4,3,2,1,0:T(8,128)}), f32[4,1,48,24,96]{4,3,2,1,0:T(8,128)S(1)}, u32[]{:S(2)}, u32[]{:S(2)}) async-start(f32[4,1,48,24,96]{4,3,2,1,0:T(8,128)} %select_select_fusion), calls=%async_computation | async-start | bytes 4718592 | tf_op jit(solution)/shard_map/all_to_all | solution.py:146
  17.5 1.6 %collective-permute-start = (f32[1,8,24,96]{3,2,1,0:T(8,128)S(1)}, f32[1,8,24,96]{3,2,1,0:T(8,128)S(1)}, u32[]{:S(2)}, u32[]{:S(2)}) collective-permute-start(f32[1,8,24,96]{3,2,1,0:T(8,128)S(1)} %slice_select_fusion.1), channel_id=1, source_target_pairs={{0,4},{4,0},{1,5},{5,1},{2,6},{6,2},{3,7},{7,3},{8,12},{12,8},{9,1... | collective-permute-start | bytes 221192 | tf_op jit(solution)/shard_map/ppermute | solution.py:25
  19.0 0.5 fusion.129
  19.6 0.5 multiply_add_fusion.1
  20.1 2.0 %collective-permute-done = f32[1,8,24,96]{3,2,1,0:T(8,128)S(1)} collective-permute-done((f32[1,8,24,96]{3,2,1,0:T(8,128)S(1)}, f32[1,8,24,96]{3,2,1,0:T(8,128)S(1)}, u32[]{:S(2)}, u32[]{:S(2)}) %collective-permute-start) | collective-permute-done | bytes 73760 | tf_op jit(solution)/shard_map/ppermute | solution.py:25
  22.2 0.8 pad_maximum_fusion.5
  23.0 2.0 %collective-permute-start.1 = (f32[1,64,8,96]{3,2,1,0:T(8,128)}, f32[1,64,8,96]{3,2,1,0:T(8,128)}, u32[]{:S(2)}, u32[]{:S(2)}) collective-permute-start(f32[1,64,8,96]{3,2,1,0:T(8,128)} %get-tuple-element.12), channel_id=1, source_target_pairs={{0,1},{1,2},{2,3},{4,5},{5,6},{6,7},{8,9},{9,10},{10,11},{12,13},{... | collective-permute-start | bytes 589832 | tf_op jit(solution)/shard_map/ppermute | solution.py:30
  25.1 1.3 collective-permute-start.2
  26.3 42.6 %all-to-all-done = f32[4,1,48,24,96]{4,3,2,1,0:T(8,128)S(1)} async-done(((f32[4,1,48,24,96]{4,3,2,1,0:T(8,128)}), f32[4,1,48,24,96]{4,3,2,1,0:T(8,128)S(1)}, u32[]{:S(2)}, u32[]{:S(2)}) %all-to-all-start) | async-done | bytes 1769504 | tf_op jit(solution)/shard_map/all_to_all | solution.py:146
  69.0 0.2 reduce_sum.26
  69.2 1.6 %collective-permute-start.5 = (f32[1,8,24,96]{3,2,1,0:T(8,128)S(1)}, f32[1,8,24,96]{3,2,1,0:T(8,128)S(1)}, u32[]{:S(2)}, u32[]{:S(2)}) collective-permute-start(f32[1,8,24,96]{3,2,1,0:T(8,128)S(1)} %slice_select_fusion), channel_id=1, source_target_pairs={{0,4},{4,0},{1,5},{5,1},{2,6},{6,2},{3,7},{7,3},{8,12},{12,8},{9,1... | collective-permute-start | bytes 221192 | tf_op jit(solution)/shard_map/ppermute | solution.py:25
  70.8 2.4 %fusion.7 = f32[64,40,96]{2,1,0:T(8,128)S(1)} fusion(f32[1,64,8,96]{3,2,1,0:T(8,128)} %collective-permute-done.2, f32[1,8,24,96]{3,2,1,0:T(8,128)} %copy-done.2, f32[1,48,24,96]{3,2,1,0:T(8,128)S(1)} %copy-done, f32[1,8,24,96]{3,2,1,0:T(8,128)} %copy-done.1, f32[1,64,8,96]{3,2,1,0:T(8,128)} %collective-permute-done.1), kind=kOutput, calls=%fused_computation.14 | convolution fusion | flops 284540928 | bytes 1966080 | tf_op jit(solution)/shard_map/dot_general | solution.py:65
  73.1 0.7 collective-permute-done.5
  74.0 1.3 collective-permute-start.6
  75.3 1.3 collective-permute-start.7
  76.6 0.8 convolution_bitcast_fusion.3
  77.4 3.0 %collective-permute-done.7 = f32[1,64,8,96]{3,2,1,0:T(8,128)S(1)} collective-permute-done((f32[1,64,8,96]{3,2,1,0:T(8,128)S(1)}, f32[1,64,8,96]{3,2,1,0:T(8,128)S(1)}, u32[]{:S(2)}, u32[]{:S(2)}) %collective-permute-start.7) | collective-permute-done | bytes 196640 | tf_op jit(solution)/shard_map/ppermute | solution.py:31
  80.4 1.2 fusion.16
  81.7 0.8 convolution_bitcast_fusion.2
  82.5 0.8 fusion.28
  83.3 0.8 convolution_multiply_fusion.1
  84.1 1.9 %convolution_bitcast_fusion = f32[8,24,1,1152]{3,1,2,0:T(8,128)} fusion(f32[1152,96,1]{1,0,2:T(8,128)S(1)} %bitcast.132, s32[8,24]{1,0:T(8,128)S(1)} %add_select_fusion.3, pred[8,24]{1,0:T(8,128)(4,1)S(1)} %copy-done.4), kind=kOutput, calls=%fused_computation.3 | convolution fusion | flops 127586304 | bytes 1328064 | tf_op jit(solution)/shard_map/dot_general | solution.py:89
  86.0 7.1 %all-to-all-start.1 = ((f32[8,24,1,1152]{3,1,2,0:T(8,128)}), f32[8,24,1,1152]{3,1,2,0:T(8,128)}, u32[]{:S(2)}, u32[]{:S(2)}) async-start(f32[8,24,1,1152]{3,1,2,0:T(8,128)} %convolution_bitcast_fusion), calls=%async_computation.1 | async-start | bytes 1769472 | tf_op jit(solution)/shard_map/all_to_all | solution.py:105
  93.4 12.5 %all-to-all-done.1 = f32[8,24,1,1152]{3,1,2,0:T(8,128)} async-done(((f32[8,24,1,1152]{3,1,2,0:T(8,128)}), f32[8,24,1,1152]{3,1,2,0:T(8,128)}, u32[]{:S(2)}, u32[]{:S(2)}) %all-to-all-start.1) | async-done | bytes 884768 | tf_op jit(solution)/shard_map/all_to_all | solution.py:105
  106.0 2.1 %reshape.380 = f32[2,4,24,1,24,48]{5,4,2,1,0,3:T(8,128)S(1)} reshape(f32[8,24,1,1152]{3,1,2,0:T(8,128)} %all-to-all-done.1) | data formatting | bytes 1769472 | tf_op jit(solution)/shard_map/reshape | solution.py:106
  108.1 3.3 %copy.47 = f32[2,4,24,1,24,48]{5,0,4,1,2,3:T(2,128)} copy(f32[2,4,24,1,24,48]{5,4,2,1,0,3:T(8,128)S(1)} %reshape.380) | data formatting | bytes 1769472 | tf_op jit(solution)/shard_map/reshape | solution.py:106
  111.3 2.7 %reshape.381 = f32[24,96,96]{2,1,0:T(8,128)S(1)} reshape(f32[24,1,4,24,2,48]{5,4,3,2,0,1:T(2,128)} %bitcast.124) | data formatting | bytes 1769472 | tf_op jit(solution)/shard_map/reshape.30
  114.1 1.9 %fusion.42 = f32[24,96,192]{1,2,0:T(8,128)S(1)} fusion(f32[24,96,96]{2,1,0:T(8,128)S(1)} %reshape.381, s32[192]{0:T(256)S(1)} %add_select_fusion.4, pred[192]{0:T(512)(128)(4,1)S(1)} %iota_compare_fusion), kind=kOutput, calls=%fused_computation.66 | convolution fusion | flops 254988288 | bytes 2655168 | tf_op jit(solution)/shard_map/dot_general | solution.py:89
  115.9 3.8 %multiply_reduce_fusion = (f32[]{:T(128)}, f32[24,192,192]{2,1,0:T(8,128)S(1)}) fusion(f32[192]{0:T(256)S(1)} %get-tuple-element.27, f32[24,192]{1,0:T(8,128)S(1)} %broadcast_add_fusion, f32[192]{0:T(256)S(1)} %get-tuple-element.26, f32[24,192]{1,0:T(8,128)S(1)} %broadcast_multiply_fusion, f32[24,96,192]{1,2,0:T(8,128)S(1)} %fusion.42, ...), kind=kOutput, calls=%fused_computation | convolution fusion | flops 516870144 | bytes 5347780 | tf_op jit(solution)/shard_map/dot_general | solution.py:89
  119.7 3.8 %fusion = f32[24,192,96]{1,2,0:T(8,128)S(1)} fusion(f32[24,192,192]{2,1,0:T(8,128)S(1)} %get-tuple-element.23, f32[192]{0:T(256)S(1)} %get-tuple-element.27, f32[24,192]{1,0:T(8,128)S(1)} %broadcast_add_fusion, f32[192]{0:T(256)S(1)} %get-tuple-element.26, f32[24,192]{1,0:T(8,128)S(1)} %broadcast_multiply_fusion, s32[192]{0:T(256)S(1)} %add_select_fusion.4, ...), kind=kOutput, calls=%fused_computation.2 | convolution fusion | flops 515100672 | bytes 5347776 | tf_op jit(solution)/shard_map/dot_general | solution.py:89
  123.5 1.6 %convolution_bitcast_fusion.1 = f32[2,4,24,1,24,48]{5,4,0,1,2,3:T(8,128)S(1)} fusion(f32[24,4,24,192,1]{3,2,4,1,0:T(8,128)S(1)} %bitcast.131, s32[192]{0:T(256)S(1)} %add_select_fusion.4, s32[2,48]{1,0:T(2,128)S(1)} %copy-done.3, pred[192]{0:T(512)(128)(4,1)S(1)} %iota_compare_fusion), kind=kOutput, calls=%fused_computation.12 | convolution fusion | flops 254988288 | bytes 2655552 | tf_op jit(solution)/shard_map/dot_general | solution.py:89
  125.3 1.6 %reshape.383 = f32[8,24,1,1152]{3,1,0,2:T(8,128)} reshape(f32[2,4,24,1,24,48]{5,4,2,1,0,3:T(8,128)S(1)} %copy.33) | data formatting | bytes 1769472 | tf_op jit(solution)/shard_map/reshape | solution.py:126
  126.9 3.5 %all-to-all-start.2 = ((f32[8,24,1,1152]{3,1,2,0:T(8,128)}), f32[8,24,1,1152]{3,1,2,0:T(8,128)S(1)}, u32[]{:S(2)}, u32[]{:S(2)}) async-start(f32[8,24,1,1152]{3,1,2,0:T(8,128)} %bitcast.126), calls=%async_computation.2 | async-start | bytes 1769472 | tf_op jit(solution)/shard_map/all_to_all | solution.py:128
  131.1 0.5 collective-permute-start.8
  131.6 1.0 collective-permute-done.8
  133.8 7.2 %collective-permute-start.9 = (f32[1]{0:T(128)}, f32[1]{0:T(128)}, u32[]{:S(2)}, u32[]{:S(2)}) collective-permute-start(f32[1]{0:T(128)} %add.504), channel_id=1, source_target_pairs={{0,2},{1,3},{2,0},{3,1},{4,6},{5,7},{6,4},{7,5},{8,10},{9,11},{10,... | collective-permute-start | bytes 20 | tf_op jit(solution)/shard_map/ppermute | solution.py:45
  141.1 2.0 %collective-permute-done.9 = f32[1]{0:T(128)} collective-permute-done((f32[1]{0:T(128)}, f32[1]{0:T(128)}, u32[]{:S(2)}, u32[]{:S(2)}) %collective-permute-start.9) | collective-permute-done | bytes 36 | tf_op jit(solution)/shard_map/ppermute | solution.py:45
  143.7 2.9 %collective-permute-start.10 = (f32[1]{0:T(128)}, f32[1]{0:T(128)}, u32[]{:S(2)}, u32[]{:S(2)}) collective-permute-start(f32[1]{0:T(128)} %add.505), channel_id=1, source_target_pairs={{0,4},{4,0},{1,5},{5,1},{2,6},{6,2},{3,7},{7,3},{8,12},{12,8},{9,1... | collective-permute-start | bytes 20 | tf_op jit(solution)/shard_map/ppermute | solution.py:45
  146.6 0.7 collective-permute-done.10
  148.0 0.4 copy.35
  148.3 1.0 fusion.27
  149.4 1.0 copy.36
  (32 shorter events, 0.6 us)
Async XLA Ops:
  1.3 4.6 %collective-permute-start.3 = (s32[4,1]{0,1:T(1,128)S(1)}, s32[4,1]{0,1:T(1,128)S(1)}, u32[]{:S(2)}, u32[]{:S(2)}) collective-permute-start(s32[4,1]{0,1:T(1,128)S(1)} %compare_select_fusion.1), channel_id=1, source_target_pairs={{0,8},{8,0},{16,24},{24,16},{1,9},{9,1},{17,25},{25,17},{2,10},{10... | collective-permute-start | bytes 56 | tf_op jit(solution)/shard_map/ppermute | solution.py:45
  5.9 4.6 %collective-permute-start.4 = (s32[4,1]{0,1:T(1,128)S(1)}, s32[4,1]{0,1:T(1,128)S(1)}, u32[]{:S(2)}, u32[]{:S(2)}) collective-permute-start(s32[4,1]{0,1:T(1,128)S(1)} %fusion.368), channel_id=1, source_target_pairs={{0,16},{8,24},{16,0},{24,8},{1,17},{9,25},{17,1},{25,9},{2,18},{10... | collective-permute-start | bytes 56 | tf_op jit(solution)/shard_map/ppermute | solution.py:45
  12.1 5.3 %copy-start = (f32[1,48,24,96]{3,2,1,0:T(8,128)S(1)}, f32[1,48,24,96]{3,2,1,0:T(8,128)}, u32[]{:S(2)}) copy-start(f32[1,48,24,96]{3,2,1,0:T(8,128)} %param.4) | copy-start | bytes 1327108
  12.1 56.9 %all-to-all-start = ((f32[4,1,48,24,96]{4,3,2,1,0:T(8,128)}), f32[4,1,48,24,96]{4,3,2,1,0:T(8,128)S(1)}, u32[]{:S(2)}, u32[]{:S(2)}) async-start(f32[4,1,48,24,96]{4,3,2,1,0:T(8,128)} %select_select_fusion), calls=%async_computation | async-start | bytes 4718592 | tf_op jit(solution)/shard_map/all_to_all | solution.py:146
  17.5 4.7 %collective-permute-start = (f32[1,8,24,96]{3,2,1,0:T(8,128)S(1)}, f32[1,8,24,96]{3,2,1,0:T(8,128)S(1)}, u32[]{:S(2)}, u32[]{:S(2)}) collective-permute-start(f32[1,8,24,96]{3,2,1,0:T(8,128)S(1)} %slice_select_fusion.1), channel_id=1, source_target_pairs={{0,4},{4,0},{1,5},{5,1},{2,6},{6,2},{3,7},{7,3},{8,12},{12,8},{9,1... | collective-permute-start | bytes 221192 | tf_op jit(solution)/shard_map/ppermute | solution.py:25
  22.2 2.9 %copy-start.1 = (f32[1,8,24,96]{3,2,1,0:T(8,128)}, f32[1,8,24,96]{3,2,1,0:T(8,128)S(1)}, u32[]{:S(2)}) copy-start(f32[1,8,24,96]{3,2,1,0:T(8,128)S(1)} %get-tuple-element.16) | copy-start | bytes 221188
  22.2 2.9 %copy-start.2 = (f32[1,8,24,96]{3,2,1,0:T(8,128)}, f32[1,8,24,96]{3,2,1,0:T(8,128)S(1)}, u32[]{:S(2)}) copy-start(f32[1,8,24,96]{3,2,1,0:T(8,128)S(1)} %get-tuple-element.17) | copy-start | bytes 221188
  23.0 47.7 %collective-permute-start.1 = (f32[1,64,8,96]{3,2,1,0:T(8,128)}, f32[1,64,8,96]{3,2,1,0:T(8,128)}, u32[]{:S(2)}, u32[]{:S(2)}) collective-permute-start(f32[1,64,8,96]{3,2,1,0:T(8,128)} %get-tuple-element.12), channel_id=1, source_target_pairs={{0,1},{1,2},{2,3},{4,5},{5,6},{6,7},{8,9},{9,10},{10,11},{12,13},{... | collective-permute-start | bytes 589832 | tf_op jit(solution)/shard_map/ppermute | solution.py:30
  25.1 45.7 %collective-permute-start.2 = (f32[1,64,8,96]{3,2,1,0:T(8,128)}, f32[1,64,8,96]{3,2,1,0:T(8,128)}, u32[]{:S(2)}, u32[]{:S(2)}) collective-permute-start(f32[1,64,8,96]{3,2,1,0:T(8,128)} %get-tuple-element.13), channel_id=1, source_target_pairs={{1,0},{2,1},{3,2},{5,4},{6,5},{7,6},{9,8},{10,9},{11,10},{13,12},{... | collective-permute-start | bytes 589832 | tf_op jit(solution)/shard_map/ppermute | solution.py:31
  69.2 4.7 %collective-permute-start.5 = (f32[1,8,24,96]{3,2,1,0:T(8,128)S(1)}, f32[1,8,24,96]{3,2,1,0:T(8,128)S(1)}, u32[]{:S(2)}, u32[]{:S(2)}) collective-permute-start(f32[1,8,24,96]{3,2,1,0:T(8,128)S(1)} %slice_select_fusion), channel_id=1, source_target_pairs={{0,4},{4,0},{1,5},{5,1},{2,6},{6,2},{3,7},{7,3},{8,12},{12,8},{9,1... | collective-permute-start | bytes 221192 | tf_op jit(solution)/shard_map/ppermute | solution.py:25
  74.0 3.4 %collective-permute-start.6 = (f32[1,64,8,96]{3,2,1,0:T(8,128)S(1)}, f32[1,64,8,96]{3,2,1,0:T(8,128)S(1)}, u32[]{:S(2)}, u32[]{:S(2)}) collective-permute-start(f32[1,64,8,96]{3,2,1,0:T(8,128)S(1)} %get-tuple-element.14), channel_id=1, source_target_pairs={{0,1},{1,2},{2,3},{4,5},{5,6},{6,7},{8,9},{9,10},{10,11},{12,13},{... | collective-permute-start | bytes 589832 | tf_op jit(solution)/shard_map/ppermute | solution.py:30
  75.3 5.2 %collective-permute-start.7 = (f32[1,64,8,96]{3,2,1,0:T(8,128)S(1)}, f32[1,64,8,96]{3,2,1,0:T(8,128)S(1)}, u32[]{:S(2)}, u32[]{:S(2)}) collective-permute-start(f32[1,64,8,96]{3,2,1,0:T(8,128)S(1)} %get-tuple-element.15), channel_id=1, source_target_pairs={{1,0},{2,1},{3,2},{5,4},{6,5},{7,6},{9,8},{10,9},{11,10},{13,12},{... | collective-permute-start | bytes 589832 | tf_op jit(solution)/shard_map/ppermute | solution.py:31
  81.7 2.4 %copy-start.4 = (pred[8,24]{1,0:T(8,128)(4,1)S(1)}, pred[8,24]{1,0:T(8,128)(4,1)}, u32[]{:S(2)}) copy-start(pred[8,24]{1,0:T(8,128)(4,1)} %fusion.129) | copy-start | bytes 580
  86.0 19.9 %all-to-all-start.1 = ((f32[8,24,1,1152]{3,1,2,0:T(8,128)}), f32[8,24,1,1152]{3,1,2,0:T(8,128)}, u32[]{:S(2)}, u32[]{:S(2)}) async-start(f32[8,24,1,1152]{3,1,2,0:T(8,128)} %convolution_bitcast_fusion), calls=%async_computation.1 | async-start | bytes 1769472 | tf_op jit(solution)/shard_map/all_to_all | solution.py:105
  119.7 3.8 %copy-start.3 = (s32[2,48]{1,0:T(2,128)S(1)}, s32[2,48]{1,0:T(2,128)}, u32[]{:S(2)}) copy-start(s32[2,48]{1,0:T(2,128)} %multiply_add_fusion.1) | copy-start | bytes 1156
  126.9 21.0 %all-to-all-start.2 = ((f32[8,24,1,1152]{3,1,2,0:T(8,128)}), f32[8,24,1,1152]{3,1,2,0:T(8,128)S(1)}, u32[]{:S(2)}, u32[]{:S(2)}) async-start(f32[8,24,1,1152]{3,1,2,0:T(8,128)} %bitcast.126), calls=%async_computation.2 | async-start | bytes 1769472 | tf_op jit(solution)/shard_map/all_to_all | solution.py:128
  131.1 1.4 collective-permute-start.8
  133.8 9.3 %collective-permute-start.9 = (f32[1]{0:T(128)}, f32[1]{0:T(128)}, u32[]{:S(2)}, u32[]{:S(2)}) collective-permute-start(f32[1]{0:T(128)} %add.504), channel_id=1, source_target_pairs={{0,2},{1,3},{2,0},{3,1},{4,6},{5,7},{6,4},{7,5},{8,10},{9,11},{10,... | collective-permute-start | bytes 20 | tf_op jit(solution)/shard_map/ppermute | solution.py:45
  143.7 3.6 %collective-permute-start.10 = (f32[1]{0:T(128)}, f32[1]{0:T(128)}, u32[]{:S(2)}, u32[]{:S(2)}) collective-permute-start(f32[1]{0:T(128)} %add.505), channel_id=1, source_target_pairs={{0,4},{4,0},{1,5},{5,1},{2,6},{6,2},{3,7},{7,3},{8,12},{12,8},{9,1... | collective-permute-start | bytes 20 | tf_op jit(solution)/shard_map/ppermute | solution.py:45

commit v14 on v13

--- a/solution.py
+++ b/solution.py
@@ -124,7 +124,22 @@
     back_z = contract(back_y, table, 2, 1)
     back = back_z.reshape(width, pair_count, count_z, rows_z, count_y, rows_y)
     back = back.transpose(4, 2, 0, 1, 3, 5).reshape(spread, width, pair_count, rows_y * rows_z)
-    energy_total = group_sum(energy_part, ("gz", "gy"))
+    rounds = [
+        (axis, 1 << bit)
+        for axis in ("gz", "gy")
+        for bit in range(lax.axis_size(axis).bit_length() - 1)
+    ]
+    if rounds and all(lax.axis_size(axis) & (lax.axis_size(axis) - 1) == 0 for axis in ("gz", "gy")):
+        energy_total = energy_part
+        for number, (axis, step) in enumerate(rounds):
+            count = lax.axis_size(axis)
+            energy_total = energy_total + lax.ppermute(
+                energy_total, axis, [(i, i ^ step) for i in range(count)]
+            )
+            if number == 0:
+                back, energy_total = lax.optimization_barrier((back, energy_total))
+    else:
+        energy_total = group_sum(energy_part, ("gz", "gy"))
     got = lax.all_to_all(back, ("gy", "gz"), 0, 0, tiled=True)
     got = got.reshape(period, pair_count, rows_y * rows_z)
     result = contract(got, table, 0, 1)

time: 152 us -> 154 us (1.013)
  starting transfers between devices: 41.7 us -> 44.3 us
    ppermute x0 -> x3, starting transfers between devices: none -> 13.2 us  [potentials(): lax.ppermute(energy_total, axis, [(i, i ^ step) for i in range(count)])]
    ppermute x5 -> x2, starting transfers between devices: 16.7 us -> 6.12 us  [group_sum(): lax.ppermute(total, axis, [(i, i ^ step) for i in range(count)])]
    ppermute x5 -> x2, waiting for transfers between devices: 5.4 us -> 1.71 us  [group_sum(): lax.ppermute(total, axis, [(i, i ^ step) for i in range(count)])]
    ppermute x0 -> x3, waiting for transfers between devices: none -> 2.74 us  [potentials(): lax.ppermute(energy_total, axis, [(i, i ^ step) for i in range(count)])]
  transfers between devices with their start and end apart: 14 -> 14, of which waited for: 10 -> 9; matrix products, arithmetic and copies ran while one was open for 5% -> 9% of each run, Pallas kernels for 0% -> 0%
where the time goes in v14:
time: 154 us; the launch traced here: 153 us
  waiting for transfers between devices  65.5 us (43%)
  starting transfers between devices  44.3 us (29%)
  matrix products  20.8 us (14%)
  local copies, waits for them, and re-layouts  12.6 us (8%)
  between operations  5.87 us (4%)
  other arithmetic  4.14 us (3%)
    all_to_all x1, waiting for transfers between devices, shards(): arrived = lax.all_to_all(slots, 'band', 0, 0, tiled=True)  42.6 us
    dot_general x6, matrix products, contract(): lax.dot_general(left, right, (((left_dim,), (right_dim,)), ((), ())), pre...  14 us
    ppermute x3, starting transfers between devices, potentials(): lax.ppermute(energy_total, axis, [(i, i ^ step) for i in range(count)])  13.2 us
    all_to_all x1, waiting for transfers between devices, potentials(): got = lax.all_to_all(send, ('gy', 'gz'), 0, 0, tiled=True)  12.5 us
    all_to_all x1, starting transfers between devices, potentials(): got = lax.all_to_all(send, ('gy', 'gz'), 0, 0, tiled=True)  7.13 us
    ppermute x2, starting transfers between devices, group_sum(): lax.ppermute(total, axis, [(i, i ^ step) for i in range(count)])  6.12 us
    reshape x2, local copies, waits for them, and re-layouts, potentials(): got = got.reshape(count_y, count_z, width, pair_count, rows_z, rows_y)  5.35 us
    all_to_all x1, starting transfers between devices, shards(): arrived = lax.all_to_all(slots, 'band', 0, 0, tiled=True)  5.33 us
  transfers between devices with their start and end apart: 14, of which 9 were waited for; matrix products, arithmetic and copies ran while one was open for 9% of the time, Pallas kernels for 0%

profile of v14, /device:TPU:0, one launch (start us, length us, event | category | flops | bytes accessed | tf_op | source)
XLA Modules:
  0.0 153.2 jit_solution(12577172647318603134)
XLA Ops:
  1.3 3.1 %collective-permute-start.3 = (s32[4,1]{0,1:T(1,128)S(1)}, s32[4,1]{0,1:T(1,128)S(1)}, u32[]{:S(2)}, u32[]{:S(2)}) collective-permute-start(s32[4,1]{0,1:T(1,128)S(1)} %compare_select_fusion.1), channel_id=1, source_target_pairs={{0,8},{8,0},{16,24},{24,16},{1,9},{9,1},{17,25},{25,17},{2,10},{10... | collective-permute-start | bytes 56 | tf_op jit(solution)/shard_map/ppermute | solution.py:45
  4.4 1.3 slice_bitcast_fusion.1
  5.7 0.2 collective-permute-done.3
  5.9 3.0 %collective-permute-start.4 = (s32[4,1]{0,1:T(1,128)S(1)}, s32[4,1]{0,1:T(1,128)S(1)}, u32[]{:S(2)}, u32[]{:S(2)}) collective-permute-start(s32[4,1]{0,1:T(1,128)S(1)} %fusion.368), channel_id=1, source_target_pairs={{0,16},{8,24},{16,0},{24,8},{1,17},{9,25},{17,1},{25,9},{2,18},{10... | collective-permute-start | bytes 56 | tf_op jit(solution)/shard_map/ppermute | solution.py:45
  8.9 1.5 collective-permute-done.4
  10.5 1.7 %select_select_fusion = f32[4,1,48,24,96]{4,3,2,1,0:T(8,128)} fusion(f32[48,24,96]{2,1,0:T(8,128)S(1)} %get-tuple-element.15, f32[48,24,96]{2,1,0:T(8,128)S(1)} %get-tuple-element.14, pred[4]{0:T(512)(128)(4,1)S(1)} %get-tuple-element.25, pred[4]{0:T(512)(128)(4,1)S(1)} %get-tuple-element.24), kind=kLoop, calls=%fused_computation.11 | loop fusion | flops 884736 | bytes 2654216 | tf_op jit(solution)/shard_map/jit(_where)/select_n | solution.py:160
  12.1 5.3 %all-to-all-start = ((f32[4,1,48,24,96]{4,3,2,1,0:T(8,128)}), f32[4,1,48,24,96]{4,3,2,1,0:T(8,128)S(1)}, u32[]{:S(2)}, u32[]{:S(2)}) async-start(f32[4,1,48,24,96]{4,3,2,1,0:T(8,128)} %select_select_fusion), calls=%async_computation | async-start | bytes 4718592 | tf_op jit(solution)/shard_map/all_to_all | solution.py:161
  17.5 1.6 %collective-permute-start = (f32[1,8,24,96]{3,2,1,0:T(8,128)S(1)}, f32[1,8,24,96]{3,2,1,0:T(8,128)S(1)}, u32[]{:S(2)}, u32[]{:S(2)}) collective-permute-start(f32[1,8,24,96]{3,2,1,0:T(8,128)S(1)} %slice_select_fusion.1), channel_id=1, source_target_pairs={{0,4},{4,0},{1,5},{5,1},{2,6},{6,2},{3,7},{7,3},{8,12},{12,8},{9,1... | collective-permute-start | bytes 221192 | tf_op jit(solution)/shard_map/ppermute | solution.py:25
  19.0 0.5 fusion.129
  19.6 0.5 multiply_add_fusion.1
  20.1 2.0 %collective-permute-done = f32[1,8,24,96]{3,2,1,0:T(8,128)S(1)} collective-permute-done((f32[1,8,24,96]{3,2,1,0:T(8,128)S(1)}, f32[1,8,24,96]{3,2,1,0:T(8,128)S(1)}, u32[]{:S(2)}, u32[]{:S(2)}) %collective-permute-start) | collective-permute-done | bytes 73760 | tf_op jit(solution)/shard_map/ppermute | solution.py:25
  22.2 0.8 pad_maximum_fusion.5
  23.0 2.0 %collective-permute-start.1 = (f32[1,64,8,96]{3,2,1,0:T(8,128)}, f32[1,64,8,96]{3,2,1,0:T(8,128)}, u32[]{:S(2)}, u32[]{:S(2)}) collective-permute-start(f32[1,64,8,96]{3,2,1,0:T(8,128)} %get-tuple-element.16), channel_id=1, source_target_pairs={{0,1},{1,2},{2,3},{4,5},{5,6},{6,7},{8,9},{9,10},{10,11},{12,13},{... | collective-permute-start | bytes 589832 | tf_op jit(solution)/shard_map/ppermute | solution.py:30
  25.1 1.3 collective-permute-start.2
  26.3 42.6 %all-to-all-done = f32[4,1,48,24,96]{4,3,2,1,0:T(8,128)S(1)} async-done(((f32[4,1,48,24,96]{4,3,2,1,0:T(8,128)}), f32[4,1,48,24,96]{4,3,2,1,0:T(8,128)S(1)}, u32[]{:S(2)}, u32[]{:S(2)}) %all-to-all-start) | async-done | bytes 1769504 | tf_op jit(solution)/shard_map/all_to_all | solution.py:161
  69.0 0.2 reduce_sum.26
  69.2 1.6 %collective-permute-start.5 = (f32[1,8,24,96]{3,2,1,0:T(8,128)S(1)}, f32[1,8,24,96]{3,2,1,0:T(8,128)S(1)}, u32[]{:S(2)}, u32[]{:S(2)}) collective-permute-start(f32[1,8,24,96]{3,2,1,0:T(8,128)S(1)} %slice_select_fusion), channel_id=1, source_target_pairs={{0,4},{4,0},{1,5},{5,1},{2,6},{6,2},{3,7},{7,3},{8,12},{12,8},{9,1... | collective-permute-start | bytes 221192 | tf_op jit(solution)/shard_map/ppermute | solution.py:25
  70.8 2.4 %fusion.7 = f32[64,40,96]{2,1,0:T(8,128)S(1)} fusion(f32[1,64,8,96]{3,2,1,0:T(8,128)} %collective-permute-done.2, f32[1,8,24,96]{3,2,1,0:T(8,128)} %copy-done.2, f32[1,48,24,96]{3,2,1,0:T(8,128)S(1)} %copy-done, f32[1,8,24,96]{3,2,1,0:T(8,128)} %copy-done.1, f32[1,64,8,96]{3,2,1,0:T(8,128)} %collective-permute-done.1), kind=kOutput, calls=%fused_computation.14 | convolution fusion | flops 284540928 | bytes 1966080 | tf_op jit(solution)/shard_map/dot_general | solution.py:65
  73.1 0.7 collective-permute-done.5
  74.0 1.3 collective-permute-start.6
  75.3 1.3 collective-permute-start.7
  76.6 0.8 convolution_bitcast_fusion.3
  77.4 3.0 %collective-permute-done.7 = f32[1,64,8,96]{3,2,1,0:T(8,128)S(1)} collective-permute-done((f32[1,64,8,96]{3,2,1,0:T(8,128)S(1)}, f32[1,64,8,96]{3,2,1,0:T(8,128)S(1)}, u32[]{:S(2)}, u32[]{:S(2)}) %collective-permute-start.7) | collective-permute-done | bytes 196640 | tf_op jit(solution)/shard_map/ppermute | solution.py:31
  80.4 1.2 fusion.16
  81.7 0.8 convolution_bitcast_fusion.2
  82.5 0.8 fusion.28
  83.3 0.8 convolution_multiply_fusion.1
  84.1 1.9 %convolution_bitcast_fusion = f32[8,24,1,1152]{3,1,2,0:T(8,128)} fusion(f32[1152,96,1]{1,0,2:T(8,128)S(1)} %bitcast.132, s32[8,24]{1,0:T(8,128)S(1)} %add_select_fusion.3, pred[8,24]{1,0:T(8,128)(4,1)S(1)} %copy-done.4), kind=kOutput, calls=%fused_computation.3 | convolution fusion | flops 127586304 | bytes 1328064 | tf_op jit(solution)/shard_map/dot_general | solution.py:89
  86.0 7.1 %all-to-all-start.1 = ((f32[8,24,1,1152]{3,1,2,0:T(8,128)}), f32[8,24,1,1152]{3,1,2,0:T(8,128)}, u32[]{:S(2)}, u32[]{:S(2)}) async-start(f32[8,24,1,1152]{3,1,2,0:T(8,128)} %convolution_bitcast_fusion), calls=%async_computation.1 | async-start | bytes 1769472 | tf_op jit(solution)/shard_map/all_to_all | solution.py:105
  93.4 12.5 %all-to-all-done.1 = f32[8,24,1,1152]{3,1,2,0:T(8,128)} async-done(((f32[8,24,1,1152]{3,1,2,0:T(8,128)}), f32[8,24,1,1152]{3,1,2,0:T(8,128)}, u32[]{:S(2)}, u32[]{:S(2)}) %all-to-all-start.1) | async-done | bytes 884768 | tf_op jit(solution)/shard_map/all_to_all | solution.py:105
  106.0 2.1 %reshape.380 = f32[2,4,24,1,24,48]{5,4,2,1,0,3:T(8,128)S(1)} reshape(f32[8,24,1,1152]{3,1,2,0:T(8,128)} %all-to-all-done.1) | data formatting | bytes 1769472 | tf_op jit(solution)/shard_map/reshape | solution.py:106
  108.1 3.3 %copy.47 = f32[2,4,24,1,24,48]{5,0,4,1,2,3:T(2,128)} copy(f32[2,4,24,1,24,48]{5,4,2,1,0,3:T(8,128)S(1)} %reshape.380) | data formatting | bytes 1769472 | tf_op jit(solution)/shard_map/reshape | solution.py:106
  111.3 2.7 %reshape.381 = f32[24,96,96]{2,1,0:T(8,128)S(1)} reshape(f32[24,1,4,24,2,48]{5,4,3,2,0,1:T(2,128)} %bitcast.124) | data formatting | bytes 1769472 | tf_op jit(solution)/shard_map/reshape.30
  114.1 1.9 %fusion.42 = f32[24,96,192]{1,2,0:T(8,128)S(1)} fusion(f32[24,96,96]{2,1,0:T(8,128)S(1)} %reshape.381, s32[192]{0:T(256)S(1)} %add_select_fusion.4, pred[192]{0:T(512)(128)(4,1)S(1)} %iota_compare_fusion), kind=kOutput, calls=%fused_computation.66 | convolution fusion | flops 254988288 | bytes 2655168 | tf_op jit(solution)/shard_map/dot_general | solution.py:89
  115.9 3.8 %multiply_reduce_fusion = (f32[]{:T(128)}, f32[24,192,192]{2,1,0:T(8,128)S(1)}) fusion(f32[192]{0:T(256)S(1)} %get-tuple-element.31, f32[24,192]{1,0:T(8,128)S(1)} %broadcast_add_fusion, f32[192]{0:T(256)S(1)} %get-tuple-element.30, f32[24,192]{1,0:T(8,128)S(1)} %broadcast_multiply_fusion, f32[24,96,192]{1,2,0:T(8,128)S(1)} %fusion.42, ...), kind=kOutput, calls=%fused_computation | convolution fusion | flops 516870144 | bytes 5347780 | tf_op jit(solution)/shard_map/dot_general | solution.py:89
  119.7 0.4 collective-permute-start.8
  120.1 3.8 %fusion = f32[24,192,96]{1,2,0:T(8,128)S(1)} fusion(f32[24,192,192]{2,1,0:T(8,128)S(1)} %get-tuple-element.27, f32[192]{0:T(256)S(1)} %get-tuple-element.31, f32[24,192]{1,0:T(8,128)S(1)} %broadcast_add_fusion, f32[192]{0:T(256)S(1)} %get-tuple-element.30, f32[24,192]{1,0:T(8,128)S(1)} %broadcast_multiply_fusion, s32[192]{0:T(256)S(1)} %add_select_fusion.4, ...), kind=kOutput, calls=%fused_computation.2 | convolution fusion | flops 515100672 | bytes 5347776 | tf_op jit(solution)/shard_map/dot_general | solution.py:89
  123.9 1.6 %convolution_bitcast_fusion.1 = f32[2,4,24,1,24,48]{5,4,0,1,2,3:T(8,128)S(1)} fusion(f32[24,4,24,192,1]{3,2,4,1,0:T(8,128)S(1)} %bitcast.131, s32[192]{0:T(256)S(1)} %add_select_fusion.4, s32[2,48]{1,0:T(2,128)S(1)} %copy-done.3, pred[192]{0:T(512)(128)(4,1)S(1)} %iota_compare_fusion), kind=kOutput, calls=%fused_computation.12 | convolution fusion | flops 254988288 | bytes 2655552 | tf_op jit(solution)/shard_map/dot_general | solution.py:89
  125.5 0.2 copy.33
  125.6 1.6 %reshape.383 = f32[8,24,1,1152]{3,1,0,2:T(8,128)} reshape(f32[2,4,24,1,24,48]{5,4,2,1,0,3:T(8,128)S(1)} %copy.33) | data formatting | bytes 1769472 | tf_op jit(solution)/shard_map/reshape | solution.py:126
  128.6 3.6 %all-to-all-start.2 = ((f32[8,24,1,1152]{3,1,2,0:T(8,128)}), f32[8,24,1,1152]{3,1,2,0:T(8,128)S(1)}, u32[]{:S(2)}, u32[]{:S(2)}) async-start(f32[8,24,1,1152]{3,1,2,0:T(8,128)} %bitcast.126), calls=%async_computation.2 | async-start | bytes 1769472 | tf_op jit(solution)/shard_map/all_to_all | solution.py:143
  132.8 9.9 %collective-permute-start.9 = (f32[1]{0:T(128)}, f32[1]{0:T(128)}, u32[]{:S(2)}, u32[]{:S(2)}) collective-permute-start(f32[1]{0:T(128)} %add.504), channel_id=1, source_target_pairs={{0,2},{1,3},{2,0},{3,1},{4,6},{5,7},{6,4},{7,5},{8,10},{9,11},{10,... | collective-permute-start | bytes 20 | tf_op jit(solution)/shard_map/ppermute | solution.py:136
  142.7 2.0 %collective-permute-done.9 = f32[1]{0:T(128)} collective-permute-done((f32[1]{0:T(128)}, f32[1]{0:T(128)}, u32[]{:S(2)}, u32[]{:S(2)}) %collective-permute-start.9) | collective-permute-done | bytes 36 | tf_op jit(solution)/shard_map/ppermute | solution.py:136
  145.4 2.9 %collective-permute-start.10 = (f32[1]{0:T(128)}, f32[1]{0:T(128)}, u32[]{:S(2)}, u32[]{:S(2)}) collective-permute-start(f32[1]{0:T(128)} %add.505), channel_id=1, source_target_pairs={{0,4},{4,0},{1,5},{5,1},{2,6},{6,2},{3,7},{7,3},{8,12},{12,8},{9,1... | collective-permute-start | bytes 20 | tf_op jit(solution)/shard_map/ppermute | solution.py:136
  148.3 0.7 collective-permute-done.10
  149.6 0.4 copy.35
  150.0 1.0 fusion.27
  151.0 1.0 copy.36
  (32 shorter events, 0.4 us)
Async XLA Ops:
  1.3 4.6 %collective-permute-start.3 = (s32[4,1]{0,1:T(1,128)S(1)}, s32[4,1]{0,1:T(1,128)S(1)}, u32[]{:S(2)}, u32[]{:S(2)}) collective-permute-start(s32[4,1]{0,1:T(1,128)S(1)} %compare_select_fusion.1), channel_id=1, source_target_pairs={{0,8},{8,0},{16,24},{24,16},{1,9},{9,1},{17,25},{25,17},{2,10},{10... | collective-permute-start | bytes 56 | tf_op jit(solution)/shard_map/ppermute | solution.py:45
  5.9 4.6 %collective-permute-start.4 = (s32[4,1]{0,1:T(1,128)S(1)}, s32[4,1]{0,1:T(1,128)S(1)}, u32[]{:S(2)}, u32[]{:S(2)}) collective-permute-start(s32[4,1]{0,1:T(1,128)S(1)} %fusion.368), channel_id=1, source_target_pairs={{0,16},{8,24},{16,0},{24,8},{1,17},{9,25},{17,1},{25,9},{2,18},{10... | collective-permute-start | bytes 56 | tf_op jit(solution)/shard_map/ppermute | solution.py:45
  12.1 5.3 %copy-start = (f32[1,48,24,96]{3,2,1,0:T(8,128)S(1)}, f32[1,48,24,96]{3,2,1,0:T(8,128)}, u32[]{:S(2)}) copy-start(f32[1,48,24,96]{3,2,1,0:T(8,128)} %param.4) | copy-start | bytes 1327108
  12.1 56.9 %all-to-all-start = ((f32[4,1,48,24,96]{4,3,2,1,0:T(8,128)}), f32[4,1,48,24,96]{4,3,2,1,0:T(8,128)S(1)}, u32[]{:S(2)}, u32[]{:S(2)}) async-start(f32[4,1,48,24,96]{4,3,2,1,0:T(8,128)} %select_select_fusion), calls=%async_computation | async-start | bytes 4718592 | tf_op jit(solution)/shard_map/all_to_all | solution.py:161
  17.5 4.7 %collective-permute-start = (f32[1,8,24,96]{3,2,1,0:T(8,128)S(1)}, f32[1,8,24,96]{3,2,1,0:T(8,128)S(1)}, u32[]{:S(2)}, u32[]{:S(2)}) collective-permute-start(f32[1,8,24,96]{3,2,1,0:T(8,128)S(1)} %slice_select_fusion.1), channel_id=1, source_target_pairs={{0,4},{4,0},{1,5},{5,1},{2,6},{6,2},{3,7},{7,3},{8,12},{12,8},{9,1... | collective-permute-start | bytes 221192 | tf_op jit(solution)/shard_map/ppermute | solution.py:25
  22.2 2.9 %copy-start.1 = (f32[1,8,24,96]{3,2,1,0:T(8,128)}, f32[1,8,24,96]{3,2,1,0:T(8,128)S(1)}, u32[]{:S(2)}) copy-start(f32[1,8,24,96]{3,2,1,0:T(8,128)S(1)} %get-tuple-element.20) | copy-start | bytes 221188
  22.2 2.9 %copy-start.2 = (f32[1,8,24,96]{3,2,1,0:T(8,128)}, f32[1,8,24,96]{3,2,1,0:T(8,128)S(1)}, u32[]{:S(2)}) copy-start(f32[1,8,24,96]{3,2,1,0:T(8,128)S(1)} %get-tuple-element.21) | copy-start | bytes 221188
  23.0 47.7 %collective-permute-start.1 = (f32[1,64,8,96]{3,2,1,0:T(8,128)}, f32[1,64,8,96]{3,2,1,0:T(8,128)}, u32[]{:S(2)}, u32[]{:S(2)}) collective-permute-start(f32[1,64,8,96]{3,2,1,0:T(8,128)} %get-tuple-element.16), channel_id=1, source_target_pairs={{0,1},{1,2},{2,3},{4,5},{5,6},{6,7},{8,9},{9,10},{10,11},{12,13},{... | collective-permute-start | bytes 589832 | tf_op jit(solution)/shard_map/ppermute | solution.py:30
  25.1 45.7 %collective-permute-start.2 = (f32[1,64,8,96]{3,2,1,0:T(8,128)}, f32[1,64,8,96]{3,2,1,0:T(8,128)}, u32[]{:S(2)}, u32[]{:S(2)}) collective-permute-start(f32[1,64,8,96]{3,2,1,0:T(8,128)} %get-tuple-element.17), channel_id=1, source_target_pairs={{1,0},{2,1},{3,2},{5,4},{6,5},{7,6},{9,8},{10,9},{11,10},{13,12},{... | collective-permute-start | bytes 589832 | tf_op jit(solution)/shard_map/ppermute | solution.py:31
  69.2 4.7 %collective-permute-start.5 = (f32[1,8,24,96]{3,2,1,0:T(8,128)S(1)}, f32[1,8,24,96]{3,2,1,0:T(8,128)S(1)}, u32[]{:S(2)}, u32[]{:S(2)}) collective-permute-start(f32[1,8,24,96]{3,2,1,0:T(8,128)S(1)} %slice_select_fusion), channel_id=1, source_target_pairs={{0,4},{4,0},{1,5},{5,1},{2,6},{6,2},{3,7},{7,3},{8,12},{12,8},{9,1... | collective-permute-start | bytes 221192 | tf_op jit(solution)/shard_map/ppermute | solution.py:25
  74.0 3.4 %collective-permute-start.6 = (f32[1,64,8,96]{3,2,1,0:T(8,128)S(1)}, f32[1,64,8,96]{3,2,1,0:T(8,128)S(1)}, u32[]{:S(2)}, u32[]{:S(2)}) collective-permute-start(f32[1,64,8,96]{3,2,1,0:T(8,128)S(1)} %get-tuple-element.18), channel_id=1, source_target_pairs={{0,1},{1,2},{2,3},{4,5},{5,6},{6,7},{8,9},{9,10},{10,11},{12,13},{... | collective-permute-start | bytes 589832 | tf_op jit(solution)/shard_map/ppermute | solution.py:30
  75.3 5.2 %collective-permute-start.7 = (f32[1,64,8,96]{3,2,1,0:T(8,128)S(1)}, f32[1,64,8,96]{3,2,1,0:T(8,128)S(1)}, u32[]{:S(2)}, u32[]{:S(2)}) collective-permute-start(f32[1,64,8,96]{3,2,1,0:T(8,128)S(1)} %get-tuple-element.19), channel_id=1, source_target_pairs={{1,0},{2,1},{3,2},{5,4},{6,5},{7,6},{9,8},{10,9},{11,10},{13,12},{... | collective-permute-start | bytes 589832 | tf_op jit(solution)/shard_map/ppermute | solution.py:31
  81.7 2.4 %copy-start.4 = (pred[8,24]{1,0:T(8,128)(4,1)S(1)}, pred[8,24]{1,0:T(8,128)(4,1)}, u32[]{:S(2)}) copy-start(pred[8,24]{1,0:T(8,128)(4,1)} %fusion.129) | copy-start | bytes 580
  86.0 19.9 %all-to-all-start.1 = ((f32[8,24,1,1152]{3,1,2,0:T(8,128)}), f32[8,24,1,1152]{3,1,2,0:T(8,128)}, u32[]{:S(2)}, u32[]{:S(2)}) async-start(f32[8,24,1,1152]{3,1,2,0:T(8,128)} %convolution_bitcast_fusion), calls=%async_computation.1 | async-start | bytes 1769472 | tf_op jit(solution)/shard_map/all_to_all | solution.py:105
  119.7 7.6 %collective-permute-start.8 = (f32[1]{0:T(128)}, f32[1]{0:T(128)}, u32[]{:S(2)}, u32[]{:S(2)}) collective-permute-start(f32[1]{0:T(128)} %bitcast.35), channel_id=1, source_target_pairs={{0,1},{1,0},{2,3},{3,2},{4,5},{5,4},{6,7},{7,6},{8,9},{9,8},{10,11... | collective-permute-start | bytes 20 | tf_op jit(solution)/shard_map/ppermute | solution.py:136
  120.1 3.8 %copy-start.3 = (s32[2,48]{1,0:T(2,128)S(1)}, s32[2,48]{1,0:T(2,128)}, u32[]{:S(2)}) copy-start(s32[2,48]{1,0:T(2,128)} %multiply_add_fusion.1) | copy-start | bytes 1156
  128.6 21.0 %all-to-all-start.2 = ((f32[8,24,1,1152]{3,1,2,0:T(8,128)}), f32[8,24,1,1152]{3,1,2,0:T(8,128)S(1)}, u32[]{:S(2)}, u32[]{:S(2)}) async-start(f32[8,24,1,1152]{3,1,2,0:T(8,128)} %bitcast.126), calls=%async_computation.2 | async-start | bytes 1769472 | tf_op jit(solution)/shard_map/all_to_all | solution.py:143
  132.8 12.0 %collective-permute-start.9 = (f32[1]{0:T(128)}, f32[1]{0:T(128)}, u32[]{:S(2)}, u32[]{:S(2)}) collective-permute-start(f32[1]{0:T(128)} %add.504), channel_id=1, source_target_pairs={{0,2},{1,3},{2,0},{3,1},{4,6},{5,7},{6,4},{7,5},{8,10},{9,11},{10,... | collective-permute-start | bytes 20 | tf_op jit(solution)/shard_map/ppermute | solution.py:136
  145.4 3.6 %collective-permute-start.10 = (f32[1]{0:T(128)}, f32[1]{0:T(128)}, u32[]{:S(2)}, u32[]{:S(2)}) collective-permute-start(f32[1]{0:T(128)} %add.505), channel_id=1, source_target_pairs={{0,4},{4,0},{1,5},{5,1},{2,6},{6,2},{3,7},{7,3},{8,12},{12,8},{9,1... | collective-permute-start | bytes 20 | tf_op jit(solution)/shard_map/ppermute | solution.py:136

commit v15 on v13

--- a/solution.py
+++ b/solution.py
@@ -104,11 +104,14 @@
     send = along_x.reshape(spread, width, pair_count, rows_y * rows_z)
     got = lax.all_to_all(send, ("gy", "gz"), 0, 0, tiled=True)
     got = got.reshape(count_y, count_z, width, pair_count, rows_z, rows_y)
-    got = got.transpose(2, 3, 1, 4, 0, 5).reshape(
-        width, pair_count, count_z * rows_z, count_y * rows_y
-    )
-    along_z = contract(got, table, 3, 0)
-    spectrum = contract(along_z, table, 2, 0)
+    table_y = table.reshape(count_y, rows_y, period)
+    along_y = contract(got[0], table_y[0], 4, 0)
+    for part in range(1, count_y):
+        along_y = along_y + contract(got[part], table_y[part], 4, 0)
+    table_z = table.reshape(count_z, rows_z, period)
+    spectrum = contract(along_y[0], table_z[0], 2, 0)
+    for part in range(1, count_z):
+        spectrum = spectrum + contract(along_y[part], table_z[part], 2, 0)
     own = lax.axis_index(("gy", "gz")) * width + jnp.arange(width, dtype=jnp.int32)
     _, lattice_x, fold_x = channel_of(own, length)
     _, lattice_all, fold_all = channel_of(jnp.arange(period, dtype=jnp.int32), length)

time: 152 us -> 154 us (1.013)
  matrix products: 20.8 us -> 29.1 us
  local copies, waits for them, and re-layouts: 12.6 us -> 5.59 us
  other arithmetic: 4.14 us -> 6.25 us
  waiting for transfers between devices: 66.4 us -> 64.6 us
    dot_general x6 -> x10, matrix products: 14 us -> 22.3 us  [contract(): lax.dot_general(left, right, (((left_dim,), (right_dim,)), ((), ())), pre...]
    reshape x2 -> x0, local copies, waits for them, and re-layouts: 5.35 us -> none  [potentials(): got = got.reshape(count_y, count_z, width, pair_count, rows_z, rows_y)]
    ppermute x2, waiting for transfers between devices: 2.78 us -> 0.96 us  [extended(): got = lax.ppermute(jnp.where(first, tail, head), axis, [(0, 1), (1, 0)])]
    another operation x1 -> x2, local copies, waits for them, and re-layouts: 2.72 us -> 1 us
  transfers between devices with their start and end apart: 14 -> 14, of which waited for: 10 -> 10; matrix products, arithmetic and copies ran while one was open for 5% -> 6% of each run, Pallas kernels for 0% -> 0%
where the time goes in v15:
time: 154 us; the launch traced here: 153 us
  waiting for transfers between devices  64.6 us (42%)
  starting transfers between devices  41.7 us (27%)
  matrix products  29.1 us (19%)
  other arithmetic  6.25 us (4%)
  between operations  6 us (4%)
  local copies, waits for them, and re-layouts  5.59 us (4%)
    all_to_all x1, waiting for transfers between devices, shards(): arrived = lax.all_to_all(slots, 'band', 0, 0, tiled=True)  42.6 us
    dot_general x10, matrix products, contract(): lax.dot_general(left, right, (((left_dim,), (right_dim,)), ((), ())), pre...  22.3 us
    ppermute x5, starting transfers between devices, group_sum(): lax.ppermute(total, axis, [(i, i ^ step) for i in range(count)])  16.7 us
    all_to_all x1, waiting for transfers between devices, potentials(): got = lax.all_to_all(send, ('gy', 'gz'), 0, 0, tiled=True)  12.6 us
    all_to_all x1, starting transfers between devices, potentials(): got = lax.all_to_all(send, ('gy', 'gz'), 0, 0, tiled=True)  7.13 us
    ppermute x5, waiting for transfers between devices, group_sum(): lax.ppermute(total, axis, [(i, i ^ step) for i in range(count)])  5.4 us
    all_to_all x1, starting transfers between devices, shards(): arrived = lax.all_to_all(slots, 'band', 0, 0, tiled=True)  5.33 us
    dot_general x2, matrix products, synthesize(): step_one = jnp.matmul(padded, matrix_x, precision=precise_mode)  3.62 us
  transfers between devices with their start and end apart: 14, of which 10 were waited for; matrix products, arithmetic and copies ran while one was open for 6% of the time, Pallas kernels for 0%

profile of v15, /device:TPU:0, one launch (start us, length us, event | category | flops | bytes accessed | tf_op | source)
XLA Modules:
  0.0 153.2 jit_solution(3142929718862435923)
XLA Ops:
  1.3 3.1 %collective-permute-start.3 = (s32[4,1]{0,1:T(1,128)S(1)}, s32[4,1]{0,1:T(1,128)S(1)}, u32[]{:S(2)}, u32[]{:S(2)}) collective-permute-start(s32[4,1]{0,1:T(1,128)S(1)} %compare_select_fusion.1), channel_id=1, source_target_pairs={{0,8},{8,0},{16,24},{24,16},{1,9},{9,1},{17,25},{25,17},{2,10},{10... | collective-permute-start | bytes 56 | tf_op jit(solution)/shard_map/ppermute | solution.py:45
  4.4 1.3 slice_bitcast_fusion.9
  5.9 3.0 %collective-permute-start.4 = (s32[4,1]{0,1:T(1,128)S(1)}, s32[4,1]{0,1:T(1,128)S(1)}, u32[]{:S(2)}, u32[]{:S(2)}) collective-permute-start(s32[4,1]{0,1:T(1,128)S(1)} %fusion.363), channel_id=1, source_target_pairs={{0,16},{8,24},{16,0},{24,8},{1,17},{9,25},{17,1},{25,9},{2,18},{10... | collective-permute-start | bytes 56 | tf_op jit(solution)/shard_map/ppermute | solution.py:45
  8.9 1.5 collective-permute-done.4
  10.5 1.7 %select_select_fusion = f32[4,1,48,24,96]{4,3,2,1,0:T(8,128)} fusion(f32[48,24,96]{2,1,0:T(8,128)S(1)} %get-tuple-element.11, f32[48,24,96]{2,1,0:T(8,128)S(1)} %get-tuple-element.10, pred[4]{0:T(512)(128)(4,1)S(1)} %get-tuple-element.23, pred[4]{0:T(512)(128)(4,1)S(1)} %get-tuple-element.22), kind=kLoop, calls=%fused_computation.11 | loop fusion | flops 884736 | bytes 2654216 | tf_op jit(solution)/shard_map/jit(_where)/select_n | solution.py:148
  12.1 5.3 %all-to-all-start = ((f32[4,1,48,24,96]{4,3,2,1,0:T(8,128)}), f32[4,1,48,24,96]{4,3,2,1,0:T(8,128)S(1)}, u32[]{:S(2)}, u32[]{:S(2)}) async-start(f32[4,1,48,24,96]{4,3,2,1,0:T(8,128)} %select_select_fusion), calls=%async_computation | async-start | bytes 4718592 | tf_op jit(solution)/shard_map/all_to_all | solution.py:149
  17.5 1.6 %collective-permute-start = (f32[1,8,24,96]{3,2,1,0:T(8,128)S(1)}, f32[1,8,24,96]{3,2,1,0:T(8,128)S(1)}, u32[]{:S(2)}, u32[]{:S(2)}) collective-permute-start(f32[1,8,24,96]{3,2,1,0:T(8,128)S(1)} %slice_select_fusion.1), channel_id=1, source_target_pairs={{0,4},{4,0},{1,5},{5,1},{2,6},{6,2},{3,7},{7,3},{8,12},{12,8},{9,1... | collective-permute-start | bytes 221192 | tf_op jit(solution)/shard_map/ppermute | solution.py:25
  19.0 0.6 iota_add_fusion.1
  19.6 0.5 fusion.129
  20.2 0.6 multiply_add_fusion.1
  20.7 0.5 or_select_fusion.1
  21.4 0.6 iota_add_fusion.2
  22.2 0.8 pad_maximum_fusion.5
  23.0 2.0 %collective-permute-start.1 = (f32[1,64,8,96]{3,2,1,0:T(8,128)}, f32[1,64,8,96]{3,2,1,0:T(8,128)}, u32[]{:S(2)}, u32[]{:S(2)}) collective-permute-start(f32[1,64,8,96]{3,2,1,0:T(8,128)} %get-tuple-element.14), channel_id=1, source_target_pairs={{0,1},{1,2},{2,3},{4,5},{5,6},{6,7},{8,9},{9,10},{10,11},{12,13},{... | collective-permute-start | bytes 589832 | tf_op jit(solution)/shard_map/ppermute | solution.py:30
  25.0 1.3 collective-permute-start.2
  26.3 42.6 %all-to-all-done = f32[4,1,48,24,96]{4,3,2,1,0:T(8,128)S(1)} async-done(((f32[4,1,48,24,96]{4,3,2,1,0:T(8,128)}), f32[4,1,48,24,96]{4,3,2,1,0:T(8,128)S(1)}, u32[]{:S(2)}, u32[]{:S(2)}) %all-to-all-start) | async-done | bytes 1769504 | tf_op jit(solution)/shard_map/all_to_all | solution.py:149
  69.2 1.6 %collective-permute-start.5 = (f32[1,8,24,96]{3,2,1,0:T(8,128)S(1)}, f32[1,8,24,96]{3,2,1,0:T(8,128)S(1)}, u32[]{:S(2)}, u32[]{:S(2)}) collective-permute-start(f32[1,8,24,96]{3,2,1,0:T(8,128)S(1)} %slice_select_fusion), channel_id=1, source_target_pairs={{0,4},{4,0},{1,5},{5,1},{2,6},{6,2},{3,7},{7,3},{8,12},{12,8},{9,1... | collective-permute-start | bytes 221192 | tf_op jit(solution)/shard_map/ppermute | solution.py:25
  70.8 2.4 %fusion.7 = f32[64,40,96]{2,1,0:T(8,128)S(1)} fusion(f32[1,64,8,96]{3,2,1,0:T(8,128)} %collective-permute-done.2, f32[1,8,24,96]{3,2,1,0:T(8,128)} %copy-done.2, f32[1,48,24,96]{3,2,1,0:T(8,128)S(1)} %copy-done, f32[1,8,24,96]{3,2,1,0:T(8,128)} %copy-done.1, f32[1,64,8,96]{3,2,1,0:T(8,128)} %collective-permute-done.1), kind=kOutput, calls=%fused_computation.15 | convolution fusion | flops 284540928 | bytes 1966080 | tf_op jit(solution)/shard_map/dot_general | solution.py:65
  73.1 0.7 collective-permute-done.5
  74.0 1.3 collective-permute-start.6
  75.3 1.3 collective-permute-start.7
  76.6 0.8 convolution_bitcast_fusion.3
  77.4 3.0 %collective-permute-done.7 = f32[1,64,8,96]{3,2,1,0:T(8,128)S(1)} collective-permute-done((f32[1,64,8,96]{3,2,1,0:T(8,128)S(1)}, f32[1,64,8,96]{3,2,1,0:T(8,128)S(1)}, u32[]{:S(2)}, u32[]{:S(2)}) %collective-permute-start.7) | collective-permute-done | bytes 196640 | tf_op jit(solution)/shard_map/ppermute | solution.py:31
  80.4 1.2 fusion.16
  81.7 0.8 convolution_bitcast_fusion.2
  82.5 0.8 fusion.28
  83.3 0.8 convolution_multiply_fusion.1
  84.1 1.9 %convolution_bitcast_fusion = f32[8,24,1,1152]{3,1,2,0:T(8,128)} fusion(f32[1152,96,1]{1,0,2:T(8,128)S(1)} %bitcast.162, s32[8,24]{1,0:T(8,128)S(1)} %add_select_fusion.3, pred[8,24]{1,0:T(8,128)(4,1)S(1)} %copy-done.6), kind=kOutput, calls=%fused_computation.4 | convolution fusion | flops 127586304 | bytes 1328064 | tf_op jit(solution)/shard_map/dot_general | solution.py:89
  86.0 7.1 %all-to-all-start.1 = ((f32[8,24,1,1152]{3,1,2,0:T(8,128)}), f32[8,24,1,1152]{3,1,2,0:T(8,128)S(1)}, u32[]{:S(2)}, u32[]{:S(2)}) async-start(f32[8,24,1,1152]{3,1,2,0:T(8,128)} %convolution_bitcast_fusion), calls=%async_computation.1 | async-start | bytes 1769472 | tf_op jit(solution)/shard_map/all_to_all | solution.py:105
  93.8 12.6 %all-to-all-done.1 = f32[8,24,1,1152]{3,1,2,0:T(8,128)S(1)} async-done(((f32[8,24,1,1152]{3,1,2,0:T(8,128)}), f32[8,24,1,1152]{3,1,2,0:T(8,128)S(1)}, u32[]{:S(2)}, u32[]{:S(2)}) %all-to-all-start.1) | async-done | bytes 884768 | tf_op jit(solution)/shard_map/all_to_all | solution.py:105
  106.4 0.5 reshape.429
  107.4 1.1 fusion.63
  108.5 1.1 convolution_add_fusion
  109.6 2.1 %fusion.32 = f32[24,192,192]{2,1,0:T(8,128)S(1)} fusion(f32[4,24,24,192]{3,2,1,0:T(8,128)S(1)} %convolution_add_fusion, f32[96,192]{1,0:T(8,128)S(1)} %sine_select_fusion), kind=kOutput, calls=%fused_computation.48 | convolution fusion | flops 127401984 | bytes 4153344 | tf_op jit(solution)/shard_map/dot_general | solution.py:89
  111.7 2.1 %fusion.33 = f32[24,192,192]{2,1,0:T(8,128)S(1)} fusion(f32[4,24,24,192]{3,2,1,0:T(8,128)S(1)} %convolution_add_fusion, f32[96,192]{1,0:T(8,128)S(1)} %sine_select_fusion), kind=kOutput, calls=%fused_computation.50 | convolution fusion | flops 127401984 | bytes 4153344 | tf_op jit(solution)/shard_map/dot_general | solution.py:89
  113.9 2.1 %fusion.31 = f32[24,192,192]{2,1,0:T(8,128)S(1)} fusion(f32[4,24,24,192]{3,2,1,0:T(8,128)S(1)} %convolution_add_fusion, f32[96,192]{1,0:T(8,128)S(1)} %sine_select_fusion), kind=kOutput, calls=%fused_computation.46 | convolution fusion | flops 127401984 | bytes 4153344 | tf_op jit(solution)/shard_map/dot_general | solution.py:89
  116.0 5.4 %multiply_reduce_fusion = (f32[]{:T(128)}, f32[24,192,192]{2,1,0:T(8,128)S(1)}) fusion(f32[192]{0:T(256)S(1)} %get-tuple-element.29, f32[24,192]{1,0:T(8,128)S(1)} %broadcast_add_fusion, f32[192]{0:T(256)S(1)} %get-tuple-element.28, f32[24,192]{1,0:T(8,128)S(1)} %broadcast_multiply_fusion, f32[96,192]{1,0:T(8,128)S(1)} %sine_select_fusion, ...), kind=kOutput, calls=%fused_computation | convolution fusion | flops 137134080 | bytes 18360324 | tf_op jit(solution)/shard_map/dot_general | solution.py:89
  121.4 3.8 %fusion = f32[24,192,96]{1,2,0:T(8,128)S(1)} fusion(f32[24,192,192]{2,1,0:T(8,128)S(1)} %get-tuple-element.25, f32[192]{0:T(256)S(1)} %get-tuple-element.29, f32[24,192]{1,0:T(8,128)S(1)} %broadcast_add_fusion, f32[192]{0:T(256)S(1)} %get-tuple-element.28, f32[24,192]{1,0:T(8,128)S(1)} %broadcast_multiply_fusion, s32[192]{0:T(256)S(1)} %add_select_fusion.4, ...), kind=kOutput, calls=%fused_computation.3 | convolution fusion | flops 515100672 | bytes 5347776 | tf_op jit(solution)/shard_map/dot_general | solution.py:89
  125.2 1.6 %convolution_bitcast_fusion.1 = f32[2,4,24,1,24,48]{5,4,0,1,2,3:T(8,128)S(1)} fusion(f32[24,4,24,192,1]{3,2,4,1,0:T(8,128)S(1)} %bitcast.161, s32[192]{0:T(256)S(1)} %add_select_fusion.4, s32[2,48]{1,0:T(2,128)S(1)} %copy-done.5, pred[192]{0:T(512)(128)(4,1)S(1)} %iota_compare_fusion), kind=kOutput, calls=%fused_computation.13 | convolution fusion | flops 254988288 | bytes 2655552 | tf_op jit(solution)/shard_map/dot_general | solution.py:89
  126.9 1.7 %reshape.436 = f32[8,24,1,1152]{3,1,0,2:T(8,128)} reshape(f32[2,4,24,1,24,48]{5,4,2,1,0,3:T(8,128)S(1)} %copy.28) | data formatting | bytes 1769472 | tf_op jit(solution)/shard_map/reshape | solution.py:129
  128.6 3.5 %all-to-all-start.2 = ((f32[8,24,1,1152]{3,1,2,0:T(8,128)}), f32[8,24,1,1152]{3,1,2,0:T(8,128)S(1)}, u32[]{:S(2)}, u32[]{:S(2)}) async-start(f32[8,24,1,1152]{3,1,2,0:T(8,128)} %bitcast.156), calls=%async_computation.2 | async-start | bytes 1769472 | tf_op jit(solution)/shard_map/all_to_all | solution.py:131
  133.3 1.0 collective-permute-done.8
  135.5 7.2 %collective-permute-start.9 = (f32[1]{0:T(128)}, f32[1]{0:T(128)}, u32[]{:S(2)}, u32[]{:S(2)}) collective-permute-start(f32[1]{0:T(128)} %add.532), channel_id=1, source_target_pairs={{0,2},{1,3},{2,0},{3,1},{4,6},{5,7},{6,4},{7,5},{8,10},{9,11},{10,... | collective-permute-start | bytes 20 | tf_op jit(solution)/shard_map/ppermute | solution.py:45
  142.8 2.0 %collective-permute-done.9 = f32[1]{0:T(128)} collective-permute-done((f32[1]{0:T(128)}, f32[1]{0:T(128)}, u32[]{:S(2)}, u32[]{:S(2)}) %collective-permute-start.9) | collective-permute-done | bytes 36 | tf_op jit(solution)/shard_map/ppermute | solution.py:45
  145.4 2.9 %collective-permute-start.10 = (f32[1]{0:T(128)}, f32[1]{0:T(128)}, u32[]{:S(2)}, u32[]{:S(2)}) collective-permute-start(f32[1]{0:T(128)} %add.533), channel_id=1, source_target_pairs={{0,4},{4,0},{1,5},{5,1},{2,6},{6,2},{3,7},{7,3},{8,12},{12,8},{9,1... | collective-permute-start | bytes 20 | tf_op jit(solution)/shard_map/ppermute | solution.py:45
  148.3 0.7 collective-permute-done.10
  150.0 1.0 fusion.27
  151.1 1.0 copy.31
  (45 shorter events, 3.0 us)
Async XLA Ops:
  1.3 4.6 %collective-permute-start.3 = (s32[4,1]{0,1:T(1,128)S(1)}, s32[4,1]{0,1:T(1,128)S(1)}, u32[]{:S(2)}, u32[]{:S(2)}) collective-permute-start(s32[4,1]{0,1:T(1,128)S(1)} %compare_select_fusion.1), channel_id=1, source_target_pairs={{0,8},{8,0},{16,24},{24,16},{1,9},{9,1},{17,25},{25,17},{2,10},{10... | collective-permute-start | bytes 56 | tf_op jit(solution)/shard_map/ppermute | solution.py:45
  5.9 4.6 %collective-permute-start.4 = (s32[4,1]{0,1:T(1,128)S(1)}, s32[4,1]{0,1:T(1,128)S(1)}, u32[]{:S(2)}, u32[]{:S(2)}) collective-permute-start(s32[4,1]{0,1:T(1,128)S(1)} %fusion.363), channel_id=1, source_target_pairs={{0,16},{8,24},{16,0},{24,8},{1,17},{9,25},{17,1},{25,9},{2,18},{10... | collective-permute-start | bytes 56 | tf_op jit(solution)/shard_map/ppermute | solution.py:45
  12.1 5.3 %copy-start = (f32[1,48,24,96]{3,2,1,0:T(8,128)S(1)}, f32[1,48,24,96]{3,2,1,0:T(8,128)}, u32[]{:S(2)}) copy-start(f32[1,48,24,96]{3,2,1,0:T(8,128)} %param.4) | copy-start | bytes 1327108
  12.1 56.9 %all-to-all-start = ((f32[4,1,48,24,96]{4,3,2,1,0:T(8,128)}), f32[4,1,48,24,96]{4,3,2,1,0:T(8,128)S(1)}, u32[]{:S(2)}, u32[]{:S(2)}) async-start(f32[4,1,48,24,96]{4,3,2,1,0:T(8,128)} %select_select_fusion), calls=%async_computation | async-start | bytes 4718592 | tf_op jit(solution)/shard_map/all_to_all | solution.py:149
  17.5 4.7 %collective-permute-start = (f32[1,8,24,96]{3,2,1,0:T(8,128)S(1)}, f32[1,8,24,96]{3,2,1,0:T(8,128)S(1)}, u32[]{:S(2)}, u32[]{:S(2)}) collective-permute-start(f32[1,8,24,96]{3,2,1,0:T(8,128)S(1)} %slice_select_fusion.1), channel_id=1, source_target_pairs={{0,4},{4,0},{1,5},{5,1},{2,6},{6,2},{3,7},{7,3},{8,12},{12,8},{9,1... | collective-permute-start | bytes 221192 | tf_op jit(solution)/shard_map/ppermute | solution.py:25
  22.2 4.1 %copy-start.1 = (f32[1,8,24,96]{3,2,1,0:T(8,128)}, f32[1,8,24,96]{3,2,1,0:T(8,128)S(1)}, u32[]{:S(2)}) copy-start(f32[1,8,24,96]{3,2,1,0:T(8,128)S(1)} %get-tuple-element.18) | copy-start | bytes 221188
  22.2 4.1 %copy-start.2 = (f32[1,8,24,96]{3,2,1,0:T(8,128)}, f32[1,8,24,96]{3,2,1,0:T(8,128)S(1)}, u32[]{:S(2)}) copy-start(f32[1,8,24,96]{3,2,1,0:T(8,128)S(1)} %get-tuple-element.19) | copy-start | bytes 221188
  23.0 47.7 %collective-permute-start.1 = (f32[1,64,8,96]{3,2,1,0:T(8,128)}, f32[1,64,8,96]{3,2,1,0:T(8,128)}, u32[]{:S(2)}, u32[]{:S(2)}) collective-permute-start(f32[1,64,8,96]{3,2,1,0:T(8,128)} %get-tuple-element.14), channel_id=1, source_target_pairs={{0,1},{1,2},{2,3},{4,5},{5,6},{6,7},{8,9},{9,10},{10,11},{12,13},{... | collective-permute-start | bytes 589832 | tf_op jit(solution)/shard_map/ppermute | solution.py:30
  25.0 45.7 %collective-permute-start.2 = (f32[1,64,8,96]{3,2,1,0:T(8,128)}, f32[1,64,8,96]{3,2,1,0:T(8,128)}, u32[]{:S(2)}, u32[]{:S(2)}) collective-permute-start(f32[1,64,8,96]{3,2,1,0:T(8,128)} %get-tuple-element.15), channel_id=1, source_target_pairs={{1,0},{2,1},{3,2},{5,4},{6,5},{7,6},{9,8},{10,9},{11,10},{13,12},{... | collective-permute-start | bytes 589832 | tf_op jit(solution)/shard_map/ppermute | solution.py:31
  69.2 7.4 %copy-start.4 = (s32[40]{0:T(128)S(1)}, s32[40]{0:T(128)}, u32[]{:S(2)}) copy-start(s32[40]{0:T(128)} %iota_add_fusion.1) | copy-start | bytes 484
  69.2 4.7 %collective-permute-start.5 = (f32[1,8,24,96]{3,2,1,0:T(8,128)S(1)}, f32[1,8,24,96]{3,2,1,0:T(8,128)S(1)}, u32[]{:S(2)}, u32[]{:S(2)}) collective-permute-start(f32[1,8,24,96]{3,2,1,0:T(8,128)S(1)} %slice_select_fusion), channel_id=1, source_target_pairs={{0,4},{4,0},{1,5},{5,1},{2,6},{6,2},{3,7},{7,3},{8,12},{12,8},{9,1... | collective-permute-start | bytes 221192 | tf_op jit(solution)/shard_map/ppermute | solution.py:25
  74.0 3.5 %collective-permute-start.6 = (f32[1,64,8,96]{3,2,1,0:T(8,128)S(1)}, f32[1,64,8,96]{3,2,1,0:T(8,128)S(1)}, u32[]{:S(2)}, u32[]{:S(2)}) collective-permute-start(f32[1,64,8,96]{3,2,1,0:T(8,128)S(1)} %get-tuple-element.16), channel_id=1, source_target_pairs={{0,1},{1,2},{2,3},{4,5},{5,6},{6,7},{8,9},{9,10},{10,11},{12,13},{... | collective-permute-start | bytes 589832 | tf_op jit(solution)/shard_map/ppermute | solution.py:30
  75.3 5.2 %collective-permute-start.7 = (f32[1,64,8,96]{3,2,1,0:T(8,128)S(1)}, f32[1,64,8,96]{3,2,1,0:T(8,128)S(1)}, u32[]{:S(2)}, u32[]{:S(2)}) collective-permute-start(f32[1,64,8,96]{3,2,1,0:T(8,128)S(1)} %get-tuple-element.17), channel_id=1, source_target_pairs={{1,0},{2,1},{3,2},{5,4},{6,5},{7,6},{9,8},{10,9},{11,10},{13,12},{... | collective-permute-start | bytes 589832 | tf_op jit(solution)/shard_map/ppermute | solution.py:31
  77.4 5.1 %copy-start.3 = (s32[64]{0:T(128)S(1)}, s32[64]{0:T(128)}, u32[]{:S(2)}) copy-start(s32[64]{0:T(128)} %iota_add_fusion.2) | copy-start | bytes 772
  81.7 2.4 %copy-start.6 = (pred[8,24]{1,0:T(8,128)(4,1)S(1)}, pred[8,24]{1,0:T(8,128)(4,1)}, u32[]{:S(2)}) copy-start(pred[8,24]{1,0:T(8,128)(4,1)} %fusion.129) | copy-start | bytes 580
  83.3 9.9 %copy-start.8 = (f32[24]{0:T(128)S(1)}, f32[24]{0:T(128)}, u32[]{:S(2)}) copy-start(f32[24]{0:T(128)} %get-tuple-element.26) | copy-start | bytes 292
  83.3 9.9 %copy-start.7 = (f32[24]{0:T(128)S(1)}, f32[24]{0:T(128)}, u32[]{:S(2)}) copy-start(f32[24]{0:T(128)} %get-tuple-element.27) | copy-start | bytes 292
  86.0 20.3 %all-to-all-start.1 = ((f32[8,24,1,1152]{3,1,2,0:T(8,128)}), f32[8,24,1,1152]{3,1,2,0:T(8,128)S(1)}, u32[]{:S(2)}, u32[]{:S(2)}) async-start(f32[8,24,1,1152]{3,1,2,0:T(8,128)} %convolution_bitcast_fusion), calls=%async_computation.1 | async-start | bytes 1769472 | tf_op jit(solution)/shard_map/all_to_all | solution.py:105
  121.3 3.8 %copy-start.5 = (s32[2,48]{1,0:T(2,128)S(1)}, s32[2,48]{1,0:T(2,128)}, u32[]{:S(2)}) copy-start(s32[2,48]{1,0:T(2,128)} %multiply_add_fusion.1) | copy-start | bytes 1156
  128.6 21.0 %all-to-all-start.2 = ((f32[8,24,1,1152]{3,1,2,0:T(8,128)}), f32[8,24,1,1152]{3,1,2,0:T(8,128)S(1)}, u32[]{:S(2)}, u32[]{:S(2)}) async-start(f32[8,24,1,1152]{3,1,2,0:T(8,128)} %bitcast.156), calls=%async_computation.2 | async-start | bytes 1769472 | tf_op jit(solution)/shard_map/all_to_all | solution.py:131
  132.8 1.4 collective-permute-start.8
  135.5 9.3 %collective-permute-start.9 = (f32[1]{0:T(128)}, f32[1]{0:T(128)}, u32[]{:S(2)}, u32[]{:S(2)}) collective-permute-start(f32[1]{0:T(128)} %add.532), channel_id=1, source_target_pairs={{0,2},{1,3},{2,0},{3,1},{4,6},{5,7},{6,4},{7,5},{8,10},{9,11},{10,... | collective-permute-start | bytes 20 | tf_op jit(solution)/shard_map/ppermute | solution.py:45
  145.4 3.6 %collective-permute-start.10 = (f32[1]{0:T(128)}, f32[1]{0:T(128)}, u32[]{:S(2)}, u32[]{:S(2)}) collective-permute-start(f32[1]{0:T(128)} %add.533), channel_id=1, source_target_pairs={{0,4},{4,0},{1,5},{5,1},{2,6},{6,2},{3,7},{7,3},{8,12},{12,8},{9,1... | collective-permute-start | bytes 20 | tf_op jit(solution)/shard_map/ppermute | solution.py:45

commit v16 on v15

--- a/solution.py
+++ b/solution.py
@@ -108,10 +108,8 @@
     along_y = contract(got[0], table_y[0], 4, 0)
     for part in range(1, count_y):
         along_y = along_y + contract(got[part], table_y[part], 4, 0)
-    table_z = table.reshape(count_z, rows_z, period)
-    spectrum = contract(along_y[0], table_z[0], 2, 0)
-    for part in range(1, count_z):
-        spectrum = spectrum + contract(along_y[part], table_z[part], 2, 0)
+    along_y = along_y.transpose(1, 2, 0, 3, 4).reshape(width, pair_count, count_z * rows_z, period)
+    spectrum = contract(along_y, table, 2, 0)
     own = lax.axis_index(("gy", "gz")) * width + jnp.arange(width, dtype=jnp.int32)
     _, lattice_x, fold_x = channel_of(own, length)
     _, lattice_all, fold_all = channel_of(jnp.arange(period, dtype=jnp.int32), length)

time: 154 us -> 147 us (0.955)
  matrix products: 29.1 us -> 22.5 us
    dot_general x10 -> x7, matrix products: 22.3 us -> 15.7 us  [contract(): lax.dot_general(left, right, (((left_dim,), (right_dim,)), ((), ())), pre...]
where the time goes in v16:
time: 147 us
  waiting for transfers between devices  64.6 us (44%)
  starting transfers between devices  41.7 us (28%)
  matrix products  22.5 us (15%)
  other arithmetic  6.25 us (4%)
  between operations  5.99 us (4%)
  local copies, waits for them, and re-layouts  5.88 us (4%)
    all_to_all x1, waiting for transfers between devices, shards(): arrived = lax.all_to_all(slots, 'band', 0, 0, tiled=True)  42.6 us
    ppermute x5, starting transfers between devices, group_sum(): lax.ppermute(total, axis, [(i, i ^ step) for i in range(count)])  16.7 us
    dot_general x7, matrix products, contract(): lax.dot_general(left, right, (((left_dim,), (right_dim,)), ((), ())), pre...  15.7 us
    all_to_all x1, waiting for transfers between devices, potentials(): got = lax.all_to_all(send, ('gy', 'gz'), 0, 0, tiled=True)  12.6 us
    all_to_all x1, starting transfers between devices, potentials(): got = lax.all_to_all(send, ('gy', 'gz'), 0, 0, tiled=True)  7.13 us
    ppermute x5, waiting for transfers between devices, group_sum(): lax.ppermute(total, axis, [(i, i ^ step) for i in range(count)])  5.4 us
    all_to_all x1, starting transfers between devices, shards(): arrived = lax.all_to_all(slots, 'band', 0, 0, tiled=True)  5.33 us
    dot_general x2, matrix products, synthesize(): step_one = jnp.matmul(padded, matrix_x, precision=precise_mode)  3.62 us
  transfers between devices with their start and end apart: 14, of which 10 were waited for; matrix products, arithmetic and copies ran while one was open for 6% of the time, Pallas kernels for 0%

profile of v16, /device:TPU:0, one launch (start us, length us, event | category | flops | bytes accessed | tf_op | source)
XLA Modules:
  0.0 146.9 jit_solution(14477961857398257623)
XLA Ops:
  1.3 3.1 %collective-permute-start.3 = (s32[4,1]{0,1:T(1,128)S(1)}, s32[4,1]{0,1:T(1,128)S(1)}, u32[]{:S(2)}, u32[]{:S(2)}) collective-permute-start(s32[4,1]{0,1:T(1,128)S(1)} %compare_select_fusion.1), channel_id=1, source_target_pairs={{0,8},{8,0},{16,24},{24,16},{1,9},{9,1},{17,25},{25,17},{2,10},{10... | collective-permute-start | bytes 56 | tf_op jit(solution)/shard_map/ppermute | solution.py:45
  4.4 1.3 slice_bitcast_fusion.1
  5.9 3.0 %collective-permute-start.4 = (s32[4,1]{0,1:T(1,128)S(1)}, s32[4,1]{0,1:T(1,128)S(1)}, u32[]{:S(2)}, u32[]{:S(2)}) collective-permute-start(s32[4,1]{0,1:T(1,128)S(1)} %fusion.366), channel_id=1, source_target_pairs={{0,16},{8,24},{16,0},{24,8},{1,17},{9,25},{17,1},{25,9},{2,18},{10... | collective-permute-start | bytes 56 | tf_op jit(solution)/shard_map/ppermute | solution.py:45
  8.9 1.5 %collective-permute-done.4 = s32[4,1]{0,1:T(1,128)S(1)} collective-permute-done((s32[4,1]{0,1:T(1,128)S(1)}, s32[4,1]{0,1:T(1,128)S(1)}, u32[]{:S(2)}, u32[]{:S(2)}) %collective-permute-start.4) | collective-permute-done | bytes 48 | tf_op jit(solution)/shard_map/ppermute | solution.py:45
  10.5 1.7 %select_select_fusion = f32[4,1,48,24,96]{4,3,2,1,0:T(8,128)} fusion(f32[48,24,96]{2,1,0:T(8,128)S(1)} %get-tuple-element.11, f32[48,24,96]{2,1,0:T(8,128)S(1)} %get-tuple-element.10, pred[4]{0:T(512)(128)(4,1)S(1)} %get-tuple-element.23, pred[4]{0:T(512)(128)(4,1)S(1)} %get-tuple-element.22), kind=kLoop, calls=%fused_computation.11 | loop fusion | flops 884736 | bytes 2654216 | tf_op jit(solution)/shard_map/jit(_where)/select_n | solution.py:146
  12.1 5.3 %all-to-all-start = ((f32[4,1,48,24,96]{4,3,2,1,0:T(8,128)}), f32[4,1,48,24,96]{4,3,2,1,0:T(8,128)S(1)}, u32[]{:S(2)}, u32[]{:S(2)}) async-start(f32[4,1,48,24,96]{4,3,2,1,0:T(8,128)} %select_select_fusion), calls=%async_computation | async-start | bytes 4718592 | tf_op jit(solution)/shard_map/all_to_all | solution.py:147
  17.5 1.6 %collective-permute-start = (f32[1,8,24,96]{3,2,1,0:T(8,128)S(1)}, f32[1,8,24,96]{3,2,1,0:T(8,128)S(1)}, u32[]{:S(2)}, u32[]{:S(2)}) collective-permute-start(f32[1,8,24,96]{3,2,1,0:T(8,128)S(1)} %slice_select_fusion.1), channel_id=1, source_target_pairs={{0,4},{4,0},{1,5},{5,1},{2,6},{6,2},{3,7},{7,3},{8,12},{12,8},{9,1... | collective-permute-start | bytes 221192 | tf_op jit(solution)/shard_map/ppermute | solution.py:25
  19.0 0.6 iota_add_fusion.1
  19.6 0.5 fusion.128
  20.2 0.6 multiply_add_fusion.1
  20.7 0.5 or_select_fusion.1
  21.4 0.6 iota_add_fusion.2
  22.2 0.8 pad_maximum_fusion.5
  23.0 2.0 %collective-permute-start.1 = (f32[1,64,8,96]{3,2,1,0:T(8,128)}, f32[1,64,8,96]{3,2,1,0:T(8,128)}, u32[]{:S(2)}, u32[]{:S(2)}) collective-permute-start(f32[1,64,8,96]{3,2,1,0:T(8,128)} %get-tuple-element.14), channel_id=1, source_target_pairs={{0,1},{1,2},{2,3},{4,5},{5,6},{6,7},{8,9},{9,10},{10,11},{12,13},{... | collective-permute-start | bytes 589832 | tf_op jit(solution)/shard_map/ppermute | solution.py:30
  25.0 1.3 collective-permute-start.2
  26.3 42.6 %all-to-all-done = f32[4,1,48,24,96]{4,3,2,1,0:T(8,128)S(1)} async-done(((f32[4,1,48,24,96]{4,3,2,1,0:T(8,128)}), f32[4,1,48,24,96]{4,3,2,1,0:T(8,128)S(1)}, u32[]{:S(2)}, u32[]{:S(2)}) %all-to-all-start) | async-done | bytes 1769504 | tf_op jit(solution)/shard_map/all_to_all | solution.py:147
  69.2 1.6 %collective-permute-start.5 = (f32[1,8,24,96]{3,2,1,0:T(8,128)S(1)}, f32[1,8,24,96]{3,2,1,0:T(8,128)S(1)}, u32[]{:S(2)}, u32[]{:S(2)}) collective-permute-start(f32[1,8,24,96]{3,2,1,0:T(8,128)S(1)} %slice_select_fusion), channel_id=1, source_target_pairs={{0,4},{4,0},{1,5},{5,1},{2,6},{6,2},{3,7},{7,3},{8,12},{12,8},{9,1... | collective-permute-start | bytes 221192 | tf_op jit(solution)/shard_map/ppermute | solution.py:25
  70.8 2.4 %fusion.7 = f32[64,40,96]{2,1,0:T(8,128)S(1)} fusion(f32[1,64,8,96]{3,2,1,0:T(8,128)} %collective-permute-done.2, f32[1,8,24,96]{3,2,1,0:T(8,128)} %copy-done.2, f32[1,48,24,96]{3,2,1,0:T(8,128)S(1)} %copy-done, f32[1,8,24,96]{3,2,1,0:T(8,128)} %copy-done.1, f32[1,64,8,96]{3,2,1,0:T(8,128)} %collective-permute-done.1), kind=kOutput, calls=%fused_computation.14 | convolution fusion | flops 284540928 | bytes 1966080 | tf_op jit(solution)/shard_map/dot_general | solution.py:65
  73.1 0.7 collective-permute-done.5
  74.0 1.3 collective-permute-start.6
  75.3 1.3 collective-permute-start.7
  76.6 0.8 convolution_bitcast_fusion.3
  77.4 3.0 %collective-permute-done.7 = f32[1,64,8,96]{3,2,1,0:T(8,128)S(1)} collective-permute-done((f32[1,64,8,96]{3,2,1,0:T(8,128)S(1)}, f32[1,64,8,96]{3,2,1,0:T(8,128)S(1)}, u32[]{:S(2)}, u32[]{:S(2)}) %collective-permute-start.7) | collective-permute-done | bytes 196640 | tf_op jit(solution)/shard_map/ppermute | solution.py:31
  80.4 1.2 fusion.16
  81.7 0.8 convolution_bitcast_fusion.2
  82.5 0.8 fusion.28
  83.3 0.8 convolution_multiply_fusion.1
  84.1 1.9 %convolution_bitcast_fusion = f32[8,24,1,1152]{3,1,2,0:T(8,128)} fusion(f32[1152,96,1]{1,0,2:T(8,128)S(1)} %bitcast.145, s32[8,24]{1,0:T(8,128)S(1)} %add_select_fusion.3, pred[8,24]{1,0:T(8,128)(4,1)S(1)} %copy-done.6), kind=kOutput, calls=%fused_computation.3 | convolution fusion | flops 127586304 | bytes 1328064 | tf_op jit(solution)/shard_map/dot_general | solution.py:89
  86.0 7.1 %all-to-all-start.1 = ((f32[8,24,1,1152]{3,1,2,0:T(8,128)}), f32[8,24,1,1152]{3,1,2,0:T(8,128)S(1)}, u32[]{:S(2)}, u32[]{:S(2)}) async-start(f32[8,24,1,1152]{3,1,2,0:T(8,128)} %convolution_bitcast_fusion), calls=%async_computation.1 | async-start | bytes 1769472 | tf_op jit(solution)/shard_map/all_to_all | solution.py:105
  93.3 0.4 sine_select_fusion
  93.8 12.6 %all-to-all-done.1 = f32[8,24,1,1152]{3,1,2,0:T(8,128)S(1)} async-done(((f32[8,24,1,1152]{3,1,2,0:T(8,128)}), f32[8,24,1,1152]{3,1,2,0:T(8,128)S(1)}, u32[]{:S(2)}, u32[]{:S(2)}) %all-to-all-start.1) | async-done | bytes 884768 | tf_op jit(solution)/shard_map/all_to_all | solution.py:105
  106.4 0.5 reshape.395
  106.9 0.5 reshape.396
  107.4 1.1 fusion.62
  108.5 1.1 add_bitcast_fusion
  109.9 5.0 %multiply_reduce_fusion = (f32[]{:T(128)}, f32[24,192,192]{2,1,0:T(8,128)S(1)}) fusion(f32[192]{0:T(256)S(1)} %get-tuple-element.29, f32[24,192]{1,0:T(8,128)S(1)} %broadcast_add_fusion, f32[192]{0:T(256)S(1)} %get-tuple-element.28, f32[24,192]{1,0:T(8,128)S(1)} %broadcast_multiply_fusion, f32[24,96,192]{2,1,0:T(8,128)S(1)} %bitcast.144, ...), kind=kOutput, calls=%fused_computation | convolution fusion | flops 516870144 | bytes 5347780 | tf_op jit(solution)/shard_map/dot_general | solution.py:89
  114.9 3.8 %fusion = f32[24,192,96]{1,2,0:T(8,128)S(1)} fusion(f32[24,192,192]{2,1,0:T(8,128)S(1)} %get-tuple-element.25, f32[192]{0:T(256)S(1)} %get-tuple-element.29, f32[24,192]{1,0:T(8,128)S(1)} %broadcast_add_fusion, f32[192]{0:T(256)S(1)} %get-tuple-element.28, f32[24,192]{1,0:T(8,128)S(1)} %broadcast_multiply_fusion, s32[192]{0:T(256)S(1)} %add_select_fusion.4, ...), kind=kOutput, calls=%fused_computation.2 | convolution fusion | flops 515100672 | bytes 5347776 | tf_op jit(solution)/shard_map/dot_general | solution.py:89
  118.7 1.8 %convolution_bitcast_fusion.1 = f32[2,4,24,1,24,48]{5,4,0,1,2,3:T(8,128)S(1)} fusion(f32[24,4,24,192,1]{3,2,4,1,0:T(8,128)S(1)} %bitcast.143, s32[192]{0:T(256)S(1)} %add_select_fusion.4, s32[2,48]{1,0:T(2,128)S(1)} %copy-done.5, pred[192]{0:T(512)(128)(4,1)S(1)} %iota_compare_fusion), kind=kOutput, calls=%fused_computation.12 | convolution fusion | flops 254988288 | bytes 2655552 | tf_op jit(solution)/shard_map/dot_general | solution.py:89
  120.7 1.7 %reshape.399 = f32[8,24,1,1152]{3,1,0,2:T(8,128)} reshape(f32[2,4,24,1,24,48]{5,4,2,1,0,3:T(8,128)S(1)} %copy.34) | data formatting | bytes 1769472 | tf_op jit(solution)/shard_map/reshape | solution.py:127
  122.3 3.5 %all-to-all-start.2 = ((f32[8,24,1,1152]{3,1,2,0:T(8,128)}), f32[8,24,1,1152]{3,1,2,0:T(8,128)S(1)}, u32[]{:S(2)}, u32[]{:S(2)}) async-start(f32[8,24,1,1152]{3,1,2,0:T(8,128)} %bitcast.138), calls=%async_computation.2 | async-start | bytes 1769472 | tf_op jit(solution)/shard_map/all_to_all | solution.py:129
  126.6 0.5 collective-permute-start.8
  127.0 1.0 collective-permute-done.8
  129.3 7.2 %collective-permute-start.9 = (f32[1]{0:T(128)}, f32[1]{0:T(128)}, u32[]{:S(2)}, u32[]{:S(2)}) collective-permute-start(f32[1]{0:T(128)} %add.514), channel_id=1, source_target_pairs={{0,2},{1,3},{2,0},{3,1},{4,6},{5,7},{6,4},{7,5},{8,10},{9,11},{10,... | collective-permute-start | bytes 20 | tf_op jit(solution)/shard_map/ppermute | solution.py:45
  136.5 2.0 %collective-permute-done.9 = f32[1]{0:T(128)} collective-permute-done((f32[1]{0:T(128)}, f32[1]{0:T(128)}, u32[]{:S(2)}, u32[]{:S(2)}) %collective-permute-start.9) | collective-permute-done | bytes 36 | tf_op jit(solution)/shard_map/ppermute | solution.py:45
  139.2 2.9 %collective-permute-start.10 = (f32[1]{0:T(128)}, f32[1]{0:T(128)}, u32[]{:S(2)}, u32[]{:S(2)}) collective-permute-start(f32[1]{0:T(128)} %add.515), channel_id=1, source_target_pairs={{0,4},{4,0},{1,5},{5,1},{2,6},{6,2},{3,7},{7,3},{8,12},{12,8},{9,1... | collective-permute-start | bytes 20 | tf_op jit(solution)/shard_map/ppermute | solution.py:45
  142.0 0.7 collective-permute-done.10
  143.8 1.0 fusion.27
  144.8 1.0 copy.37
  (43 shorter events, 1.9 us)
Async XLA Ops:
  1.3 4.6 %collective-permute-start.3 = (s32[4,1]{0,1:T(1,128)S(1)}, s32[4,1]{0,1:T(1,128)S(1)}, u32[]{:S(2)}, u32[]{:S(2)}) collective-permute-start(s32[4,1]{0,1:T(1,128)S(1)} %compare_select_fusion.1), channel_id=1, source_target_pairs={{0,8},{8,0},{16,24},{24,16},{1,9},{9,1},{17,25},{25,17},{2,10},{10... | collective-permute-start | bytes 56 | tf_op jit(solution)/shard_map/ppermute | solution.py:45
  5.9 4.6 %collective-permute-start.4 = (s32[4,1]{0,1:T(1,128)S(1)}, s32[4,1]{0,1:T(1,128)S(1)}, u32[]{:S(2)}, u32[]{:S(2)}) collective-permute-start(s32[4,1]{0,1:T(1,128)S(1)} %fusion.366), channel_id=1, source_target_pairs={{0,16},{8,24},{16,0},{24,8},{1,17},{9,25},{17,1},{25,9},{2,18},{10... | collective-permute-start | bytes 56 | tf_op jit(solution)/shard_map/ppermute | solution.py:45
  12.1 5.3 %copy-start = (f32[1,48,24,96]{3,2,1,0:T(8,128)S(1)}, f32[1,48,24,96]{3,2,1,0:T(8,128)}, u32[]{:S(2)}) copy-start(f32[1,48,24,96]{3,2,1,0:T(8,128)} %param.4) | copy-start | bytes 1327108
  12.1 56.9 %all-to-all-start = ((f32[4,1,48,24,96]{4,3,2,1,0:T(8,128)}), f32[4,1,48,24,96]{4,3,2,1,0:T(8,128)S(1)}, u32[]{:S(2)}, u32[]{:S(2)}) async-start(f32[4,1,48,24,96]{4,3,2,1,0:T(8,128)} %select_select_fusion), calls=%async_computation | async-start | bytes 4718592 | tf_op jit(solution)/shard_map/all_to_all | solution.py:147
  17.5 4.7 %collective-permute-start = (f32[1,8,24,96]{3,2,1,0:T(8,128)S(1)}, f32[1,8,24,96]{3,2,1,0:T(8,128)S(1)}, u32[]{:S(2)}, u32[]{:S(2)}) collective-permute-start(f32[1,8,24,96]{3,2,1,0:T(8,128)S(1)} %slice_select_fusion.1), channel_id=1, source_target_pairs={{0,4},{4,0},{1,5},{5,1},{2,6},{6,2},{3,7},{7,3},{8,12},{12,8},{9,1... | collective-permute-start | bytes 221192 | tf_op jit(solution)/shard_map/ppermute | solution.py:25
  22.2 4.1 %copy-start.1 = (f32[1,8,24,96]{3,2,1,0:T(8,128)}, f32[1,8,24,96]{3,2,1,0:T(8,128)S(1)}, u32[]{:S(2)}) copy-start(f32[1,8,24,96]{3,2,1,0:T(8,128)S(1)} %get-tuple-element.18) | copy-start | bytes 221188
  22.2 4.1 %copy-start.2 = (f32[1,8,24,96]{3,2,1,0:T(8,128)}, f32[1,8,24,96]{3,2,1,0:T(8,128)S(1)}, u32[]{:S(2)}) copy-start(f32[1,8,24,96]{3,2,1,0:T(8,128)S(1)} %get-tuple-element.19) | copy-start | bytes 221188
  23.0 47.7 %collective-permute-start.1 = (f32[1,64,8,96]{3,2,1,0:T(8,128)}, f32[1,64,8,96]{3,2,1,0:T(8,128)}, u32[]{:S(2)}, u32[]{:S(2)}) collective-permute-start(f32[1,64,8,96]{3,2,1,0:T(8,128)} %get-tuple-element.14), channel_id=1, source_target_pairs={{0,1},{1,2},{2,3},{4,5},{5,6},{6,7},{8,9},{9,10},{10,11},{12,13},{... | collective-permute-start | bytes 589832 | tf_op jit(solution)/shard_map/ppermute | solution.py:30
  25.0 45.7 %collective-permute-start.2 = (f32[1,64,8,96]{3,2,1,0:T(8,128)}, f32[1,64,8,96]{3,2,1,0:T(8,128)}, u32[]{:S(2)}, u32[]{:S(2)}) collective-permute-start(f32[1,64,8,96]{3,2,1,0:T(8,128)} %get-tuple-element.15), channel_id=1, source_target_pairs={{1,0},{2,1},{3,2},{5,4},{6,5},{7,6},{9,8},{10,9},{11,10},{13,12},{... | collective-permute-start | bytes 589832 | tf_op jit(solution)/shard_map/ppermute | solution.py:31
  69.2 7.4 %copy-start.4 = (s32[40]{0:T(128)S(1)}, s32[40]{0:T(128)}, u32[]{:S(2)}) copy-start(s32[40]{0:T(128)} %iota_add_fusion.1) | copy-start | bytes 484
  69.2 4.7 %collective-permute-start.5 = (f32[1,8,24,96]{3,2,1,0:T(8,128)S(1)}, f32[1,8,24,96]{3,2,1,0:T(8,128)S(1)}, u32[]{:S(2)}, u32[]{:S(2)}) collective-permute-start(f32[1,8,24,96]{3,2,1,0:T(8,128)S(1)} %slice_select_fusion), channel_id=1, source_target_pairs={{0,4},{4,0},{1,5},{5,1},{2,6},{6,2},{3,7},{7,3},{8,12},{12,8},{9,1... | collective-permute-start | bytes 221192 | tf_op jit(solution)/shard_map/ppermute | solution.py:25
  74.0 3.5 %collective-permute-start.6 = (f32[1,64,8,96]{3,2,1,0:T(8,128)S(1)}, f32[1,64,8,96]{3,2,1,0:T(8,128)S(1)}, u32[]{:S(2)}, u32[]{:S(2)}) collective-permute-start(f32[1,64,8,96]{3,2,1,0:T(8,128)S(1)} %get-tuple-element.16), channel_id=1, source_target_pairs={{0,1},{1,2},{2,3},{4,5},{5,6},{6,7},{8,9},{9,10},{10,11},{12,13},{... | collective-permute-start | bytes 589832 | tf_op jit(solution)/shard_map/ppermute | solution.py:30
  75.3 5.2 %collective-permute-start.7 = (f32[1,64,8,96]{3,2,1,0:T(8,128)S(1)}, f32[1,64,8,96]{3,2,1,0:T(8,128)S(1)}, u32[]{:S(2)}, u32[]{:S(2)}) collective-permute-start(f32[1,64,8,96]{3,2,1,0:T(8,128)S(1)} %get-tuple-element.17), channel_id=1, source_target_pairs={{1,0},{2,1},{3,2},{5,4},{6,5},{7,6},{9,8},{10,9},{11,10},{13,12},{... | collective-permute-start | bytes 589832 | tf_op jit(solution)/shard_map/ppermute | solution.py:31
  77.4 5.1 %copy-start.3 = (s32[64]{0:T(128)S(1)}, s32[64]{0:T(128)}, u32[]{:S(2)}) copy-start(s32[64]{0:T(128)} %iota_add_fusion.2) | copy-start | bytes 772
  81.7 2.4 %copy-start.6 = (pred[8,24]{1,0:T(8,128)(4,1)S(1)}, pred[8,24]{1,0:T(8,128)(4,1)}, u32[]{:S(2)}) copy-start(pred[8,24]{1,0:T(8,128)(4,1)} %fusion.128) | copy-start | bytes 580
  83.3 9.9 %copy-start.8 = (f32[24]{0:T(128)S(1)}, f32[24]{0:T(128)}, u32[]{:S(2)}) copy-start(f32[24]{0:T(128)} %get-tuple-element.26) | copy-start | bytes 292
  83.3 9.9 %copy-start.7 = (f32[24]{0:T(128)S(1)}, f32[24]{0:T(128)}, u32[]{:S(2)}) copy-start(f32[24]{0:T(128)} %get-tuple-element.27) | copy-start | bytes 292
  86.0 20.3 %all-to-all-start.1 = ((f32[8,24,1,1152]{3,1,2,0:T(8,128)}), f32[8,24,1,1152]{3,1,2,0:T(8,128)S(1)}, u32[]{:S(2)}, u32[]{:S(2)}) async-start(f32[8,24,1,1152]{3,1,2,0:T(8,128)} %convolution_bitcast_fusion), calls=%async_computation.1 | async-start | bytes 1769472 | tf_op jit(solution)/shard_map/all_to_all | solution.py:105
  114.9 3.8 %copy-start.5 = (s32[2,48]{1,0:T(2,128)S(1)}, s32[2,48]{1,0:T(2,128)}, u32[]{:S(2)}) copy-start(s32[2,48]{1,0:T(2,128)} %multiply_add_fusion.1) | copy-start | bytes 1156
  122.3 21.0 %all-to-all-start.2 = ((f32[8,24,1,1152]{3,1,2,0:T(8,128)}), f32[8,24,1,1152]{3,1,2,0:T(8,128)S(1)}, u32[]{:S(2)}, u32[]{:S(2)}) async-start(f32[8,24,1,1152]{3,1,2,0:T(8,128)} %bitcast.138), calls=%async_computation.2 | async-start | bytes 1769472 | tf_op jit(solution)/shard_map/all_to_all | solution.py:129
  126.6 1.4 collective-permute-start.8
  129.3 9.3 %collective-permute-start.9 = (f32[1]{0:T(128)}, f32[1]{0:T(128)}, u32[]{:S(2)}, u32[]{:S(2)}) collective-permute-start(f32[1]{0:T(128)} %add.514), channel_id=1, source_target_pairs={{0,2},{1,3},{2,0},{3,1},{4,6},{5,7},{6,4},{7,5},{8,10},{9,11},{10,... | collective-permute-start | bytes 20 | tf_op jit(solution)/shard_map/ppermute | solution.py:45
  139.2 3.6 %collective-permute-start.10 = (f32[1]{0:T(128)}, f32[1]{0:T(128)}, u32[]{:S(2)}, u32[]{:S(2)}) collective-permute-start(f32[1]{0:T(128)} %add.515), channel_id=1, source_target_pairs={{0,4},{4,0},{1,5},{5,1},{2,6},{6,2},{3,7},{7,3},{8,12},{12,8},{9,1... | collective-permute-start | bytes 20 | tf_op jit(solution)/shard_map/ppermute | solution.py:45

commit v17 on v16

--- a/solution.py
+++ b/solution.py
@@ -91,7 +91,22 @@
     )
 
 
-def potentials(density):
+def channel_weight(length):
+    period = 2 * length
+    width = period // (lax.axis_size("gy") * lax.axis_size("gz"))
+    own = lax.axis_index(("gy", "gz")) * width + jnp.arange(width, dtype=jnp.int32)
+    _, lattice_x, fold_x = channel_of(own, length)
+    _, lattice_all, fold_all = channel_of(jnp.arange(period, dtype=jnp.int32), length)
+    weight = (
+        fold_x[:, None, None] * fold_all[None, :, None] * fold_all[None, None, :]
+    ) / (
+        (lattice_x[:, None, None] + lattice_all[None, :, None] + lattice_all[None, None, :] + SCREEN)
+        * float(period**3)
+    )
+    return weight
+
+
+def potentials(density, weight):
     pair_count, rows_y, rows_z, length = density.shape
     period = 2 * length
     count_y = lax.axis_size("gy")
@@ -110,15 +125,6 @@
         along_y = along_y + contract(got[part], table_y[part], 4, 0)
     along_y = along_y.transpose(1, 2, 0, 3, 4).reshape(width, pair_count, count_z * rows_z, period)
     spectrum = contract(along_y, table, 2, 0)
-    own = lax.axis_index(("gy", "gz")) * width + jnp.arange(width, dtype=jnp.int32)
-    _, lattice_x, fold_x = channel_of(own, length)
-    _, lattice_all, fold_all = channel_of(jnp.arange(period, dtype=jnp.int32), length)
-    weight = (
-        fold_x[:, None, None] * fold_all[None, :, None] * fold_all[None, None, :]
-    ) / (
-        (lattice_x[:, None, None] + lattice_all[None, :, None] + lattice_all[None, None, :] + SCREEN)
-        * float(period**3)
-    )
     weighted = spectrum * weight[:, None]
     energy_part = jnp.sum(weighted * spectrum, axis=(0, 2, 3))
     back_y = contract(weighted, table, 3, 1)
@@ -145,10 +151,11 @@
         hit = (wanted == first_owned + number)[:, :, None, None, None]
         slots = jnp.where(hit, j_coeff[number][None, None], slots)
     arrived = lax.all_to_all(slots, "band", 0, 0, tiled=True)
+    arrived, weight = lax.optimization_barrier((arrived, channel_weight(j_coeff.shape[3])))
     own_orbital = synthesize(extended(i_coeff, sides, 8))[0]
     partner = synthesize(extended(jnp.sum(arrived, axis=0), sides, 8))
     density = own_orbital[None] * partner
-    potential, energy_part = potentials(density)
+    potential, energy_part = potentials(density, weight)
     weights = pair_occ[0].astype(jnp.float32)
     applied = -jnp.sum(weights[:, None, None, None] * potential * partner, axis=0)
     length = own_orbital.shape[2]

time: 147 us -> 145 us (0.986)
  matrix products: 22.5 us -> 19.7 us
    div x0 -> x1, other arithmetic: none -> 3.25 us  [channel_weight(): fold_x[:, None, None] * fold_all[None, :, None] * fold_all[None, None, :]...]
    dot_general x7, matrix products: 15.7 us -> 12.9 us  [contract(): lax.dot_general(left, right, (((left_dim,), (right_dim,)), ((), ())), pre...]
  transfers between devices with their start and end apart: 14 -> 14, of which waited for: 10 -> 9; matrix products, arithmetic and copies ran while one was open for 6% -> 7% of each run, Pallas kernels for 0% -> 0%
where the time goes in v17:
time: 145 us; the launch traced here: 144 us
  waiting for transfers between devices  64.6 us (45%)
  starting transfers between devices  41.6 us (29%)
  matrix products  19.7 us (14%)
  other arithmetic  6.8 us (5%)
  local copies, waits for them, and re-layouts  5.91 us (4%)
  between operations  5.77 us (4%)
    all_to_all x1, waiting for transfers between devices, shards(): arrived = lax.all_to_all(slots, 'band', 0, 0, tiled=True)  42.2 us
    ppermute x5, starting transfers between devices, group_sum(): lax.ppermute(total, axis, [(i, i ^ step) for i in range(count)])  16.6 us
    dot_general x7, matrix products, contract(): lax.dot_general(left, right, (((left_dim,), (right_dim,)), ((), ())), pre...  12.9 us
    all_to_all x1, waiting for transfers between devices, potentials(): got = lax.all_to_all(send, ('gy', 'gz'), 0, 0, tiled=True)  12.7 us
    all_to_all x1, starting transfers between devices, potentials(): got = lax.all_to_all(send, ('gy', 'gz'), 0, 0, tiled=True)  7.13 us
    ppermute x5, waiting for transfers between devices, group_sum(): lax.ppermute(total, axis, [(i, i ^ step) for i in range(count)])  5.84 us
    all_to_all x1, starting transfers between devices, shards(): arrived = lax.all_to_all(slots, 'band', 0, 0, tiled=True)  5.33 us
    dot_general x2, matrix products, synthesize(): step_one = jnp.matmul(padded, matrix_x, precision=precise_mode)  3.62 us
  transfers between devices with their start and end apart: 14, of which 9 were waited for; matrix products, arithmetic and copies ran while one was open for 7% of the time, Pallas kernels for 0%

profile of v17, /device:TPU:0, one launch (start us, length us, event | category | flops | bytes accessed | tf_op | source)
XLA Modules:
  0.0 144.3 jit_solution(16178619296690111072)
XLA Ops:
  1.3 3.1 %collective-permute-start.3 = (s32[4,1]{0,1:T(1,128)S(1)}, s32[4,1]{0,1:T(1,128)S(1)}, u32[]{:S(2)}, u32[]{:S(2)}) collective-permute-start(s32[4,1]{0,1:T(1,128)S(1)} %compare_select_fusion.1), channel_id=1, source_target_pairs={{0,8},{8,0},{16,24},{24,16},{1,9},{9,1},{17,25},{25,17},{2,10},{10... | collective-permute-start | bytes 56 | tf_op jit(solution)/shard_map/ppermute | solution.py:45
  4.4 1.3 slice_bitcast_fusion.1
  5.7 0.2 collective-permute-done.3
  5.9 3.0 %collective-permute-start.4 = (s32[4,1]{0,1:T(1,128)S(1)}, s32[4,1]{0,1:T(1,128)S(1)}, u32[]{:S(2)}, u32[]{:S(2)}) collective-permute-start(s32[4,1]{0,1:T(1,128)S(1)} %fusion.359), channel_id=1, source_target_pairs={{0,16},{8,24},{16,0},{24,8},{1,17},{9,25},{17,1},{25,9},{2,18},{10... | collective-permute-start | bytes 56 | tf_op jit(solution)/shard_map/ppermute | solution.py:45
  8.9 1.5 %collective-permute-done.4 = s32[4,1]{0,1:T(1,128)S(1)} collective-permute-done((s32[4,1]{0,1:T(1,128)S(1)}, s32[4,1]{0,1:T(1,128)S(1)}, u32[]{:S(2)}, u32[]{:S(2)}) %collective-permute-start.4) | collective-permute-done | bytes 48 | tf_op jit(solution)/shard_map/ppermute | solution.py:45
  10.5 1.7 %select_select_fusion = f32[4,1,48,24,96]{4,3,2,1,0:T(8,128)} fusion(f32[48,24,96]{2,1,0:T(8,128)S(1)} %get-tuple-element.13, f32[48,24,96]{2,1,0:T(8,128)S(1)} %get-tuple-element.12, pred[4]{0:T(512)(128)(4,1)S(1)} %get-tuple-element.25, pred[4]{0:T(512)(128)(4,1)S(1)} %get-tuple-element.24), kind=kLoop, calls=%fused_computation.6 | loop fusion | flops 884736 | bytes 2654216 | tf_op jit(solution)/shard_map/jit(_where)/select_n | solution.py:152
  12.1 5.3 %all-to-all-start = ((f32[4,1,48,24,96]{4,3,2,1,0:T(8,128)}), f32[4,1,48,24,96]{4,3,2,1,0:T(8,128)S(1)}, u32[]{:S(2)}, u32[]{:S(2)}) async-start(f32[4,1,48,24,96]{4,3,2,1,0:T(8,128)} %select_select_fusion), calls=%async_computation | async-start | bytes 4718592 | tf_op jit(solution)/shard_map/all_to_all | solution.py:153
  17.5 1.6 %collective-permute-start = (f32[1,8,24,96]{3,2,1,0:T(8,128)S(1)}, f32[1,8,24,96]{3,2,1,0:T(8,128)S(1)}, u32[]{:S(2)}, u32[]{:S(2)}) collective-permute-start(f32[1,8,24,96]{3,2,1,0:T(8,128)S(1)} %slice_select_fusion.1), channel_id=1, source_target_pairs={{0,4},{4,0},{1,5},{5,1},{2,6},{6,2},{3,7},{7,3},{8,12},{12,8},{9,1... | collective-permute-start | bytes 221192 | tf_op jit(solution)/shard_map/ppermute | solution.py:25
  19.3 3.2 %multiply_divide_fusion = f32[24,192,192]{2,1,0:T(8,128)} fusion(f32[192]{0:T(256)S(1)} %get-tuple-element.31, f32[24,192]{1,0:T(8,128)S(1)} %broadcast_add_fusion, f32[192]{0:T(256)S(1)} %get-tuple-element.30, f32[24,192]{1,0:T(8,128)S(1)} %broadcast_multiply_fusion), kind=kLoop, calls=%fused_computation.1 | loop fusion | flops 4423680 | bytes 3577344 | tf_op jit(solution)/shard_map/div | solution.py:100
  22.6 0.9 pad_maximum_fusion.5
  23.5 2.0 %collective-permute-start.1 = (f32[1,64,8,96]{3,2,1,0:T(8,128)}, f32[1,64,8,96]{3,2,1,0:T(8,128)}, u32[]{:S(2)}, u32[]{:S(2)}) collective-permute-start(f32[1,64,8,96]{3,2,1,0:T(8,128)} %get-tuple-element.16), channel_id=1, source_target_pairs={{0,1},{1,2},{2,3},{4,5},{5,6},{6,7},{8,9},{9,10},{10,11},{12,13},{... | collective-permute-start | bytes 589832 | tf_op jit(solution)/shard_map/ppermute | solution.py:30
  25.5 1.3 collective-permute-start.2
  26.8 42.2 %all-to-all-done = f32[4,1,48,24,96]{4,3,2,1,0:T(8,128)S(1)} async-done(((f32[4,1,48,24,96]{4,3,2,1,0:T(8,128)}), f32[4,1,48,24,96]{4,3,2,1,0:T(8,128)S(1)}, u32[]{:S(2)}, u32[]{:S(2)}) %all-to-all-start) | async-done | bytes 1769504 | tf_op jit(solution)/shard_map/all_to_all | solution.py:153
  69.0 0.2 reduce_sum.26
  69.2 1.6 %collective-permute-start.5 = (f32[1,8,24,96]{3,2,1,0:T(8,128)S(1)}, f32[1,8,24,96]{3,2,1,0:T(8,128)S(1)}, u32[]{:S(2)}, u32[]{:S(2)}) collective-permute-start(f32[1,8,24,96]{3,2,1,0:T(8,128)S(1)} %slice_select_fusion), channel_id=1, source_target_pairs={{0,4},{4,0},{1,5},{5,1},{2,6},{6,2},{3,7},{7,3},{8,12},{12,8},{9,1... | collective-permute-start | bytes 221192 | tf_op jit(solution)/shard_map/ppermute | solution.py:25
  70.8 2.4 %fusion.2 = f32[64,40,96]{2,1,0:T(8,128)S(1)} fusion(f32[1,64,8,96]{3,2,1,0:T(8,128)} %collective-permute-done.2, f32[1,8,24,96]{3,2,1,0:T(8,128)} %copy-done.2, f32[1,48,24,96]{3,2,1,0:T(8,128)S(1)} %copy-done, f32[1,8,24,96]{3,2,1,0:T(8,128)} %copy-done.1, f32[1,64,8,96]{3,2,1,0:T(8,128)} %collective-permute-done.1), kind=kOutput, calls=%fused_computation.9 | convolution fusion | flops 284540928 | bytes 1966080 | tf_op jit(solution)/shard_map/dot_general | solution.py:65
  73.2 0.7 collective-permute-done.5
  74.0 1.3 collective-permute-start.6
  75.3 1.3 collective-permute-start.7
  76.6 0.8 convolution_bitcast_fusion.3
  77.4 3.0 %collective-permute-done.7 = f32[1,64,8,96]{3,2,1,0:T(8,128)S(1)} collective-permute-done((f32[1,64,8,96]{3,2,1,0:T(8,128)S(1)}, f32[1,64,8,96]{3,2,1,0:T(8,128)S(1)}, u32[]{:S(2)}, u32[]{:S(2)}) %collective-permute-start.7) | collective-permute-done | bytes 196640 | tf_op jit(solution)/shard_map/ppermute | solution.py:31
  80.5 1.2 fusion.11
  81.7 0.8 convolution_bitcast_fusion.2
  82.5 0.8 fusion.23
  83.3 0.8 convolution_multiply_fusion.1
  84.1 1.9 %convolution_bitcast_fusion = f32[8,24,1,1152]{3,1,2,0:T(8,128)} fusion(f32[1152,96,1]{1,0,2:T(8,128)S(1)} %bitcast.147, s32[8,24]{1,0:T(8,128)S(1)} %add_select_fusion.3, pred[8,24]{1,0:T(8,128)(4,1)S(1)} %fusion.123), kind=kOutput, calls=%fused_computation.4 | convolution fusion | flops 127586304 | bytes 1328064 | tf_op jit(solution)/shard_map/dot_general | solution.py:89
  86.0 7.1 %all-to-all-start.1 = ((f32[8,24,1,1152]{3,1,2,0:T(8,128)}), f32[8,24,1,1152]{3,1,2,0:T(8,128)S(1)}, u32[]{:S(2)}, u32[]{:S(2)}) async-start(f32[8,24,1,1152]{3,1,2,0:T(8,128)} %convolution_bitcast_fusion), calls=%async_computation.1 | async-start | bytes 1769472 | tf_op jit(solution)/shard_map/all_to_all | solution.py:120
  93.2 0.4 sine_select_fusion
  93.6 12.7 %all-to-all-done.1 = f32[8,24,1,1152]{3,1,2,0:T(8,128)S(1)} async-done(((f32[8,24,1,1152]{3,1,2,0:T(8,128)}), f32[8,24,1,1152]{3,1,2,0:T(8,128)S(1)}, u32[]{:S(2)}, u32[]{:S(2)}) %all-to-all-start.1) | async-done | bytes 884768 | tf_op jit(solution)/shard_map/all_to_all | solution.py:120
  106.4 0.5 reshape.395
  106.9 0.5 reshape.396
  107.4 1.1 fusion.57
  108.5 1.1 add_bitcast_fusion
  109.6 0.3 copy.22
  109.9 3.3 %multiply_reduce_fusion = (f32[]{:T(128)}, f32[24,192,192]{2,1,0:T(8,128)S(1)}) fusion(f32[24,192,192]{2,1,0:T(8,128)S(1)} %bitcast.138, f32[24,96,192]{2,1,0:T(8,128)S(1)} %bitcast.139, s32[192]{0:T(256)S(1)} %add_select_fusion.4, pred[192]{0:T(512)(128)(4,1)S(1)} %iota_compare_fusion), kind=kOutput, calls=%fused_computation | convolution fusion | flops 512446464 | bytes 8848324 | tf_op jit(solution)/shard_map/dot_general | solution.py:89
  113.3 2.8 %fusion = f32[24,192,96]{1,2,0:T(8,128)S(1)} fusion(f32[24,192,192]{2,1,0:T(8,128)S(1)} %get-tuple-element.27, f32[24,192,192]{2,1,0:T(8,128)S(1)} %bitcast.138, s32[192]{0:T(256)S(1)} %add_select_fusion.4, pred[192]{0:T(512)(128)(4,1)S(1)} %iota_compare_fusion), kind=kOutput, calls=%fused_computation.2 | convolution fusion | flops 510676992 | bytes 8848320 | tf_op jit(solution)/shard_map/dot_general | solution.py:89
  116.1 1.6 %convolution_bitcast_fusion.1 = f32[2,4,24,1,24,48]{5,4,0,1,2,3:T(8,128)S(1)} fusion(f32[24,4,24,192,1]{3,2,4,1,0:T(8,128)S(1)} %bitcast.140, s32[192]{0:T(256)S(1)} %add_select_fusion.4, s32[2,48]{1,0:T(2,128)S(1)} %multiply_add_fusion.1, pred[192]{0:T(512)(128)(4,1)S(1)} %iota_compare_fusion), kind=kOutput, calls=%fused_computation.7 | convolution fusion | flops 254988288 | bytes 2655552 | tf_op jit(solution)/shard_map/dot_general | solution.py:89
  117.9 1.7 %reshape.399 = f32[8,24,1,1152]{3,1,0,2:T(8,128)} reshape(f32[2,4,24,1,24,48]{5,4,2,1,0,3:T(8,128)S(1)} %copy.24) | data formatting | bytes 1769472 | tf_op jit(solution)/shard_map/reshape | solution.py:133
  119.5 3.5 %all-to-all-start.2 = ((f32[8,24,1,1152]{3,1,2,0:T(8,128)}), f32[8,24,1,1152]{3,1,2,0:T(8,128)S(1)}, u32[]{:S(2)}, u32[]{:S(2)}) async-start(f32[8,24,1,1152]{3,1,2,0:T(8,128)} %bitcast.142), calls=%async_computation.2 | async-start | bytes 1769472 | tf_op jit(solution)/shard_map/all_to_all | solution.py:135
  123.7 0.5 collective-permute-start.8
  124.2 1.1 collective-permute-done.8
  126.5 7.2 %collective-permute-start.9 = (f32[1]{0:T(128)}, f32[1]{0:T(128)}, u32[]{:S(2)}, u32[]{:S(2)}) collective-permute-start(f32[1]{0:T(128)} %add.514), channel_id=1, source_target_pairs={{0,2},{1,3},{2,0},{3,1},{4,6},{5,7},{6,4},{7,5},{8,10},{9,11},{10,... | collective-permute-start | bytes 20 | tf_op jit(solution)/shard_map/ppermute | solution.py:45
  133.7 2.2 %collective-permute-done.9 = f32[1]{0:T(128)} collective-permute-done((f32[1]{0:T(128)}, f32[1]{0:T(128)}, u32[]{:S(2)}, u32[]{:S(2)}) %collective-permute-start.9) | collective-permute-done | bytes 36 | tf_op jit(solution)/shard_map/ppermute | solution.py:45
  136.5 2.9 %collective-permute-start.10 = (f32[1]{0:T(128)}, f32[1]{0:T(128)}, u32[]{:S(2)}, u32[]{:S(2)}) collective-permute-start(f32[1]{0:T(128)} %add.515), channel_id=1, source_target_pairs={{0,4},{4,0},{1,5},{5,1},{2,6},{6,2},{3,7},{7,3},{8,12},{12,8},{9,1... | collective-permute-start | bytes 20 | tf_op jit(solution)/shard_map/ppermute | solution.py:45
  139.3 0.9 collective-permute-done.10
  140.8 0.4 copy.26
  141.1 1.0 fusion.22
  142.2 1.0 copy.27
  (37 shorter events, 0.7 us)
Async XLA Ops:
  1.3 4.6 %collective-permute-start.3 = (s32[4,1]{0,1:T(1,128)S(1)}, s32[4,1]{0,1:T(1,128)S(1)}, u32[]{:S(2)}, u32[]{:S(2)}) collective-permute-start(s32[4,1]{0,1:T(1,128)S(1)} %compare_select_fusion.1), channel_id=1, source_target_pairs={{0,8},{8,0},{16,24},{24,16},{1,9},{9,1},{17,25},{25,17},{2,10},{10... | collective-permute-start | bytes 56 | tf_op jit(solution)/shard_map/ppermute | solution.py:45
  5.9 4.6 %collective-permute-start.4 = (s32[4,1]{0,1:T(1,128)S(1)}, s32[4,1]{0,1:T(1,128)S(1)}, u32[]{:S(2)}, u32[]{:S(2)}) collective-permute-start(s32[4,1]{0,1:T(1,128)S(1)} %fusion.359), channel_id=1, source_target_pairs={{0,16},{8,24},{16,0},{24,8},{1,17},{9,25},{17,1},{25,9},{2,18},{10... | collective-permute-start | bytes 56 | tf_op jit(solution)/shard_map/ppermute | solution.py:45
  12.1 5.3 %copy-start = (f32[1,48,24,96]{3,2,1,0:T(8,128)S(1)}, f32[1,48,24,96]{3,2,1,0:T(8,128)}, u32[]{:S(2)}) copy-start(f32[1,48,24,96]{3,2,1,0:T(8,128)} %param.4) | copy-start | bytes 1327108
  12.1 56.9 %all-to-all-start = ((f32[4,1,48,24,96]{4,3,2,1,0:T(8,128)}), f32[4,1,48,24,96]{4,3,2,1,0:T(8,128)S(1)}, u32[]{:S(2)}, u32[]{:S(2)}) async-start(f32[4,1,48,24,96]{4,3,2,1,0:T(8,128)} %select_select_fusion), calls=%async_computation | async-start | bytes 4718592 | tf_op jit(solution)/shard_map/all_to_all | solution.py:153
  17.5 5.1 %collective-permute-start = (f32[1,8,24,96]{3,2,1,0:T(8,128)S(1)}, f32[1,8,24,96]{3,2,1,0:T(8,128)S(1)}, u32[]{:S(2)}, u32[]{:S(2)}) collective-permute-start(f32[1,8,24,96]{3,2,1,0:T(8,128)S(1)} %slice_select_fusion.1), channel_id=1, source_target_pairs={{0,4},{4,0},{1,5},{5,1},{2,6},{6,2},{3,7},{7,3},{8,12},{12,8},{9,1... | collective-permute-start | bytes 221192 | tf_op jit(solution)/shard_map/ppermute | solution.py:25
  22.6 4.2 %copy-start.1 = (f32[1,8,24,96]{3,2,1,0:T(8,128)}, f32[1,8,24,96]{3,2,1,0:T(8,128)S(1)}, u32[]{:S(2)}) copy-start(f32[1,8,24,96]{3,2,1,0:T(8,128)S(1)} %get-tuple-element.20) | copy-start | bytes 221188
  22.6 4.2 %copy-start.2 = (f32[1,8,24,96]{3,2,1,0:T(8,128)}, f32[1,8,24,96]{3,2,1,0:T(8,128)S(1)}, u32[]{:S(2)}) copy-start(f32[1,8,24,96]{3,2,1,0:T(8,128)S(1)} %get-tuple-element.21) | copy-start | bytes 221188
  23.5 47.3 %collective-permute-start.1 = (f32[1,64,8,96]{3,2,1,0:T(8,128)}, f32[1,64,8,96]{3,2,1,0:T(8,128)}, u32[]{:S(2)}, u32[]{:S(2)}) collective-permute-start(f32[1,64,8,96]{3,2,1,0:T(8,128)} %get-tuple-element.16), channel_id=1, source_target_pairs={{0,1},{1,2},{2,3},{4,5},{5,6},{6,7},{8,9},{9,10},{10,11},{12,13},{... | collective-permute-start | bytes 589832 | tf_op jit(solution)/shard_map/ppermute | solution.py:30
  25.5 45.3 %collective-permute-start.2 = (f32[1,64,8,96]{3,2,1,0:T(8,128)}, f32[1,64,8,96]{3,2,1,0:T(8,128)}, u32[]{:S(2)}, u32[]{:S(2)}) collective-permute-start(f32[1,64,8,96]{3,2,1,0:T(8,128)} %get-tuple-element.17), channel_id=1, source_target_pairs={{1,0},{2,1},{3,2},{5,4},{6,5},{7,6},{9,8},{10,9},{11,10},{13,12},{... | collective-permute-start | bytes 589832 | tf_op jit(solution)/shard_map/ppermute | solution.py:31
  69.2 4.7 %collective-permute-start.5 = (f32[1,8,24,96]{3,2,1,0:T(8,128)S(1)}, f32[1,8,24,96]{3,2,1,0:T(8,128)S(1)}, u32[]{:S(2)}, u32[]{:S(2)}) collective-permute-start(f32[1,8,24,96]{3,2,1,0:T(8,128)S(1)} %slice_select_fusion), channel_id=1, source_target_pairs={{0,4},{4,0},{1,5},{5,1},{2,6},{6,2},{3,7},{7,3},{8,12},{12,8},{9,1... | collective-permute-start | bytes 221192 | tf_op jit(solution)/shard_map/ppermute | solution.py:25
  74.0 3.5 %collective-permute-start.6 = (f32[1,64,8,96]{3,2,1,0:T(8,128)S(1)}, f32[1,64,8,96]{3,2,1,0:T(8,128)S(1)}, u32[]{:S(2)}, u32[]{:S(2)}) collective-permute-start(f32[1,64,8,96]{3,2,1,0:T(8,128)S(1)} %get-tuple-element.18), channel_id=1, source_target_pairs={{0,1},{1,2},{2,3},{4,5},{5,6},{6,7},{8,9},{9,10},{10,11},{12,13},{... | collective-permute-start | bytes 589832 | tf_op jit(solution)/shard_map/ppermute | solution.py:30
  75.3 5.2 %collective-permute-start.7 = (f32[1,64,8,96]{3,2,1,0:T(8,128)S(1)}, f32[1,64,8,96]{3,2,1,0:T(8,128)S(1)}, u32[]{:S(2)}, u32[]{:S(2)}) collective-permute-start(f32[1,64,8,96]{3,2,1,0:T(8,128)S(1)} %get-tuple-element.19), channel_id=1, source_target_pairs={{1,0},{2,1},{3,2},{5,4},{6,5},{7,6},{9,8},{10,9},{11,10},{13,12},{... | collective-permute-start | bytes 589832 | tf_op jit(solution)/shard_map/ppermute | solution.py:31
  86.0 20.3 %all-to-all-start.1 = ((f32[8,24,1,1152]{3,1,2,0:T(8,128)}), f32[8,24,1,1152]{3,1,2,0:T(8,128)S(1)}, u32[]{:S(2)}, u32[]{:S(2)}) async-start(f32[8,24,1,1152]{3,1,2,0:T(8,128)} %convolution_bitcast_fusion), calls=%async_computation.1 | async-start | bytes 1769472 | tf_op jit(solution)/shard_map/all_to_all | solution.py:120
  107.4 2.5 %slice-start = ((s8[4718592]{0:T(1024)(128)(4,1)}), s8[4194304]{0:T(1024)(128)(4,1)S(1)}, s32[]{:S(2)}) async-start(s8[4718592]{0:T(1024)(128)(4,1)} %bitcast.137), calls=%async_computation.3 | async-start | bytes 8388608
  108.5 1.4 %slice-start.1 = ((s8[4718592]{0:T(1024)(128)(4,1)}), s8[524288]{0:T(1024)(128)(4,1)S(1)}, s32[]{:S(2)}) async-start(s8[4718592]{0:T(1024)(128)(4,1)} %bitcast.137), calls=%async_computation.4 | async-start | bytes 1048576
  119.5 21.2 %all-to-all-start.2 = ((f32[8,24,1,1152]{3,1,2,0:T(8,128)}), f32[8,24,1,1152]{3,1,2,0:T(8,128)S(1)}, u32[]{:S(2)}, u32[]{:S(2)}) async-start(f32[8,24,1,1152]{3,1,2,0:T(8,128)} %bitcast.142), calls=%async_computation.2 | async-start | bytes 1769472 | tf_op jit(solution)/shard_map/all_to_all | solution.py:135
  123.7 1.6 %collective-permute-start.8 = (f32[1]{0:T(128)}, f32[1]{0:T(128)}, u32[]{:S(2)}, u32[]{:S(2)}) collective-permute-start(f32[1]{0:T(128)} %bitcast.48), channel_id=1, source_target_pairs={{0,1},{1,0},{2,3},{3,2},{4,5},{5,4},{6,7},{7,6},{8,9},{9,8},{10,11... | collective-permute-start | bytes 20 | tf_op jit(solution)/shard_map/ppermute | solution.py:45
  126.5 9.4 %collective-permute-start.9 = (f32[1]{0:T(128)}, f32[1]{0:T(128)}, u32[]{:S(2)}, u32[]{:S(2)}) collective-permute-start(f32[1]{0:T(128)} %add.514), channel_id=1, source_target_pairs={{0,2},{1,3},{2,0},{3,1},{4,6},{5,7},{6,4},{7,5},{8,10},{9,11},{10,... | collective-permute-start | bytes 20 | tf_op jit(solution)/shard_map/ppermute | solution.py:45
  136.5 3.7 %collective-permute-start.10 = (f32[1]{0:T(128)}, f32[1]{0:T(128)}, u32[]{:S(2)}, u32[]{:S(2)}) collective-permute-start(f32[1]{0:T(128)} %add.515), channel_id=1, source_target_pairs={{0,4},{4,0},{1,5},{5,1},{2,6},{6,2},{3,7},{7,3},{8,12},{12,8},{9,1... | collective-permute-start | bytes 20 | tf_op jit(solution)/shard_map/ppermute | solution.py:45

commit v18 on v17

--- a/solution.py
+++ b/solution.py
@@ -153,7 +153,7 @@
     arrived = lax.all_to_all(slots, "band", 0, 0, tiled=True)
     arrived, weight = lax.optimization_barrier((arrived, channel_weight(j_coeff.shape[3])))
     own_orbital = synthesize(extended(i_coeff, sides, 8))[0]
-    partner = synthesize(extended(jnp.sum(arrived, axis=0), sides, 8))
+    partner = synthesize(extended(jnp.sum(arrived, axis=0), sides[::-1], 8))
     density = own_orbital[None] * partner
     potential, energy_part = potentials(density, weight)
     weights = pair_occ[0].astype(jnp.float32)

time: 145 us -> 144 us (level)
    ppermute x2, waiting for transfers between devices: 0.74 us -> 3 us  [extended(): got = lax.ppermute(jnp.where(first, tail, head), axis, [(0, 1), (1, 0)])]
    ppermute x2, waiting for transfers between devices: 3.03 us -> 1.36 us  [extended(): after = lax.ppermute(head, axis, [(i + 1, i) for i in range(count - 1)])]
where the time goes in v18:
time: 144 us
  waiting for transfers between devices  64.8 us (45%)
  starting transfers between devices  40.6 us (28%)
  matrix products  19.7 us (14%)
  other arithmetic  6.77 us (5%)
  local copies, waits for them, and re-layouts  5.92 us (4%)
  between operations  5.78 us (4%)
    all_to_all x1, waiting for transfers between devices, shards(): arrived = lax.all_to_all(slots, 'band', 0, 0, tiled=True)  42.2 us
    ppermute x5, starting transfers between devices, group_sum(): lax.ppermute(total, axis, [(i, i ^ step) for i in range(count)])  16.6 us
    dot_general x7, matrix products, contract(): lax.dot_general(left, right, (((left_dim,), (right_dim,)), ((), ())), pre...  12.9 us
    all_to_all x1, waiting for transfers between devices, potentials(): got = lax.all_to_all(send, ('gy', 'gz'), 0, 0, tiled=True)  12.4 us
    all_to_all x1, starting transfers between devices, potentials(): got = lax.all_to_all(send, ('gy', 'gz'), 0, 0, tiled=True)  6.08 us
    ppermute x5, waiting for transfers between devices, group_sum(): lax.ppermute(total, axis, [(i, i ^ step) for i in range(count)])  5.84 us
    all_to_all x1, starting transfers between devices, shards(): arrived = lax.all_to_all(slots, 'band', 0, 0, tiled=True)  5.33 us
    dot_general x2, matrix products, synthesize(): step_one = jnp.matmul(padded, matrix_x, precision=precise_mode)  3.63 us
  transfers between devices with their start and end apart: 14, of which 9 were waited for; matrix products, arithmetic and copies ran while one was open for 7% of the time, Pallas kernels for 0%

profile of v18, /device:TPU:0, one launch (start us, length us, event | category | flops | bytes accessed | tf_op | source)
XLA Modules:
  0.0 143.6 jit_solution(13179085002763858650)
XLA Ops:
  1.3 3.1 %collective-permute-start.3 = (s32[4,1]{0,1:T(1,128)S(1)}, s32[4,1]{0,1:T(1,128)S(1)}, u32[]{:S(2)}, u32[]{:S(2)}) collective-permute-start(s32[4,1]{0,1:T(1,128)S(1)} %compare_select_fusion.1), channel_id=1, source_target_pairs={{0,8},{8,0},{16,24},{24,16},{1,9},{9,1},{17,25},{25,17},{2,10},{10... | collective-permute-start | bytes 56 | tf_op jit(solution)/shard_map/ppermute | solution.py:45
  4.4 1.3 slice_bitcast_fusion.1
  5.7 0.2 collective-permute-done.3
  5.9 3.0 %collective-permute-start.4 = (s32[4,1]{0,1:T(1,128)S(1)}, s32[4,1]{0,1:T(1,128)S(1)}, u32[]{:S(2)}, u32[]{:S(2)}) collective-permute-start(s32[4,1]{0,1:T(1,128)S(1)} %fusion.361), channel_id=1, source_target_pairs={{0,16},{8,24},{16,0},{24,8},{1,17},{9,25},{17,1},{25,9},{2,18},{10... | collective-permute-start | bytes 56 | tf_op jit(solution)/shard_map/ppermute | solution.py:45
  8.9 1.5 %collective-permute-done.4 = s32[4,1]{0,1:T(1,128)S(1)} collective-permute-done((s32[4,1]{0,1:T(1,128)S(1)}, s32[4,1]{0,1:T(1,128)S(1)}, u32[]{:S(2)}, u32[]{:S(2)}) %collective-permute-start.4) | collective-permute-done | bytes 48 | tf_op jit(solution)/shard_map/ppermute | solution.py:45
  10.5 1.7 %select_select_fusion = f32[4,1,48,24,96]{4,3,2,1,0:T(8,128)} fusion(f32[48,24,96]{2,1,0:T(8,128)S(1)} %get-tuple-element.13, f32[48,24,96]{2,1,0:T(8,128)S(1)} %get-tuple-element.12, pred[4]{0:T(512)(128)(4,1)S(1)} %get-tuple-element.25, pred[4]{0:T(512)(128)(4,1)S(1)} %get-tuple-element.24), kind=kLoop, calls=%fused_computation.6 | loop fusion | flops 884736 | bytes 2654216 | tf_op jit(solution)/shard_map/jit(_where)/select_n | solution.py:152
  12.1 5.3 %all-to-all-start = ((f32[4,1,48,24,96]{4,3,2,1,0:T(8,128)}), f32[4,1,48,24,96]{4,3,2,1,0:T(8,128)S(1)}, u32[]{:S(2)}, u32[]{:S(2)}) async-start(f32[4,1,48,24,96]{4,3,2,1,0:T(8,128)} %select_select_fusion), calls=%async_computation | async-start | bytes 4718592 | tf_op jit(solution)/shard_map/all_to_all | solution.py:153
  17.5 1.6 %collective-permute-start = (f32[1,8,24,96]{3,2,1,0:T(8,128)S(1)}, f32[1,8,24,96]{3,2,1,0:T(8,128)S(1)}, u32[]{:S(2)}, u32[]{:S(2)}) collective-permute-start(f32[1,8,24,96]{3,2,1,0:T(8,128)S(1)} %slice_select_fusion), channel_id=1, source_target_pairs={{0,4},{4,0},{1,5},{5,1},{2,6},{6,2},{3,7},{7,3},{8,12},{12,8},{9,1... | collective-permute-start | bytes 221192 | tf_op jit(solution)/shard_map/ppermute | solution.py:25
  19.3 3.2 %multiply_divide_fusion = f32[24,192,192]{2,1,0:T(8,128)} fusion(f32[192]{0:T(256)S(1)} %get-tuple-element.31, f32[24,192]{1,0:T(8,128)S(1)} %broadcast_add_fusion, f32[192]{0:T(256)S(1)} %get-tuple-element.30, f32[24,192]{1,0:T(8,128)S(1)} %broadcast_multiply_fusion), kind=kLoop, calls=%fused_computation.1 | loop fusion | flops 4423680 | bytes 3577344 | tf_op jit(solution)/shard_map/div | solution.py:100
  22.6 0.9 pad_maximum_fusion.2
  23.5 2.0 %collective-permute-start.1 = (f32[1,64,8,96]{3,2,1,0:T(8,128)}, f32[1,64,8,96]{3,2,1,0:T(8,128)}, u32[]{:S(2)}, u32[]{:S(2)}) collective-permute-start(f32[1,64,8,96]{3,2,1,0:T(8,128)} %get-tuple-element.16), channel_id=1, source_target_pairs={{0,1},{1,2},{2,3},{4,5},{5,6},{6,7},{8,9},{9,10},{10,11},{12,13},{... | collective-permute-start | bytes 589832 | tf_op jit(solution)/shard_map/ppermute | solution.py:30
  25.5 1.3 collective-permute-start.2
  26.8 42.2 %all-to-all-done = f32[4,1,48,24,96]{4,3,2,1,0:T(8,128)S(1)} async-done(((f32[4,1,48,24,96]{4,3,2,1,0:T(8,128)}), f32[4,1,48,24,96]{4,3,2,1,0:T(8,128)S(1)}, u32[]{:S(2)}, u32[]{:S(2)}) %all-to-all-start) | async-done | bytes 1769504 | tf_op jit(solution)/shard_map/all_to_all | solution.py:153
  69.0 0.2 reduce_sum.26
  69.2 1.3 collective-permute-start.5
  70.5 1.3 collective-permute-start.6
  71.9 2.4 %fusion.2 = f32[64,40,96]{2,1,0:T(8,128)S(1)} fusion(f32[1,64,8,96]{3,2,1,0:T(8,128)} %collective-permute-done.2, f32[1,8,24,96]{3,2,1,0:T(8,128)} %copy-done.2, f32[1,48,24,96]{3,2,1,0:T(8,128)S(1)} %copy-done, f32[1,8,24,96]{3,2,1,0:T(8,128)} %copy-done.1, f32[1,64,8,96]{3,2,1,0:T(8,128)} %collective-permute-done.1), kind=kOutput, calls=%fused_computation.9 | convolution fusion | flops 284540928 | bytes 1966080 | tf_op jit(solution)/shard_map/dot_general | solution.py:65
  74.3 1.4 collective-permute-done.6
  75.6 1.6 %collective-permute-start.7 = (f32[1,8,40,96]{3,2,1,0:T(8,128)S(1)}, f32[1,8,40,96]{3,2,1,0:T(8,128)S(1)}, u32[]{:S(2)}, u32[]{:S(2)}) collective-permute-start(f32[1,8,40,96]{3,2,1,0:T(8,128)S(1)} %fusion.26), channel_id=1, source_target_pairs={{0,4},{4,0},{1,5},{5,1},{2,6},{6,2},{3,7},{7,3},{8,12},{12,8},{9,1... | collective-permute-start | bytes 368648 | tf_op jit(solution)/shard_map/ppermute | solution.py:25
  77.2 0.8 convolution_bitcast_fusion.3
  78.0 3.0 %collective-permute-done.7 = f32[1,8,40,96]{3,2,1,0:T(8,128)S(1)} collective-permute-done((f32[1,8,40,96]{3,2,1,0:T(8,128)S(1)}, f32[1,8,40,96]{3,2,1,0:T(8,128)S(1)}, u32[]{:S(2)}, u32[]{:S(2)}) %collective-permute-start.7) | collective-permute-done | bytes 122912 | tf_op jit(solution)/shard_map/ppermute | solution.py:25
  81.1 1.2 fusion.11
  82.3 0.8 convolution_bitcast_fusion.2
  83.2 0.8 fusion.23
  83.9 0.8 convolution_multiply_fusion.1
  84.7 1.9 %convolution_bitcast_fusion = f32[8,24,1,1152]{3,1,2,0:T(8,128)} fusion(f32[1152,96,1]{1,0,2:T(8,128)S(1)} %bitcast.147, s32[8,24]{1,0:T(8,128)S(1)} %add_select_fusion.3, pred[8,24]{1,0:T(8,128)(4,1)S(1)} %fusion.124), kind=kOutput, calls=%fused_computation.4 | convolution fusion | flops 127586304 | bytes 1328064 | tf_op jit(solution)/shard_map/dot_general | solution.py:89
  86.6 6.1 %all-to-all-start.1 = ((f32[8,24,1,1152]{3,1,2,0:T(8,128)}), f32[8,24,1,1152]{3,1,2,0:T(8,128)S(1)}, u32[]{:S(2)}, u32[]{:S(2)}) async-start(f32[8,24,1,1152]{3,1,2,0:T(8,128)} %convolution_bitcast_fusion), calls=%async_computation.1 | async-start | bytes 1769472 | tf_op jit(solution)/shard_map/all_to_all | solution.py:120
  92.7 0.4 sine_select_fusion
  93.2 12.4 %all-to-all-done.1 = f32[8,24,1,1152]{3,1,2,0:T(8,128)S(1)} async-done(((f32[8,24,1,1152]{3,1,2,0:T(8,128)}), f32[8,24,1,1152]{3,1,2,0:T(8,128)S(1)}, u32[]{:S(2)}, u32[]{:S(2)}) %all-to-all-start.1) | async-done | bytes 884768 | tf_op jit(solution)/shard_map/all_to_all | solution.py:120
  105.7 0.5 reshape.395
  106.2 0.5 reshape.396
  106.7 1.1 fusion.58
  107.8 1.1 add_bitcast_fusion
  108.9 0.3 copy.22
  109.2 3.3 %multiply_reduce_fusion = (f32[]{:T(128)}, f32[24,192,192]{2,1,0:T(8,128)S(1)}) fusion(f32[24,192,192]{2,1,0:T(8,128)S(1)} %bitcast.138, f32[24,96,192]{2,1,0:T(8,128)S(1)} %bitcast.139, s32[192]{0:T(256)S(1)} %add_select_fusion.4, pred[192]{0:T(512)(128)(4,1)S(1)} %iota_compare_fusion), kind=kOutput, calls=%fused_computation | convolution fusion | flops 512446464 | bytes 8848324 | tf_op jit(solution)/shard_map/dot_general | solution.py:89
  112.5 2.8 %fusion = f32[24,192,96]{1,2,0:T(8,128)S(1)} fusion(f32[24,192,192]{2,1,0:T(8,128)S(1)} %get-tuple-element.27, f32[24,192,192]{2,1,0:T(8,128)S(1)} %bitcast.138, s32[192]{0:T(256)S(1)} %add_select_fusion.4, pred[192]{0:T(512)(128)(4,1)S(1)} %iota_compare_fusion), kind=kOutput, calls=%fused_computation.2 | convolution fusion | flops 510676992 | bytes 8848320 | tf_op jit(solution)/shard_map/dot_general | solution.py:89
  115.4 1.6 %convolution_bitcast_fusion.1 = f32[2,4,24,1,24,48]{5,4,0,1,2,3:T(8,128)S(1)} fusion(f32[24,4,24,192,1]{3,2,4,1,0:T(8,128)S(1)} %bitcast.140, s32[192]{0:T(256)S(1)} %add_select_fusion.4, s32[2,48]{1,0:T(2,128)S(1)} %multiply_add_fusion.1, pred[192]{0:T(512)(128)(4,1)S(1)} %iota_compare_fusion), kind=kOutput, calls=%fused_computation.7 | convolution fusion | flops 254988288 | bytes 2655552 | tf_op jit(solution)/shard_map/dot_general | solution.py:89
  117.1 1.7 %reshape.399 = f32[8,24,1,1152]{3,1,0,2:T(8,128)} reshape(f32[2,4,24,1,24,48]{5,4,2,1,0,3:T(8,128)S(1)} %copy.24) | data formatting | bytes 1769472 | tf_op jit(solution)/shard_map/reshape | solution.py:133
  118.8 3.5 %all-to-all-start.2 = ((f32[8,24,1,1152]{3,1,2,0:T(8,128)}), f32[8,24,1,1152]{3,1,2,0:T(8,128)S(1)}, u32[]{:S(2)}, u32[]{:S(2)}) async-start(f32[8,24,1,1152]{3,1,2,0:T(8,128)} %bitcast.145), calls=%async_computation.2 | async-start | bytes 1769472 | tf_op jit(solution)/shard_map/all_to_all | solution.py:135
  123.0 0.5 collective-permute-start.8
  123.5 1.1 collective-permute-done.8
  125.8 7.2 %collective-permute-start.9 = (f32[1]{0:T(128)}, f32[1]{0:T(128)}, u32[]{:S(2)}, u32[]{:S(2)}) collective-permute-start(f32[1]{0:T(128)} %add.514), channel_id=1, source_target_pairs={{0,2},{1,3},{2,0},{3,1},{4,6},{5,7},{6,4},{7,5},{8,10},{9,11},{10,... | collective-permute-start | bytes 20 | tf_op jit(solution)/shard_map/ppermute | solution.py:45
  132.9 2.2 %collective-permute-done.9 = f32[1]{0:T(128)} collective-permute-done((f32[1]{0:T(128)}, f32[1]{0:T(128)}, u32[]{:S(2)}, u32[]{:S(2)}) %collective-permute-start.9) | collective-permute-done | bytes 36 | tf_op jit(solution)/shard_map/ppermute | solution.py:45
  135.7 2.9 %collective-permute-start.10 = (f32[1]{0:T(128)}, f32[1]{0:T(128)}, u32[]{:S(2)}, u32[]{:S(2)}) collective-permute-start(f32[1]{0:T(128)} %add.515), channel_id=1, source_target_pairs={{0,4},{4,0},{1,5},{5,1},{2,6},{6,2},{3,7},{7,3},{8,12},{12,8},{9,1... | collective-permute-start | bytes 20 | tf_op jit(solution)/shard_map/ppermute | solution.py:45
  138.6 0.9 collective-permute-done.10
  140.0 0.4 copy.26
  140.4 1.0 fusion.22
  141.4 1.0 copy.27
  (37 shorter events, 0.7 us)
Async XLA Ops:
  1.3 4.6 %collective-permute-start.3 = (s32[4,1]{0,1:T(1,128)S(1)}, s32[4,1]{0,1:T(1,128)S(1)}, u32[]{:S(2)}, u32[]{:S(2)}) collective-permute-start(s32[4,1]{0,1:T(1,128)S(1)} %compare_select_fusion.1), channel_id=1, source_target_pairs={{0,8},{8,0},{16,24},{24,16},{1,9},{9,1},{17,25},{25,17},{2,10},{10... | collective-permute-start | bytes 56 | tf_op jit(solution)/shard_map/ppermute | solution.py:45
  5.9 4.6 %collective-permute-start.4 = (s32[4,1]{0,1:T(1,128)S(1)}, s32[4,1]{0,1:T(1,128)S(1)}, u32[]{:S(2)}, u32[]{:S(2)}) collective-permute-start(s32[4,1]{0,1:T(1,128)S(1)} %fusion.361), channel_id=1, source_target_pairs={{0,16},{8,24},{16,0},{24,8},{1,17},{9,25},{17,1},{25,9},{2,18},{10... | collective-permute-start | bytes 56 | tf_op jit(solution)/shard_map/ppermute | solution.py:45
  12.1 5.3 %copy-start = (f32[1,48,24,96]{3,2,1,0:T(8,128)S(1)}, f32[1,48,24,96]{3,2,1,0:T(8,128)}, u32[]{:S(2)}) copy-start(f32[1,48,24,96]{3,2,1,0:T(8,128)} %param.4) | copy-start | bytes 1327108
  12.1 56.9 %all-to-all-start = ((f32[4,1,48,24,96]{4,3,2,1,0:T(8,128)}), f32[4,1,48,24,96]{4,3,2,1,0:T(8,128)S(1)}, u32[]{:S(2)}, u32[]{:S(2)}) async-start(f32[4,1,48,24,96]{4,3,2,1,0:T(8,128)} %select_select_fusion), calls=%async_computation | async-start | bytes 4718592 | tf_op jit(solution)/shard_map/all_to_all | solution.py:153
  17.5 5.1 %collective-permute-start = (f32[1,8,24,96]{3,2,1,0:T(8,128)S(1)}, f32[1,8,24,96]{3,2,1,0:T(8,128)S(1)}, u32[]{:S(2)}, u32[]{:S(2)}) collective-permute-start(f32[1,8,24,96]{3,2,1,0:T(8,128)S(1)} %slice_select_fusion), channel_id=1, source_target_pairs={{0,4},{4,0},{1,5},{5,1},{2,6},{6,2},{3,7},{7,3},{8,12},{12,8},{9,1... | collective-permute-start | bytes 221192 | tf_op jit(solution)/shard_map/ppermute | solution.py:25
  22.6 4.2 %copy-start.1 = (f32[1,8,24,96]{3,2,1,0:T(8,128)}, f32[1,8,24,96]{3,2,1,0:T(8,128)S(1)}, u32[]{:S(2)}) copy-start(f32[1,8,24,96]{3,2,1,0:T(8,128)S(1)} %get-tuple-element.22) | copy-start | bytes 221188
  22.6 4.2 %copy-start.2 = (f32[1,8,24,96]{3,2,1,0:T(8,128)}, f32[1,8,24,96]{3,2,1,0:T(8,128)S(1)}, u32[]{:S(2)}) copy-start(f32[1,8,24,96]{3,2,1,0:T(8,128)S(1)} %get-tuple-element.23) | copy-start | bytes 221188
  23.5 48.4 %collective-permute-start.1 = (f32[1,64,8,96]{3,2,1,0:T(8,128)}, f32[1,64,8,96]{3,2,1,0:T(8,128)}, u32[]{:S(2)}, u32[]{:S(2)}) collective-permute-start(f32[1,64,8,96]{3,2,1,0:T(8,128)} %get-tuple-element.16), channel_id=1, source_target_pairs={{0,1},{1,2},{2,3},{4,5},{5,6},{6,7},{8,9},{9,10},{10,11},{12,13},{... | collective-permute-start | bytes 589832 | tf_op jit(solution)/shard_map/ppermute | solution.py:30
  25.5 46.4 %collective-permute-start.2 = (f32[1,64,8,96]{3,2,1,0:T(8,128)}, f32[1,64,8,96]{3,2,1,0:T(8,128)}, u32[]{:S(2)}, u32[]{:S(2)}) collective-permute-start(f32[1,64,8,96]{3,2,1,0:T(8,128)} %get-tuple-element.17), channel_id=1, source_target_pairs={{1,0},{2,1},{3,2},{5,4},{6,5},{7,6},{9,8},{10,9},{11,10},{13,12},{... | collective-permute-start | bytes 589832 | tf_op jit(solution)/shard_map/ppermute | solution.py:31
  69.2 5.0 %collective-permute-start.5 = (f32[1,48,8,96]{3,2,1,0:T(8,128)S(1)}, f32[1,48,8,96]{3,2,1,0:T(8,128)S(1)}, u32[]{:S(2)}, u32[]{:S(2)}) collective-permute-start(f32[1,48,8,96]{3,2,1,0:T(8,128)S(1)} %get-tuple-element.18), channel_id=1, source_target_pairs={{0,1},{1,2},{2,3},{4,5},{5,6},{6,7},{8,9},{9,10},{10,11},{12,13},{... | collective-permute-start | bytes 442376 | tf_op jit(solution)/shard_map/ppermute | solution.py:30
  70.5 5.1 %collective-permute-start.6 = (f32[1,48,8,96]{3,2,1,0:T(8,128)S(1)}, f32[1,48,8,96]{3,2,1,0:T(8,128)S(1)}, u32[]{:S(2)}, u32[]{:S(2)}) collective-permute-start(f32[1,48,8,96]{3,2,1,0:T(8,128)S(1)} %get-tuple-element.19), channel_id=1, source_target_pairs={{1,0},{2,1},{3,2},{5,4},{6,5},{7,6},{9,8},{10,9},{11,10},{13,12},{... | collective-permute-start | bytes 442376 | tf_op jit(solution)/shard_map/ppermute | solution.py:31
  75.6 5.4 %collective-permute-start.7 = (f32[1,8,40,96]{3,2,1,0:T(8,128)S(1)}, f32[1,8,40,96]{3,2,1,0:T(8,128)S(1)}, u32[]{:S(2)}, u32[]{:S(2)}) collective-permute-start(f32[1,8,40,96]{3,2,1,0:T(8,128)S(1)} %fusion.26), channel_id=1, source_target_pairs={{0,4},{4,0},{1,5},{5,1},{2,6},{6,2},{3,7},{7,3},{8,12},{12,8},{9,1... | collective-permute-start | bytes 368648 | tf_op jit(solution)/shard_map/ppermute | solution.py:25
  86.6 19.0 %all-to-all-start.1 = ((f32[8,24,1,1152]{3,1,2,0:T(8,128)}), f32[8,24,1,1152]{3,1,2,0:T(8,128)S(1)}, u32[]{:S(2)}, u32[]{:S(2)}) async-start(f32[8,24,1,1152]{3,1,2,0:T(8,128)} %convolution_bitcast_fusion), calls=%async_computation.1 | async-start | bytes 1769472 | tf_op jit(solution)/shard_map/all_to_all | solution.py:120
  106.7 2.5 %slice-start = ((s8[4718592]{0:T(1024)(128)(4,1)}), s8[4194304]{0:T(1024)(128)(4,1)S(1)}, s32[]{:S(2)}) async-start(s8[4718592]{0:T(1024)(128)(4,1)} %bitcast.137), calls=%async_computation.3 | async-start | bytes 8388608
  107.8 1.4 %slice-start.1 = ((s8[4718592]{0:T(1024)(128)(4,1)}), s8[524288]{0:T(1024)(128)(4,1)S(1)}, s32[]{:S(2)}) async-start(s8[4718592]{0:T(1024)(128)(4,1)} %bitcast.137), calls=%async_computation.4 | async-start | bytes 1048576
  118.8 21.2 %all-to-all-start.2 = ((f32[8,24,1,1152]{3,1,2,0:T(8,128)}), f32[8,24,1,1152]{3,1,2,0:T(8,128)S(1)}, u32[]{:S(2)}, u32[]{:S(2)}) async-start(f32[8,24,1,1152]{3,1,2,0:T(8,128)} %bitcast.145), calls=%async_computation.2 | async-start | bytes 1769472 | tf_op jit(solution)/shard_map/all_to_all | solution.py:135
  123.0 1.6 %collective-permute-start.8 = (f32[1]{0:T(128)}, f32[1]{0:T(128)}, u32[]{:S(2)}, u32[]{:S(2)}) collective-permute-start(f32[1]{0:T(128)} %bitcast.48), channel_id=1, source_target_pairs={{0,1},{1,0},{2,3},{3,2},{4,5},{5,4},{6,7},{7,6},{8,9},{9,8},{10,11... | collective-permute-start | bytes 20 | tf_op jit(solution)/shard_map/ppermute | solution.py:45
  125.8 9.4 %collective-permute-start.9 = (f32[1]{0:T(128)}, f32[1]{0:T(128)}, u32[]{:S(2)}, u32[]{:S(2)}) collective-permute-start(f32[1]{0:T(128)} %add.514), channel_id=1, source_target_pairs={{0,2},{1,3},{2,0},{3,1},{4,6},{5,7},{6,4},{7,5},{8,10},{9,11},{10,... | collective-permute-start | bytes 20 | tf_op jit(solution)/shard_map/ppermute | solution.py:45
  135.7 3.7 %collective-permute-start.10 = (f32[1]{0:T(128)}, f32[1]{0:T(128)}, u32[]{:S(2)}, u32[]{:S(2)}) collective-permute-start(f32[1]{0:T(128)} %add.515), channel_id=1, source_target_pairs={{0,4},{4,0},{1,5},{5,1},{2,6},{6,2},{3,7},{7,3},{8,12},{12,8},{9,1... | collective-permute-start | bytes 20 | tf_op jit(solution)/shard_map/ppermute | solution.py:45

commit v19 on v18

--- a/solution.py
+++ b/solution.py
@@ -55,6 +55,19 @@
     for number in range(16):
         picked = picked + jnp.where(offset == number - 8, float(FILTER_TAPS[number]), 0.0)
     return picked
+
+
+def filter_x(cells):
+    length = cells.shape[3]
+    return jnp.matmul(cells, band_matrix(length, length, 0), precision=precise_mode)
+
+
+def filter_yz(padded):
+    wide_y, wide_z = padded.shape[1], padded.shape[2]
+    matrix_y = band_matrix(wide_y, wide_y - 16, 8)
+    matrix_z = band_matrix(wide_z, wide_z - 16, 8)
+    step_one = jnp.einsum("oyqx,qz->oyzx", padded, matrix_z, precision=precise_mode)
+    return jnp.einsum("oqzx,qy->oyzx", step_one, matrix_y, precision=precise_mode)
 
 
 def synthesize(padded):
@@ -153,7 +166,7 @@
     arrived = lax.all_to_all(slots, "band", 0, 0, tiled=True)
     arrived, weight = lax.optimization_barrier((arrived, channel_weight(j_coeff.shape[3])))
     own_orbital = synthesize(extended(i_coeff, sides, 8))[0]
-    partner = synthesize(extended(jnp.sum(arrived, axis=0), sides[::-1], 8))
+    partner = filter_yz(extended(filter_x(jnp.sum(arrived, axis=0)), sides[::-1], 8))
     density = own_orbital[None] * partner
     potential, energy_part = potentials(density, weight)
     weights = pair_occ[0].astype(jnp.float32)

time: 144 us -> 144 us (level)
    dot_general x0 -> x3, matrix products: none -> 3.01 us  [the longest x1 1.55 us: filter_yz(): jnp.einsum('oyqx,qz->oyzx', padded, matrix_z, precision=precise_mode)]
    dot_general x2 -> x1, matrix products: 3.63 us -> 2.39 us  [synthesize(): step_one = jnp.matmul(padded, matrix_x, precision=precise_mode)]
where the time goes in v19:
time: 144 us
  waiting for transfers between devices  64.8 us (45%)
  starting transfers between devices  40.6 us (28%)
  matrix products  19.9 us (14%)
  other arithmetic  6.92 us (5%)
  local copies, waits for them, and re-layouts  5.92 us (4%)
  between operations  5.79 us (4%)
    all_to_all x1, waiting for transfers between devices, shards(): arrived = lax.all_to_all(slots, 'band', 0, 0, tiled=True)  42.2 us
    ppermute x5, starting transfers between devices, group_sum(): lax.ppermute(total, axis, [(i, i ^ step) for i in range(count)])  16.6 us
    dot_general x7, matrix products, contract(): lax.dot_general(left, right, (((left_dim,), (right_dim,)), ((), ())), pre...  12.9 us
    all_to_all x1, waiting for transfers between devices, potentials(): got = lax.all_to_all(send, ('gy', 'gz'), 0, 0, tiled=True)  12.4 us
    all_to_all x1, starting transfers between devices, potentials(): got = lax.all_to_all(send, ('gy', 'gz'), 0, 0, tiled=True)  6.08 us
    ppermute x5, waiting for transfers between devices, group_sum(): lax.ppermute(total, axis, [(i, i ^ step) for i in range(count)])  5.84 us
    all_to_all x1, starting transfers between devices, shards(): arrived = lax.all_to_all(slots, 'band', 0, 0, tiled=True)  5.33 us
    all_to_all x1, starting transfers between devices, potentials(): got = lax.all_to_all(back, ('gy', 'gz'), 0, 0, tiled=True)  3.55 us
  transfers between devices with their start and end apart: 14, of which 9 were waited for; matrix products, arithmetic and copies ran while one was open for 7% of the time, Pallas kernels for 0%

profile of v19, /device:TPU:0, one launch (start us, length us, event | category | flops | bytes accessed | tf_op | source)
XLA Modules:
  0.0 143.9 jit_solution(13777507530928726484)
XLA Ops:
  1.3 3.1 %collective-permute-start.3 = (s32[4,1]{0,1:T(1,128)S(1)}, s32[4,1]{0,1:T(1,128)S(1)}, u32[]{:S(2)}, u32[]{:S(2)}) collective-permute-start(s32[4,1]{0,1:T(1,128)S(1)} %compare_select_fusion.1), channel_id=1, source_target_pairs={{0,8},{8,0},{16,24},{24,16},{1,9},{9,1},{17,25},{25,17},{2,10},{10... | collective-permute-start | bytes 56 | tf_op jit(solution)/shard_map/ppermute | solution.py:45
  4.4 1.3 slice_bitcast_fusion.1
  5.7 0.2 collective-permute-done.3
  5.9 3.0 %collective-permute-start.4 = (s32[4,1]{0,1:T(1,128)S(1)}, s32[4,1]{0,1:T(1,128)S(1)}, u32[]{:S(2)}, u32[]{:S(2)}) collective-permute-start(s32[4,1]{0,1:T(1,128)S(1)} %fusion.356), channel_id=1, source_target_pairs={{0,16},{8,24},{16,0},{24,8},{1,17},{9,25},{17,1},{25,9},{2,18},{10... | collective-permute-start | bytes 56 | tf_op jit(solution)/shard_map/ppermute | solution.py:45
  8.9 1.5 %collective-permute-done.4 = s32[4,1]{0,1:T(1,128)S(1)} collective-permute-done((s32[4,1]{0,1:T(1,128)S(1)}, s32[4,1]{0,1:T(1,128)S(1)}, u32[]{:S(2)}, u32[]{:S(2)}) %collective-permute-start.4) | collective-permute-done | bytes 48 | tf_op jit(solution)/shard_map/ppermute | solution.py:45
  10.5 1.7 %select_select_fusion = f32[4,1,48,24,96]{4,3,2,1,0:T(8,128)} fusion(f32[48,24,96]{2,1,0:T(8,128)S(1)} %get-tuple-element.13, f32[48,24,96]{2,1,0:T(8,128)S(1)} %get-tuple-element.12, pred[4]{0:T(512)(128)(4,1)S(1)} %get-tuple-element.25, pred[4]{0:T(512)(128)(4,1)S(1)} %get-tuple-element.24), kind=kLoop, calls=%fused_computation.6 | loop fusion | flops 884736 | bytes 2654216 | tf_op jit(solution)/shard_map/jit(_where)/select_n | solution.py:165
  12.1 5.3 %all-to-all-start = ((f32[4,1,48,24,96]{4,3,2,1,0:T(8,128)}), f32[4,1,48,24,96]{4,3,2,1,0:T(8,128)S(1)}, u32[]{:S(2)}, u32[]{:S(2)}) async-start(f32[4,1,48,24,96]{4,3,2,1,0:T(8,128)} %select_select_fusion), calls=%async_computation | async-start | bytes 4718592 | tf_op jit(solution)/shard_map/all_to_all | solution.py:166
  17.5 1.6 %collective-permute-start = (f32[1,8,24,96]{3,2,1,0:T(8,128)S(1)}, f32[1,8,24,96]{3,2,1,0:T(8,128)S(1)}, u32[]{:S(2)}, u32[]{:S(2)}) collective-permute-start(f32[1,8,24,96]{3,2,1,0:T(8,128)S(1)} %slice_select_fusion), channel_id=1, source_target_pairs={{0,4},{4,0},{1,5},{5,1},{2,6},{6,2},{3,7},{7,3},{8,12},{12,8},{9,1... | collective-permute-start | bytes 221192 | tf_op jit(solution)/shard_map/ppermute | solution.py:25
  19.3 3.2 %multiply_divide_fusion = f32[24,192,192]{2,1,0:T(8,128)} fusion(f32[192]{0:T(256)S(1)} %get-tuple-element.31, f32[24,192]{1,0:T(8,128)S(1)} %broadcast_add_fusion, f32[192]{0:T(256)S(1)} %get-tuple-element.30, f32[24,192]{1,0:T(8,128)S(1)} %broadcast_multiply_fusion), kind=kLoop, calls=%fused_computation.1 | loop fusion | flops 4423680 | bytes 3577344 | tf_op jit(solution)/shard_map/div | solution.py:113
  22.6 0.9 pad_maximum_fusion.2
  23.5 2.0 %collective-permute-start.1 = (f32[1,64,8,96]{3,2,1,0:T(8,128)}, f32[1,64,8,96]{3,2,1,0:T(8,128)}, u32[]{:S(2)}, u32[]{:S(2)}) collective-permute-start(f32[1,64,8,96]{3,2,1,0:T(8,128)} %get-tuple-element.16), channel_id=1, source_target_pairs={{0,1},{1,2},{2,3},{4,5},{5,6},{6,7},{8,9},{9,10},{10,11},{12,13},{... | collective-permute-start | bytes 589832 | tf_op jit(solution)/shard_map/ppermute | solution.py:30
  25.5 1.3 collective-permute-start.2
  26.8 42.2 %all-to-all-done = f32[4,1,48,24,96]{4,3,2,1,0:T(8,128)S(1)} async-done(((f32[4,1,48,24,96]{4,3,2,1,0:T(8,128)}), f32[4,1,48,24,96]{4,3,2,1,0:T(8,128)S(1)}, u32[]{:S(2)}, u32[]{:S(2)}) %all-to-all-start) | async-done | bytes 1769504 | tf_op jit(solution)/shard_map/all_to_all | solution.py:166
  69.0 0.2 reduce_sum.24
  69.2 0.7 convolution_bitcast_fusion.3
  69.9 1.3 collective-permute-start.5
  71.2 1.3 collective-permute-start.6
  72.6 2.4 %fusion.2 = f32[64,40,96]{2,1,0:T(8,128)S(1)} fusion(f32[1,64,8,96]{3,2,1,0:T(8,128)} %collective-permute-done.2, f32[1,8,24,96]{3,2,1,0:T(8,128)} %copy-done.2, f32[1,48,24,96]{3,2,1,0:T(8,128)S(1)} %copy-done, f32[1,8,24,96]{3,2,1,0:T(8,128)} %copy-done.1, f32[1,64,8,96]{3,2,1,0:T(8,128)} %collective-permute-done.1), kind=kOutput, calls=%fused_computation.9 | convolution fusion | flops 284540928 | bytes 1966080 | tf_op jit(solution)/shard_map/dot_general | solution.py:78
  75.0 1.3 collective-permute-done.6
  76.4 1.6 %collective-permute-start.7 = (f32[1,8,40,96]{3,1,2,0:T(8,128)S(1)}, f32[1,8,40,96]{3,1,2,0:T(8,128)S(1)}, u32[]{:S(2)}, u32[]{:S(2)}) collective-permute-start(f32[1,8,40,96]{3,1,2,0:T(8,128)S(1)} %fusion.23), channel_id=1, source_target_pairs={{0,4},{4,0},{1,5},{5,1},{2,6},{6,2},{3,7},{7,3},{8,12},{12,8},{9,1... | collective-permute-start | bytes 368648 | tf_op jit(solution)/shard_map/ppermute | solution.py:25
  77.9 0.8 convolution_bitcast_fusion.2
  78.7 3.0 %collective-permute-done.7 = f32[1,8,40,96]{3,1,2,0:T(8,128)S(1)} collective-permute-done((f32[1,8,40,96]{3,1,2,0:T(8,128)S(1)}, f32[1,8,40,96]{3,1,2,0:T(8,128)S(1)}, u32[]{:S(2)}, u32[]{:S(2)}) %collective-permute-start.7) | collective-permute-done | bytes 122912 | tf_op jit(solution)/shard_map/ppermute | solution.py:25
  81.9 1.6 %fusion.13 = f32[64,24,96]{2,1,0:T(8,128)S(1)} fusion(f32[64,40,96]{2,0,1:T(8,128)S(1)} %maximum_bitcast_fusion.2, s32[40]{0:T(128)S(1)} %iota_add_fusion.1), kind=kOutput, calls=%fused_computation.21 | convolution fusion | flops 70824960 | bytes 1573024 | tf_op jit(solution)/shard_map/oyqx,qz->oyzx/dot_general | solution.py:69
  83.5 0.8 fusion.19
  84.2 0.8 convolution_multiply_fusion.1
  85.0 1.9 %convolution_bitcast_fusion = f32[8,24,1,1152]{3,1,2,0:T(8,128)} fusion(f32[1152,96,1]{1,0,2:T(8,128)S(1)} %bitcast.143, s32[8,24]{1,0:T(8,128)S(1)} %add_select_fusion.3, pred[8,24]{1,0:T(8,128)(4,1)S(1)} %fusion.121), kind=kOutput, calls=%fused_computation.4 | convolution fusion | flops 127586304 | bytes 1328064 | tf_op jit(solution)/shard_map/dot_general | solution.py:102
  86.9 6.1 %all-to-all-start.1 = ((f32[8,24,1,1152]{3,1,2,0:T(8,128)}), f32[8,24,1,1152]{3,1,2,0:T(8,128)S(1)}, u32[]{:S(2)}, u32[]{:S(2)}) async-start(f32[8,24,1,1152]{3,1,2,0:T(8,128)} %convolution_bitcast_fusion), calls=%async_computation.1 | async-start | bytes 1769472 | tf_op jit(solution)/shard_map/all_to_all | solution.py:133
  93.1 0.4 sine_select_fusion
  93.5 12.4 %all-to-all-done.1 = f32[8,24,1,1152]{3,1,2,0:T(8,128)S(1)} async-done(((f32[8,24,1,1152]{3,1,2,0:T(8,128)}), f32[8,24,1,1152]{3,1,2,0:T(8,128)S(1)}, u32[]{:S(2)}, u32[]{:S(2)}) %all-to-all-start.1) | async-done | bytes 884768 | tf_op jit(solution)/shard_map/all_to_all | solution.py:133
  106.0 0.5 reshape.395
  106.5 0.5 reshape.396
  107.0 1.1 fusion.55
  108.1 1.1 add_bitcast_fusion
  109.2 0.3 copy.26
  109.5 3.3 %multiply_reduce_fusion = (f32[]{:T(128)}, f32[24,192,192]{2,1,0:T(8,128)S(1)}) fusion(f32[24,192,192]{2,1,0:T(8,128)S(1)} %bitcast.137, f32[24,96,192]{2,1,0:T(8,128)S(1)} %bitcast.138, s32[192]{0:T(256)S(1)} %add_select_fusion.4, pred[192]{0:T(512)(128)(4,1)S(1)} %iota_compare_fusion), kind=kOutput, calls=%fused_computation | convolution fusion | flops 512446464 | bytes 8848324 | tf_op jit(solution)/shard_map/dot_general | solution.py:102
  112.9 2.8 %fusion = f32[24,192,96]{1,2,0:T(8,128)S(1)} fusion(f32[24,192,192]{2,1,0:T(8,128)S(1)} %get-tuple-element.27, f32[24,192,192]{2,1,0:T(8,128)S(1)} %bitcast.137, s32[192]{0:T(256)S(1)} %add_select_fusion.4, pred[192]{0:T(512)(128)(4,1)S(1)} %iota_compare_fusion), kind=kOutput, calls=%fused_computation.2 | convolution fusion | flops 510676992 | bytes 8848320 | tf_op jit(solution)/shard_map/dot_general | solution.py:102
  115.7 1.6 %convolution_bitcast_fusion.1 = f32[2,4,24,1,24,48]{5,4,0,1,2,3:T(8,128)S(1)} fusion(f32[24,4,24,192,1]{3,2,4,1,0:T(8,128)S(1)} %bitcast.139, s32[192]{0:T(256)S(1)} %add_select_fusion.4, s32[2,48]{1,0:T(2,128)S(1)} %multiply_add_fusion.1, pred[192]{0:T(512)(128)(4,1)S(1)} %iota_compare_fusion), kind=kOutput, calls=%fused_computation.7 | convolution fusion | flops 254988288 | bytes 2655552 | tf_op jit(solution)/shard_map/dot_general | solution.py:102
  117.5 1.7 %reshape.399 = f32[8,24,1,1152]{3,1,0,2:T(8,128)} reshape(f32[2,4,24,1,24,48]{5,4,2,1,0,3:T(8,128)S(1)} %copy.28) | data formatting | bytes 1769472 | tf_op jit(solution)/shard_map/reshape | solution.py:146
  119.1 3.5 %all-to-all-start.2 = ((f32[8,24,1,1152]{3,1,2,0:T(8,128)}), f32[8,24,1,1152]{3,1,2,0:T(8,128)S(1)}, u32[]{:S(2)}, u32[]{:S(2)}) async-start(f32[8,24,1,1152]{3,1,2,0:T(8,128)} %bitcast.141), calls=%async_computation.2 | async-start | bytes 1769472 | tf_op jit(solution)/shard_map/all_to_all | solution.py:148
  123.3 0.5 collective-permute-start.8
  123.8 1.1 collective-permute-done.8
  126.1 7.2 %collective-permute-start.9 = (f32[1]{0:T(128)}, f32[1]{0:T(128)}, u32[]{:S(2)}, u32[]{:S(2)}) collective-permute-start(f32[1]{0:T(128)} %add.514), channel_id=1, source_target_pairs={{0,2},{1,3},{2,0},{3,1},{4,6},{5,7},{6,4},{7,5},{8,10},{9,11},{10,... | collective-permute-start | bytes 20 | tf_op jit(solution)/shard_map/ppermute | solution.py:45
  133.3 2.2 %collective-permute-done.9 = f32[1]{0:T(128)} collective-permute-done((f32[1]{0:T(128)}, f32[1]{0:T(128)}, u32[]{:S(2)}, u32[]{:S(2)}) %collective-permute-start.9) | collective-permute-done | bytes 36 | tf_op jit(solution)/shard_map/ppermute | solution.py:45
  136.0 2.9 %collective-permute-start.10 = (f32[1]{0:T(128)}, f32[1]{0:T(128)}, u32[]{:S(2)}, u32[]{:S(2)}) collective-permute-start(f32[1]{0:T(128)} %add.515), channel_id=1, source_target_pairs={{0,4},{4,0},{1,5},{5,1},{2,6},{6,2},{3,7},{7,3},{8,12},{12,8},{9,1... | collective-permute-start | bytes 20 | tf_op jit(solution)/shard_map/ppermute | solution.py:45
  138.9 0.9 collective-permute-done.10
  140.3 0.4 copy.30
  140.7 1.0 fusion.18
  141.8 1.0 copy.31
  (38 shorter events, 0.8 us)
Async XLA Ops:
  1.3 4.6 %collective-permute-start.3 = (s32[4,1]{0,1:T(1,128)S(1)}, s32[4,1]{0,1:T(1,128)S(1)}, u32[]{:S(2)}, u32[]{:S(2)}) collective-permute-start(s32[4,1]{0,1:T(1,128)S(1)} %compare_select_fusion.1), channel_id=1, source_target_pairs={{0,8},{8,0},{16,24},{24,16},{1,9},{9,1},{17,25},{25,17},{2,10},{10... | collective-permute-start | bytes 56 | tf_op jit(solution)/shard_map/ppermute | solution.py:45
  5.9 4.6 %collective-permute-start.4 = (s32[4,1]{0,1:T(1,128)S(1)}, s32[4,1]{0,1:T(1,128)S(1)}, u32[]{:S(2)}, u32[]{:S(2)}) collective-permute-start(s32[4,1]{0,1:T(1,128)S(1)} %fusion.356), channel_id=1, source_target_pairs={{0,16},{8,24},{16,0},{24,8},{1,17},{9,25},{17,1},{25,9},{2,18},{10... | collective-permute-start | bytes 56 | tf_op jit(solution)/shard_map/ppermute | solution.py:45
  12.1 5.3 %copy-start = (f32[1,48,24,96]{3,2,1,0:T(8,128)S(1)}, f32[1,48,24,96]{3,2,1,0:T(8,128)}, u32[]{:S(2)}) copy-start(f32[1,48,24,96]{3,2,1,0:T(8,128)} %param.4) | copy-start | bytes 1327108
  12.1 56.9 %all-to-all-start = ((f32[4,1,48,24,96]{4,3,2,1,0:T(8,128)}), f32[4,1,48,24,96]{4,3,2,1,0:T(8,128)S(1)}, u32[]{:S(2)}, u32[]{:S(2)}) async-start(f32[4,1,48,24,96]{4,3,2,1,0:T(8,128)} %select_select_fusion), calls=%async_computation | async-start | bytes 4718592 | tf_op jit(solution)/shard_map/all_to_all | solution.py:166
  17.5 5.1 %collective-permute-start = (f32[1,8,24,96]{3,2,1,0:T(8,128)S(1)}, f32[1,8,24,96]{3,2,1,0:T(8,128)S(1)}, u32[]{:S(2)}, u32[]{:S(2)}) collective-permute-start(f32[1,8,24,96]{3,2,1,0:T(8,128)S(1)} %slice_select_fusion), channel_id=1, source_target_pairs={{0,4},{4,0},{1,5},{5,1},{2,6},{6,2},{3,7},{7,3},{8,12},{12,8},{9,1... | collective-permute-start | bytes 221192 | tf_op jit(solution)/shard_map/ppermute | solution.py:25
  22.6 4.2 %copy-start.1 = (f32[1,8,24,96]{3,2,1,0:T(8,128)}, f32[1,8,24,96]{3,2,1,0:T(8,128)S(1)}, u32[]{:S(2)}) copy-start(f32[1,8,24,96]{3,2,1,0:T(8,128)S(1)} %get-tuple-element.22) | copy-start | bytes 221188
  22.6 4.2 %copy-start.2 = (f32[1,8,24,96]{3,2,1,0:T(8,128)}, f32[1,8,24,96]{3,2,1,0:T(8,128)S(1)}, u32[]{:S(2)}) copy-start(f32[1,8,24,96]{3,2,1,0:T(8,128)S(1)} %get-tuple-element.23) | copy-start | bytes 221188
  23.5 49.1 %collective-permute-start.1 = (f32[1,64,8,96]{3,2,1,0:T(8,128)}, f32[1,64,8,96]{3,2,1,0:T(8,128)}, u32[]{:S(2)}, u32[]{:S(2)}) collective-permute-start(f32[1,64,8,96]{3,2,1,0:T(8,128)} %get-tuple-element.16), channel_id=1, source_target_pairs={{0,1},{1,2},{2,3},{4,5},{5,6},{6,7},{8,9},{9,10},{10,11},{12,13},{... | collective-permute-start | bytes 589832 | tf_op jit(solution)/shard_map/ppermute | solution.py:30
  25.5 47.1 %collective-permute-start.2 = (f32[1,64,8,96]{3,2,1,0:T(8,128)}, f32[1,64,8,96]{3,2,1,0:T(8,128)}, u32[]{:S(2)}, u32[]{:S(2)}) collective-permute-start(f32[1,64,8,96]{3,2,1,0:T(8,128)} %get-tuple-element.17), channel_id=1, source_target_pairs={{1,0},{2,1},{3,2},{5,4},{6,5},{7,6},{9,8},{10,9},{11,10},{13,12},{... | collective-permute-start | bytes 589832 | tf_op jit(solution)/shard_map/ppermute | solution.py:31
  69.9 5.0 %collective-permute-start.5 = (f32[1,48,8,96]{3,1,2,0:T(8,128)S(1)}, f32[1,48,8,96]{3,1,2,0:T(8,128)S(1)}, u32[]{:S(2)}, u32[]{:S(2)}) collective-permute-start(f32[1,48,8,96]{3,1,2,0:T(8,128)S(1)} %get-tuple-element.18), channel_id=1, source_target_pairs={{0,1},{1,2},{2,3},{4,5},{5,6},{6,7},{8,9},{9,10},{10,11},{12,13},{... | collective-permute-start | bytes 442376 | tf_op jit(solution)/shard_map/ppermute | solution.py:30
  71.2 5.1 %collective-permute-start.6 = (f32[1,48,8,96]{3,1,2,0:T(8,128)S(1)}, f32[1,48,8,96]{3,1,2,0:T(8,128)S(1)}, u32[]{:S(2)}, u32[]{:S(2)}) collective-permute-start(f32[1,48,8,96]{3,1,2,0:T(8,128)S(1)} %get-tuple-element.19), channel_id=1, source_target_pairs={{1,0},{2,1},{3,2},{5,4},{6,5},{7,6},{9,8},{10,9},{11,10},{13,12},{... | collective-permute-start | bytes 442376 | tf_op jit(solution)/shard_map/ppermute | solution.py:31
  76.4 5.4 %collective-permute-start.7 = (f32[1,8,40,96]{3,1,2,0:T(8,128)S(1)}, f32[1,8,40,96]{3,1,2,0:T(8,128)S(1)}, u32[]{:S(2)}, u32[]{:S(2)}) collective-permute-start(f32[1,8,40,96]{3,1,2,0:T(8,128)S(1)} %fusion.23), channel_id=1, source_target_pairs={{0,4},{4,0},{1,5},{5,1},{2,6},{6,2},{3,7},{7,3},{8,12},{12,8},{9,1... | collective-permute-start | bytes 368648 | tf_op jit(solution)/shard_map/ppermute | solution.py:25
  86.9 19.0 %all-to-all-start.1 = ((f32[8,24,1,1152]{3,1,2,0:T(8,128)}), f32[8,24,1,1152]{3,1,2,0:T(8,128)S(1)}, u32[]{:S(2)}, u32[]{:S(2)}) async-start(f32[8,24,1,1152]{3,1,2,0:T(8,128)} %convolution_bitcast_fusion), calls=%async_computation.1 | async-start | bytes 1769472 | tf_op jit(solution)/shard_map/all_to_all | solution.py:133
  107.0 2.5 %slice-start = ((s8[4718592]{0:T(1024)(128)(4,1)}), s8[4194304]{0:T(1024)(128)(4,1)S(1)}, s32[]{:S(2)}) async-start(s8[4718592]{0:T(1024)(128)(4,1)} %bitcast.136), calls=%async_computation.3 | async-start | bytes 8388608
  108.1 1.4 %slice-start.1 = ((s8[4718592]{0:T(1024)(128)(4,1)}), s8[524288]{0:T(1024)(128)(4,1)S(1)}, s32[]{:S(2)}) async-start(s8[4718592]{0:T(1024)(128)(4,1)} %bitcast.136), calls=%async_computation.4 | async-start | bytes 1048576
  119.1 21.2 %all-to-all-start.2 = ((f32[8,24,1,1152]{3,1,2,0:T(8,128)}), f32[8,24,1,1152]{3,1,2,0:T(8,128)S(1)}, u32[]{:S(2)}, u32[]{:S(2)}) async-start(f32[8,24,1,1152]{3,1,2,0:T(8,128)} %bitcast.141), calls=%async_computation.2 | async-start | bytes 1769472 | tf_op jit(solution)/shard_map/all_to_all | solution.py:148
  123.3 1.6 %collective-permute-start.8 = (f32[1]{0:T(128)}, f32[1]{0:T(128)}, u32[]{:S(2)}, u32[]{:S(2)}) collective-permute-start(f32[1]{0:T(128)} %bitcast.48), channel_id=1, source_target_pairs={{0,1},{1,0},{2,3},{3,2},{4,5},{5,4},{6,7},{7,6},{8,9},{9,8},{10,11... | collective-permute-start | bytes 20 | tf_op jit(solution)/shard_map/ppermute | solution.py:45
  126.1 9.4 %collective-permute-start.9 = (f32[1]{0:T(128)}, f32[1]{0:T(128)}, u32[]{:S(2)}, u32[]{:S(2)}) collective-permute-start(f32[1]{0:T(128)} %add.514), channel_id=1, source_target_pairs={{0,2},{1,3},{2,0},{3,1},{4,6},{5,7},{6,4},{7,5},{8,10},{9,11},{10,... | collective-permute-start | bytes 20 | tf_op jit(solution)/shard_map/ppermute | solution.py:45
  136.0 3.7 %collective-permute-start.10 = (f32[1]{0:T(128)}, f32[1]{0:T(128)}, u32[]{:S(2)}, u32[]{:S(2)}) collective-permute-start(f32[1]{0:T(128)} %add.515), channel_id=1, source_target_pairs={{0,4},{4,0},{1,5},{5,1},{2,6},{6,2},{3,7},{7,3},{8,12},{12,8},{9,1... | collective-permute-start | bytes 20 | tf_op jit(solution)/shard_map/ppermute | solution.py:45

commit v20 on v18

--- a/solution.py
+++ b/solution.py
@@ -57,11 +57,18 @@
     return picked
 
 
-def synthesize(padded):
-    wide_y, wide_z, length = (padded.shape[1], padded.shape[2], padded.shape[3])
-    matrix_y = band_matrix(wide_y, wide_y - 16, 8)
-    matrix_z = band_matrix(wide_z, wide_z - 16, 8)
-    matrix_x = band_matrix(length, length, 0)
+def filter_matrices(wide_y, wide_z, length):
+    return (
+        band_matrix(wide_y, wide_y - 16, 8),
+        band_matrix(wide_z, wide_z - 16, 8),
+        band_matrix(length, length, 0),
+    )
+
+
+def synthesize(padded, matrices=None):
+    if matrices is None:
+        matrices = filter_matrices(padded.shape[1], padded.shape[2], padded.shape[3])
+    matrix_y, matrix_z, matrix_x = matrices
     step_one = jnp.matmul(padded, matrix_x, precision=precise_mode)
     step_two = jnp.einsum("oyqx,qz->oyzx", step_one, matrix_z, precision=precise_mode)
     return jnp.einsum("oqzx,qy->oyzx", step_two, matrix_y, precision=precise_mode)
@@ -151,9 +158,12 @@
         hit = (wanted == first_owned + number)[:, :, None, None, None]
         slots = jnp.where(hit, j_coeff[number][None, None], slots)
     arrived = lax.all_to_all(slots, "band", 0, 0, tiled=True)
-    arrived, weight = lax.optimization_barrier((arrived, channel_weight(j_coeff.shape[3])))
+    matrices = filter_matrices(j_coeff.shape[1] + 16, j_coeff.shape[2] + 16, j_coeff.shape[3])
+    arrived, weight, matrices = lax.optimization_barrier(
+        (arrived, channel_weight(j_coeff.shape[3]), matrices)
+    )
     own_orbital = synthesize(extended(i_coeff, sides, 8))[0]
-    partner = synthesize(extended(jnp.sum(arrived, axis=0), sides[::-1], 8))
+    partner = synthesize(extended(jnp.sum(arrived, axis=0), sides[::-1], 8), matrices)
     density = own_orbital[None] * partner
     potential, energy_part = potentials(density, weight)
     weights = pair_occ[0].astype(jnp.float32)

time: 144 us -> 144 us (level)
  waiting for transfers between devices: 64.8 us -> 63 us
  transfers between devices with their start and end apart: 14 -> 14, of which waited for: 9 -> 9; matrix products, arithmetic and copies ran while one was open for 7% -> 8% of each run, Pallas kernels for 0% -> 0%
where the time goes in v20:
time: 144 us; the launch traced here: 143 us
  waiting for transfers between devices  63 us (44%)
  starting transfers between devices  40.6 us (28%)
  matrix products  19.6 us (14%)
  other arithmetic  8.16 us (6%)
  between operations  6.04 us (4%)
  local copies, waits for them, and re-layouts  5.93 us (4%)
    all_to_all x1, waiting for transfers between devices, shards(): arrived = lax.all_to_all(slots, 'band', 0, 0, tiled=True)  40.8 us
    ppermute x5, starting transfers between devices, group_sum(): lax.ppermute(total, axis, [(i, i ^ step) for i in range(count)])  16.7 us
    dot_general x7, matrix products, contract(): lax.dot_general(left, right, (((left_dim,), (right_dim,)), ((), ())), pre...  12.9 us
    all_to_all x1, waiting for transfers between devices, potentials(): got = lax.all_to_all(send, ('gy', 'gz'), 0, 0, tiled=True)  12.4 us
    all_to_all x1, starting transfers between devices, potentials(): got = lax.all_to_all(send, ('gy', 'gz'), 0, 0, tiled=True)  6.08 us
    ppermute x5, waiting for transfers between devices, group_sum(): lax.ppermute(total, axis, [(i, i ^ step) for i in range(count)])  5.4 us
    all_to_all x1, starting transfers between devices, shards(): arrived = lax.all_to_all(slots, 'band', 0, 0, tiled=True)  5.33 us
    all_to_all x1, starting transfers between devices, potentials(): got = lax.all_to_all(back, ('gy', 'gz'), 0, 0, tiled=True)  3.55 us
  transfers between devices with their start and end apart: 14, of which 9 were waited for; matrix products, arithmetic and copies ran while one was open for 8% of the time, Pallas kernels for 0%

profile of v20, /device:TPU:0, one launch (start us, length us, event | category | flops | bytes accessed | tf_op | source)
XLA Modules:
  0.0 143.3 jit_solution(6965012138217455575)
XLA Ops:
  1.3 3.1 %collective-permute-start.3 = (s32[4,1]{0,1:T(1,128)S(1)}, s32[4,1]{0,1:T(1,128)S(1)}, u32[]{:S(2)}, u32[]{:S(2)}) collective-permute-start(s32[4,1]{0,1:T(1,128)S(1)} %compare_select_fusion.1), channel_id=1, source_target_pairs={{0,8},{8,0},{16,24},{24,16},{1,9},{9,1},{17,25},{25,17},{2,10},{10... | collective-permute-start | bytes 56 | tf_op jit(solution)/shard_map/ppermute | solution.py:45
  4.4 1.3 slice_bitcast_fusion.1
  5.9 3.0 %collective-permute-start.4 = (s32[4,1]{0,1:T(1,128)S(1)}, s32[4,1]{0,1:T(1,128)S(1)}, u32[]{:S(2)}, u32[]{:S(2)}) collective-permute-start(s32[4,1]{0,1:T(1,128)S(1)} %fusion.262), channel_id=1, source_target_pairs={{0,16},{8,24},{16,0},{24,8},{1,17},{9,25},{17,1},{25,9},{2,18},{10... | collective-permute-start | bytes 56 | tf_op jit(solution)/shard_map/ppermute | solution.py:45
  8.9 1.5 %collective-permute-done.4 = s32[4,1]{0,1:T(1,128)S(1)} collective-permute-done((s32[4,1]{0,1:T(1,128)S(1)}, s32[4,1]{0,1:T(1,128)S(1)}, u32[]{:S(2)}, u32[]{:S(2)}) %collective-permute-start.4) | collective-permute-done | bytes 48 | tf_op jit(solution)/shard_map/ppermute | solution.py:45
  10.5 1.7 %select_select_fusion = f32[4,1,48,24,96]{4,3,2,1,0:T(8,128)} fusion(f32[48,24,96]{2,1,0:T(8,128)S(1)} %get-tuple-element.19, f32[48,24,96]{2,1,0:T(8,128)S(1)} %get-tuple-element.18, pred[4]{0:T(512)(128)(4,1)S(1)} %get-tuple-element.31, pred[4]{0:T(512)(128)(4,1)S(1)} %get-tuple-element.30), kind=kLoop, calls=%fused_computation.6 | loop fusion | flops 884736 | bytes 2654216 | tf_op jit(solution)/shard_map/jit(_where)/select_n | solution.py:159
  12.2 5.3 %all-to-all-start = ((f32[4,1,48,24,96]{4,3,2,1,0:T(8,128)}), f32[4,1,48,24,96]{4,3,2,1,0:T(8,128)S(1)}, u32[]{:S(2)}, u32[]{:S(2)}) async-start(f32[4,1,48,24,96]{4,3,2,1,0:T(8,128)} %select_select_fusion), calls=%async_computation | async-start | bytes 4718592 | tf_op jit(solution)/shard_map/all_to_all | solution.py:160
  17.5 1.6 %collective-permute-start = (f32[1,8,24,96]{3,2,1,0:T(8,128)S(1)}, f32[1,8,24,96]{3,2,1,0:T(8,128)S(1)}, u32[]{:S(2)}, u32[]{:S(2)}) collective-permute-start(f32[1,8,24,96]{3,2,1,0:T(8,128)S(1)} %slice_select_fusion), channel_id=1, source_target_pairs={{0,4},{4,0},{1,5},{5,1},{2,6},{6,2},{3,7},{7,3},{8,12},{12,8},{9,1... | collective-permute-start | bytes 221192 | tf_op jit(solution)/shard_map/ppermute | solution.py:25
  19.2 0.7 select_add_fusion
  19.9 0.6 select_add_fusion.1
  20.7 3.2 %multiply_divide_fusion = f32[24,192,192]{2,1,0:T(8,128)} fusion(f32[192]{0:T(256)S(1)} %get-tuple-element.37, f32[24,192]{1,0:T(8,128)S(1)} %broadcast_add_fusion, f32[192]{0:T(256)S(1)} %get-tuple-element.36, f32[24,192]{1,0:T(8,128)S(1)} %broadcast_multiply_fusion), kind=kLoop, calls=%fused_computation.1 | loop fusion | flops 4423680 | bytes 3577344 | tf_op jit(solution)/shard_map/div | solution.py:107
  24.0 0.9 pad_maximum_fusion.2
  24.9 2.0 %collective-permute-start.1 = (f32[1,64,8,96]{3,2,1,0:T(8,128)}, f32[1,64,8,96]{3,2,1,0:T(8,128)}, u32[]{:S(2)}, u32[]{:S(2)}) collective-permute-start(f32[1,64,8,96]{3,2,1,0:T(8,128)} %get-tuple-element.22), channel_id=1, source_target_pairs={{0,1},{1,2},{2,3},{4,5},{5,6},{6,7},{8,9},{9,10},{10,11},{12,13},{... | collective-permute-start | bytes 589832 | tf_op jit(solution)/shard_map/ppermute | solution.py:30
  26.9 1.3 collective-permute-start.2
  28.2 40.8 %all-to-all-done = f32[4,1,48,24,96]{4,3,2,1,0:T(8,128)S(1)} async-done(((f32[4,1,48,24,96]{4,3,2,1,0:T(8,128)}), f32[4,1,48,24,96]{4,3,2,1,0:T(8,128)S(1)}, u32[]{:S(2)}, u32[]{:S(2)}) %all-to-all-start) | async-done | bytes 1769504 | tf_op jit(solution)/shard_map/all_to_all | solution.py:160
  69.3 1.3 collective-permute-start.5
  70.6 1.3 collective-permute-start.6
  71.9 2.4 %fusion.2 = f32[64,40,96]{2,1,0:T(8,128)S(1)} fusion(f32[1,64,8,96]{3,2,1,0:T(8,128)} %collective-permute-done.2, f32[1,8,24,96]{3,2,1,0:T(8,128)} %copy-done.2, f32[1,48,24,96]{3,2,1,0:T(8,128)S(1)} %copy-done, f32[1,8,24,96]{3,2,1,0:T(8,128)} %copy-done.1, f32[1,64,8,96]{3,2,1,0:T(8,128)} %collective-permute-done.1), kind=kOutput, calls=%fused_computation.9 | convolution fusion | flops 284540928 | bytes 1966080 | tf_op jit(solution)/shard_map/dot_general | solution.py:72
  74.3 1.3 collective-permute-done.6
  75.7 1.6 %collective-permute-start.7 = (f32[1,8,40,96]{3,2,1,0:T(8,128)S(1)}, f32[1,8,40,96]{3,2,1,0:T(8,128)S(1)}, u32[]{:S(2)}, u32[]{:S(2)}) collective-permute-start(f32[1,8,40,96]{3,2,1,0:T(8,128)S(1)} %fusion.26), channel_id=1, source_target_pairs={{0,4},{4,0},{1,5},{5,1},{2,6},{6,2},{3,7},{7,3},{8,12},{12,8},{9,1... | collective-permute-start | bytes 368648 | tf_op jit(solution)/shard_map/ppermute | solution.py:25
  77.2 0.8 convolution_bitcast_fusion.3
  78.1 3.0 %collective-permute-done.7 = f32[1,8,40,96]{3,2,1,0:T(8,128)S(1)} collective-permute-done((f32[1,8,40,96]{3,2,1,0:T(8,128)S(1)}, f32[1,8,40,96]{3,2,1,0:T(8,128)S(1)}, u32[]{:S(2)}, u32[]{:S(2)}) %collective-permute-start.7) | collective-permute-done | bytes 122912 | tf_op jit(solution)/shard_map/ppermute | solution.py:25
  81.1 1.2 fusion.11
  82.3 0.8 convolution_bitcast_fusion.2
  83.1 0.8 fusion.23
  83.9 0.8 convolution_multiply_fusion.1
  84.7 1.9 %convolution_bitcast_fusion = f32[8,24,1,1152]{3,1,2,0:T(8,128)} fusion(f32[1152,96,1]{1,0,2:T(8,128)S(1)} %bitcast.150, s32[8,24]{1,0:T(8,128)S(1)} %add_select_fusion.3, pred[8,24]{1,0:T(8,128)(4,1)S(1)} %fusion.124), kind=kOutput, calls=%fused_computation.4 | convolution fusion | flops 127586304 | bytes 1328064 | tf_op jit(solution)/shard_map/dot_general | solution.py:96
  86.6 6.1 %all-to-all-start.1 = ((f32[8,24,1,1152]{3,1,2,0:T(8,128)}), f32[8,24,1,1152]{3,1,2,0:T(8,128)S(1)}, u32[]{:S(2)}, u32[]{:S(2)}) async-start(f32[8,24,1,1152]{3,1,2,0:T(8,128)} %convolution_bitcast_fusion), calls=%async_computation.1 | async-start | bytes 1769472 | tf_op jit(solution)/shard_map/all_to_all | solution.py:127
  92.7 0.4 sine_select_fusion
  93.1 12.4 %all-to-all-done.1 = f32[8,24,1,1152]{3,1,2,0:T(8,128)S(1)} async-done(((f32[8,24,1,1152]{3,1,2,0:T(8,128)}), f32[8,24,1,1152]{3,1,2,0:T(8,128)S(1)}, u32[]{:S(2)}, u32[]{:S(2)}) %all-to-all-start.1) | async-done | bytes 884768 | tf_op jit(solution)/shard_map/all_to_all | solution.py:127
  105.6 0.5 reshape.395
  106.1 0.5 reshape.396
  106.7 1.1 fusion.58
  107.7 1.1 add_bitcast_fusion
  108.8 0.3 copy.22
  109.2 3.3 %multiply_reduce_fusion = (f32[]{:T(128)}, f32[24,192,192]{2,1,0:T(8,128)S(1)}) fusion(f32[24,192,192]{2,1,0:T(8,128)S(1)} %bitcast.141, f32[24,96,192]{2,1,0:T(8,128)S(1)} %bitcast.142, s32[192]{0:T(256)S(1)} %add_select_fusion.4, pred[192]{0:T(512)(128)(4,1)S(1)} %iota_compare_fusion), kind=kOutput, calls=%fused_computation | convolution fusion | flops 512446464 | bytes 8848324 | tf_op jit(solution)/shard_map/dot_general | solution.py:96
  112.5 2.8 %fusion = f32[24,192,96]{1,2,0:T(8,128)S(1)} fusion(f32[24,192,192]{2,1,0:T(8,128)S(1)} %get-tuple-element.33, f32[24,192,192]{2,1,0:T(8,128)S(1)} %bitcast.141, s32[192]{0:T(256)S(1)} %add_select_fusion.4, pred[192]{0:T(512)(128)(4,1)S(1)} %iota_compare_fusion), kind=kOutput, calls=%fused_computation.2 | convolution fusion | flops 510676992 | bytes 8848320 | tf_op jit(solution)/shard_map/dot_general | solution.py:96
  115.4 1.6 %convolution_bitcast_fusion.1 = f32[2,4,24,1,24,48]{5,4,0,1,2,3:T(8,128)S(1)} fusion(f32[24,4,24,192,1]{3,2,4,1,0:T(8,128)S(1)} %bitcast.143, s32[192]{0:T(256)S(1)} %add_select_fusion.4, s32[2,48]{1,0:T(2,128)S(1)} %multiply_add_fusion.1, pred[192]{0:T(512)(128)(4,1)S(1)} %iota_compare_fusion), kind=kOutput, calls=%fused_computation.7 | convolution fusion | flops 254988288 | bytes 2655552 | tf_op jit(solution)/shard_map/dot_general | solution.py:96
  117.1 1.6 %reshape.399 = f32[8,24,1,1152]{3,1,0,2:T(8,128)} reshape(f32[2,4,24,1,24,48]{5,4,2,1,0,3:T(8,128)S(1)} %copy.24) | data formatting | bytes 1769472 | tf_op jit(solution)/shard_map/reshape | solution.py:140
  118.8 3.5 %all-to-all-start.2 = ((f32[8,24,1,1152]{3,1,2,0:T(8,128)}), f32[8,24,1,1152]{3,1,2,0:T(8,128)S(1)}, u32[]{:S(2)}, u32[]{:S(2)}) async-start(f32[8,24,1,1152]{3,1,2,0:T(8,128)} %bitcast.148), calls=%async_computation.2 | async-start | bytes 1769472 | tf_op jit(solution)/shard_map/all_to_all | solution.py:142
  123.0 0.5 collective-permute-start.8
  123.4 1.0 collective-permute-done.8
  125.7 7.2 %collective-permute-start.9 = (f32[1]{0:T(128)}, f32[1]{0:T(128)}, u32[]{:S(2)}, u32[]{:S(2)}) collective-permute-start(f32[1]{0:T(128)} %add.514), channel_id=1, source_target_pairs={{0,2},{1,3},{2,0},{3,1},{4,6},{5,7},{6,4},{7,5},{8,10},{9,11},{10,... | collective-permute-start | bytes 20 | tf_op jit(solution)/shard_map/ppermute | solution.py:45
  132.9 2.0 %collective-permute-done.9 = f32[1]{0:T(128)} collective-permute-done((f32[1]{0:T(128)}, f32[1]{0:T(128)}, u32[]{:S(2)}, u32[]{:S(2)}) %collective-permute-start.9) | collective-permute-done | bytes 36 | tf_op jit(solution)/shard_map/ppermute | solution.py:45
  135.6 2.9 %collective-permute-start.10 = (f32[1]{0:T(128)}, f32[1]{0:T(128)}, u32[]{:S(2)}, u32[]{:S(2)}) collective-permute-start(f32[1]{0:T(128)} %add.515), channel_id=1, source_target_pairs={{0,4},{4,0},{1,5},{5,1},{2,6},{6,2},{3,7},{7,3},{8,12},{12,8},{9,1... | collective-permute-start | bytes 20 | tf_op jit(solution)/shard_map/ppermute | solution.py:45
  138.4 0.7 collective-permute-done.10
  139.8 0.4 copy.26
  140.2 1.0 fusion.22
  141.2 1.0 copy.27
  (52 shorter events, 1.1 us)
Async XLA Ops:
  1.3 4.6 %collective-permute-start.3 = (s32[4,1]{0,1:T(1,128)S(1)}, s32[4,1]{0,1:T(1,128)S(1)}, u32[]{:S(2)}, u32[]{:S(2)}) collective-permute-start(s32[4,1]{0,1:T(1,128)S(1)} %compare_select_fusion.1), channel_id=1, source_target_pairs={{0,8},{8,0},{16,24},{24,16},{1,9},{9,1},{17,25},{25,17},{2,10},{10... | collective-permute-start | bytes 56 | tf_op jit(solution)/shard_map/ppermute | solution.py:45
  5.9 4.6 %collective-permute-start.4 = (s32[4,1]{0,1:T(1,128)S(1)}, s32[4,1]{0,1:T(1,128)S(1)}, u32[]{:S(2)}, u32[]{:S(2)}) collective-permute-start(s32[4,1]{0,1:T(1,128)S(1)} %fusion.262), channel_id=1, source_target_pairs={{0,16},{8,24},{16,0},{24,8},{1,17},{9,25},{17,1},{25,9},{2,18},{10... | collective-permute-start | bytes 56 | tf_op jit(solution)/shard_map/ppermute | solution.py:45
  12.2 5.3 %copy-start = (f32[1,48,24,96]{3,2,1,0:T(8,128)S(1)}, f32[1,48,24,96]{3,2,1,0:T(8,128)}, u32[]{:S(2)}) copy-start(f32[1,48,24,96]{3,2,1,0:T(8,128)} %param.4) | copy-start | bytes 1327108
  12.2 56.9 %all-to-all-start = ((f32[4,1,48,24,96]{4,3,2,1,0:T(8,128)}), f32[4,1,48,24,96]{4,3,2,1,0:T(8,128)S(1)}, u32[]{:S(2)}, u32[]{:S(2)}) async-start(f32[4,1,48,24,96]{4,3,2,1,0:T(8,128)} %select_select_fusion), calls=%async_computation | async-start | bytes 4718592 | tf_op jit(solution)/shard_map/all_to_all | solution.py:160
  17.5 6.5 %collective-permute-start = (f32[1,8,24,96]{3,2,1,0:T(8,128)S(1)}, f32[1,8,24,96]{3,2,1,0:T(8,128)S(1)}, u32[]{:S(2)}, u32[]{:S(2)}) collective-permute-start(f32[1,8,24,96]{3,2,1,0:T(8,128)S(1)} %slice_select_fusion), channel_id=1, source_target_pairs={{0,4},{4,0},{1,5},{5,1},{2,6},{6,2},{3,7},{7,3},{8,12},{12,8},{9,1... | collective-permute-start | bytes 221192 | tf_op jit(solution)/shard_map/ppermute | solution.py:25
  19.1 4.9 %copy-start.5 = (s32[64]{0:T(128)}, s32[64]{0:T(128)S(1)}, u32[]{:S(2)}) copy-start(s32[64]{0:T(128)S(1)} %iota_add_fusion.2) | copy-start | bytes 772
  19.1 4.9 %copy-start.7 = (s32[40]{0:T(128)}, s32[40]{0:T(128)S(1)}, u32[]{:S(2)}) copy-start(s32[40]{0:T(128)S(1)} %iota_add_fusion.1) | copy-start | bytes 484
  24.0 4.2 %copy-start.1 = (f32[1,8,24,96]{3,2,1,0:T(8,128)}, f32[1,8,24,96]{3,2,1,0:T(8,128)S(1)}, u32[]{:S(2)}) copy-start(f32[1,8,24,96]{3,2,1,0:T(8,128)S(1)} %get-tuple-element.28) | copy-start | bytes 221188
  24.0 4.2 %copy-start.2 = (f32[1,8,24,96]{3,2,1,0:T(8,128)}, f32[1,8,24,96]{3,2,1,0:T(8,128)S(1)}, u32[]{:S(2)}) copy-start(f32[1,8,24,96]{3,2,1,0:T(8,128)S(1)} %get-tuple-element.29) | copy-start | bytes 221188
  24.9 47.0 %collective-permute-start.1 = (f32[1,64,8,96]{3,2,1,0:T(8,128)}, f32[1,64,8,96]{3,2,1,0:T(8,128)}, u32[]{:S(2)}, u32[]{:S(2)}) collective-permute-start(f32[1,64,8,96]{3,2,1,0:T(8,128)} %get-tuple-element.22), channel_id=1, source_target_pairs={{0,1},{1,2},{2,3},{4,5},{5,6},{6,7},{8,9},{9,10},{10,11},{12,13},{... | collective-permute-start | bytes 589832 | tf_op jit(solution)/shard_map/ppermute | solution.py:30
  26.9 45.0 %collective-permute-start.2 = (f32[1,64,8,96]{3,2,1,0:T(8,128)}, f32[1,64,8,96]{3,2,1,0:T(8,128)}, u32[]{:S(2)}, u32[]{:S(2)}) collective-permute-start(f32[1,64,8,96]{3,2,1,0:T(8,128)} %get-tuple-element.23), channel_id=1, source_target_pairs={{1,0},{2,1},{3,2},{5,4},{6,5},{7,6},{9,8},{10,9},{11,10},{13,12},{... | collective-permute-start | bytes 589832 | tf_op jit(solution)/shard_map/ppermute | solution.py:31
  69.2 8.0 %copy-start.8 = (s32[40]{0:T(128)S(1)}, s32[40]{0:T(128)}, u32[]{:S(2)}) copy-start(s32[40]{0:T(128)} %copy-done.7) | copy-start | bytes 484
  69.3 5.0 %collective-permute-start.5 = (f32[1,48,8,96]{3,2,1,0:T(8,128)S(1)}, f32[1,48,8,96]{3,2,1,0:T(8,128)S(1)}, u32[]{:S(2)}, u32[]{:S(2)}) collective-permute-start(f32[1,48,8,96]{3,2,1,0:T(8,128)S(1)} %get-tuple-element.24), channel_id=1, source_target_pairs={{0,1},{1,2},{2,3},{4,5},{5,6},{6,7},{8,9},{9,10},{10,11},{12,13},{... | collective-permute-start | bytes 442376 | tf_op jit(solution)/shard_map/ppermute | solution.py:30
  70.6 5.1 %collective-permute-start.6 = (f32[1,48,8,96]{3,2,1,0:T(8,128)S(1)}, f32[1,48,8,96]{3,2,1,0:T(8,128)S(1)}, u32[]{:S(2)}, u32[]{:S(2)}) collective-permute-start(f32[1,48,8,96]{3,2,1,0:T(8,128)S(1)} %get-tuple-element.25), channel_id=1, source_target_pairs={{1,0},{2,1},{3,2},{5,4},{6,5},{7,6},{9,8},{10,9},{11,10},{13,12},{... | collective-permute-start | bytes 442376 | tf_op jit(solution)/shard_map/ppermute | solution.py:31
  74.3 6.8 %copy-start.4 = (f32[96,96]{1,0:T(8,128)S(1)}, f32[96,96]{1,0:T(8,128)}, u32[]{:S(2)}) copy-start(f32[96,96]{1,0:T(8,128)} %select_add_fusion) | copy-start | bytes 110596
  75.7 5.4 %collective-permute-start.7 = (f32[1,8,40,96]{3,2,1,0:T(8,128)S(1)}, f32[1,8,40,96]{3,2,1,0:T(8,128)S(1)}, u32[]{:S(2)}, u32[]{:S(2)}) collective-permute-start(f32[1,8,40,96]{3,2,1,0:T(8,128)S(1)} %fusion.26), channel_id=1, source_target_pairs={{0,4},{4,0},{1,5},{5,1},{2,6},{6,2},{3,7},{7,3},{8,12},{12,8},{9,1... | collective-permute-start | bytes 368648 | tf_op jit(solution)/shard_map/ppermute | solution.py:25
  81.1 2.0 %copy-start.3 = (f32[64,48]{0,1:T(8,128)S(1)}, f32[64,48]{0,1:T(8,128)}, u32[]{:S(2)}) copy-start(f32[64,48]{0,1:T(8,128)} %select_add_fusion.1) | copy-start | bytes 36868
  82.3 1.6 %copy-start.6 = (s32[64]{0:T(128)S(1)}, s32[64]{0:T(128)}, u32[]{:S(2)}) copy-start(s32[64]{0:T(128)} %copy-done.5) | copy-start | bytes 772
  86.6 19.0 %all-to-all-start.1 = ((f32[8,24,1,1152]{3,1,2,0:T(8,128)}), f32[8,24,1,1152]{3,1,2,0:T(8,128)S(1)}, u32[]{:S(2)}, u32[]{:S(2)}) async-start(f32[8,24,1,1152]{3,1,2,0:T(8,128)} %convolution_bitcast_fusion), calls=%async_computation.1 | async-start | bytes 1769472 | tf_op jit(solution)/shard_map/all_to_all | solution.py:127
  106.6 2.5 %slice-start = ((s8[4718592]{0:T(1024)(128)(4,1)}), s8[4194304]{0:T(1024)(128)(4,1)S(1)}, s32[]{:S(2)}) async-start(s8[4718592]{0:T(1024)(128)(4,1)} %bitcast.140), calls=%async_computation.3 | async-start | bytes 8388608
  107.7 1.4 %slice-start.1 = ((s8[4718592]{0:T(1024)(128)(4,1)}), s8[524288]{0:T(1024)(128)(4,1)S(1)}, s32[]{:S(2)}) async-start(s8[4718592]{0:T(1024)(128)(4,1)} %bitcast.140), calls=%async_computation.4 | async-start | bytes 1048576
  118.8 21.0 %all-to-all-start.2 = ((f32[8,24,1,1152]{3,1,2,0:T(8,128)}), f32[8,24,1,1152]{3,1,2,0:T(8,128)S(1)}, u32[]{:S(2)}, u32[]{:S(2)}) async-start(f32[8,24,1,1152]{3,1,2,0:T(8,128)} %bitcast.148), calls=%async_computation.2 | async-start | bytes 1769472 | tf_op jit(solution)/shard_map/all_to_all | solution.py:142
  123.0 1.4 collective-permute-start.8
  125.7 9.3 %collective-permute-start.9 = (f32[1]{0:T(128)}, f32[1]{0:T(128)}, u32[]{:S(2)}, u32[]{:S(2)}) collective-permute-start(f32[1]{0:T(128)} %add.514), channel_id=1, source_target_pairs={{0,2},{1,3},{2,0},{3,1},{4,6},{5,7},{6,4},{7,5},{8,10},{9,11},{10,... | collective-permute-start | bytes 20 | tf_op jit(solution)/shard_map/ppermute | solution.py:45
  135.6 3.6 %collective-permute-start.10 = (f32[1]{0:T(128)}, f32[1]{0:T(128)}, u32[]{:S(2)}, u32[]{:S(2)}) collective-permute-start(f32[1]{0:T(128)} %add.515), channel_id=1, source_target_pairs={{0,4},{4,0},{1,5},{5,1},{2,6},{6,2},{3,7},{7,3},{8,12},{12,8},{9,1... | collective-permute-start | bytes 20 | tf_op jit(solution)/shard_map/ppermute | solution.py:45
